TPU v7x, 512 devices: a whole 4x4x16 slice. The times are simulated.
512 devices in a mesh: tm: 32 (over z, core), band: 4 (over y), fsdp: 4 (over x).
Axes of the slice: x: 4, y: 4, z: 16, core: 2. Of those that a mesh axis runs over, the one named last changes fastest.
Arguments:
- video: bfloat16 [128, 64, 128, 256], P('tm', 'band', 'fsdp'), may hold values from -8 to 8
- clip_lengths: int32 [16], replicated, may hold values from 1 to 31, 128 in all
- norm_gains: float32 [2, 256], replicated, may hold values from 0.1 to 1.9
- spatial_kernel_weight: bfloat16 [256, 2304], P(('band', 'fsdp')), may hold values from -0.125 to 0.125
- w_time: bfloat16 [256, 768], P(('band', 'fsdp')), may hold values from -0.21875 to 0.21875
- w_qkv: bfloat16 [256, 768], P(('band', 'fsdp')), may hold values from -4 to 4
- w_out: bfloat16 [256, 256], P(('band', 'fsdp')), may hold values from -0.375 to 0.375
Outputs:
- mixed: bfloat16 [4, 4, 512, 128, 256], P('band', 'fsdp', 'tm')
Inputs may be any that keep to these rules, and one draw needn't show every extreme that they name: `clip_lengths`: every clip has at least one frame and the lengths sum to 128.
All inputs are finite; a program needn't handle non-finite values.
Results may differ from a plain program's by a relative error of at most 0.0064.
Values may be sent and summed in bfloat16 or wider, within the bound.
No kernel may reach another device: no remote copies, remote signals or barrier semaphores. Data moves between devices by JAX's collectives and lax.ppermute only.
A program may use at most 64 MiB of HBM per device.

v0:
```python
import math

import jax
import jax.numpy as jnp
from jax import lax
from jax.sharding import PartitionSpec as P

GROUPS = 32


EPS = 1e-06


def with_halo(x, sides, width):
    for axis, dim in sides:
        size, length = (lax.axis_size(axis), x.shape[dim])
        up = [(i, (i + 1) % size) for i in range(size - 1)]
        down = [(j, i) for i, j in up]
        last = lax.slice_in_dim(x, length - width, length, axis=dim)
        initial = lax.slice_in_dim(x, 0, width, axis=dim)
        before = lax.ppermute(last, axis, up)
        after = lax.ppermute(initial, axis, down)
        x = jnp.concatenate([before, x, after], axis=dim)
    return x


def from_behind(x, axis, by):
    length = lax.axis_size(axis)
    pairs = [(i, i + by) for i in range(length) if 0 <= i + by < length]
    return lax.ppermute(x, axis, pairs)


def frame_starts(clip_lengths, total):
    ends = jnp.cumsum(clip_lengths)
    begins = ends - clip_lengths
    index = jnp.arange(total, dtype=jnp.int32)
    chosen = jnp.where(begins[None, :] <= index[:, None], begins[None, :], 0)
    return jnp.max(chosen, axis=1)


def group_moments(field):
    frames, height, width, chans = field.shape
    group_width = chans // GROUPS
    vals = field.astype(jnp.float32).reshape(frames, height * width, GROUPS, group_width)
    sums = jnp.sum(vals, axis=(1, 3))
    squares = jnp.sum(vals * vals, axis=(1, 3))
    sums, squares = lax.psum((sums, squares), ("band", "fsdp"))
    count = height * width * group_width * lax.axis_size("band") * lax.axis_size("fsdp")
    mean = sums / count
    scale = lax.rsqrt(squares / count - mean * mean + EPS)
    return (mean, scale)


def apply_norm(field, mean, scale, gain):
    shape = field.shape
    chans = shape[-1]
    group_width = chans // GROUPS
    vals = field.astype(jnp.float32).reshape(shape[0], -1, GROUPS, group_width)
    normed = (vals - mean[:, None, :, None]) * scale[:, None, :, None]
    return normed.reshape(shape) * gain


def body(video, clip_lengths, norm_gains, spatial_kernel_weight, w_time, w_qkv, w_out):
    space_full, time_full, qkv_full, output_complete = (
        lax.all_gather(spatial_kernel_weight, ("band", "fsdp"), axis=0, tiled=True),
        lax.all_gather(w_time, ("band", "fsdp"), axis=0, tiled=True),
        lax.all_gather(w_qkv, ("band", "fsdp"), axis=0, tiled=True),
        lax.all_gather(w_out, ("band", "fsdp"), axis=0, tiled=True),
    )
    frames, height, width, chans = video.shape
    ranks = lax.axis_size("tm")
    total_frames = frames * ranks
    first = lax.axis_index("tm") * frames
    starts = frame_starts(clip_lengths, total_frames)
    local_starts = lax.dynamic_slice_in_dim(starts, first, frames)
    mean_one, scale_one = group_moments(video)
    act = jax.nn.silu(apply_norm(video, mean_one, scale_one, norm_gains[0])).astype(jnp.bfloat16)
    padded = with_halo(act, (("band", 1), ("fsdp", 2)), 1)
    spatial = jnp.zeros((frames, height, width, chans), jnp.float32)
    for tap in range(9):
        shift_y = tap // 3
        shift_x = tap % 3
        spatial = spatial + jnp.einsum(
            "fhwc,cd->fhwd",
            padded[:, shift_y : shift_y + height, shift_x : shift_x + width],
            space_full[:, tap * chans : (tap + 1) * chans],
            preferred_element_type=jnp.float32,
        )
    spatial = spatial.astype(jnp.bfloat16)
    carried = from_behind(spatial[frames - 2 :], "tm", 1)
    extended = jnp.concatenate([carried, spatial], axis=0)
    position = first + jnp.arange(frames, dtype=jnp.int32)
    slots = jnp.arange(frames + 2, dtype=jnp.int32)
    temporal = jnp.zeros((frames, height, width, chans), jnp.float32)
    for tap in range(3):
        source = jnp.maximum(position - 2 + tap, local_starts) - first + 2
        select = (source[:, None] == slots[None, :]).astype(jnp.bfloat16)
        picked = jnp.einsum(
            "fe,ehwc->fhwc", select, extended, preferred_element_type=jnp.float32
        ).astype(jnp.bfloat16)
        temporal = temporal + jnp.einsum(
            "fhwc,cd->fhwd",
            picked,
            time_full[:, tap * chans : (tap + 1) * chans],
            preferred_element_type=jnp.float32,
        )
    resid = (video.astype(jnp.float32) + temporal).astype(jnp.bfloat16)
    mean_two, scale_two = group_moments(resid)
    pixels = height * width
    flat_resid = resid.reshape(frames, pixels, chans)
    flat_norm = (
        apply_norm(resid, mean_two, scale_two, norm_gains[1])
        .astype(jnp.bfloat16)
        .reshape(frames, pixels, chans)
    )
    qkv = jnp.einsum("fpc,cd->fpd", flat_norm, qkv_full, preferred_element_type=jnp.float32).astype(
        jnp.bfloat16
    )
    qkv_time, resid_time = (
        lax.all_to_all(qkv, "tm", split_axis=1, concat_axis=0, tiled=True),
        lax.all_to_all(flat_resid, "tm", split_axis=1, concat_axis=0, tiled=True),
    )
    query = qkv_time[..., :chans]
    keys = qkv_time[..., chans : 2 * chans]
    value_rows = qkv_time[..., 2 * chans :]
    index = jnp.arange(total_frames, dtype=jnp.int32)
    allowed = (index[None, :] <= index[:, None]) & (index[None, :] >= starts[:, None])
    scores = jnp.einsum(
        "fpc,gpc->pfg", query, keys, preferred_element_type=jnp.float32
    ) / math.sqrt(chans)
    scores = jnp.where(allowed[None], scores, -1e30)
    top = jnp.max(scores, axis=-1, keepdims=True)
    expo = jnp.where(allowed[None], jnp.exp(scores - top), 0.0)
    attention_probabilities = (expo / jnp.sum(expo, axis=-1, keepdims=True)).astype(jnp.bfloat16)
    attention_output = jnp.einsum(
        "boh,hba->boa", attention_probabilities, value_rows, preferred_element_type=jnp.float32
    ).astype(jnp.bfloat16)
    projected_output = jnp.einsum(
        "axi,iy->axy", attention_output, output_complete, preferred_element_type=jnp.float32
    )
    mixed = (jnp.swapaxes(resid_time, 0, 1).astype(jnp.float32) + projected_output).astype(
        jnp.bfloat16
    )
    return mixed.reshape(1, 1, mixed.shape[0], total_frames, chans)


def solution(mesh):
    return jax.shard_map(
        body,
        mesh=mesh,
        in_specs=(
            P("tm", "band", "fsdp", None),
            P(),
            P(),
            P(("band", "fsdp"), None),
            P(("band", "fsdp"), None),
            P(("band", "fsdp"), None),
            P(("band", "fsdp"), None),
        ),
        out_specs=P("band", "fsdp", "tm", None, None),
        check_vma=False,
    )
```

profile of v0, /device:TPU:1, one launch (start us, length us, event | category | flops | bytes accessed | tf_op | source)
XLA Modules:
  0.0 365.6 jit_solution(13306108738331257121)
XLA Ops:
  6.5 0.7 all-gather.2.cloned.1.call-update
  7.3 1.5 convert_reduce_fusion
  9.2 34.3 %all-reduce.1 = (f32[4,32]{1,0:T(4,128)S(1)}, f32[4,32]{1,0:T(4,128)S(1)}) all-reduce(f32[4,32]{1,0:T(4,128)S(1)} %reduce_sum.62, f32[4,32]{1,0:T(4,128)S(1)} %reduce_sum.59), channel_id=1, replica_groups=mesh['tm'=32,'band'=4,'fsdp'=4] {'band','fsdp'}, use_global_device_ids=true, to_apply=%region_7.8 | all-reduce | flops 256 | bytes 2048 | tf_op jit(solution)/shard_map/psum | solution.py:47
  43.8 0.8 fusion.85
  44.6 0.7 fusion.18
  45.3 1.3 collective-permute-start
  46.6 1.3 collective-permute-start.1
  47.9 3.7 %collective-permute-done.1 = bf16[4,1,32,256]{3,2,1,0:T(8,128)(2,1)S(1)} collective-permute-done((bf16[4,1,32,256]{3,2,1,0:T(8,128)(2,1)S(1)}, bf16[4,1,32,256]{3,2,1,0:T(8,128)(2,1)S(1)}, u32[]{:S(2)}, u32[]{:S(2)}) %collective-permute-start.1) | collective-permute-done | bytes 65568 | tf_op jit(solution)/shard_map/ppermute | solution.py:22
  51.7 1.3 collective-permute-start.2
  53.0 1.3 collective-permute-start.3
  54.4 3.7 %collective-permute-done.3 = bf16[4,18,1,256]{3,2,1,0:T(2,128)(2,1)S(1)} collective-permute-done((bf16[4,18,1,256]{3,2,1,0:T(2,128)(2,1)S(1)}, bf16[4,18,1,256]{3,2,1,0:T(2,128)(2,1)S(1)}, u32[]{:S(2)}, u32[]{:S(2)}) %collective-permute-start.3) | collective-permute-done | bytes 36896 | tf_op jit(solution)/shard_map/ppermute | solution.py:22
  58.1 1.8 pad_maximum_fusion.1
  59.9 12.3 %all-gather.2.cloned.1.call-done = bf16[256,2304]{1,0:T(8,128)(2,1)} async-done(((bf16[16,2304]{1,0:T(8,128)(2,1)}), bf16[256,2304]{1,0:T(8,128)(2,1)}) %all-gather.2.cloned.1.call-update) | async-done | bytes 1179664 | tf_op jit(solution)/shard_map/all_gather | solution.py:65
  72.1 1.5 fusion.54
  73.6 0.5 fusion.58
  74.1 0.9 copy-done
  75.0 0.4 fusion.56
  75.4 0.4 fusion.60
  75.8 0.4 fusion.52
  76.3 0.4 fusion.36
  76.7 0.4 fusion.40
  77.2 0.4 fusion.70
  77.6 1.1 add_convert_fusion
  78.8 5.3 %collective-permute-start.4 = (bf16[2,16,32,256]{3,2,1,0:T(8,128)(2,1)S(1)}, bf16[2,16,32,256]{3,2,1,0:T(8,128)(2,1)S(1)}, u32[]{:S(2)}, u32[]{:S(2)}) collective-permute-start(bf16[2,16,32,256]{3,2,1,0:T(8,128)(2,1)S(1)} %slice.145), channel_id=1, source_target_pairs={{0,16},{16,32},{32,48},{48,64},{64,80},{80,96},{96,112},{112,128},... | collective-permute-start | bytes 1572872 | tf_op jit(solution)/shard_map/ppermute | solution.py:30
  84.4 18.0 %all_gather.13 = bf16[256,768]{1,0:T(8,128)(2,1)S(1)} all-gather(bf16[16,768]{1,0:T(8,128)(2,1)S(1)} %copy-done.4), channel_id=1, replica_groups=mesh['tm'=32,'band'=4,'fsdp'=4] {'band','fsdp'}, dimensions={0}, use_global_device_ids=true | all-gather | bytes 417792 | tf_op jit(solution)/shard_map/all_gather | solution.py:66
  102.6 0.1 pad_maximum_fusion
  102.7 1.2 fusion.25
  103.9 1.2 fusion.22
  105.1 0.4 fusion.63
  105.6 0.4 fusion.65
  106.0 1.2 fusion.28
  107.2 0.8 convert_reduce_fusion.1
  108.1 1.8 copy.33
  109.8 16.8 %all-to-all-start = ((bf16[4,512,256]{2,0,1:T(4,128)(2,1)}), bf16[4,512,256]{2,0,1:T(4,128)(2,1)}, u32[]{:S(2)}, u32[]{:S(2)}) async-start(bf16[4,512,256]{2,0,1:T(4,128)(2,1)} %copy.33), calls=%async_computation | async-start | bytes 2097152 | tf_op jit(solution)/shard_map/all_to_all | solution.py:121
  126.7 18.6 %all_gather.14 = bf16[256,768]{1,0:T(8,128)(2,1)S(1)} all-gather(bf16[16,768]{1,0:T(8,128)(2,1)S(1)} %copy-done.5), channel_id=1, replica_groups=mesh['tm'=32,'band'=4,'fsdp'=4] {'band','fsdp'}, dimensions={0}, use_global_device_ids=true | all-gather | bytes 417792 | tf_op jit(solution)/shard_map/all_gather | solution.py:67
  145.7 32.7 %all-reduce = (f32[4,32]{1,0:T(4,128)S(1)}, f32[4,32]{1,0:T(4,128)S(1)}) all-reduce(f32[4,32]{1,0:T(4,128)S(1)} %reduce_sum.84, f32[4,32]{1,0:T(4,128)S(1)} %reduce_sum.81), channel_id=1, replica_groups=mesh['tm'=32,'band'=4,'fsdp'=4] {'band','fsdp'}, use_global_device_ids=true, to_apply=%region_13.14 | all-reduce | flops 256 | bytes 2048 | tf_op jit(solution)/shard_map/psum | solution.py:47
  178.8 0.3 fusion.9
  179.1 1.0 convolution_convert_fusion
  180.1 4.1 %copy.35 = bf16[4,512,768]{2,0,1:T(4,128)(2,1)} copy(bf16[4,512,768]{2,1,0:T(8,128)(2,1)S(1)} %convolution_convert_fusion) | data formatting | bytes 6291456 | tf_op jit(solution)/shard_map/convert_element_type | solution.py:116
  184.2 20.8 %all-to-all-start.1 = ((bf16[4,512,768]{2,0,1:T(4,128)(2,1)}), bf16[4,512,768]{2,0,1:T(4,128)(2,1)S(1)}, u32[]{:S(2)}, u32[]{:S(2)}) async-start(bf16[4,512,768]{2,0,1:T(4,128)(2,1)} %copy.35), calls=%async_computation.1 | async-start | bytes 6291456 | tf_op jit(solution)/shard_map/all_to_all | solution.py:120
  205.1 16.8 %all_gather.15 = bf16[256,256]{1,0:T(8,128)(2,1)S(1)} all-gather(bf16[16,256]{1,0:T(8,128)(2,1)S(1)} %copy-done.6), channel_id=1, replica_groups=mesh['tm'=32,'band'=4,'fsdp'=4] {'band','fsdp'}, dimensions={0}, use_global_device_ids=true | all-gather | bytes 139264 | tf_op jit(solution)/shard_map/all_gather | solution.py:68
  221.9 3.2 copy_bitcast_fusion.1
  225.0 3.0 reshape.101
  228.0 117.9 %all-to-all-done.1 = bf16[4,512,768]{2,0,1:T(4,128)(2,1)S(1)} async-done(((bf16[4,512,768]{2,0,1:T(4,128)(2,1)}), bf16[4,512,768]{2,0,1:T(4,128)(2,1)S(1)}, u32[]{:S(2)}, u32[]{:S(2)}) %all-to-all-start.1) | async-done | bytes 3145760 | tf_op jit(solution)/shard_map/all_to_all | solution.py:120
  345.9 3.2 copy.76
  349.1 4.5 %all_to_all.24 = bf16[128,16,768]{2,0,1:T(8,128)(2,1)S(1)} reshape(bf16[32,4,16,768]{3,1,0,2:T(4,128)(2,1)} %bitcast.111) | data formatting | bytes 6291456 | tf_op jit(solution)/shard_map/all_to_all | solution.py:120
  353.6 1.5 fusion.86
  355.1 3.7 %fusion.34 = bf16[1,1,16,128,256]{4,3,2,1,0:T(8,128)(2,1)} fusion(f32[128,16,256]{2,0,1:T(8,128)} %reshape.101, bf16[128,16,768]{2,0,1:T(8,128)(2,1)S(1)} %all_to_all.24, f32[16,128,128]{1,2,0:T(8,128)} %get-tuple-element.30, f32[16,128]{1,0:T(8,128)S(1)} %get-tuple-element.29, bf16[256,256]{1,0:T(8,128)(2,1)S(1)} %all_gather.15), kind=kOutput, calls=%fused_computation.44 | convolution fusion | flops 404750336 | bytes 5382144 | tf_op jit(solution)/shard_map/axi,iy->axy/dot_general | solution.py:138
  (48 shorter events, 2.2 us)
Async XLA Ops:
  6.5 38.0 %copy-start.1 = (bf16[4,16,32,256]{3,2,1,0:T(8,128)(2,1)S(1)}, bf16[4,16,32,256]{3,2,1,0:T(8,128)(2,1)}, u32[]{:S(2)}) copy-start(bf16[4,16,32,256]{3,2,1,0:T(8,128)(2,1)} %param.7) | copy-start | bytes 3145732
  6.5 65.6 %all-gather.2.cloned.1.call-start = ((), (), s32[]{:S(2)}) async-start(), calls=%async_computation.2 | async-start | bytes 1253376 | tf_op jit(solution)/shard_map/all_gather | solution.py:65
  45.3 2.6 collective-permute-start
  46.6 5.0 %collective-permute-start.1 = (bf16[4,1,32,256]{3,2,1,0:T(8,128)(2,1)S(1)}, bf16[4,1,32,256]{3,2,1,0:T(8,128)(2,1)S(1)}, u32[]{:S(2)}, u32[]{:S(2)}) collective-permute-start(bf16[4,1,32,256]{3,2,1,0:T(8,128)(2,1)S(1)} %get-tuple-element.18), channel_id=1, source_target_pairs={{4,0},{8,4},{12,8},{5,1},{9,5},{13,9},{6,2},{10,6},{14,10},{7,3},{... | collective-permute-start | bytes 196616 | tf_op jit(solution)/shard_map/ppermute | solution.py:22
  51.7 2.7 collective-permute-start.2
  53.0 5.1 %collective-permute-start.3 = (bf16[4,18,1,256]{3,2,1,0:T(2,128)(2,1)S(1)}, bf16[4,18,1,256]{3,2,1,0:T(2,128)(2,1)S(1)}, u32[]{:S(2)}, u32[]{:S(2)}) collective-permute-start(bf16[4,18,1,256]{3,2,1,0:T(2,128)(2,1)S(1)} %get-tuple-element.15), channel_id=1, source_target_pairs={{1,0},{2,1},{3,2},{5,4},{6,5},{7,6},{9,8},{10,9},{11,10},{13,12},{... | collective-permute-start | bytes 110600 | tf_op jit(solution)/shard_map/ppermute | solution.py:22
  72.1 1.5 copy-start.3
  73.6 1.4 copy-start
  77.6 6.5 %copy-start.7 = (s32[16]{0:T(128)S(1)}, s32[16]{0:T(128)}, u32[]{:S(2)}) copy-start(s32[16]{0:T(128)} %param.8) | copy-start | bytes 196
  77.6 6.8 %copy-start.4 = (bf16[16,768]{1,0:T(8,128)(2,1)S(1)}, bf16[16,768]{1,0:T(8,128)(2,1)}, u32[]{:S(2)}) copy-start(bf16[16,768]{1,0:T(8,128)(2,1)} %param.11) | copy-start | bytes 73732
  78.8 23.8 %collective-permute-start.4 = (bf16[2,16,32,256]{3,2,1,0:T(8,128)(2,1)S(1)}, bf16[2,16,32,256]{3,2,1,0:T(8,128)(2,1)S(1)}, u32[]{:S(2)}, u32[]{:S(2)}) collective-permute-start(bf16[2,16,32,256]{3,2,1,0:T(8,128)(2,1)S(1)} %slice.145), channel_id=1, source_target_pairs={{0,16},{16,32},{32,48},{48,64},{64,80},{80,96},{96,112},{112,128},... | collective-permute-start | bytes 1572872 | tf_op jit(solution)/shard_map/ppermute | solution.py:30
  106.0 1.2 copy-start.2
  108.0 18.6 %copy-start.5 = (bf16[16,768]{1,0:T(8,128)(2,1)S(1)}, bf16[16,768]{1,0:T(8,128)(2,1)}, u32[]{:S(2)}) copy-start(bf16[16,768]{1,0:T(8,128)(2,1)} %param.12) | copy-start | bytes 73732
  109.8 74.4 %all-to-all-start = ((bf16[4,512,256]{2,0,1:T(4,128)(2,1)}), bf16[4,512,256]{2,0,1:T(4,128)(2,1)}, u32[]{:S(2)}, u32[]{:S(2)}) async-start(bf16[4,512,256]{2,0,1:T(4,128)(2,1)} %copy.33), calls=%async_computation | async-start | bytes 2097152 | tf_op jit(solution)/shard_map/all_to_all | solution.py:121
  184.2 20.8 %copy-start.6 = (bf16[16,256]{1,0:T(8,128)(2,1)S(1)}, bf16[16,256]{1,0:T(8,128)(2,1)}, u32[]{:S(2)}) copy-start(bf16[16,256]{1,0:T(8,128)(2,1)} %param.13) | copy-start | bytes 24580
  184.2 161.7 %all-to-all-start.1 = ((bf16[4,512,768]{2,0,1:T(4,128)(2,1)}), bf16[4,512,768]{2,0,1:T(4,128)(2,1)S(1)}, u32[]{:S(2)}, u32[]{:S(2)}) async-start(bf16[4,512,768]{2,0,1:T(4,128)(2,1)} %copy.35), calls=%async_computation.1 | async-start | bytes 6291456 | tf_op jit(solution)/shard_map/all_to_all | solution.py:120
Sparse Core Ops, SparseCore 0:
  10.3 61.7 all-gather.1
where the time goes:
time: 369 us; the launch traced here: 366 us
  waiting for transfers between devices  138 us (37%)
  blocking collectives  120 us (33%)
  starting transfers between devices  48.1 us (13%)
  local copies, waits for them, and re-layouts  19.5 us (5%)
  matrix products  17.1 us (5%)
  between operations  13.7 us (4%)
  other arithmetic  8.43 us (2%)
    all_to_all x1, waiting for transfers between devices, body(): lax.all_to_all(qkv, 'tm', split_axis=1, concat_axis=0, tiled=True)  118 us
    psum x2, blocking collectives, group_moments(): sums, squares = lax.psum((sums, squares), ('band', 'fsdp'))  67 us
    all_to_all x1, starting transfers between devices, body(): lax.all_to_all(qkv, 'tm', split_axis=1, concat_axis=0, tiled=True)  20.8 us
    all_gather x1, blocking collectives, body(): lax.all_gather(w_qkv, ('band', 'fsdp'), axis=0, tiled=True)  18.6 us
    all_gather x1, blocking collectives, body(): lax.all_gather(w_time, ('band', 'fsdp'), axis=0, tiled=True)  18 us
    all_to_all x1, starting transfers between devices, body(): lax.all_to_all(flat_resid, 'tm', split_axis=1, concat_axis=0, tiled=True)  16.8 us
    all_gather x1, blocking collectives, body(): lax.all_gather(w_out, ('band', 'fsdp'), axis=0, tiled=True)  16.8 us
    all_gather x1, waiting for transfers between devices, body(): lax.all_gather(spatial_kernel_weight, ('band', 'fsdp'), axis=0, tiled=True)  12.3 us
  transfers between devices with their start and end apart: 8, of which 5 were waited for; matrix products, arithmetic and copies ran while one was open for 5% of the time, Pallas kernels for 0%

commit v1 on v0

--- a/solution.py
+++ b/solution.py
@@ -30,6 +30,17 @@
     return lax.ppermute(x, axis, pairs)
 
 
+def butterfly_sum(x, axes):
+    for axis in axes:
+        size = lax.axis_size(axis)
+        step = 1
+        while step < size:
+            pairs = [(i, i ^ step) for i in range(size)]
+            x = x + lax.ppermute(x, axis, pairs)
+            step *= 2
+    return x
+
+
 def frame_starts(clip_lengths, total):
     ends = jnp.cumsum(clip_lengths)
     begins = ends - clip_lengths
@@ -44,7 +55,8 @@
     vals = field.astype(jnp.float32).reshape(frames, height * width, GROUPS, group_width)
     sums = jnp.sum(vals, axis=(1, 3))
     squares = jnp.sum(vals * vals, axis=(1, 3))
-    sums, squares = lax.psum((sums, squares), ("band", "fsdp"))
+    both = butterfly_sum(jnp.stack([sums, squares]), ("band", "fsdp"))
+    sums, squares = both[0], both[1]
     count = height * width * group_width * lax.axis_size("band") * lax.axis_size("fsdp")
     mean = sums / count
     scale = lax.rsqrt(squares / count - mean * mean + EPS)
@@ -60,14 +72,28 @@
     return normed.reshape(shape) * gain
 
 
+def split3(x):
+    hi = lax.reduce_precision(x, exponent_bits=8, mantissa_bits=7)
+    rest = x - hi
+    mid = lax.reduce_precision(rest, exponent_bits=8, mantissa_bits=7)
+    lo = rest - mid
+    return jnp.stack([hi, mid, lo]).astype(jnp.bfloat16)
+
+
+def join3(pieces):
+    pieces = pieces.astype(jnp.float32)
+    return (pieces[0] + pieces[1]) + pieces[2]
+
+
 def body(video, clip_lengths, norm_gains, spatial_kernel_weight, w_time, w_qkv, w_out):
-    space_full, time_full, qkv_full, output_complete = (
-        lax.all_gather(spatial_kernel_weight, ("band", "fsdp"), axis=0, tiled=True),
-        lax.all_gather(w_time, ("band", "fsdp"), axis=0, tiled=True),
-        lax.all_gather(w_qkv, ("band", "fsdp"), axis=0, tiled=True),
-        lax.all_gather(w_out, ("band", "fsdp"), axis=0, tiled=True),
-    )
     frames, height, width, chans = video.shape
+    widths = [w.shape[1] for w in (spatial_kernel_weight, w_time, w_qkv, w_out)]
+    packed = jnp.concatenate([spatial_kernel_weight, w_time, w_qkv, w_out], axis=1)
+    gathered = lax.all_gather(packed, ("band", "fsdp"), axis=0, tiled=True)
+    offsets = [sum(widths[:i]) for i in range(4)]
+    space_full, time_full, qkv_full, output_complete = [
+        gathered[:, o : o + w] for o, w in zip(offsets, widths)
+    ]
     ranks = lax.axis_size("tm")
     total_frames = frames * ranks
     first = lax.axis_index("tm") * frames
@@ -107,19 +133,22 @@
     resid = (video.astype(jnp.float32) + temporal).astype(jnp.bfloat16)
     mean_two, scale_two = group_moments(resid)
     pixels = height * width
-    flat_resid = resid.reshape(frames, pixels, chans)
-    flat_norm = (
-        apply_norm(resid, mean_two, scale_two, norm_gains[1])
-        .astype(jnp.bfloat16)
-        .reshape(frames, pixels, chans)
-    )
-    qkv = jnp.einsum("fpc,cd->fpd", flat_norm, qkv_full, preferred_element_type=jnp.float32).astype(
-        jnp.bfloat16
-    )
-    qkv_time, resid_time = (
-        lax.all_to_all(qkv, "tm", split_axis=1, concat_axis=0, tiled=True),
-        lax.all_to_all(flat_resid, "tm", split_axis=1, concat_axis=0, tiled=True),
-    )
+    group_pixels = pixels // ranks
+    flat_resid = resid.reshape(frames, ranks, group_pixels, chans).transpose(1, 0, 2, 3)
+    stats = split3(jnp.concatenate([mean_two, scale_two], axis=1))
+    stats = stats.transpose(1, 0, 2).reshape(frames, 3 * 2 * GROUPS)
+    stats = jnp.pad(stats, ((0, 0), (0, chans - stats.shape[1])))
+    stats_rows = jnp.broadcast_to(stats[None, :, None, :], (ranks, frames, 1, chans))
+    payload = jnp.concatenate([flat_resid, stats_rows], axis=2)
+    received = lax.all_to_all(payload, "tm", split_axis=0, concat_axis=0, tiled=True)
+    resid_time = received[:, :, :group_pixels, :].reshape(total_frames, group_pixels, chans)
+    got = received[:, :, group_pixels, : 3 * 2 * GROUPS].reshape(total_frames, 3, 2 * GROUPS)
+    moments = join3(got.transpose(1, 0, 2))
+    mean_all, scale_all = moments[:, :GROUPS], moments[:, GROUPS:]
+    flat_norm = apply_norm(resid_time, mean_all, scale_all, norm_gains[1]).astype(jnp.bfloat16)
+    qkv_time = jnp.einsum(
+        "fpc,cd->fpd", flat_norm, qkv_full, preferred_element_type=jnp.float32
+    ).astype(jnp.bfloat16)
     query = qkv_time[..., :chans]
     keys = qkv_time[..., chans : 2 * chans]
     value_rows = qkv_time[..., 2 * chans :]

time: 369 us -> 222 us (0.60)
  blocking collectives: 120 us -> 0 us
  waiting for transfers between devices: 138 us -> 105 us
  starting transfers between devices: 48.1 us -> 63.9 us
  local copies, waits for them, and re-layouts: 19.5 us -> 4.97 us
  matrix products: 17.1 us -> 24.5 us
    psum x2 -> x0, blocking collectives: 67 us -> none  [group_moments(): sums, squares = lax.psum((sums, squares), ('band', 'fsdp'))]
    all_to_all x2 -> x1, waiting for transfers between devices: 118 us -> 58.5 us  [body(): lax.all_to_all(payload, 'tm', split_axis=0, concat_axis=0, tiled=True)]
    all_gather x3 -> x0, blocking collectives: 53.4 us -> none  [the longest x1 18.6 us: body(): lax.all_gather(w_qkv, ('band', 'fsdp'), axis=0, tiled=True)]
    ppermute x0 -> x8, starting transfers between devices: none -> 30.1 us  [butterfly_sum(): x = x + lax.ppermute(x, axis, pairs)]
    all_to_all x2 -> x1, starting transfers between devices: 37.6 us -> 19.5 us  [body(): lax.all_to_all(payload, 'tm', split_axis=0, concat_axis=0, tiled=True)]
    all_gather x1, waiting for transfers between devices: 12.3 us -> 23.3 us  [body(): gathered = lax.all_gather(packed, ('band', 'fsdp'), axis=0, tiled=True)]
    ppermute x0 -> x8, waiting for transfers between devices: none -> 9.79 us  [butterfly_sum(): x = x + lax.ppermute(x, axis, pairs)]
    all_to_all x2 -> x0, local copies, waits for them, and re-layouts: 7.7 us -> none  [body(): lax.all_to_all(qkv, 'tm', split_axis=1, concat_axis=0, tiled=True)]
  transfers between devices with their start and end apart: 8 -> 15, of which waited for: 5 -> 14; matrix products, arithmetic and copies ran while one was open for 5% -> 3% of each run, Pallas kernels for 0% -> 0%
where the time goes in v1:
time: 222 us; the launch traced here: 221 us
  waiting for transfers between devices  105 us (47%)
  starting transfers between devices  63.9 us (29%)
  matrix products  24.5 us (11%)
  between operations  13.8 us (6%)
  other arithmetic  8.96 us (4%)
  local copies, waits for them, and re-layouts  4.97 us (2%)
    all_to_all x1, waiting for transfers between devices, body(): lax.all_to_all(payload, 'tm', split_axis=0, concat_axis=0, tiled=True)  58.5 us
    ppermute x8, starting transfers between devices, butterfly_sum(): x = x + lax.ppermute(x, axis, pairs)  30.1 us
    all_gather x1, waiting for transfers between devices, body(): gathered = lax.all_gather(packed, ('band', 'fsdp'), axis=0, tiled=True)  23.3 us
    all_to_all x1, starting transfers between devices, body(): lax.all_to_all(payload, 'tm', split_axis=0, concat_axis=0, tiled=True)  19.5 us
    ppermute x8, waiting for transfers between devices, butterfly_sum(): x = x + lax.ppermute(x, axis, pairs)  9.79 us
    ppermute x2, waiting for transfers between devices, with_halo(): after = lax.ppermute(initial, axis, down)  7.84 us
    ppermute x2, starting transfers between devices, with_halo(): before = lax.ppermute(last, axis, up)  6.45 us
    dot_general x9, matrix products, body(): jnp.einsum('fhwc,cd->fhwd', padded[:, shift_y:shift_y + height, shift_x:s...  5.7 us
  transfers between devices with their start and end apart: 15, of which 14 were waited for; matrix products, arithmetic and copies ran while one was open for 3% of the time, Pallas kernels for 0%

profile of v1, /device:TPU:1, one launch (start us, length us, event | category | flops | bytes accessed | tf_op | source)
XLA Modules:
  0.0 221.3 jit_solution(12626729914974555118)
XLA Ops:
  6.5 1.7 pad_maximum_fusion.3
  8.3 1.5 convert_reduce_fusion
  10.2 4.0 %collective-permute-start = (f32[2,4,32]{2,1,0:T(4,128)S(1)}, f32[2,4,32]{2,1,0:T(4,128)S(1)}, u32[]{:S(2)}, u32[]{:S(2)}) collective-permute-start(f32[2,4,32]{2,1,0:T(4,128)S(1)} %pad_maximum_fusion.7), channel_id=1, source_target_pairs={{0,4},{4,0},{8,12},{12,8},{1,5},{5,1},{9,13},{13,9},{2,6},{6,2},{1... | collective-permute-start | bytes 3080 | tf_op jit(solution)/shard_map/ppermute | solution.py:39
  14.2 1.0 collective-permute-done
  15.2 5.0 %collective-permute-start.1 = (f32[2,4,32]{2,1,0:T(4,128)S(1)}, f32[2,4,32]{2,1,0:T(4,128)S(1)}, u32[]{:S(2)}, u32[]{:S(2)}) collective-permute-start(f32[2,4,32]{2,1,0:T(4,128)S(1)} %fusion.92), channel_id=1, source_target_pairs={{0,8},{4,12},{8,0},{12,4},{1,9},{5,13},{9,1},{13,5},{2,10},{6,14},... | collective-permute-start | bytes 3080 | tf_op jit(solution)/shard_map/ppermute | solution.py:39
  20.2 1.0 collective-permute-done.1
  21.2 3.2 %collective-permute-start.2 = (f32[2,4,32]{2,1,0:T(4,128)S(1)}, f32[2,4,32]{2,1,0:T(4,128)S(1)}, u32[]{:S(2)}, u32[]{:S(2)}) collective-permute-start(f32[2,4,32]{2,1,0:T(4,128)S(1)} %fusion.103), channel_id=1, source_target_pairs={{0,1},{1,0},{2,3},{3,2},{4,5},{5,4},{6,7},{7,6},{8,9},{9,8},{10,11... | collective-permute-start | bytes 3080 | tf_op jit(solution)/shard_map/ppermute | solution.py:39
  24.3 1.2 collective-permute-done.2
  25.5 4.7 %collective-permute-start.3 = (f32[2,4,32]{2,1,0:T(4,128)S(1)}, f32[2,4,32]{2,1,0:T(4,128)S(1)}, u32[]{:S(2)}, u32[]{:S(2)}) collective-permute-start(f32[2,4,32]{2,1,0:T(4,128)S(1)} %add.122), channel_id=1, source_target_pairs={{0,2},{1,3},{2,0},{3,1},{4,6},{5,7},{6,4},{7,5},{8,10},{9,11},{10,... | collective-permute-start | bytes 3080 | tf_op jit(solution)/shard_map/ppermute | solution.py:39
  30.2 0.8 fusion.95
  31.8 0.7 fusion.16
  32.4 3.2 %collective-permute-start.4 = (bf16[4,1,32,256]{3,2,1,0:T(8,128)(2,1)S(1)}, bf16[4,1,32,256]{3,2,1,0:T(8,128)(2,1)S(1)}, u32[]{:S(2)}, u32[]{:S(2)}) collective-permute-start(bf16[4,1,32,256]{3,2,1,0:T(8,128)(2,1)S(1)} %get-tuple-element.13), channel_id=1, source_target_pairs={{0,4},{4,8},{8,12},{1,5},{5,9},{9,13},{2,6},{6,10},{10,14},{3,7},{... | collective-permute-start | bytes 196616 | tf_op jit(solution)/shard_map/ppermute | solution.py:21
  35.7 1.3 collective-permute-start.5
  37.0 4.1 %collective-permute-done.5 = bf16[4,1,32,256]{3,2,1,0:T(8,128)(2,1)S(1)} collective-permute-done((bf16[4,1,32,256]{3,2,1,0:T(8,128)(2,1)S(1)}, bf16[4,1,32,256]{3,2,1,0:T(8,128)(2,1)S(1)}, u32[]{:S(2)}, u32[]{:S(2)}) %collective-permute-start.5) | collective-permute-done | bytes 65568 | tf_op jit(solution)/shard_map/ppermute | solution.py:22
  41.3 3.2 %collective-permute-start.6 = (bf16[4,18,1,256]{3,2,1,0:T(2,128)(2,1)S(1)}, bf16[4,18,1,256]{3,2,1,0:T(2,128)(2,1)S(1)}, u32[]{:S(2)}, u32[]{:S(2)}) collective-permute-start(bf16[4,18,1,256]{3,2,1,0:T(2,128)(2,1)S(1)} %get-tuple-element.12), channel_id=1, source_target_pairs={{0,1},{1,2},{2,3},{4,5},{5,6},{6,7},{8,9},{9,10},{10,11},{12,13},{... | collective-permute-start | bytes 110600 | tf_op jit(solution)/shard_map/ppermute | solution.py:21
  44.5 1.3 collective-permute-start.7
  45.9 3.7 %collective-permute-done.7 = bf16[4,18,1,256]{3,2,1,0:T(2,128)(2,1)S(1)} collective-permute-done((bf16[4,18,1,256]{3,2,1,0:T(2,128)(2,1)S(1)}, bf16[4,18,1,256]{3,2,1,0:T(2,128)(2,1)S(1)}, u32[]{:S(2)}, u32[]{:S(2)}) %collective-permute-start.7) | collective-permute-done | bytes 36896 | tf_op jit(solution)/shard_map/ppermute | solution.py:22
  49.6 1.8 pad_maximum_fusion.1
  51.3 23.3 %all-gather.2.cloned.1.call-done = bf16[256,4096]{1,0:T(8,128)(2,1)} async-done(((bf16[16,4096]{1,0:T(8,128)(2,1)}), bf16[256,4096]{1,0:T(8,128)(2,1)}) %all-gather.2.cloned.1.call-update) | async-done | bytes 2097168 | tf_op jit(solution)/shard_map/all_gather | solution.py:92
  74.7 1.5 fusion.51
  76.3 0.4 fusion.55
  76.8 0.9 copy-done
  78.6 0.4 fusion.49
  80.4 1.1 add_convert_fusion
  81.5 5.3 %collective-permute-start.8 = (bf16[2,16,32,256]{3,2,1,0:T(8,128)(2,1)S(1)}, bf16[2,16,32,256]{3,2,1,0:T(8,128)(2,1)S(1)}, u32[]{:S(2)}, u32[]{:S(2)}) collective-permute-start(bf16[2,16,32,256]{3,2,1,0:T(8,128)(2,1)S(1)} %slice.213), channel_id=1, source_target_pairs={{0,16},{16,32},{32,48},{48,64},{64,80},{80,96},{96,112},{112,128},... | collective-permute-start | bytes 1572872 | tf_op jit(solution)/shard_map/ppermute | solution.py:30
  87.2 5.7 %collective-permute-done.8 = bf16[2,16,32,256]{3,2,1,0:T(8,128)(2,1)S(1)} collective-permute-done((bf16[2,16,32,256]{3,2,1,0:T(8,128)(2,1)S(1)}, bf16[2,16,32,256]{3,2,1,0:T(8,128)(2,1)S(1)}, u32[]{:S(2)}, u32[]{:S(2)}) %collective-permute-start.8) | collective-permute-done | bytes 524320 | tf_op jit(solution)/shard_map/ppermute | solution.py:30
  93.0 1.2 fusion.22
  94.2 1.2 fusion.19
  95.4 1.2 fusion.25
  96.6 1.3 fusion.60
  98.0 1.4 fusion.62
  99.4 1.7 convert_reduce_fusion.1
  101.6 3.0 %collective-permute-start.9 = (f32[2,4,32]{2,1,0:T(4,128)S(1)}, f32[2,4,32]{2,1,0:T(4,128)S(1)}, u32[]{:S(2)}, u32[]{:S(2)}) collective-permute-start(f32[2,4,32]{2,1,0:T(4,128)S(1)} %pad_maximum_fusion.8), channel_id=1, source_target_pairs={{0,4},{4,0},{8,12},{12,8},{1,5},{5,1},{9,13},{13,9},{2,6},{6,2},{1... | collective-permute-start | bytes 3080 | tf_op jit(solution)/shard_map/ppermute | solution.py:39
  104.6 1.4 collective-permute-done.9
  105.9 3.7 %collective-permute-start.10 = (f32[2,4,32]{2,1,0:T(4,128)S(1)}, f32[2,4,32]{2,1,0:T(4,128)S(1)}, u32[]{:S(2)}, u32[]{:S(2)}) collective-permute-start(f32[2,4,32]{2,1,0:T(4,128)S(1)} %fusion.91), channel_id=1, source_target_pairs={{0,8},{4,12},{8,0},{12,4},{1,9},{5,13},{9,1},{13,5},{2,10},{6,14},... | collective-permute-start | bytes 3080 | tf_op jit(solution)/shard_map/ppermute | solution.py:39
  109.7 2.1 collective-permute-done.10
  111.8 2.8 %collective-permute-start.11 = (f32[2,4,32]{2,1,0:T(4,128)S(1)}, f32[2,4,32]{2,1,0:T(4,128)S(1)}, u32[]{:S(2)}, u32[]{:S(2)}) collective-permute-start(f32[2,4,32]{2,1,0:T(4,128)S(1)} %fusion.102), channel_id=1, source_target_pairs={{0,1},{1,0},{2,3},{3,2},{4,5},{5,4},{6,7},{7,6},{8,9},{9,8},{10,11... | collective-permute-start | bytes 3080 | tf_op jit(solution)/shard_map/ppermute | solution.py:39
  114.6 1.5 collective-permute-done.11
  116.1 3.8 %collective-permute-start.12 = (f32[2,4,32]{2,1,0:T(4,128)S(1)}, f32[2,4,32]{2,1,0:T(4,128)S(1)}, u32[]{:S(2)}, u32[]{:S(2)}) collective-permute-start(f32[2,4,32]{2,1,0:T(4,128)S(1)} %add.143), channel_id=1, source_target_pairs={{0,2},{1,3},{2,0},{3,1},{4,6},{5,7},{6,4},{7,5},{8,10},{9,11},{10,... | collective-permute-start | bytes 3080 | tf_op jit(solution)/shard_map/ppermute | solution.py:39
  119.9 0.8 copy.107
  120.7 1.3 collective-permute-done.12
  122.2 1.7 pad_maximum_fusion.2
  123.9 19.5 %all-to-all-start = ((bf16[32,4,17,256]{3,1,2,0:T(4,128)(2,1)}), bf16[32,4,17,256]{3,1,2,0:T(4,128)(2,1)S(1)}, u32[]{:S(2)}, u32[]{:S(2)}) async-start(bf16[32,4,17,256]{3,1,2,0:T(4,128)(2,1)} %pad_maximum_fusion.2), calls=%async_computation | async-start | bytes 2228224 | tf_op jit(solution)/shard_map/all_to_all | solution.py:143
  143.4 58.5 %all-to-all-done = bf16[32,4,17,256]{3,1,2,0:T(4,128)(2,1)S(1)} async-done(((bf16[32,4,17,256]{3,1,2,0:T(4,128)(2,1)}), bf16[32,4,17,256]{3,1,2,0:T(4,128)(2,1)S(1)}, u32[]{:S(2)}, u32[]{:S(2)}) %all-to-all-start) | async-done | bytes 1114144 | tf_op jit(solution)/shard_map/all_to_all | solution.py:143
  201.9 0.5 slice.219
  203.8 4.6 %convolution_convert_fusion = bf16[128,16,768]{2,0,1:T(8,128)(2,1)} fusion(f32[128,16,256]{2,1,0:T(8,128)S(1)} %bitcast_convert_fusion, f32[256]{0:T(256)S(1)} %bitcast.144, f32[128,256]{1,0:T(8,128)S(1)} %copy.62, f32[128,256]{1,0:T(8,128)S(1)} %copy.59, bf16[256,4096]{1,0:T(8,128)(2,1)} %all-gather.2.cloned.1.call-done), kind=kOutput, calls=%fused_computation.7 | convolution fusion | flops 808976384 | bytes 5899264 | tf_op jit(solution)/shard_map/fpc,cd->fpd/dot_general | solution.py:149
  208.4 2.1 fusion.96
  210.5 3.9 %fusion.31 = bf16[1,1,16,128,256]{4,3,2,1,0:T(8,128)(2,1)} fusion(f32[128,16,256]{2,1,0:T(8,128)S(1)} %bitcast_convert_fusion, bf16[128,16,768]{2,0,1:T(8,128)(2,1)} %convolution_convert_fusion, f32[16,128,128]{1,2,0:T(8,128)S(1)} %get-tuple-element.29, f32[16,128]{1,0:T(8,128)S(1)} %get-tuple-element.28, bf16[256,4096]{1,0:T(8,128)(2,1)} %all-gather.2.cloned.1.call-done), kind=kOutput, calls=%fused_computation.39 | convolution fusion | flops 404750336 | bytes 5382144 | tf_op jit(solution)/shard_map/axi,iy->axy/dot_general | solution.py:167
  (73 shorter events, 6.3 us)
Async XLA Ops:
  6.5 25.2 %copy-start.1 = (bf16[4,16,32,256]{3,2,1,0:T(8,128)(2,1)S(1)}, bf16[4,16,32,256]{3,2,1,0:T(8,128)(2,1)}, u32[]{:S(2)}) copy-start(bf16[4,16,32,256]{3,2,1,0:T(8,128)(2,1)} %param.7) | copy-start | bytes 3145732
  6.5 68.1 %all-gather.2.cloned.1.call-start = ((), (), s32[]{:S(2)}) async-start(), calls=%async_computation.1 | async-start | bytes 2228224 | tf_op jit(solution)/shard_map/all_gather | solution.py:92
  10.2 5.0 %collective-permute-start = (f32[2,4,32]{2,1,0:T(4,128)S(1)}, f32[2,4,32]{2,1,0:T(4,128)S(1)}, u32[]{:S(2)}, u32[]{:S(2)}) collective-permute-start(f32[2,4,32]{2,1,0:T(4,128)S(1)} %pad_maximum_fusion.7), channel_id=1, source_target_pairs={{0,4},{4,0},{8,12},{12,8},{1,5},{5,1},{9,13},{13,9},{2,6},{6,2},{1... | collective-permute-start | bytes 3080 | tf_op jit(solution)/shard_map/ppermute | solution.py:39
  15.2 6.0 %collective-permute-start.1 = (f32[2,4,32]{2,1,0:T(4,128)S(1)}, f32[2,4,32]{2,1,0:T(4,128)S(1)}, u32[]{:S(2)}, u32[]{:S(2)}) collective-permute-start(f32[2,4,32]{2,1,0:T(4,128)S(1)} %fusion.92), channel_id=1, source_target_pairs={{0,8},{4,12},{8,0},{12,4},{1,9},{5,13},{9,1},{13,5},{2,10},{6,14},... | collective-permute-start | bytes 3080 | tf_op jit(solution)/shard_map/ppermute | solution.py:39
  21.2 4.3 %collective-permute-start.2 = (f32[2,4,32]{2,1,0:T(4,128)S(1)}, f32[2,4,32]{2,1,0:T(4,128)S(1)}, u32[]{:S(2)}, u32[]{:S(2)}) collective-permute-start(f32[2,4,32]{2,1,0:T(4,128)S(1)} %fusion.103), channel_id=1, source_target_pairs={{0,1},{1,0},{2,3},{3,2},{4,5},{5,4},{6,7},{7,6},{8,9},{9,8},{10,11... | collective-permute-start | bytes 3080 | tf_op jit(solution)/shard_map/ppermute | solution.py:39
  25.5 5.8 %collective-permute-start.3 = (f32[2,4,32]{2,1,0:T(4,128)S(1)}, f32[2,4,32]{2,1,0:T(4,128)S(1)}, u32[]{:S(2)}, u32[]{:S(2)}) collective-permute-start(f32[2,4,32]{2,1,0:T(4,128)S(1)} %add.122), channel_id=1, source_target_pairs={{0,2},{1,3},{2,0},{3,1},{4,6},{5,7},{6,4},{7,5},{8,10},{9,11},{10,... | collective-permute-start | bytes 3080 | tf_op jit(solution)/shard_map/ppermute | solution.py:39
  32.4 4.6 %collective-permute-start.4 = (bf16[4,1,32,256]{3,2,1,0:T(8,128)(2,1)S(1)}, bf16[4,1,32,256]{3,2,1,0:T(8,128)(2,1)S(1)}, u32[]{:S(2)}, u32[]{:S(2)}) collective-permute-start(bf16[4,1,32,256]{3,2,1,0:T(8,128)(2,1)S(1)} %get-tuple-element.13), channel_id=1, source_target_pairs={{0,4},{4,8},{8,12},{1,5},{5,9},{9,13},{2,6},{6,10},{10,14},{3,7},{... | collective-permute-start | bytes 196616 | tf_op jit(solution)/shard_map/ppermute | solution.py:21
  35.7 5.4 %collective-permute-start.5 = (bf16[4,1,32,256]{3,2,1,0:T(8,128)(2,1)S(1)}, bf16[4,1,32,256]{3,2,1,0:T(8,128)(2,1)S(1)}, u32[]{:S(2)}, u32[]{:S(2)}) collective-permute-start(bf16[4,1,32,256]{3,2,1,0:T(8,128)(2,1)S(1)} %get-tuple-element.14), channel_id=1, source_target_pairs={{4,0},{8,4},{12,8},{5,1},{9,5},{13,9},{6,2},{10,6},{14,10},{7,3},{... | collective-permute-start | bytes 196616 | tf_op jit(solution)/shard_map/ppermute | solution.py:22
  41.3 4.6 %collective-permute-start.6 = (bf16[4,18,1,256]{3,2,1,0:T(2,128)(2,1)S(1)}, bf16[4,18,1,256]{3,2,1,0:T(2,128)(2,1)S(1)}, u32[]{:S(2)}, u32[]{:S(2)}) collective-permute-start(bf16[4,18,1,256]{3,2,1,0:T(2,128)(2,1)S(1)} %get-tuple-element.12), channel_id=1, source_target_pairs={{0,1},{1,2},{2,3},{4,5},{5,6},{6,7},{8,9},{9,10},{10,11},{12,13},{... | collective-permute-start | bytes 110600 | tf_op jit(solution)/shard_map/ppermute | solution.py:21
  44.5 5.1 %collective-permute-start.7 = (bf16[4,18,1,256]{3,2,1,0:T(2,128)(2,1)S(1)}, bf16[4,18,1,256]{3,2,1,0:T(2,128)(2,1)S(1)}, u32[]{:S(2)}, u32[]{:S(2)}) collective-permute-start(bf16[4,18,1,256]{3,2,1,0:T(2,128)(2,1)S(1)} %get-tuple-element.11), channel_id=1, source_target_pairs={{1,0},{2,1},{3,2},{5,4},{6,5},{7,6},{9,8},{10,9},{11,10},{13,12},{... | collective-permute-start | bytes 110600 | tf_op jit(solution)/shard_map/ppermute | solution.py:22
  74.6 1.7 copy-start.3
  76.3 1.4 copy-start
  80.4 6.4 %copy-start.4 = (s32[16]{0:T(128)S(1)}, s32[16]{0:T(128)}, u32[]{:S(2)}) copy-start(s32[16]{0:T(128)} %param.8) | copy-start | bytes 196
  81.5 11.4 %collective-permute-start.8 = (bf16[2,16,32,256]{3,2,1,0:T(8,128)(2,1)S(1)}, bf16[2,16,32,256]{3,2,1,0:T(8,128)(2,1)S(1)}, u32[]{:S(2)}, u32[]{:S(2)}) collective-permute-start(bf16[2,16,32,256]{3,2,1,0:T(8,128)(2,1)S(1)} %slice.213), channel_id=1, source_target_pairs={{0,16},{16,32},{32,48},{48,64},{64,80},{80,96},{96,112},{112,128},... | collective-permute-start | bytes 1572872 | tf_op jit(solution)/shard_map/ppermute | solution.py:30
  98.0 1.4 copy-start.2
  101.6 4.4 %collective-permute-start.9 = (f32[2,4,32]{2,1,0:T(4,128)S(1)}, f32[2,4,32]{2,1,0:T(4,128)S(1)}, u32[]{:S(2)}, u32[]{:S(2)}) collective-permute-start(f32[2,4,32]{2,1,0:T(4,128)S(1)} %pad_maximum_fusion.8), channel_id=1, source_target_pairs={{0,4},{4,0},{8,12},{12,8},{1,5},{5,1},{9,13},{13,9},{2,6},{6,2},{1... | collective-permute-start | bytes 3080 | tf_op jit(solution)/shard_map/ppermute | solution.py:39
  105.9 5.8 %collective-permute-start.10 = (f32[2,4,32]{2,1,0:T(4,128)S(1)}, f32[2,4,32]{2,1,0:T(4,128)S(1)}, u32[]{:S(2)}, u32[]{:S(2)}) collective-permute-start(f32[2,4,32]{2,1,0:T(4,128)S(1)} %fusion.91), channel_id=1, source_target_pairs={{0,8},{4,12},{8,0},{12,4},{1,9},{5,13},{9,1},{13,5},{2,10},{6,14},... | collective-permute-start | bytes 3080 | tf_op jit(solution)/shard_map/ppermute | solution.py:39
  111.8 4.3 %collective-permute-start.11 = (f32[2,4,32]{2,1,0:T(4,128)S(1)}, f32[2,4,32]{2,1,0:T(4,128)S(1)}, u32[]{:S(2)}, u32[]{:S(2)}) collective-permute-start(f32[2,4,32]{2,1,0:T(4,128)S(1)} %fusion.102), channel_id=1, source_target_pairs={{0,1},{1,0},{2,3},{3,2},{4,5},{5,4},{6,7},{7,6},{8,9},{9,8},{10,11... | collective-permute-start | bytes 3080 | tf_op jit(solution)/shard_map/ppermute | solution.py:39
  116.1 5.8 %collective-permute-start.12 = (f32[2,4,32]{2,1,0:T(4,128)S(1)}, f32[2,4,32]{2,1,0:T(4,128)S(1)}, u32[]{:S(2)}, u32[]{:S(2)}) collective-permute-start(f32[2,4,32]{2,1,0:T(4,128)S(1)} %add.143), channel_id=1, source_target_pairs={{0,2},{1,3},{2,0},{3,1},{4,6},{5,7},{6,4},{7,5},{8,10},{9,11},{10,... | collective-permute-start | bytes 3080 | tf_op jit(solution)/shard_map/ppermute | solution.py:39
  123.9 78.0 %all-to-all-start = ((bf16[32,4,17,256]{3,1,2,0:T(4,128)(2,1)}), bf16[32,4,17,256]{3,1,2,0:T(4,128)(2,1)S(1)}, u32[]{:S(2)}, u32[]{:S(2)}) async-start(bf16[32,4,17,256]{3,1,2,0:T(4,128)(2,1)} %pad_maximum_fusion.2), calls=%async_computation | async-start | bytes 2228224 | tf_op jit(solution)/shard_map/all_to_all | solution.py:143
Sparse Core Ops, SparseCore 0:
  10.3 64.2 all-gather.1

commit v2 on v1

--- a/solution.py
+++ b/solution.py
@@ -72,19 +72,6 @@
     return normed.reshape(shape) * gain
 
 
-def split3(x):
-    hi = lax.reduce_precision(x, exponent_bits=8, mantissa_bits=7)
-    rest = x - hi
-    mid = lax.reduce_precision(rest, exponent_bits=8, mantissa_bits=7)
-    lo = rest - mid
-    return jnp.stack([hi, mid, lo]).astype(jnp.bfloat16)
-
-
-def join3(pieces):
-    pieces = pieces.astype(jnp.float32)
-    return (pieces[0] + pieces[1]) + pieces[2]
-
-
 def body(video, clip_lengths, norm_gains, spatial_kernel_weight, w_time, w_qkv, w_out):
     frames, height, width, chans = video.shape
     widths = [w.shape[1] for w in (spatial_kernel_weight, w_time, w_qkv, w_out)]
@@ -131,19 +118,15 @@
             preferred_element_type=jnp.float32,
         )
     resid = (video.astype(jnp.float32) + temporal).astype(jnp.bfloat16)
-    mean_two, scale_two = group_moments(resid)
     pixels = height * width
     group_pixels = pixels // ranks
     flat_resid = resid.reshape(frames, ranks, group_pixels, chans).transpose(1, 0, 2, 3)
-    stats = split3(jnp.concatenate([mean_two, scale_two], axis=1))
-    stats = stats.transpose(1, 0, 2).reshape(frames, 3 * 2 * GROUPS)
-    stats = jnp.pad(stats, ((0, 0), (0, chans - stats.shape[1])))
-    stats_rows = jnp.broadcast_to(stats[None, :, None, :], (ranks, frames, 1, chans))
-    payload = jnp.concatenate([flat_resid, stats_rows], axis=2)
-    received = lax.all_to_all(payload, "tm", split_axis=0, concat_axis=0, tiled=True)
-    resid_time = received[:, :, :group_pixels, :].reshape(total_frames, group_pixels, chans)
-    got = received[:, :, group_pixels, : 3 * 2 * GROUPS].reshape(total_frames, 3, 2 * GROUPS)
-    moments = join3(got.transpose(1, 0, 2))
+    received = lax.all_to_all(flat_resid, "tm", split_axis=0, concat_axis=0, tiled=True)
+    resid_time = received.reshape(total_frames, group_pixels, chans)
+    mean_two, scale_two = group_moments(resid)
+    moments = lax.all_gather(
+        jnp.concatenate([mean_two, scale_two], axis=1), "tm", axis=0, tiled=True
+    )
     mean_all, scale_all = moments[:, :GROUPS], moments[:, GROUPS:]
     flat_norm = apply_norm(resid_time, mean_all, scale_all, norm_gains[1]).astype(jnp.bfloat16)
     qkv_time = jnp.einsum(

time: 222 us -> 209 us (0.941)
  waiting for transfers between devices: 105 us -> 48.9 us
  blocking collectives: 0 us -> 50.1 us
  starting transfers between devices: 63.9 us -> 59.2 us
    all_to_all x1, waiting for transfers between devices: 58.5 us -> 0.01 us  [body(): lax.all_to_all(flat_resid, 'tm', split_axis=0, concat_axis=0, tiled=True)]
    all_gather x0 -> x1, blocking collectives: none -> 50.1 us  [body(): lax.all_gather(jnp.concatenate([mean_two, scale_two], axis=1), 'tm', axis...]
    all_to_all x1, starting transfers between devices: 19.5 us -> 15.1 us  [body(): lax.all_to_all(flat_resid, 'tm', split_axis=0, concat_axis=0, tiled=True)]
  transfers between devices with their start and end apart: 15 -> 15, of which waited for: 14 -> 13; matrix products, arithmetic and copies ran while one was open for 3% -> 3% of each run, Pallas kernels for 0% -> 0%
where the time goes in v2:
time: 209 us; the launch traced here: 208 us
  starting transfers between devices  59.2 us (28%)
  blocking collectives  50.1 us (24%)
  waiting for transfers between devices  48.9 us (23%)
  matrix products  24.5 us (12%)
  between operations  13.8 us (7%)
  other arithmetic  7.11 us (3%)
  local copies, waits for them, and re-layouts  4.26 us (2%)
    all_gather x1, blocking collectives, body(): lax.all_gather(jnp.concatenate([mean_two, scale_two], axis=1), 'tm', axis...  50.1 us
    ppermute x8, starting transfers between devices, butterfly_sum(): x = x + lax.ppermute(x, axis, pairs)  29.9 us
    all_gather x1, waiting for transfers between devices, body(): gathered = lax.all_gather(packed, ('band', 'fsdp'), axis=0, tiled=True)  23.3 us
    all_to_all x1, starting transfers between devices, body(): lax.all_to_all(flat_resid, 'tm', split_axis=0, concat_axis=0, tiled=True)  15.1 us
    ppermute x8, waiting for transfers between devices, butterfly_sum(): x = x + lax.ppermute(x, axis, pairs)  12 us
    ppermute x2, waiting for transfers between devices, with_halo(): after = lax.ppermute(initial, axis, down)  7.84 us
    ppermute x2, starting transfers between devices, with_halo(): before = lax.ppermute(last, axis, up)  6.45 us
    dot_general x9, matrix products, body(): jnp.einsum('fhwc,cd->fhwd', padded[:, shift_y:shift_y + height, shift_x:s...  5.7 us
  transfers between devices with their start and end apart: 15, of which 13 were waited for; matrix products, arithmetic and copies ran while one was open for 3% of the time, Pallas kernels for 0%

profile of v2, /device:TPU:1, one launch (start us, length us, event | category | flops | bytes accessed | tf_op | source)
XLA Modules:
  0.0 207.9 jit_solution(15241322184960660251)
XLA Ops:
  6.5 1.7 pad_maximum_fusion.2
  8.3 1.5 convert_reduce_fusion
  10.2 4.0 %collective-permute-start = (f32[2,4,32]{2,1,0:T(4,128)S(1)}, f32[2,4,32]{2,1,0:T(4,128)S(1)}, u32[]{:S(2)}, u32[]{:S(2)}) collective-permute-start(f32[2,4,32]{2,1,0:T(4,128)S(1)} %pad_maximum_fusion.6), channel_id=1, source_target_pairs={{0,4},{4,0},{8,12},{12,8},{1,5},{5,1},{9,13},{13,9},{2,6},{6,2},{1... | collective-permute-start | bytes 3080 | tf_op jit(solution)/shard_map/ppermute | solution.py:39
  14.2 1.0 collective-permute-done
  15.2 5.0 %collective-permute-start.1 = (f32[2,4,32]{2,1,0:T(4,128)S(1)}, f32[2,4,32]{2,1,0:T(4,128)S(1)}, u32[]{:S(2)}, u32[]{:S(2)}) collective-permute-start(f32[2,4,32]{2,1,0:T(4,128)S(1)} %fusion.93), channel_id=1, source_target_pairs={{0,8},{4,12},{8,0},{12,4},{1,9},{5,13},{9,1},{13,5},{2,10},{6,14},... | collective-permute-start | bytes 3080 | tf_op jit(solution)/shard_map/ppermute | solution.py:39
  20.2 1.0 collective-permute-done.1
  21.2 3.2 %collective-permute-start.2 = (f32[2,4,32]{2,1,0:T(4,128)S(1)}, f32[2,4,32]{2,1,0:T(4,128)S(1)}, u32[]{:S(2)}, u32[]{:S(2)}) collective-permute-start(f32[2,4,32]{2,1,0:T(4,128)S(1)} %fusion.104), channel_id=1, source_target_pairs={{0,1},{1,0},{2,3},{3,2},{4,5},{5,4},{6,7},{7,6},{8,9},{9,8},{10,11... | collective-permute-start | bytes 3080 | tf_op jit(solution)/shard_map/ppermute | solution.py:39
  24.3 1.2 collective-permute-done.2
  25.5 4.7 %collective-permute-start.3 = (f32[2,4,32]{2,1,0:T(4,128)S(1)}, f32[2,4,32]{2,1,0:T(4,128)S(1)}, u32[]{:S(2)}, u32[]{:S(2)}) collective-permute-start(f32[2,4,32]{2,1,0:T(4,128)S(1)} %add.109), channel_id=1, source_target_pairs={{0,2},{1,3},{2,0},{3,1},{4,6},{5,7},{6,4},{7,5},{8,10},{9,11},{10,... | collective-permute-start | bytes 3080 | tf_op jit(solution)/shard_map/ppermute | solution.py:39
  30.2 0.8 fusion.96
  31.8 0.7 fusion.16
  32.4 3.2 %collective-permute-start.4 = (bf16[4,1,32,256]{3,2,1,0:T(8,128)(2,1)S(1)}, bf16[4,1,32,256]{3,2,1,0:T(8,128)(2,1)S(1)}, u32[]{:S(2)}, u32[]{:S(2)}) collective-permute-start(bf16[4,1,32,256]{3,2,1,0:T(8,128)(2,1)S(1)} %get-tuple-element.13), channel_id=1, source_target_pairs={{0,4},{4,8},{8,12},{1,5},{5,9},{9,13},{2,6},{6,10},{10,14},{3,7},{... | collective-permute-start | bytes 196616 | tf_op jit(solution)/shard_map/ppermute | solution.py:21
  35.7 1.3 collective-permute-start.5
  37.0 4.1 %collective-permute-done.5 = bf16[4,1,32,256]{3,2,1,0:T(8,128)(2,1)S(1)} collective-permute-done((bf16[4,1,32,256]{3,2,1,0:T(8,128)(2,1)S(1)}, bf16[4,1,32,256]{3,2,1,0:T(8,128)(2,1)S(1)}, u32[]{:S(2)}, u32[]{:S(2)}) %collective-permute-start.5) | collective-permute-done | bytes 65568 | tf_op jit(solution)/shard_map/ppermute | solution.py:22
  41.3 3.2 %collective-permute-start.6 = (bf16[4,18,1,256]{3,2,1,0:T(2,128)(2,1)S(1)}, bf16[4,18,1,256]{3,2,1,0:T(2,128)(2,1)S(1)}, u32[]{:S(2)}, u32[]{:S(2)}) collective-permute-start(bf16[4,18,1,256]{3,2,1,0:T(2,128)(2,1)S(1)} %get-tuple-element.12), channel_id=1, source_target_pairs={{0,1},{1,2},{2,3},{4,5},{5,6},{6,7},{8,9},{9,10},{10,11},{12,13},{... | collective-permute-start | bytes 110600 | tf_op jit(solution)/shard_map/ppermute | solution.py:21
  44.5 1.3 collective-permute-start.7
  45.9 3.7 %collective-permute-done.7 = bf16[4,18,1,256]{3,2,1,0:T(2,128)(2,1)S(1)} collective-permute-done((bf16[4,18,1,256]{3,2,1,0:T(2,128)(2,1)S(1)}, bf16[4,18,1,256]{3,2,1,0:T(2,128)(2,1)S(1)}, u32[]{:S(2)}, u32[]{:S(2)}) %collective-permute-start.7) | collective-permute-done | bytes 36896 | tf_op jit(solution)/shard_map/ppermute | solution.py:22
  49.6 1.8 pad_maximum_fusion.1
  51.3 23.3 %all-gather.3.cloned.1.call-done = bf16[256,4096]{1,0:T(8,128)(2,1)} async-done(((bf16[16,4096]{1,0:T(8,128)(2,1)}), bf16[256,4096]{1,0:T(8,128)(2,1)}) %all-gather.3.cloned.1.call-update) | async-done | bytes 2097168 | tf_op jit(solution)/shard_map/all_gather | solution.py:79
  74.7 1.5 fusion.51
  76.3 0.4 fusion.55
  76.8 0.9 copy-done
  77.7 0.4 fusion.53
  78.6 0.4 fusion.49
  79.0 0.4 fusion.33
  80.4 1.1 add_convert_fusion
  81.5 5.3 %collective-permute-start.8 = (bf16[2,16,32,256]{3,2,1,0:T(8,128)(2,1)S(1)}, bf16[2,16,32,256]{3,2,1,0:T(8,128)(2,1)S(1)}, u32[]{:S(2)}, u32[]{:S(2)}) collective-permute-start(bf16[2,16,32,256]{3,2,1,0:T(8,128)(2,1)S(1)} %slice.193), channel_id=1, source_target_pairs={{0,16},{16,32},{32,48},{48,64},{64,80},{80,96},{96,112},{112,128},... | collective-permute-start | bytes 1572872 | tf_op jit(solution)/shard_map/ppermute | solution.py:30
  87.2 5.7 %collective-permute-done.8 = bf16[2,16,32,256]{3,2,1,0:T(8,128)(2,1)S(1)} collective-permute-done((bf16[2,16,32,256]{3,2,1,0:T(8,128)(2,1)S(1)}, bf16[2,16,32,256]{3,2,1,0:T(8,128)(2,1)S(1)}, u32[]{:S(2)}, u32[]{:S(2)}) %collective-permute-start.8) | collective-permute-done | bytes 524320 | tf_op jit(solution)/shard_map/ppermute | solution.py:30
  93.0 1.2 fusion.22
  94.2 1.2 fusion.19
  95.4 1.2 fusion.25
  96.6 1.3 fusion.60
  98.0 1.4 fusion.62
  99.4 1.7 convert_reduce_fusion.1
  101.2 1.1 copy.89
  102.3 15.1 %all-to-all-start = ((bf16[32,4,16,256]{3,2,1,0:T(8,128)(2,1)}), bf16[32,4,16,256]{3,2,1,0:T(8,128)(2,1)S(1)}, u32[]{:S(2)}, u32[]{:S(2)}) async-start(bf16[32,4,16,256]{3,2,1,0:T(8,128)(2,1)} %bitcast.136), calls=%async_computation | async-start | bytes 2097152 | tf_op jit(solution)/shard_map/all_to_all | solution.py:124
  117.8 2.8 %collective-permute-start.9 = (f32[2,4,32]{2,1,0:T(4,128)S(1)}, f32[2,4,32]{2,1,0:T(4,128)S(1)}, u32[]{:S(2)}, u32[]{:S(2)}) collective-permute-start(f32[2,4,32]{2,1,0:T(4,128)S(1)} %pad_maximum_fusion.7), channel_id=1, source_target_pairs={{0,4},{4,0},{8,12},{12,8},{1,5},{5,1},{9,13},{13,9},{2,6},{6,2},{1... | collective-permute-start | bytes 3080 | tf_op jit(solution)/shard_map/ppermute | solution.py:39
  120.6 1.8 collective-permute-done.9
  122.4 3.7 %collective-permute-start.10 = (f32[2,4,32]{2,1,0:T(4,128)S(1)}, f32[2,4,32]{2,1,0:T(4,128)S(1)}, u32[]{:S(2)}, u32[]{:S(2)}) collective-permute-start(f32[2,4,32]{2,1,0:T(4,128)S(1)} %fusion.92), channel_id=1, source_target_pairs={{0,8},{4,12},{8,0},{12,4},{1,9},{5,13},{9,1},{13,5},{2,10},{6,14},... | collective-permute-start | bytes 3080 | tf_op jit(solution)/shard_map/ppermute | solution.py:39
  126.1 2.4 %collective-permute-done.10 = f32[2,4,32]{2,1,0:T(4,128)S(1)} collective-permute-done((f32[2,4,32]{2,1,0:T(4,128)S(1)}, f32[2,4,32]{2,1,0:T(4,128)S(1)}, u32[]{:S(2)}, u32[]{:S(2)}) %collective-permute-start.10) | collective-permute-done | bytes 1056 | tf_op jit(solution)/shard_map/ppermute | solution.py:39
  128.6 2.8 %collective-permute-start.11 = (f32[2,4,32]{2,1,0:T(4,128)S(1)}, f32[2,4,32]{2,1,0:T(4,128)S(1)}, u32[]{:S(2)}, u32[]{:S(2)}) collective-permute-start(f32[2,4,32]{2,1,0:T(4,128)S(1)} %fusion.103), channel_id=1, source_target_pairs={{0,1},{1,0},{2,3},{3,2},{4,5},{5,4},{6,7},{7,6},{8,9},{9,8},{10,11... | collective-permute-start | bytes 3080 | tf_op jit(solution)/shard_map/ppermute | solution.py:39
  131.3 1.8 collective-permute-done.11
  133.2 3.7 %collective-permute-start.12 = (f32[2,4,32]{2,1,0:T(4,128)S(1)}, f32[2,4,32]{2,1,0:T(4,128)S(1)}, u32[]{:S(2)}, u32[]{:S(2)}) collective-permute-start(f32[2,4,32]{2,1,0:T(4,128)S(1)} %add.130), channel_id=1, source_target_pairs={{0,2},{1,3},{2,0},{3,1},{4,6},{5,7},{6,4},{7,5},{8,10},{9,11},{10,... | collective-permute-start | bytes 3080 | tf_op jit(solution)/shard_map/ppermute | solution.py:39
  137.0 2.4 %collective-permute-done.12 = f32[2,4,32]{2,1,0:T(4,128)S(1)} collective-permute-done((f32[2,4,32]{2,1,0:T(4,128)S(1)}, f32[2,4,32]{2,1,0:T(4,128)S(1)}, u32[]{:S(2)}, u32[]{:S(2)}) %collective-permute-start.12) | collective-permute-done | bytes 1056 | tf_op jit(solution)/shard_map/ppermute | solution.py:39
  139.4 50.1 %all-gather = f32[32,4,64]{2,1,0:T(4,128)S(1)} all-gather(f32[1,4,64]{2,1,0:T(4,128)S(1)} %maximum_bitcast_fusion), channel_id=1, replica_groups=mesh['tm'=32,'band'=4,'fsdp'=4] {'tm'}, dimensions={0}, use_global_device_ids=true | all-gather | bytes 33792 | tf_op jit(solution)/shard_map/all_gather | solution.py:127
  190.4 4.6 %convolution_convert_fusion = bf16[128,16,768]{2,0,1:T(8,128)(2,1)} fusion(f32[128,16,256]{2,1,0:T(8,128)S(1)} %bitcast_convert_fusion, f32[256]{0:T(256)S(1)} %bitcast.151, f32[128,256]{1,0:T(8,128)S(1)} %copy.42, f32[128,256]{1,0:T(8,128)S(1)} %copy.40, bf16[256,4096]{1,0:T(8,128)(2,1)} %all-gather.3.cloned.1.call-done), kind=kOutput, calls=%fused_computation.7 | convolution fusion | flops 808976384 | bytes 5899264 | tf_op jit(solution)/shard_map/fpc,cd->fpd/dot_general | solution.py:132
  195.0 2.1 %fusion.97 = (f32[16,128]{1,0:T(8,128)S(1)}, f32[16,128,128]{1,2,0:T(8,128)S(1)}) fusion(pred[128,128]{0,1:T(8,128)(4,1)S(1)} %fusion.70, bf16[128,16,768]{2,0,1:T(8,128)(2,1)} %convolution_convert_fusion), kind=kOutput, calls=%fused_computation.140 | convolution fusion | flops 135528576 | bytes 3186688 | tf_op jit(solution)/shard_map/sub | solution.py:145
  197.2 3.9 %fusion.31 = bf16[1,1,16,128,256]{4,3,2,1,0:T(8,128)(2,1)} fusion(f32[128,16,256]{2,1,0:T(8,128)S(1)} %bitcast_convert_fusion, bf16[128,16,768]{2,0,1:T(8,128)(2,1)} %convolution_convert_fusion, f32[16,128,128]{1,2,0:T(8,128)S(1)} %get-tuple-element.24, f32[16,128]{1,0:T(8,128)S(1)} %get-tuple-element.23, bf16[256,4096]{1,0:T(8,128)(2,1)} %all-gather.3.cloned.1.call-done), kind=kOutput, calls=%fused_computation.39 | convolution fusion | flops 404750336 | bytes 5382144 | tf_op jit(solution)/shard_map/axi,iy->axy/dot_general | solution.py:150
  (64 shorter events, 4.8 us)
Async XLA Ops:
  6.5 25.2 %copy-start.1 = (bf16[4,16,32,256]{3,2,1,0:T(8,128)(2,1)S(1)}, bf16[4,16,32,256]{3,2,1,0:T(8,128)(2,1)}, u32[]{:S(2)}) copy-start(bf16[4,16,32,256]{3,2,1,0:T(8,128)(2,1)} %param.7) | copy-start | bytes 3145732
  6.5 68.1 %all-gather.3.cloned.1.call-start = ((), (), s32[]{:S(2)}) async-start(), calls=%async_computation.1 | async-start | bytes 2228224 | tf_op jit(solution)/shard_map/all_gather | solution.py:79
  10.2 5.0 %collective-permute-start = (f32[2,4,32]{2,1,0:T(4,128)S(1)}, f32[2,4,32]{2,1,0:T(4,128)S(1)}, u32[]{:S(2)}, u32[]{:S(2)}) collective-permute-start(f32[2,4,32]{2,1,0:T(4,128)S(1)} %pad_maximum_fusion.6), channel_id=1, source_target_pairs={{0,4},{4,0},{8,12},{12,8},{1,5},{5,1},{9,13},{13,9},{2,6},{6,2},{1... | collective-permute-start | bytes 3080 | tf_op jit(solution)/shard_map/ppermute | solution.py:39
  15.2 6.0 %collective-permute-start.1 = (f32[2,4,32]{2,1,0:T(4,128)S(1)}, f32[2,4,32]{2,1,0:T(4,128)S(1)}, u32[]{:S(2)}, u32[]{:S(2)}) collective-permute-start(f32[2,4,32]{2,1,0:T(4,128)S(1)} %fusion.93), channel_id=1, source_target_pairs={{0,8},{4,12},{8,0},{12,4},{1,9},{5,13},{9,1},{13,5},{2,10},{6,14},... | collective-permute-start | bytes 3080 | tf_op jit(solution)/shard_map/ppermute | solution.py:39
  21.2 4.3 %collective-permute-start.2 = (f32[2,4,32]{2,1,0:T(4,128)S(1)}, f32[2,4,32]{2,1,0:T(4,128)S(1)}, u32[]{:S(2)}, u32[]{:S(2)}) collective-permute-start(f32[2,4,32]{2,1,0:T(4,128)S(1)} %fusion.104), channel_id=1, source_target_pairs={{0,1},{1,0},{2,3},{3,2},{4,5},{5,4},{6,7},{7,6},{8,9},{9,8},{10,11... | collective-permute-start | bytes 3080 | tf_op jit(solution)/shard_map/ppermute | solution.py:39
  25.5 5.8 %collective-permute-start.3 = (f32[2,4,32]{2,1,0:T(4,128)S(1)}, f32[2,4,32]{2,1,0:T(4,128)S(1)}, u32[]{:S(2)}, u32[]{:S(2)}) collective-permute-start(f32[2,4,32]{2,1,0:T(4,128)S(1)} %add.109), channel_id=1, source_target_pairs={{0,2},{1,3},{2,0},{3,1},{4,6},{5,7},{6,4},{7,5},{8,10},{9,11},{10,... | collective-permute-start | bytes 3080 | tf_op jit(solution)/shard_map/ppermute | solution.py:39
  32.4 4.6 %collective-permute-start.4 = (bf16[4,1,32,256]{3,2,1,0:T(8,128)(2,1)S(1)}, bf16[4,1,32,256]{3,2,1,0:T(8,128)(2,1)S(1)}, u32[]{:S(2)}, u32[]{:S(2)}) collective-permute-start(bf16[4,1,32,256]{3,2,1,0:T(8,128)(2,1)S(1)} %get-tuple-element.13), channel_id=1, source_target_pairs={{0,4},{4,8},{8,12},{1,5},{5,9},{9,13},{2,6},{6,10},{10,14},{3,7},{... | collective-permute-start | bytes 196616 | tf_op jit(solution)/shard_map/ppermute | solution.py:21
  35.7 5.4 %collective-permute-start.5 = (bf16[4,1,32,256]{3,2,1,0:T(8,128)(2,1)S(1)}, bf16[4,1,32,256]{3,2,1,0:T(8,128)(2,1)S(1)}, u32[]{:S(2)}, u32[]{:S(2)}) collective-permute-start(bf16[4,1,32,256]{3,2,1,0:T(8,128)(2,1)S(1)} %get-tuple-element.14), channel_id=1, source_target_pairs={{4,0},{8,4},{12,8},{5,1},{9,5},{13,9},{6,2},{10,6},{14,10},{7,3},{... | collective-permute-start | bytes 196616 | tf_op jit(solution)/shard_map/ppermute | solution.py:22
  41.3 4.6 %collective-permute-start.6 = (bf16[4,18,1,256]{3,2,1,0:T(2,128)(2,1)S(1)}, bf16[4,18,1,256]{3,2,1,0:T(2,128)(2,1)S(1)}, u32[]{:S(2)}, u32[]{:S(2)}) collective-permute-start(bf16[4,18,1,256]{3,2,1,0:T(2,128)(2,1)S(1)} %get-tuple-element.12), channel_id=1, source_target_pairs={{0,1},{1,2},{2,3},{4,5},{5,6},{6,7},{8,9},{9,10},{10,11},{12,13},{... | collective-permute-start | bytes 110600 | tf_op jit(solution)/shard_map/ppermute | solution.py:21
  44.5 5.1 %collective-permute-start.7 = (bf16[4,18,1,256]{3,2,1,0:T(2,128)(2,1)S(1)}, bf16[4,18,1,256]{3,2,1,0:T(2,128)(2,1)S(1)}, u32[]{:S(2)}, u32[]{:S(2)}) collective-permute-start(bf16[4,18,1,256]{3,2,1,0:T(2,128)(2,1)S(1)} %get-tuple-element.11), channel_id=1, source_target_pairs={{1,0},{2,1},{3,2},{5,4},{6,5},{7,6},{9,8},{10,9},{11,10},{13,12},{... | collective-permute-start | bytes 110600 | tf_op jit(solution)/shard_map/ppermute | solution.py:22
  74.6 1.7 copy-start.3
  76.3 1.4 copy-start
  80.4 6.4 %copy-start.4 = (s32[16]{0:T(128)S(1)}, s32[16]{0:T(128)}, u32[]{:S(2)}) copy-start(s32[16]{0:T(128)} %param.8) | copy-start | bytes 196
  81.5 11.4 %collective-permute-start.8 = (bf16[2,16,32,256]{3,2,1,0:T(8,128)(2,1)S(1)}, bf16[2,16,32,256]{3,2,1,0:T(8,128)(2,1)S(1)}, u32[]{:S(2)}, u32[]{:S(2)}) collective-permute-start(bf16[2,16,32,256]{3,2,1,0:T(8,128)(2,1)S(1)} %slice.193), channel_id=1, source_target_pairs={{0,16},{16,32},{32,48},{48,64},{64,80},{80,96},{96,112},{112,128},... | collective-permute-start | bytes 1572872 | tf_op jit(solution)/shard_map/ppermute | solution.py:30
  98.0 1.4 copy-start.2
  102.3 87.7 %all-to-all-start = ((bf16[32,4,16,256]{3,2,1,0:T(8,128)(2,1)}), bf16[32,4,16,256]{3,2,1,0:T(8,128)(2,1)S(1)}, u32[]{:S(2)}, u32[]{:S(2)}) async-start(bf16[32,4,16,256]{3,2,1,0:T(8,128)(2,1)} %bitcast.136), calls=%async_computation | async-start | bytes 2097152 | tf_op jit(solution)/shard_map/all_to_all | solution.py:124
  117.8 4.6 %collective-permute-start.9 = (f32[2,4,32]{2,1,0:T(4,128)S(1)}, f32[2,4,32]{2,1,0:T(4,128)S(1)}, u32[]{:S(2)}, u32[]{:S(2)}) collective-permute-start(f32[2,4,32]{2,1,0:T(4,128)S(1)} %pad_maximum_fusion.7), channel_id=1, source_target_pairs={{0,4},{4,0},{8,12},{12,8},{1,5},{5,1},{9,13},{13,9},{2,6},{6,2},{1... | collective-permute-start | bytes 3080 | tf_op jit(solution)/shard_map/ppermute | solution.py:39
  122.4 6.1 %collective-permute-start.10 = (f32[2,4,32]{2,1,0:T(4,128)S(1)}, f32[2,4,32]{2,1,0:T(4,128)S(1)}, u32[]{:S(2)}, u32[]{:S(2)}) collective-permute-start(f32[2,4,32]{2,1,0:T(4,128)S(1)} %fusion.92), channel_id=1, source_target_pairs={{0,8},{4,12},{8,0},{12,4},{1,9},{5,13},{9,1},{13,5},{2,10},{6,14},... | collective-permute-start | bytes 3080 | tf_op jit(solution)/shard_map/ppermute | solution.py:39
  128.6 4.6 %collective-permute-start.11 = (f32[2,4,32]{2,1,0:T(4,128)S(1)}, f32[2,4,32]{2,1,0:T(4,128)S(1)}, u32[]{:S(2)}, u32[]{:S(2)}) collective-permute-start(f32[2,4,32]{2,1,0:T(4,128)S(1)} %fusion.103), channel_id=1, source_target_pairs={{0,1},{1,0},{2,3},{3,2},{4,5},{5,4},{6,7},{7,6},{8,9},{9,8},{10,11... | collective-permute-start | bytes 3080 | tf_op jit(solution)/shard_map/ppermute | solution.py:39
  133.2 6.1 %collective-permute-start.12 = (f32[2,4,32]{2,1,0:T(4,128)S(1)}, f32[2,4,32]{2,1,0:T(4,128)S(1)}, u32[]{:S(2)}, u32[]{:S(2)}) collective-permute-start(f32[2,4,32]{2,1,0:T(4,128)S(1)} %add.130), channel_id=1, source_target_pairs={{0,2},{1,3},{2,0},{3,1},{4,6},{5,7},{6,4},{7,5},{8,10},{9,11},{10,... | collective-permute-start | bytes 3080 | tf_op jit(solution)/shard_map/ppermute | solution.py:39
Sparse Core Ops, SparseCore 0:
  10.3 64.2 all-gather.2

commit v3 on v2

--- a/solution.py
+++ b/solution.py
@@ -124,9 +124,10 @@
     received = lax.all_to_all(flat_resid, "tm", split_axis=0, concat_axis=0, tiled=True)
     resid_time = received.reshape(total_frames, group_pixels, chans)
     mean_two, scale_two = group_moments(resid)
-    moments = lax.all_gather(
-        jnp.concatenate([mean_two, scale_two], axis=1), "tm", axis=0, tiled=True
-    )
+    mine = jnp.concatenate([mean_two, scale_two], axis=1)
+    placed = jnp.zeros((ranks, frames, 2 * GROUPS), jnp.float32)
+    placed = lax.dynamic_update_index_in_dim(placed, mine, lax.axis_index("tm"), 0)
+    moments = butterfly_sum(placed, ("tm",)).reshape(total_frames, 2 * GROUPS)
     mean_all, scale_all = moments[:, :GROUPS], moments[:, GROUPS:]
     flat_norm = apply_norm(resid_time, mean_all, scale_all, norm_gains[1]).astype(jnp.bfloat16)
     qkv_time = jnp.einsum(

time: 209 us -> 219 us (1.048)
  the two profiles are of different devices: /device:TPU:1 before, /device:TPU:2 now
where the time goes in v3:
time: 219 us; the launch traced here: 218 us
  starting transfers between devices  92.3 us (42%)
  waiting for transfers between devices  75.5 us (34%)
  matrix products  24.5 us (11%)
  between operations  13.8 us (6%)
  other arithmetic  7.28 us (3%)
  local copies, waits for them, and re-layouts  4.27 us (2%)
    ppermute x13, starting transfers between devices, butterfly_sum(): x = x + lax.ppermute(x, axis, pairs)  60.4 us
    ppermute x13, waiting for transfers between devices, butterfly_sum(): x = x + lax.ppermute(x, axis, pairs)  50.5 us
    all_to_all x1, starting transfers between devices, body(): lax.all_to_all(flat_resid, 'tm', split_axis=0, concat_axis=0, tiled=True)  21.6 us
    all_gather x1, waiting for transfers between devices, body(): gathered = lax.all_gather(packed, ('band', 'fsdp'), axis=0, tiled=True)  16.8 us
    ppermute x2, waiting for transfers between devices, with_halo(): after = lax.ppermute(initial, axis, down)  6.2 us
    dot_general x9, matrix products, body(): jnp.einsum('fhwc,cd->fhwd', padded[:, shift_y:shift_y + height, shift_x:s...  5.7 us
    ppermute x2, starting transfers between devices, with_halo(): after = lax.ppermute(initial, axis, down)  5.21 us
    dot_general x1, matrix products, body(): jnp.einsum('fpc,cd->fpd', flat_norm, qkv_full, preferred_element_type=jnp...  4.63 us
  transfers between devices with their start and end apart: 20, of which 19 were waited for; matrix products, arithmetic and copies ran while one was open for 3% of the time, Pallas kernels for 0%

profile of v3, /device:TPU:2, one launch (start us, length us, event | category | flops | bytes accessed | tf_op | source)
XLA Modules:
  0.0 217.6 jit_solution(15398916996960577577)
XLA Ops:
  6.5 1.7 pad_maximum_fusion.2
  8.3 1.5 convert_reduce_fusion
  10.2 3.5 %collective-permute-start = (f32[2,4,32]{2,1,0:T(4,128)S(1)}, f32[2,4,32]{2,1,0:T(4,128)S(1)}, u32[]{:S(2)}, u32[]{:S(2)}) collective-permute-start(f32[2,4,32]{2,1,0:T(4,128)S(1)} %pad_maximum_fusion.6), channel_id=1, source_target_pairs={{0,4},{4,0},{8,12},{12,8},{1,5},{5,1},{9,13},{13,9},{2,6},{6,2},{1... | collective-permute-start | bytes 3080 | tf_op jit(solution)/shard_map/ppermute | solution.py:39
  13.7 2.0 collective-permute-done
  15.7 5.1 %collective-permute-start.1 = (f32[2,4,32]{2,1,0:T(4,128)S(1)}, f32[2,4,32]{2,1,0:T(4,128)S(1)}, u32[]{:S(2)}, u32[]{:S(2)}) collective-permute-start(f32[2,4,32]{2,1,0:T(4,128)S(1)} %fusion.93), channel_id=1, source_target_pairs={{0,8},{4,12},{8,0},{12,4},{1,9},{5,13},{9,1},{13,5},{2,10},{6,14},... | collective-permute-start | bytes 3080 | tf_op jit(solution)/shard_map/ppermute | solution.py:39
  20.8 1.9 collective-permute-done.1
  22.7 7.8 %collective-permute-start.2 = (f32[2,4,32]{2,1,0:T(4,128)S(1)}, f32[2,4,32]{2,1,0:T(4,128)S(1)}, u32[]{:S(2)}, u32[]{:S(2)}) collective-permute-start(f32[2,4,32]{2,1,0:T(4,128)S(1)} %fusion.104), channel_id=1, source_target_pairs={{0,1},{1,0},{2,3},{3,2},{4,5},{5,4},{6,7},{7,6},{8,9},{9,8},{10,11... | collective-permute-start | bytes 3080 | tf_op jit(solution)/shard_map/ppermute | solution.py:39
  30.5 1.6 collective-permute-done.2
  32.0 1.9 collective-permute-start.3
  34.7 4.4 %collective-permute-done.3 = f32[2,4,32]{2,1,0:T(4,128)S(1)} collective-permute-done((f32[2,4,32]{2,1,0:T(4,128)S(1)}, f32[2,4,32]{2,1,0:T(4,128)S(1)}, u32[]{:S(2)}, u32[]{:S(2)}) %collective-permute-start.3) | collective-permute-done | bytes 1056 | tf_op jit(solution)/shard_map/ppermute | solution.py:39
  40.2 1.8 collective-permute-start.4
  42.1 1.3 collective-permute-start.5
  43.9 4.3 %collective-permute-done.5 = bf16[4,1,32,256]{3,2,1,0:T(8,128)(2,1)S(1)} collective-permute-done((bf16[4,1,32,256]{3,2,1,0:T(8,128)(2,1)S(1)}, bf16[4,1,32,256]{3,2,1,0:T(8,128)(2,1)S(1)}, u32[]{:S(2)}, u32[]{:S(2)}) %collective-permute-start.5) | collective-permute-done | bytes 65568 | tf_op jit(solution)/shard_map/ppermute | solution.py:22
  48.3 1.9 collective-permute-start.6
  50.3 3.9 %collective-permute-start.7 = (bf16[4,18,1,256]{3,2,1,0:T(2,128)(2,1)S(1)}, bf16[4,18,1,256]{3,2,1,0:T(2,128)(2,1)S(1)}, u32[]{:S(2)}, u32[]{:S(2)}) collective-permute-start(bf16[4,18,1,256]{3,2,1,0:T(2,128)(2,1)S(1)} %get-tuple-element.11), channel_id=1, source_target_pairs={{1,0},{2,1},{3,2},{5,4},{6,5},{7,6},{9,8},{10,9},{11,10},{13,12},{... | collective-permute-start | bytes 110600 | tf_op jit(solution)/shard_map/ppermute | solution.py:22
  54.6 1.9 collective-permute-done.7
  56.5 1.8 pad_maximum_fusion.1
  58.3 16.8 %all-gather.2.cloned.1.call-done = bf16[256,4096]{1,0:T(8,128)(2,1)} async-done(((bf16[16,4096]{1,0:T(8,128)(2,1)}), bf16[256,4096]{1,0:T(8,128)(2,1)}) %all-gather.2.cloned.1.call-update) | async-done | bytes 2097168 | tf_op jit(solution)/shard_map/all_gather | solution.py:79
  75.1 1.5 fusion.51
  81.9 1.3 collective-permute-start.8
  84.9 1.2 fusion.22
  86.1 1.2 fusion.19
  87.3 1.2 fusion.25
  88.5 1.3 fusion.60
  89.8 1.4 fusion.62
  91.3 1.7 convert_reduce_fusion.1
  94.1 21.6 %all-to-all-start = ((bf16[32,4,16,256]{3,2,1,0:T(8,128)(2,1)}), bf16[32,4,16,256]{3,2,1,0:T(8,128)(2,1)S(1)}, u32[]{:S(2)}, u32[]{:S(2)}) async-start(bf16[32,4,16,256]{3,2,1,0:T(8,128)(2,1)} %bitcast.140), calls=%async_computation | async-start | bytes 2097152 | tf_op jit(solution)/shard_map/all_to_all | solution.py:124
  116.2 2.2 collective-permute-start.9
  118.3 3.3 %collective-permute-done.9 = f32[2,4,32]{2,1,0:T(4,128)S(1)} collective-permute-done((f32[2,4,32]{2,1,0:T(4,128)S(1)}, f32[2,4,32]{2,1,0:T(4,128)S(1)}, u32[]{:S(2)}, u32[]{:S(2)}) %collective-permute-start.9) | collective-permute-done | bytes 1056 | tf_op jit(solution)/shard_map/ppermute | solution.py:39
  121.7 3.4 %collective-permute-start.10 = (f32[2,4,32]{2,1,0:T(4,128)S(1)}, f32[2,4,32]{2,1,0:T(4,128)S(1)}, u32[]{:S(2)}, u32[]{:S(2)}) collective-permute-start(f32[2,4,32]{2,1,0:T(4,128)S(1)} %fusion.92), channel_id=1, source_target_pairs={{0,8},{4,12},{8,0},{12,4},{1,9},{5,13},{9,1},{13,5},{2,10},{6,14},... | collective-permute-start | bytes 3080 | tf_op jit(solution)/shard_map/ppermute | solution.py:39
  125.0 3.6 %collective-permute-done.10 = f32[2,4,32]{2,1,0:T(4,128)S(1)} collective-permute-done((f32[2,4,32]{2,1,0:T(4,128)S(1)}, f32[2,4,32]{2,1,0:T(4,128)S(1)}, u32[]{:S(2)}, u32[]{:S(2)}) %collective-permute-start.10) | collective-permute-done | bytes 1056 | tf_op jit(solution)/shard_map/ppermute | solution.py:39
  128.7 2.8 %collective-permute-start.11 = (f32[2,4,32]{2,1,0:T(4,128)S(1)}, f32[2,4,32]{2,1,0:T(4,128)S(1)}, u32[]{:S(2)}, u32[]{:S(2)}) collective-permute-start(f32[2,4,32]{2,1,0:T(4,128)S(1)} %fusion.103), channel_id=1, source_target_pairs={{0,1},{1,0},{2,3},{3,2},{4,5},{5,4},{6,7},{7,6},{8,9},{9,8},{10,11... | collective-permute-start | bytes 3080 | tf_op jit(solution)/shard_map/ppermute | solution.py:39
  131.4 2.7 %collective-permute-done.11 = f32[2,4,32]{2,1,0:T(4,128)S(1)} collective-permute-done((f32[2,4,32]{2,1,0:T(4,128)S(1)}, f32[2,4,32]{2,1,0:T(4,128)S(1)}, u32[]{:S(2)}, u32[]{:S(2)}) %collective-permute-start.11) | collective-permute-done | bytes 1056 | tf_op jit(solution)/shard_map/ppermute | solution.py:39
  134.2 4.0 %collective-permute-start.12 = (f32[2,4,32]{2,1,0:T(4,128)S(1)}, f32[2,4,32]{2,1,0:T(4,128)S(1)}, u32[]{:S(2)}, u32[]{:S(2)}) collective-permute-start(f32[2,4,32]{2,1,0:T(4,128)S(1)} %add.150), channel_id=1, source_target_pairs={{0,2},{1,3},{2,0},{3,1},{4,6},{5,7},{6,4},{7,5},{8,10},{9,11},{10,... | collective-permute-start | bytes 3080 | tf_op jit(solution)/shard_map/ppermute | solution.py:39
  138.2 3.0 %collective-permute-done.12 = f32[2,4,32]{2,1,0:T(4,128)S(1)} collective-permute-done((f32[2,4,32]{2,1,0:T(4,128)S(1)}, f32[2,4,32]{2,1,0:T(4,128)S(1)}, u32[]{:S(2)}, u32[]{:S(2)}) %collective-permute-start.12) | collective-permute-done | bytes 1056 | tf_op jit(solution)/shard_map/ppermute | solution.py:39
  141.3 1.9 collective-permute-start.13
  143.2 1.2 collective-permute-done.13
  144.5 3.7 %collective-permute-start.14 = (f32[32,4,64]{2,1,0:T(4,128)S(1)}, f32[32,4,64]{2,1,0:T(4,128)S(1)}, u32[]{:S(2)}, u32[]{:S(2)}) collective-permute-start(f32[32,4,64]{2,1,0:T(4,128)S(1)} %add_dynamic-update-slice_fusion), channel_id=1, source_target_pairs={{0,32},{16,48},{32,0},{48,16},{64,96},{80,112},{96,64},{112,80},{1... | collective-permute-start | bytes 98312 | tf_op jit(solution)/shard_map/ppermute | solution.py:39
  148.2 15.3 %collective-permute-done.14 = f32[32,4,64]{2,1,0:T(4,128)S(1)} collective-permute-done((f32[32,4,64]{2,1,0:T(4,128)S(1)}, f32[32,4,64]{2,1,0:T(4,128)S(1)}, u32[]{:S(2)}, u32[]{:S(2)}) %collective-permute-start.14) | collective-permute-done | bytes 32800 | tf_op jit(solution)/shard_map/ppermute | solution.py:39
  163.5 4.5 %collective-permute-start.15 = (f32[32,4,64]{2,1,0:T(4,128)S(1)}, f32[32,4,64]{2,1,0:T(4,128)S(1)}, u32[]{:S(2)}, u32[]{:S(2)}) collective-permute-start(f32[32,4,64]{2,1,0:T(4,128)S(1)} %add.155), channel_id=1, source_target_pairs={{0,64},{16,80},{32,96},{48,112},{64,0},{80,16},{96,32},{112,48},{1... | collective-permute-start | bytes 98312 | tf_op jit(solution)/shard_map/ppermute | solution.py:39
  168.1 3.8 %collective-permute-done.15 = f32[32,4,64]{2,1,0:T(4,128)S(1)} collective-permute-done((f32[32,4,64]{2,1,0:T(4,128)S(1)}, f32[32,4,64]{2,1,0:T(4,128)S(1)}, u32[]{:S(2)}, u32[]{:S(2)}) %collective-permute-start.15) | collective-permute-done | bytes 32800 | tf_op jit(solution)/shard_map/ppermute | solution.py:39
  171.9 7.2 %collective-permute-start.16 = (f32[32,4,64]{2,1,0:T(4,128)S(1)}, f32[32,4,64]{2,1,0:T(4,128)S(1)}, u32[]{:S(2)}, u32[]{:S(2)}) collective-permute-start(f32[32,4,64]{2,1,0:T(4,128)S(1)} %add.156), channel_id=1, source_target_pairs={{0,128},{16,144},{32,160},{48,176},{64,192},{80,208},{96,224},{112... | collective-permute-start | bytes 98312 | tf_op jit(solution)/shard_map/ppermute | solution.py:39
  179.1 5.0 %collective-permute-done.16 = f32[32,4,64]{2,1,0:T(4,128)S(1)} collective-permute-done((f32[32,4,64]{2,1,0:T(4,128)S(1)}, f32[32,4,64]{2,1,0:T(4,128)S(1)}, u32[]{:S(2)}, u32[]{:S(2)}) %collective-permute-start.16) | collective-permute-done | bytes 32800 | tf_op jit(solution)/shard_map/ppermute | solution.py:39
  184.1 12.5 %collective-permute-start.17 = (f32[32,4,64]{2,1,0:T(4,128)S(1)}, f32[32,4,64]{2,1,0:T(4,128)S(1)}, u32[]{:S(2)}, u32[]{:S(2)}) collective-permute-start(f32[32,4,64]{2,1,0:T(4,128)S(1)} %add.157), channel_id=1, source_target_pairs={{0,256},{16,272},{32,288},{48,304},{64,320},{80,336},{96,352},{112... | collective-permute-start | bytes 98312 | tf_op jit(solution)/shard_map/ppermute | solution.py:39
  196.6 2.6 %collective-permute-done.17 = f32[32,4,64]{2,1,0:T(4,128)S(1)} collective-permute-done((f32[32,4,64]{2,1,0:T(4,128)S(1)}, f32[32,4,64]{2,1,0:T(4,128)S(1)}, u32[]{:S(2)}, u32[]{:S(2)}) %collective-permute-start.17) | collective-permute-done | bytes 32800 | tf_op jit(solution)/shard_map/ppermute | solution.py:39
  200.1 4.6 %convolution_convert_fusion = bf16[128,16,768]{2,0,1:T(8,128)(2,1)} fusion(f32[128,16,256]{2,1,0:T(8,128)S(1)} %bitcast_convert_fusion, f32[256]{0:T(256)S(1)} %bitcast.155, f32[128,256]{1,0:T(8,128)S(1)} %copy.42, f32[128,256]{1,0:T(8,128)S(1)} %copy.40, bf16[256,4096]{1,0:T(8,128)(2,1)} %all-gather.2.cloned.1.call-done), kind=kOutput, calls=%fused_computation.7 | convolution fusion | flops 808976384 | bytes 5899264 | tf_op jit(solution)/shard_map/fpc,cd->fpd/dot_general | solution.py:133
  204.8 2.1 fusion.97
  206.9 3.9 %fusion.31 = bf16[1,1,16,128,256]{4,3,2,1,0:T(8,128)(2,1)} fusion(f32[128,16,256]{2,1,0:T(8,128)S(1)} %bitcast_convert_fusion, bf16[128,16,768]{2,0,1:T(8,128)(2,1)} %convolution_convert_fusion, f32[16,128,128]{1,2,0:T(8,128)S(1)} %get-tuple-element.24, f32[16,128]{1,0:T(8,128)S(1)} %get-tuple-element.23, bf16[256,4096]{1,0:T(8,128)(2,1)} %all-gather.2.cloned.1.call-done), kind=kOutput, calls=%fused_computation.39 | convolution fusion | flops 404750336 | bytes 5382144 | tf_op jit(solution)/shard_map/axi,iy->axy/dot_general | solution.py:151
  (79 shorter events, 12.8 us)
Async XLA Ops:
  6.5 33.0 %copy-start.1 = (bf16[4,16,32,256]{3,2,1,0:T(8,128)(2,1)S(1)}, bf16[4,16,32,256]{3,2,1,0:T(8,128)(2,1)}, u32[]{:S(2)}) copy-start(bf16[4,16,32,256]{3,2,1,0:T(8,128)(2,1)} %param.7) | copy-start | bytes 3145732
  6.5 68.5 %all-gather.2.cloned.1.call-start = ((), (), s32[]{:S(2)}) async-start(), calls=%async_computation.1 | async-start | bytes 2228224 | tf_op jit(solution)/shard_map/all_gather | solution.py:79
  10.2 5.5 %collective-permute-start = (f32[2,4,32]{2,1,0:T(4,128)S(1)}, f32[2,4,32]{2,1,0:T(4,128)S(1)}, u32[]{:S(2)}, u32[]{:S(2)}) collective-permute-start(f32[2,4,32]{2,1,0:T(4,128)S(1)} %pad_maximum_fusion.6), channel_id=1, source_target_pairs={{0,4},{4,0},{8,12},{12,8},{1,5},{5,1},{9,13},{13,9},{2,6},{6,2},{1... | collective-permute-start | bytes 3080 | tf_op jit(solution)/shard_map/ppermute | solution.py:39
  15.7 7.0 %collective-permute-start.1 = (f32[2,4,32]{2,1,0:T(4,128)S(1)}, f32[2,4,32]{2,1,0:T(4,128)S(1)}, u32[]{:S(2)}, u32[]{:S(2)}) collective-permute-start(f32[2,4,32]{2,1,0:T(4,128)S(1)} %fusion.93), channel_id=1, source_target_pairs={{0,8},{4,12},{8,0},{12,4},{1,9},{5,13},{9,1},{13,5},{2,10},{6,14},... | collective-permute-start | bytes 3080 | tf_op jit(solution)/shard_map/ppermute | solution.py:39
  22.7 9.4 %collective-permute-start.2 = (f32[2,4,32]{2,1,0:T(4,128)S(1)}, f32[2,4,32]{2,1,0:T(4,128)S(1)}, u32[]{:S(2)}, u32[]{:S(2)}) collective-permute-start(f32[2,4,32]{2,1,0:T(4,128)S(1)} %fusion.104), channel_id=1, source_target_pairs={{0,1},{1,0},{2,3},{3,2},{4,5},{5,4},{6,7},{7,6},{8,9},{9,8},{10,11... | collective-permute-start | bytes 3080 | tf_op jit(solution)/shard_map/ppermute | solution.py:39
  32.0 7.1 %collective-permute-start.3 = (f32[2,4,32]{2,1,0:T(4,128)S(1)}, f32[2,4,32]{2,1,0:T(4,128)S(1)}, u32[]{:S(2)}, u32[]{:S(2)}) collective-permute-start(f32[2,4,32]{2,1,0:T(4,128)S(1)} %add.129), channel_id=1, source_target_pairs={{0,2},{1,3},{2,0},{3,1},{4,6},{5,7},{6,4},{7,5},{8,10},{9,11},{10,... | collective-permute-start | bytes 3080 | tf_op jit(solution)/shard_map/ppermute | solution.py:39
  40.2 3.7 %collective-permute-start.4 = (bf16[4,1,32,256]{3,2,1,0:T(8,128)(2,1)S(1)}, bf16[4,1,32,256]{3,2,1,0:T(8,128)(2,1)S(1)}, u32[]{:S(2)}, u32[]{:S(2)}) collective-permute-start(bf16[4,1,32,256]{3,2,1,0:T(8,128)(2,1)S(1)} %get-tuple-element.13), channel_id=1, source_target_pairs={{0,4},{4,8},{8,12},{1,5},{5,9},{9,13},{2,6},{6,10},{10,14},{3,7},{... | collective-permute-start | bytes 196616 | tf_op jit(solution)/shard_map/ppermute | solution.py:21
  42.1 6.2 %collective-permute-start.5 = (bf16[4,1,32,256]{3,2,1,0:T(8,128)(2,1)S(1)}, bf16[4,1,32,256]{3,2,1,0:T(8,128)(2,1)S(1)}, u32[]{:S(2)}, u32[]{:S(2)}) collective-permute-start(bf16[4,1,32,256]{3,2,1,0:T(8,128)(2,1)S(1)} %get-tuple-element.14), channel_id=1, source_target_pairs={{4,0},{8,4},{12,8},{5,1},{9,5},{13,9},{6,2},{10,6},{14,10},{7,3},{... | collective-permute-start | bytes 196616 | tf_op jit(solution)/shard_map/ppermute | solution.py:22
  48.3 6.2 %collective-permute-start.6 = (bf16[4,18,1,256]{3,2,1,0:T(2,128)(2,1)S(1)}, bf16[4,18,1,256]{3,2,1,0:T(2,128)(2,1)S(1)}, u32[]{:S(2)}, u32[]{:S(2)}) collective-permute-start(bf16[4,18,1,256]{3,2,1,0:T(2,128)(2,1)S(1)} %get-tuple-element.12), channel_id=1, source_target_pairs={{0,1},{1,2},{2,3},{4,5},{5,6},{6,7},{8,9},{9,10},{10,11},{12,13},{... | collective-permute-start | bytes 110600 | tf_op jit(solution)/shard_map/ppermute | solution.py:21
  50.3 6.2 %collective-permute-start.7 = (bf16[4,18,1,256]{3,2,1,0:T(2,128)(2,1)S(1)}, bf16[4,18,1,256]{3,2,1,0:T(2,128)(2,1)S(1)}, u32[]{:S(2)}, u32[]{:S(2)}) collective-permute-start(bf16[4,18,1,256]{3,2,1,0:T(2,128)(2,1)S(1)} %get-tuple-element.11), channel_id=1, source_target_pairs={{1,0},{2,1},{3,2},{5,4},{6,5},{7,6},{9,8},{10,9},{11,10},{13,12},{... | collective-permute-start | bytes 110600 | tf_op jit(solution)/shard_map/ppermute | solution.py:22
  75.1 1.7 copy-start.3
  76.7 1.4 copy-start
  80.8 2.5 %copy-start.4 = (s32[16]{0:T(128)S(1)}, s32[16]{0:T(128)}, u32[]{:S(2)}) copy-start(s32[16]{0:T(128)} %param.8) | copy-start | bytes 196
  81.9 2.8 %collective-permute-start.8 = (bf16[2,16,32,256]{3,2,1,0:T(8,128)(2,1)S(1)}, bf16[2,16,32,256]{3,2,1,0:T(8,128)(2,1)S(1)}, u32[]{:S(2)}, u32[]{:S(2)}) collective-permute-start(bf16[2,16,32,256]{3,2,1,0:T(8,128)(2,1)S(1)} %slice.193), channel_id=1, source_target_pairs={{0,16},{16,32},{32,48},{48,64},{64,80},{80,96},{96,112},{112,128},... | collective-permute-start | bytes 1572872 | tf_op jit(solution)/shard_map/ppermute | solution.py:30
  89.8 1.4 copy-start.2
  94.1 105.6 %all-to-all-start = ((bf16[32,4,16,256]{3,2,1,0:T(8,128)(2,1)}), bf16[32,4,16,256]{3,2,1,0:T(8,128)(2,1)S(1)}, u32[]{:S(2)}, u32[]{:S(2)}) async-start(bf16[32,4,16,256]{3,2,1,0:T(8,128)(2,1)} %bitcast.140), calls=%async_computation | async-start | bytes 2097152 | tf_op jit(solution)/shard_map/all_to_all | solution.py:124
  116.2 5.5 %collective-permute-start.9 = (f32[2,4,32]{2,1,0:T(4,128)S(1)}, f32[2,4,32]{2,1,0:T(4,128)S(1)}, u32[]{:S(2)}, u32[]{:S(2)}) collective-permute-start(f32[2,4,32]{2,1,0:T(4,128)S(1)} %pad_maximum_fusion.7), channel_id=1, source_target_pairs={{0,4},{4,0},{8,12},{12,8},{1,5},{5,1},{9,13},{13,9},{2,6},{6,2},{1... | collective-permute-start | bytes 3080 | tf_op jit(solution)/shard_map/ppermute | solution.py:39
  121.7 7.0 %collective-permute-start.10 = (f32[2,4,32]{2,1,0:T(4,128)S(1)}, f32[2,4,32]{2,1,0:T(4,128)S(1)}, u32[]{:S(2)}, u32[]{:S(2)}) collective-permute-start(f32[2,4,32]{2,1,0:T(4,128)S(1)} %fusion.92), channel_id=1, source_target_pairs={{0,8},{4,12},{8,0},{12,4},{1,9},{5,13},{9,1},{13,5},{2,10},{6,14},... | collective-permute-start | bytes 3080 | tf_op jit(solution)/shard_map/ppermute | solution.py:39
  128.7 5.5 %collective-permute-start.11 = (f32[2,4,32]{2,1,0:T(4,128)S(1)}, f32[2,4,32]{2,1,0:T(4,128)S(1)}, u32[]{:S(2)}, u32[]{:S(2)}) collective-permute-start(f32[2,4,32]{2,1,0:T(4,128)S(1)} %fusion.103), channel_id=1, source_target_pairs={{0,1},{1,0},{2,3},{3,2},{4,5},{5,4},{6,7},{7,6},{8,9},{9,8},{10,11... | collective-permute-start | bytes 3080 | tf_op jit(solution)/shard_map/ppermute | solution.py:39
  134.2 7.0 %collective-permute-start.12 = (f32[2,4,32]{2,1,0:T(4,128)S(1)}, f32[2,4,32]{2,1,0:T(4,128)S(1)}, u32[]{:S(2)}, u32[]{:S(2)}) collective-permute-start(f32[2,4,32]{2,1,0:T(4,128)S(1)} %add.150), channel_id=1, source_target_pairs={{0,2},{1,3},{2,0},{3,1},{4,6},{5,7},{6,4},{7,5},{8,10},{9,11},{10,... | collective-permute-start | bytes 3080 | tf_op jit(solution)/shard_map/ppermute | solution.py:39
  141.3 3.1 %collective-permute-start.13 = (f32[32,4,64]{2,1,0:T(4,128)S(1)}, f32[32,4,64]{2,1,0:T(4,128)S(1)}, u32[]{:S(2)}, u32[]{:S(2)}) collective-permute-start(f32[32,4,64]{2,1,0:T(4,128)S(1)} %constant_dynamic-update-slice_fusion), channel_id=1, source_target_pairs={{0,16},{16,0},{32,48},{48,32},{64,80},{80,64},{96,112},{112,96},{1... | collective-permute-start | bytes 98312 | tf_op jit(solution)/shard_map/ppermute | solution.py:39
  144.5 19.0 %collective-permute-start.14 = (f32[32,4,64]{2,1,0:T(4,128)S(1)}, f32[32,4,64]{2,1,0:T(4,128)S(1)}, u32[]{:S(2)}, u32[]{:S(2)}) collective-permute-start(f32[32,4,64]{2,1,0:T(4,128)S(1)} %add_dynamic-update-slice_fusion), channel_id=1, source_target_pairs={{0,32},{16,48},{32,0},{48,16},{64,96},{80,112},{96,64},{112,80},{1... | collective-permute-start | bytes 98312 | tf_op jit(solution)/shard_map/ppermute | solution.py:39
  163.5 8.3 %collective-permute-start.15 = (f32[32,4,64]{2,1,0:T(4,128)S(1)}, f32[32,4,64]{2,1,0:T(4,128)S(1)}, u32[]{:S(2)}, u32[]{:S(2)}) collective-permute-start(f32[32,4,64]{2,1,0:T(4,128)S(1)} %add.155), channel_id=1, source_target_pairs={{0,64},{16,80},{32,96},{48,112},{64,0},{80,16},{96,32},{112,48},{1... | collective-permute-start | bytes 98312 | tf_op jit(solution)/shard_map/ppermute | solution.py:39
  171.9 12.2 %collective-permute-start.16 = (f32[32,4,64]{2,1,0:T(4,128)S(1)}, f32[32,4,64]{2,1,0:T(4,128)S(1)}, u32[]{:S(2)}, u32[]{:S(2)}) collective-permute-start(f32[32,4,64]{2,1,0:T(4,128)S(1)} %add.156), channel_id=1, source_target_pairs={{0,128},{16,144},{32,160},{48,176},{64,192},{80,208},{96,224},{112... | collective-permute-start | bytes 98312 | tf_op jit(solution)/shard_map/ppermute | solution.py:39
  184.1 15.1 %collective-permute-start.17 = (f32[32,4,64]{2,1,0:T(4,128)S(1)}, f32[32,4,64]{2,1,0:T(4,128)S(1)}, u32[]{:S(2)}, u32[]{:S(2)}) collective-permute-start(f32[32,4,64]{2,1,0:T(4,128)S(1)} %add.157), channel_id=1, source_target_pairs={{0,256},{16,272},{32,288},{48,304},{64,320},{80,336},{96,352},{112... | collective-permute-start | bytes 98312 | tf_op jit(solution)/shard_map/ppermute | solution.py:39
Sparse Core Ops, SparseCore 0:
  10.3 64.6 all-gather.1

commit v4 on v3

--- a/solution.py
+++ b/solution.py
@@ -125,9 +125,9 @@
     resid_time = received.reshape(total_frames, group_pixels, chans)
     mean_two, scale_two = group_moments(resid)
     mine = jnp.concatenate([mean_two, scale_two], axis=1)
-    placed = jnp.zeros((ranks, frames, 2 * GROUPS), jnp.float32)
-    placed = lax.dynamic_update_index_in_dim(placed, mine, lax.axis_index("tm"), 0)
-    moments = butterfly_sum(placed, ("tm",)).reshape(total_frames, 2 * GROUPS)
+    big = jnp.pad(mine, ((0, 8 - frames), (0, 1024 - 2 * GROUPS)))
+    moments = lax.all_gather(big, "tm", axis=0, tiled=True).reshape(ranks, 8, 1024)[:, :frames, : 2 * GROUPS]
+    moments = moments.reshape(total_frames, 2 * GROUPS)
     mean_all, scale_all = moments[:, :GROUPS], moments[:, GROUPS:]
     flat_norm = apply_norm(resid_time, mean_all, scale_all, norm_gains[1]).astype(jnp.bfloat16)
     qkv_time = jnp.einsum(

time: 219 us -> 234 us (1.068)
  the two profiles are of different devices: /device:TPU:2 before, /device:TPU:1 now
where the time goes in v4:
time: 234 us; the launch traced here: 233 us
  waiting for transfers between devices  123 us (53%)
  starting transfers between devices  59.3 us (25%)
  matrix products  24.5 us (10%)
  between operations  13.8 us (6%)
  other arithmetic  7.72 us (3%)
  local copies, waits for them, and re-layouts  5.18 us (2%)
    all_gather x1, waiting for transfers between devices, body(): lax.all_gather(big, 'tm', axis=0, tiled=True).reshape(ranks, 8, 1024)  73.9 us
    ppermute x8, starting transfers between devices, butterfly_sum(): x = x + lax.ppermute(x, axis, pairs)  29.9 us
    all_gather x1, waiting for transfers between devices, body(): gathered = lax.all_gather(packed, ('band', 'fsdp'), axis=0, tiled=True)  23.3 us
    all_to_all x1, starting transfers between devices, body(): lax.all_to_all(flat_resid, 'tm', split_axis=0, concat_axis=0, tiled=True)  15.1 us
    ppermute x8, waiting for transfers between devices, butterfly_sum(): x = x + lax.ppermute(x, axis, pairs)  12 us
    ppermute x2, waiting for transfers between devices, with_halo(): after = lax.ppermute(initial, axis, down)  7.84 us
    ppermute x2, starting transfers between devices, with_halo(): before = lax.ppermute(last, axis, up)  6.45 us
    dot_general x9, matrix products, body(): jnp.einsum('fhwc,cd->fhwd', padded[:, shift_y:shift_y + height, shift_x:s...  5.7 us
  transfers between devices with their start and end apart: 16, of which 14 were waited for; matrix products, arithmetic and copies ran while one was open for 4% of the time, Pallas kernels for 0%

profile of v4, /device:TPU:1, one launch (start us, length us, event | category | flops | bytes accessed | tf_op | source)
XLA Modules:
  0.0 233.3 jit_solution(3845554850148898094)
XLA Ops:
  6.5 1.7 pad_maximum_fusion.2
  8.3 1.5 convert_reduce_fusion
  10.2 4.0 %collective-permute-start = (f32[2,4,32]{2,1,0:T(4,128)S(1)}, f32[2,4,32]{2,1,0:T(4,128)S(1)}, u32[]{:S(2)}, u32[]{:S(2)}) collective-permute-start(f32[2,4,32]{2,1,0:T(4,128)S(1)} %pad_maximum_fusion.6), channel_id=1, source_target_pairs={{0,4},{4,0},{8,12},{12,8},{1,5},{5,1},{9,13},{13,9},{2,6},{6,2},{1... | collective-permute-start | bytes 3080 | tf_op jit(solution)/shard_map/ppermute | solution.py:39
  14.2 1.0 collective-permute-done
  15.2 5.0 %collective-permute-start.1 = (f32[2,4,32]{2,1,0:T(4,128)S(1)}, f32[2,4,32]{2,1,0:T(4,128)S(1)}, u32[]{:S(2)}, u32[]{:S(2)}) collective-permute-start(f32[2,4,32]{2,1,0:T(4,128)S(1)} %fusion.93), channel_id=1, source_target_pairs={{0,8},{4,12},{8,0},{12,4},{1,9},{5,13},{9,1},{13,5},{2,10},{6,14},... | collective-permute-start | bytes 3080 | tf_op jit(solution)/shard_map/ppermute | solution.py:39
  20.2 1.0 collective-permute-done.1
  21.2 3.2 %collective-permute-start.2 = (f32[2,4,32]{2,1,0:T(4,128)S(1)}, f32[2,4,32]{2,1,0:T(4,128)S(1)}, u32[]{:S(2)}, u32[]{:S(2)}) collective-permute-start(f32[2,4,32]{2,1,0:T(4,128)S(1)} %fusion.104), channel_id=1, source_target_pairs={{0,1},{1,0},{2,3},{3,2},{4,5},{5,4},{6,7},{7,6},{8,9},{9,8},{10,11... | collective-permute-start | bytes 3080 | tf_op jit(solution)/shard_map/ppermute | solution.py:39
  24.3 1.2 collective-permute-done.2
  25.5 4.7 %collective-permute-start.3 = (f32[2,4,32]{2,1,0:T(4,128)S(1)}, f32[2,4,32]{2,1,0:T(4,128)S(1)}, u32[]{:S(2)}, u32[]{:S(2)}) collective-permute-start(f32[2,4,32]{2,1,0:T(4,128)S(1)} %add.111), channel_id=1, source_target_pairs={{0,2},{1,3},{2,0},{3,1},{4,6},{5,7},{6,4},{7,5},{8,10},{9,11},{10,... | collective-permute-start | bytes 3080 | tf_op jit(solution)/shard_map/ppermute | solution.py:39
  30.2 0.8 fusion.96
  31.8 0.7 fusion.16
  32.4 3.2 %collective-permute-start.4 = (bf16[4,1,32,256]{3,2,1,0:T(8,128)(2,1)S(1)}, bf16[4,1,32,256]{3,2,1,0:T(8,128)(2,1)S(1)}, u32[]{:S(2)}, u32[]{:S(2)}) collective-permute-start(bf16[4,1,32,256]{3,2,1,0:T(8,128)(2,1)S(1)} %get-tuple-element.13), channel_id=1, source_target_pairs={{0,4},{4,8},{8,12},{1,5},{5,9},{9,13},{2,6},{6,10},{10,14},{3,7},{... | collective-permute-start | bytes 196616 | tf_op jit(solution)/shard_map/ppermute | solution.py:21
  35.7 1.3 collective-permute-start.5
  37.0 4.1 %collective-permute-done.5 = bf16[4,1,32,256]{3,2,1,0:T(8,128)(2,1)S(1)} collective-permute-done((bf16[4,1,32,256]{3,2,1,0:T(8,128)(2,1)S(1)}, bf16[4,1,32,256]{3,2,1,0:T(8,128)(2,1)S(1)}, u32[]{:S(2)}, u32[]{:S(2)}) %collective-permute-start.5) | collective-permute-done | bytes 65568 | tf_op jit(solution)/shard_map/ppermute | solution.py:22
  41.3 3.2 %collective-permute-start.6 = (bf16[4,18,1,256]{3,2,1,0:T(2,128)(2,1)S(1)}, bf16[4,18,1,256]{3,2,1,0:T(2,128)(2,1)S(1)}, u32[]{:S(2)}, u32[]{:S(2)}) collective-permute-start(bf16[4,18,1,256]{3,2,1,0:T(2,128)(2,1)S(1)} %get-tuple-element.12), channel_id=1, source_target_pairs={{0,1},{1,2},{2,3},{4,5},{5,6},{6,7},{8,9},{9,10},{10,11},{12,13},{... | collective-permute-start | bytes 110600 | tf_op jit(solution)/shard_map/ppermute | solution.py:21
  44.5 1.3 collective-permute-start.7
  45.9 3.7 %collective-permute-done.7 = bf16[4,18,1,256]{3,2,1,0:T(2,128)(2,1)S(1)} collective-permute-done((bf16[4,18,1,256]{3,2,1,0:T(2,128)(2,1)S(1)}, bf16[4,18,1,256]{3,2,1,0:T(2,128)(2,1)S(1)}, u32[]{:S(2)}, u32[]{:S(2)}) %collective-permute-start.7) | collective-permute-done | bytes 36896 | tf_op jit(solution)/shard_map/ppermute | solution.py:22
  49.6 1.8 pad_maximum_fusion.1
  51.3 23.3 %all-gather.3.cloned.1.call-done = bf16[256,4096]{1,0:T(8,128)(2,1)} async-done(((bf16[16,4096]{1,0:T(8,128)(2,1)}), bf16[256,4096]{1,0:T(8,128)(2,1)}) %all-gather.3.cloned.1.call-update) | async-done | bytes 2097168 | tf_op jit(solution)/shard_map/all_gather | solution.py:79
  74.7 1.5 fusion.51
  76.3 0.4 fusion.55
  76.8 0.9 copy-done
  78.6 0.4 fusion.49
  80.4 1.1 add_convert_fusion
  81.5 5.3 %collective-permute-start.8 = (bf16[2,16,32,256]{3,2,1,0:T(8,128)(2,1)S(1)}, bf16[2,16,32,256]{3,2,1,0:T(8,128)(2,1)S(1)}, u32[]{:S(2)}, u32[]{:S(2)}) collective-permute-start(bf16[2,16,32,256]{3,2,1,0:T(8,128)(2,1)S(1)} %slice.197), channel_id=1, source_target_pairs={{0,16},{16,32},{32,48},{48,64},{64,80},{80,96},{96,112},{112,128},... | collective-permute-start | bytes 1572872 | tf_op jit(solution)/shard_map/ppermute | solution.py:30
  87.2 5.7 %collective-permute-done.8 = bf16[2,16,32,256]{3,2,1,0:T(8,128)(2,1)S(1)} collective-permute-done((bf16[2,16,32,256]{3,2,1,0:T(8,128)(2,1)S(1)}, bf16[2,16,32,256]{3,2,1,0:T(8,128)(2,1)S(1)}, u32[]{:S(2)}, u32[]{:S(2)}) %collective-permute-start.8) | collective-permute-done | bytes 524320 | tf_op jit(solution)/shard_map/ppermute | solution.py:30
  93.0 1.2 fusion.22
  94.2 1.2 fusion.19
  95.4 1.2 fusion.25
  96.6 1.3 fusion.60
  98.0 1.4 fusion.62
  99.4 1.7 convert_reduce_fusion.1
  101.2 1.1 copy.89
  102.3 15.1 %all-to-all-start = ((bf16[32,4,16,256]{3,2,1,0:T(8,128)(2,1)}), bf16[32,4,16,256]{3,2,1,0:T(8,128)(2,1)S(1)}, u32[]{:S(2)}, u32[]{:S(2)}) async-start(bf16[32,4,16,256]{3,2,1,0:T(8,128)(2,1)} %bitcast.135), calls=%async_computation | async-start | bytes 2097152 | tf_op jit(solution)/shard_map/all_to_all | solution.py:124
  117.8 2.8 %collective-permute-start.9 = (f32[2,4,32]{2,1,0:T(4,128)S(1)}, f32[2,4,32]{2,1,0:T(4,128)S(1)}, u32[]{:S(2)}, u32[]{:S(2)}) collective-permute-start(f32[2,4,32]{2,1,0:T(4,128)S(1)} %pad_maximum_fusion.7), channel_id=1, source_target_pairs={{0,4},{4,0},{8,12},{12,8},{1,5},{5,1},{9,13},{13,9},{2,6},{6,2},{1... | collective-permute-start | bytes 3080 | tf_op jit(solution)/shard_map/ppermute | solution.py:39
  120.6 1.8 collective-permute-done.9
  122.5 3.7 %collective-permute-start.10 = (f32[2,4,32]{2,1,0:T(4,128)S(1)}, f32[2,4,32]{2,1,0:T(4,128)S(1)}, u32[]{:S(2)}, u32[]{:S(2)}) collective-permute-start(f32[2,4,32]{2,1,0:T(4,128)S(1)} %fusion.92), channel_id=1, source_target_pairs={{0,8},{4,12},{8,0},{12,4},{1,9},{5,13},{9,1},{13,5},{2,10},{6,14},... | collective-permute-start | bytes 3080 | tf_op jit(solution)/shard_map/ppermute | solution.py:39
  126.2 2.4 %collective-permute-done.10 = f32[2,4,32]{2,1,0:T(4,128)S(1)} collective-permute-done((f32[2,4,32]{2,1,0:T(4,128)S(1)}, f32[2,4,32]{2,1,0:T(4,128)S(1)}, u32[]{:S(2)}, u32[]{:S(2)}) %collective-permute-start.10) | collective-permute-done | bytes 1056 | tf_op jit(solution)/shard_map/ppermute | solution.py:39
  128.6 2.8 %collective-permute-start.11 = (f32[2,4,32]{2,1,0:T(4,128)S(1)}, f32[2,4,32]{2,1,0:T(4,128)S(1)}, u32[]{:S(2)}, u32[]{:S(2)}) collective-permute-start(f32[2,4,32]{2,1,0:T(4,128)S(1)} %fusion.103), channel_id=1, source_target_pairs={{0,1},{1,0},{2,3},{3,2},{4,5},{5,4},{6,7},{7,6},{8,9},{9,8},{10,11... | collective-permute-start | bytes 3080 | tf_op jit(solution)/shard_map/ppermute | solution.py:39
  131.4 1.8 collective-permute-done.11
  133.2 3.7 %collective-permute-start.12 = (f32[2,4,32]{2,1,0:T(4,128)S(1)}, f32[2,4,32]{2,1,0:T(4,128)S(1)}, u32[]{:S(2)}, u32[]{:S(2)}) collective-permute-start(f32[2,4,32]{2,1,0:T(4,128)S(1)} %add.132), channel_id=1, source_target_pairs={{0,2},{1,3},{2,0},{3,1},{4,6},{5,7},{6,4},{7,5},{8,10},{9,11},{10,... | collective-permute-start | bytes 3080 | tf_op jit(solution)/shard_map/ppermute | solution.py:39
  137.0 2.4 %collective-permute-done.12 = f32[2,4,32]{2,1,0:T(4,128)S(1)} collective-permute-done((f32[2,4,32]{2,1,0:T(4,128)S(1)}, f32[2,4,32]{2,1,0:T(4,128)S(1)}, u32[]{:S(2)}, u32[]{:S(2)}) %collective-permute-start.12) | collective-permute-done | bytes 1056 | tf_op jit(solution)/shard_map/ppermute | solution.py:39
  139.4 0.7 select_maximum_fusion
  140.1 73.9 %all-gather.5.cloned.1.call-done = f32[256,1024]{1,0:T(8,128)} async-done(((f32[8,1024]{1,0:T(8,128)}), f32[256,1024]{1,0:T(8,128)}) %all-gather.5.cloned.1.call-update) | async-done | bytes 1048592 | tf_op jit(solution)/shard_map/all_gather | solution.py:129
  214.0 0.9 slice.203
  215.8 4.6 %convolution_convert_fusion = bf16[128,16,768]{2,0,1:T(8,128)(2,1)} fusion(f32[128,16,256]{2,1,0:T(8,128)S(1)} %bitcast_convert_fusion, f32[256]{0:T(256)S(1)} %bitcast.150, f32[128,256]{1,0:T(8,128)S(1)} %copy.42, f32[128,256]{1,0:T(8,128)S(1)} %copy.40, bf16[256,4096]{1,0:T(8,128)(2,1)} %all-gather.3.cloned.1.call-done), kind=kOutput, calls=%fused_computation.7 | convolution fusion | flops 808976384 | bytes 5899264 | tf_op jit(solution)/shard_map/fpc,cd->fpd/dot_general | solution.py:133
  220.4 2.1 fusion.97
  222.5 3.9 %fusion.31 = bf16[1,1,16,128,256]{4,3,2,1,0:T(8,128)(2,1)} fusion(f32[128,16,256]{2,1,0:T(8,128)S(1)} %bitcast_convert_fusion, bf16[128,16,768]{2,0,1:T(8,128)(2,1)} %convolution_convert_fusion, f32[16,128,128]{1,2,0:T(8,128)S(1)} %get-tuple-element.24, f32[16,128]{1,0:T(8,128)S(1)} %get-tuple-element.23, bf16[256,4096]{1,0:T(8,128)(2,1)} %all-gather.3.cloned.1.call-done), kind=kOutput, calls=%fused_computation.39 | convolution fusion | flops 404750336 | bytes 5382144 | tf_op jit(solution)/shard_map/axi,iy->axy/dot_general | solution.py:151
  (67 shorter events, 5.7 us)
Async XLA Ops:
  6.5 25.2 %copy-start.1 = (bf16[4,16,32,256]{3,2,1,0:T(8,128)(2,1)S(1)}, bf16[4,16,32,256]{3,2,1,0:T(8,128)(2,1)}, u32[]{:S(2)}) copy-start(bf16[4,16,32,256]{3,2,1,0:T(8,128)(2,1)} %param.7) | copy-start | bytes 3145732
  6.5 68.1 %all-gather.3.cloned.1.call-start = ((), (), s32[]{:S(2)}) async-start(), calls=%async_computation.1 | async-start | bytes 2228224 | tf_op jit(solution)/shard_map/all_gather | solution.py:79
  10.2 5.0 %collective-permute-start = (f32[2,4,32]{2,1,0:T(4,128)S(1)}, f32[2,4,32]{2,1,0:T(4,128)S(1)}, u32[]{:S(2)}, u32[]{:S(2)}) collective-permute-start(f32[2,4,32]{2,1,0:T(4,128)S(1)} %pad_maximum_fusion.6), channel_id=1, source_target_pairs={{0,4},{4,0},{8,12},{12,8},{1,5},{5,1},{9,13},{13,9},{2,6},{6,2},{1... | collective-permute-start | bytes 3080 | tf_op jit(solution)/shard_map/ppermute | solution.py:39
  15.2 6.0 %collective-permute-start.1 = (f32[2,4,32]{2,1,0:T(4,128)S(1)}, f32[2,4,32]{2,1,0:T(4,128)S(1)}, u32[]{:S(2)}, u32[]{:S(2)}) collective-permute-start(f32[2,4,32]{2,1,0:T(4,128)S(1)} %fusion.93), channel_id=1, source_target_pairs={{0,8},{4,12},{8,0},{12,4},{1,9},{5,13},{9,1},{13,5},{2,10},{6,14},... | collective-permute-start | bytes 3080 | tf_op jit(solution)/shard_map/ppermute | solution.py:39
  21.2 4.3 %collective-permute-start.2 = (f32[2,4,32]{2,1,0:T(4,128)S(1)}, f32[2,4,32]{2,1,0:T(4,128)S(1)}, u32[]{:S(2)}, u32[]{:S(2)}) collective-permute-start(f32[2,4,32]{2,1,0:T(4,128)S(1)} %fusion.104), channel_id=1, source_target_pairs={{0,1},{1,0},{2,3},{3,2},{4,5},{5,4},{6,7},{7,6},{8,9},{9,8},{10,11... | collective-permute-start | bytes 3080 | tf_op jit(solution)/shard_map/ppermute | solution.py:39
  25.5 5.8 %collective-permute-start.3 = (f32[2,4,32]{2,1,0:T(4,128)S(1)}, f32[2,4,32]{2,1,0:T(4,128)S(1)}, u32[]{:S(2)}, u32[]{:S(2)}) collective-permute-start(f32[2,4,32]{2,1,0:T(4,128)S(1)} %add.111), channel_id=1, source_target_pairs={{0,2},{1,3},{2,0},{3,1},{4,6},{5,7},{6,4},{7,5},{8,10},{9,11},{10,... | collective-permute-start | bytes 3080 | tf_op jit(solution)/shard_map/ppermute | solution.py:39
  32.4 4.6 %collective-permute-start.4 = (bf16[4,1,32,256]{3,2,1,0:T(8,128)(2,1)S(1)}, bf16[4,1,32,256]{3,2,1,0:T(8,128)(2,1)S(1)}, u32[]{:S(2)}, u32[]{:S(2)}) collective-permute-start(bf16[4,1,32,256]{3,2,1,0:T(8,128)(2,1)S(1)} %get-tuple-element.13), channel_id=1, source_target_pairs={{0,4},{4,8},{8,12},{1,5},{5,9},{9,13},{2,6},{6,10},{10,14},{3,7},{... | collective-permute-start | bytes 196616 | tf_op jit(solution)/shard_map/ppermute | solution.py:21
  35.7 5.4 %collective-permute-start.5 = (bf16[4,1,32,256]{3,2,1,0:T(8,128)(2,1)S(1)}, bf16[4,1,32,256]{3,2,1,0:T(8,128)(2,1)S(1)}, u32[]{:S(2)}, u32[]{:S(2)}) collective-permute-start(bf16[4,1,32,256]{3,2,1,0:T(8,128)(2,1)S(1)} %get-tuple-element.14), channel_id=1, source_target_pairs={{4,0},{8,4},{12,8},{5,1},{9,5},{13,9},{6,2},{10,6},{14,10},{7,3},{... | collective-permute-start | bytes 196616 | tf_op jit(solution)/shard_map/ppermute | solution.py:22
  41.3 4.6 %collective-permute-start.6 = (bf16[4,18,1,256]{3,2,1,0:T(2,128)(2,1)S(1)}, bf16[4,18,1,256]{3,2,1,0:T(2,128)(2,1)S(1)}, u32[]{:S(2)}, u32[]{:S(2)}) collective-permute-start(bf16[4,18,1,256]{3,2,1,0:T(2,128)(2,1)S(1)} %get-tuple-element.12), channel_id=1, source_target_pairs={{0,1},{1,2},{2,3},{4,5},{5,6},{6,7},{8,9},{9,10},{10,11},{12,13},{... | collective-permute-start | bytes 110600 | tf_op jit(solution)/shard_map/ppermute | solution.py:21
  44.5 5.1 %collective-permute-start.7 = (bf16[4,18,1,256]{3,2,1,0:T(2,128)(2,1)S(1)}, bf16[4,18,1,256]{3,2,1,0:T(2,128)(2,1)S(1)}, u32[]{:S(2)}, u32[]{:S(2)}) collective-permute-start(bf16[4,18,1,256]{3,2,1,0:T(2,128)(2,1)S(1)} %get-tuple-element.11), channel_id=1, source_target_pairs={{1,0},{2,1},{3,2},{5,4},{6,5},{7,6},{9,8},{10,9},{11,10},{13,12},{... | collective-permute-start | bytes 110600 | tf_op jit(solution)/shard_map/ppermute | solution.py:22
  74.6 1.7 copy-start.3
  76.3 1.4 copy-start
  80.4 6.4 %copy-start.4 = (s32[16]{0:T(128)S(1)}, s32[16]{0:T(128)}, u32[]{:S(2)}) copy-start(s32[16]{0:T(128)} %param.8) | copy-start | bytes 196
  81.5 11.4 %collective-permute-start.8 = (bf16[2,16,32,256]{3,2,1,0:T(8,128)(2,1)S(1)}, bf16[2,16,32,256]{3,2,1,0:T(8,128)(2,1)S(1)}, u32[]{:S(2)}, u32[]{:S(2)}) collective-permute-start(bf16[2,16,32,256]{3,2,1,0:T(8,128)(2,1)S(1)} %slice.197), channel_id=1, source_target_pairs={{0,16},{16,32},{32,48},{48,64},{64,80},{80,96},{96,112},{112,128},... | collective-permute-start | bytes 1572872 | tf_op jit(solution)/shard_map/ppermute | solution.py:30
  98.0 1.4 copy-start.2
  102.3 113.1 %all-to-all-start = ((bf16[32,4,16,256]{3,2,1,0:T(8,128)(2,1)}), bf16[32,4,16,256]{3,2,1,0:T(8,128)(2,1)S(1)}, u32[]{:S(2)}, u32[]{:S(2)}) async-start(bf16[32,4,16,256]{3,2,1,0:T(8,128)(2,1)} %bitcast.135), calls=%async_computation | async-start | bytes 2097152 | tf_op jit(solution)/shard_map/all_to_all | solution.py:124
  117.4 96.7 %all-gather.5.cloned.1.call-start = ((), (), s32[]{:S(2)}) async-start(), calls=%async_computation.2 | async-start | bytes 1081344 | tf_op jit(solution)/shard_map/all_gather | solution.py:129
  117.8 4.6 %collective-permute-start.9 = (f32[2,4,32]{2,1,0:T(4,128)S(1)}, f32[2,4,32]{2,1,0:T(4,128)S(1)}, u32[]{:S(2)}, u32[]{:S(2)}) collective-permute-start(f32[2,4,32]{2,1,0:T(4,128)S(1)} %pad_maximum_fusion.7), channel_id=1, source_target_pairs={{0,4},{4,0},{8,12},{12,8},{1,5},{5,1},{9,13},{13,9},{2,6},{6,2},{1... | collective-permute-start | bytes 3080 | tf_op jit(solution)/shard_map/ppermute | solution.py:39
  122.5 6.1 %collective-permute-start.10 = (f32[2,4,32]{2,1,0:T(4,128)S(1)}, f32[2,4,32]{2,1,0:T(4,128)S(1)}, u32[]{:S(2)}, u32[]{:S(2)}) collective-permute-start(f32[2,4,32]{2,1,0:T(4,128)S(1)} %fusion.92), channel_id=1, source_target_pairs={{0,8},{4,12},{8,0},{12,4},{1,9},{5,13},{9,1},{13,5},{2,10},{6,14},... | collective-permute-start | bytes 3080 | tf_op jit(solution)/shard_map/ppermute | solution.py:39
  128.6 4.6 %collective-permute-start.11 = (f32[2,4,32]{2,1,0:T(4,128)S(1)}, f32[2,4,32]{2,1,0:T(4,128)S(1)}, u32[]{:S(2)}, u32[]{:S(2)}) collective-permute-start(f32[2,4,32]{2,1,0:T(4,128)S(1)} %fusion.103), channel_id=1, source_target_pairs={{0,1},{1,0},{2,3},{3,2},{4,5},{5,4},{6,7},{7,6},{8,9},{9,8},{10,11... | collective-permute-start | bytes 3080 | tf_op jit(solution)/shard_map/ppermute | solution.py:39
  133.2 6.1 %collective-permute-start.12 = (f32[2,4,32]{2,1,0:T(4,128)S(1)}, f32[2,4,32]{2,1,0:T(4,128)S(1)}, u32[]{:S(2)}, u32[]{:S(2)}) collective-permute-start(f32[2,4,32]{2,1,0:T(4,128)S(1)} %add.132), channel_id=1, source_target_pairs={{0,2},{1,3},{2,0},{3,1},{4,6},{5,7},{6,4},{7,5},{8,10},{9,11},{10,... | collective-permute-start | bytes 3080 | tf_op jit(solution)/shard_map/ppermute | solution.py:39
Sparse Core Ops, SparseCore 0:
  10.3 64.2 all-gather.2
  140.2 73.7 all-gather.4

commit v5 on v2

--- a/solution.py
+++ b/solution.py
@@ -41,6 +41,17 @@
     return x
 
 
+def ring_gather(x, axis):
+    size = lax.axis_size(axis)
+    me = lax.axis_index(axis)
+    got = [x]
+    for shift in range(1, size):
+        got.append(lax.ppermute(x, axis, [(i, (i + shift) % size) for i in range(size)]))
+    order = jnp.stack(got[::-1] + got[::-1])
+    blocks = lax.dynamic_slice_in_dim(order, (size - 1 - me) % size, size, axis=0)
+    return blocks.reshape((size * x.shape[0],) + x.shape[1:])
+
+
 def frame_starts(clip_lengths, total):
     ends = jnp.cumsum(clip_lengths)
     begins = ends - clip_lengths
@@ -76,7 +87,7 @@
     frames, height, width, chans = video.shape
     widths = [w.shape[1] for w in (spatial_kernel_weight, w_time, w_qkv, w_out)]
     packed = jnp.concatenate([spatial_kernel_weight, w_time, w_qkv, w_out], axis=1)
-    gathered = lax.all_gather(packed, ("band", "fsdp"), axis=0, tiled=True)
+    gathered = ring_gather(ring_gather(packed, "fsdp"), "band")
     offsets = [sum(widths[:i]) for i in range(4)]
     space_full, time_full, qkv_full, output_complete = [
         gathered[:, o : o + w] for o, w in zip(offsets, widths)

time: 209 us -> 212 us (1.014)
  starting transfers between devices: 59.2 us -> 76.1 us
  between operations: 13.8 us -> 0.62 us
  local copies, waits for them, and re-layouts: 4.26 us -> 6.89 us
    all_gather x1 -> x0, waiting for transfers between devices: 23.3 us -> none  [body(): gathered = lax.all_gather(packed, ('band', 'fsdp'), axis=0, tiled=True)]
    ppermute x0 -> x6, waiting for transfers between devices: none -> 21.3 us  [ring_gather(): lax.ppermute(x, axis, [(i, (i + shift) % size) for i in range(size)])]
    ppermute x0 -> x6, starting transfers between devices: none -> 16.3 us  [ring_gather(): lax.ppermute(x, axis, [(i, (i + shift) % size) for i in range(size)])]
    ppermute x8, starting transfers between devices: 29.9 us -> 24.8 us  [butterfly_sum(): x = x + lax.ppermute(x, axis, pairs)]
    ppermute x8, waiting for transfers between devices: 12 us -> 15.5 us  [butterfly_sum(): x = x + lax.ppermute(x, axis, pairs)]
    all_to_all x1, starting transfers between devices: 15.1 us -> 17.4 us  [body(): lax.all_to_all(flat_resid, 'tm', split_axis=0, concat_axis=0, tiled=True)]
  transfers between devices with their start and end apart: 15 -> 20, of which waited for: 13 -> 11; matrix products, arithmetic and copies ran while one was open for 3% -> 4% of each run, Pallas kernels for 0% -> 0%
where the time goes in v5:
time: 212 us; the launch traced here: 211 us
  starting transfers between devices  76.1 us (36%)
  blocking collectives  49.7 us (23%)
  waiting for transfers between devices  49.1 us (23%)
  matrix products  23.3 us (11%)
  local copies, waits for them, and re-layouts  6.89 us (3%)
  other arithmetic  5.35 us (3%)
    all_gather x1, blocking collectives, body(): lax.all_gather(jnp.concatenate([mean_two, scale_two], axis=1), 'tm', axis...  49.7 us
    ppermute x8, starting transfers between devices, butterfly_sum(): x = x + lax.ppermute(x, axis, pairs)  24.8 us
    ppermute x6, waiting for transfers between devices, ring_gather(): lax.ppermute(x, axis, [(i, (i + shift) % size) for i in range(size)])  21.3 us
    all_to_all x1, starting transfers between devices, body(): lax.all_to_all(flat_resid, 'tm', split_axis=0, concat_axis=0, tiled=True)  17.4 us
    ppermute x6, starting transfers between devices, ring_gather(): lax.ppermute(x, axis, [(i, (i + shift) % size) for i in range(size)])  16.3 us
    ppermute x8, waiting for transfers between devices, butterfly_sum(): x = x + lax.ppermute(x, axis, pairs)  15.5 us
    ppermute x2, starting transfers between devices, with_halo(): before = lax.ppermute(last, axis, up)  7.97 us
    ppermute x1, starting transfers between devices, from_behind(): return lax.ppermute(x, axis, pairs)  7.07 us
  transfers between devices with their start and end apart: 20, of which 11 were waited for; matrix products, arithmetic and copies ran while one was open for 4% of the time, Pallas kernels for 0%

profile of v5, /device:TPU:1, one launch (start us, length us, event | category | flops | bytes accessed | tf_op | source)
XLA Modules:
  0.0 211.1 jit_solution(2255216260325291511)
XLA Ops:
  0.0 1.6 convert_reduce_fusion
  2.0 4.0 %collective-permute-start = (f32[2,4,32]{2,1,0:T(4,128)S(1)}, f32[2,4,32]{2,1,0:T(4,128)S(1)}, u32[]{:S(2)}, u32[]{:S(2)}) collective-permute-start(f32[2,4,32]{2,1,0:T(4,128)S(1)} %pad_maximum_fusion.5), channel_id=1, source_target_pairs={{0,4},{4,0},{8,12},{12,8},{1,5},{5,1},{9,13},{13,9},{2,6},{6,2},{1... | collective-permute-start | bytes 3080 | tf_op jit(solution)/shard_map/ppermute | solution.py:39
  6.0 0.9 constant_dynamic-update-slice_fusion.3
  6.9 0.7 constant_dynamic-update-slice_fusion.2
  8.4 4.5 %collective-permute-start.1 = (f32[2,4,32]{2,1,0:T(4,128)S(1)}, f32[2,4,32]{2,1,0:T(4,128)S(1)}, u32[]{:S(2)}, u32[]{:S(2)}) collective-permute-start(f32[2,4,32]{2,1,0:T(4,128)S(1)} %fusion.93), channel_id=1, source_target_pairs={{0,8},{4,12},{8,0},{12,4},{1,9},{5,13},{9,1},{13,5},{2,10},{6,14},... | collective-permute-start | bytes 3080 | tf_op jit(solution)/shard_map/ppermute | solution.py:39
  13.7 3.1 %collective-permute-start.9 = (bf16[16,4096]{1,0:T(8,128)(2,1)S(1)}, bf16[16,4096]{1,0:T(8,128)(2,1)S(1)}, u32[]{:S(2)}, u32[]{:S(2)}) collective-permute-start(bf16[16,4096]{1,0:T(8,128)(2,1)S(1)} %constant_dynamic-update-slice_fusion), channel_id=1, source_target_pairs={{0,1},{1,2},{2,3},{3,0},{4,5},{5,6},{6,7},{7,4},{8,9},{9,10},{10,1... | collective-permute-start | bytes 393224 | tf_op jit(solution)/shard_map/ppermute | solution.py:49
  16.8 4.4 %collective-permute-start.8 = (bf16[16,4096]{1,0:T(8,128)(2,1)S(1)}, bf16[16,4096]{1,0:T(8,128)(2,1)S(1)}, u32[]{:S(2)}, u32[]{:S(2)}) collective-permute-start(bf16[16,4096]{1,0:T(8,128)(2,1)S(1)} %constant_dynamic-update-slice_fusion), channel_id=1, source_target_pairs={{0,2},{1,3},{2,0},{3,1},{4,6},{5,7},{6,4},{7,5},{8,10},{9,11},{10,... | collective-permute-start | bytes 393224 | tf_op jit(solution)/shard_map/ppermute | solution.py:49
  21.1 3.1 %collective-permute-start.7 = (bf16[16,4096]{1,0:T(8,128)(2,1)S(1)}, bf16[16,4096]{1,0:T(8,128)(2,1)S(1)}, u32[]{:S(2)}, u32[]{:S(2)}) collective-permute-start(bf16[16,4096]{1,0:T(8,128)(2,1)S(1)} %constant_dynamic-update-slice_fusion), channel_id=1, source_target_pairs={{0,3},{1,0},{2,1},{3,2},{4,7},{5,4},{6,5},{7,6},{8,11},{9,8},{10,9... | collective-permute-start | bytes 393224 | tf_op jit(solution)/shard_map/ppermute | solution.py:49
  24.2 2.2 %collective-permute-start.2 = (f32[2,4,32]{2,1,0:T(4,128)S(1)}, f32[2,4,32]{2,1,0:T(4,128)S(1)}, u32[]{:S(2)}, u32[]{:S(2)}) collective-permute-start(f32[2,4,32]{2,1,0:T(4,128)S(1)} %fusion.104), channel_id=1, source_target_pairs={{0,1},{1,0},{2,3},{3,2},{4,5},{5,4},{6,7},{7,6},{8,9},{9,8},{10,11... | collective-permute-start | bytes 3080 | tf_op jit(solution)/shard_map/ppermute | solution.py:39
  26.5 0.8 fusion.96
  27.2 1.7 collective-permute-done.2
  28.9 2.1 %collective-permute-start.3 = (f32[2,4,32]{2,1,0:T(4,128)S(1)}, f32[2,4,32]{2,1,0:T(4,128)S(1)}, u32[]{:S(2)}, u32[]{:S(2)}) collective-permute-start(f32[2,4,32]{2,1,0:T(4,128)S(1)} %add.122), channel_id=1, source_target_pairs={{0,2},{1,3},{2,0},{3,1},{4,6},{5,7},{6,4},{7,5},{8,10},{9,11},{10,... | collective-permute-start | bytes 3080 | tf_op jit(solution)/shard_map/ppermute | solution.py:39
  31.1 3.7 %collective-permute-done.3 = f32[2,4,32]{2,1,0:T(4,128)S(1)} collective-permute-done((f32[2,4,32]{2,1,0:T(4,128)S(1)}, f32[2,4,32]{2,1,0:T(4,128)S(1)}, u32[]{:S(2)}, u32[]{:S(2)}) %collective-permute-start.3) | collective-permute-done | bytes 1056 | tf_op jit(solution)/shard_map/ppermute | solution.py:39
  36.1 1.9 collective-permute-start.10
  38.0 3.4 %collective-permute-start.4 = (bf16[4,1,32,256]{3,2,1,0:T(8,128)(2,1)S(1)}, bf16[4,1,32,256]{3,2,1,0:T(8,128)(2,1)S(1)}, u32[]{:S(2)}, u32[]{:S(2)}) collective-permute-start(bf16[4,1,32,256]{3,2,1,0:T(8,128)(2,1)S(1)} %get-tuple-element.13), channel_id=1, source_target_pairs={{0,4},{4,8},{8,12},{1,5},{5,9},{9,13},{2,6},{6,10},{10,14},{3,7},{... | collective-permute-start | bytes 196616 | tf_op jit(solution)/shard_map/ppermute | solution.py:21
  41.4 1.3 collective-permute-start.5
  42.7 6.1 %collective-permute-done.5 = bf16[4,1,32,256]{3,2,1,0:T(8,128)(2,1)S(1)} collective-permute-done((bf16[4,1,32,256]{3,2,1,0:T(8,128)(2,1)S(1)}, bf16[4,1,32,256]{3,2,1,0:T(8,128)(2,1)S(1)}, u32[]{:S(2)}, u32[]{:S(2)}) %collective-permute-start.5) | collective-permute-done | bytes 65568 | tf_op jit(solution)/shard_map/ppermute | solution.py:22
  48.9 1.3 collective-permute-start.13
  50.2 4.6 %collective-permute-start.6 = (bf16[4,18,1,256]{3,2,1,0:T(2,128)(2,1)S(1)}, bf16[4,18,1,256]{3,2,1,0:T(2,128)(2,1)}, u32[]{:S(2)}, u32[]{:S(2)}) collective-permute-start(bf16[4,18,1,256]{3,2,1,0:T(2,128)(2,1)S(1)} %get-tuple-element.12), channel_id=1, source_target_pairs={{0,1},{1,2},{2,3},{4,5},{5,6},{6,7},{8,9},{9,10},{10,11},{12,13},{... | collective-permute-start | bytes 110600 | tf_op jit(solution)/shard_map/ppermute | solution.py:21
  54.9 0.8 collective-permute-done.6
  55.6 1.6 pad_maximum_fusion.1
  57.2 1.9 collective-permute-start.12
  59.2 1.9 collective-permute-start.11
  61.1 14.6 %collective-permute-done.11 = bf16[64,4096]{1,0:T(8,128)(2,1)S(1)} collective-permute-done((bf16[64,4096]{1,0:T(8,128)(2,1)S(1)}, bf16[64,4096]{1,0:T(8,128)(2,1)S(1)}, u32[]{:S(2)}, u32[]{:S(2)}) %collective-permute-start.11) | collective-permute-done | bytes 524320 | tf_op jit(solution)/shard_map/ppermute | solution.py:49
  75.8 6.6 %collective-permute-done.12 = bf16[64,4096]{1,0:T(8,128)(2,1)S(1)} collective-permute-done((bf16[64,4096]{1,0:T(8,128)(2,1)S(1)}, bf16[64,4096]{1,0:T(8,128)(2,1)S(1)}, u32[]{:S(2)}, u32[]{:S(2)}) %collective-permute-start.12) | collective-permute-done | bytes 524320 | tf_op jit(solution)/shard_map/ppermute | solution.py:49
  86.5 1.1 add_convert_fusion
  87.6 7.1 %collective-permute-start.14 = (bf16[2,16,32,256]{3,2,1,0:T(8,128)(2,1)S(1)}, bf16[2,16,32,256]{3,2,1,0:T(8,128)(2,1)S(1)}, u32[]{:S(2)}, u32[]{:S(2)}) collective-permute-start(bf16[2,16,32,256]{3,2,1,0:T(8,128)(2,1)S(1)} %slice.193), channel_id=1, source_target_pairs={{0,16},{16,32},{32,48},{48,64},{64,80},{80,96},{96,112},{112,128},... | collective-permute-start | bytes 1572872 | tf_op jit(solution)/shard_map/ppermute | solution.py:30
  95.1 5.5 %collective-permute-done.14 = bf16[2,16,32,256]{3,2,1,0:T(8,128)(2,1)S(1)} collective-permute-done((bf16[2,16,32,256]{3,2,1,0:T(8,128)(2,1)S(1)}, bf16[2,16,32,256]{3,2,1,0:T(8,128)(2,1)S(1)}, u32[]{:S(2)}, u32[]{:S(2)}) %collective-permute-start.14) | collective-permute-done | bytes 524320 | tf_op jit(solution)/shard_map/ppermute | solution.py:30
  100.8 1.2 fusion.22
  102.0 1.2 fusion.25
  103.2 1.2 fusion.19
  104.4 1.3 fusion.62
  105.7 1.3 fusion.60
  107.0 1.8 convert_reduce_fusion.1
  108.8 1.1 copy.89
  109.9 17.4 %all-to-all-start = ((bf16[32,4,16,256]{3,2,1,0:T(8,128)(2,1)}), bf16[32,4,16,256]{3,2,1,0:T(8,128)(2,1)S(1)}, u32[]{:S(2)}, u32[]{:S(2)}) async-start(bf16[32,4,16,256]{3,2,1,0:T(8,128)(2,1)} %bitcast.162), calls=%async_computation | async-start | bytes 2097152 | tf_op jit(solution)/shard_map/all_to_all | solution.py:135
  127.8 1.9 collective-permute-start.15
  129.7 2.7 %collective-permute-done.15 = f32[2,4,32]{2,1,0:T(4,128)S(1)} collective-permute-done((f32[2,4,32]{2,1,0:T(4,128)S(1)}, f32[2,4,32]{2,1,0:T(4,128)S(1)}, u32[]{:S(2)}, u32[]{:S(2)}) %collective-permute-start.15) | collective-permute-done | bytes 1056 | tf_op jit(solution)/shard_map/ppermute | solution.py:39
  132.4 2.3 %collective-permute-start.16 = (f32[2,4,32]{2,1,0:T(4,128)S(1)}, f32[2,4,32]{2,1,0:T(4,128)S(1)}, u32[]{:S(2)}, u32[]{:S(2)}) collective-permute-start(f32[2,4,32]{2,1,0:T(4,128)S(1)} %fusion.92), channel_id=1, source_target_pairs={{0,8},{4,12},{8,0},{12,4},{1,9},{5,13},{9,1},{13,5},{2,10},{6,14},... | collective-permute-start | bytes 3080 | tf_op jit(solution)/shard_map/ppermute | solution.py:39
  134.7 3.9 %collective-permute-done.16 = f32[2,4,32]{2,1,0:T(4,128)S(1)} collective-permute-done((f32[2,4,32]{2,1,0:T(4,128)S(1)}, f32[2,4,32]{2,1,0:T(4,128)S(1)}, u32[]{:S(2)}, u32[]{:S(2)}) %collective-permute-start.16) | collective-permute-done | bytes 1056 | tf_op jit(solution)/shard_map/ppermute | solution.py:39
  138.6 3.8 %collective-permute-start.17 = (f32[2,4,32]{2,1,0:T(4,128)S(1)}, f32[2,4,32]{2,1,0:T(4,128)S(1)}, u32[]{:S(2)}, u32[]{:S(2)}) collective-permute-start(f32[2,4,32]{2,1,0:T(4,128)S(1)} %fusion.103), channel_id=1, source_target_pairs={{0,1},{1,0},{2,3},{3,2},{4,5},{5,4},{6,7},{7,6},{8,9},{9,8},{10,11... | collective-permute-start | bytes 3080 | tf_op jit(solution)/shard_map/ppermute | solution.py:39
  142.4 1.3 collective-permute-done.17
  143.6 3.9 %collective-permute-start.18 = (f32[2,4,32]{2,1,0:T(4,128)S(1)}, f32[2,4,32]{2,1,0:T(4,128)S(1)}, u32[]{:S(2)}, u32[]{:S(2)}) collective-permute-start(f32[2,4,32]{2,1,0:T(4,128)S(1)} %add.147), channel_id=1, source_target_pairs={{0,2},{1,3},{2,0},{3,1},{4,6},{5,7},{6,4},{7,5},{8,10},{9,11},{10,... | collective-permute-start | bytes 3080 | tf_op jit(solution)/shard_map/ppermute | solution.py:39
  147.6 2.2 %collective-permute-done.18 = f32[2,4,32]{2,1,0:T(4,128)S(1)} collective-permute-done((f32[2,4,32]{2,1,0:T(4,128)S(1)}, f32[2,4,32]{2,1,0:T(4,128)S(1)}, u32[]{:S(2)}, u32[]{:S(2)}) %collective-permute-start.18) | collective-permute-done | bytes 1056 | tf_op jit(solution)/shard_map/ppermute | solution.py:39
  149.9 49.7 %all-gather = f32[32,4,64]{2,1,0:T(4,128)S(1)} all-gather(f32[1,4,64]{2,1,0:T(4,128)S(1)} %maximum_bitcast_fusion), channel_id=1, replica_groups=mesh['tm'=32,'band'=4,'fsdp'=4] {'tm'}, dimensions={0}, use_global_device_ids=true | all-gather | bytes 33792 | tf_op jit(solution)/shard_map/all_gather | solution.py:138
  200.4 4.6 %convolution_convert_fusion = bf16[128,16,768]{2,0,1:T(8,128)(2,1)} fusion(f32[128,16,256]{2,1,0:T(8,128)S(1)} %bitcast_convert_fusion, f32[256]{0:T(256)S(1)} %bitcast.198, f32[128,256]{1,0:T(8,128)S(1)} %copy.42, f32[128,256]{1,0:T(8,128)S(1)} %copy.40, bf16[256,4096]{1,0:T(8,128)(2,1)} %bitcast.177), kind=kOutput, calls=%fused_computation.7 | convolution fusion | flops 808976384 | bytes 5899264 | tf_op jit(solution)/shard_map/fpc,cd->fpd/dot_general | solution.py:143
  205.0 2.1 %fusion.97 = (f32[16,128]{1,0:T(8,128)S(1)}, f32[16,128,128]{1,2,0:T(8,128)S(1)}) fusion(pred[128,128]{0,1:T(8,128)(4,1)S(1)} %fusion.70, bf16[128,16,768]{2,0,1:T(8,128)(2,1)} %convolution_convert_fusion), kind=kOutput, calls=%fused_computation.161 | convolution fusion | flops 135528576 | bytes 3186688 | tf_op jit(solution)/shard_map/sub | solution.py:156
  207.2 3.9 %fusion.31 = bf16[1,1,16,128,256]{4,3,2,1,0:T(8,128)(2,1)} fusion(f32[128,16,256]{2,1,0:T(8,128)S(1)} %bitcast_convert_fusion, bf16[128,16,768]{2,0,1:T(8,128)(2,1)} %convolution_convert_fusion, f32[16,128,128]{1,2,0:T(8,128)S(1)} %get-tuple-element.24, f32[16,128]{1,0:T(8,128)S(1)} %get-tuple-element.23, bf16[256,4096]{1,0:T(8,128)(2,1)} %bitcast.178), kind=kOutput, calls=%fused_computation.39 | convolution fusion | flops 404750336 | bytes 5382144 | tf_op jit(solution)/shard_map/axi,iy->axy/dot_general | solution.py:161
  (90 shorter events, 9.1 us)
Async XLA Ops:
  0.0 35.2 %copy-start = (bf16[4,16,32,256]{3,2,1,0:T(8,128)(2,1)S(1)}, bf16[4,16,32,256]{3,2,1,0:T(8,128)(2,1)}, u32[]{:S(2)}) copy-start(bf16[4,16,32,256]{3,2,1,0:T(8,128)(2,1)} %param.7) | copy-start | bytes 3145732
  2.0 6.4 %collective-permute-start = (f32[2,4,32]{2,1,0:T(4,128)S(1)}, f32[2,4,32]{2,1,0:T(4,128)S(1)}, u32[]{:S(2)}, u32[]{:S(2)}) collective-permute-start(f32[2,4,32]{2,1,0:T(4,128)S(1)} %pad_maximum_fusion.5), channel_id=1, source_target_pairs={{0,4},{4,0},{8,12},{12,8},{1,5},{5,1},{9,13},{13,9},{2,6},{6,2},{1... | collective-permute-start | bytes 3080 | tf_op jit(solution)/shard_map/ppermute | solution.py:39
  8.4 15.8 %collective-permute-start.1 = (f32[2,4,32]{2,1,0:T(4,128)S(1)}, f32[2,4,32]{2,1,0:T(4,128)S(1)}, u32[]{:S(2)}, u32[]{:S(2)}) collective-permute-start(f32[2,4,32]{2,1,0:T(4,128)S(1)} %fusion.93), channel_id=1, source_target_pairs={{0,8},{4,12},{8,0},{12,4},{1,9},{5,13},{9,1},{13,5},{2,10},{6,14},... | collective-permute-start | bytes 3080 | tf_op jit(solution)/shard_map/ppermute | solution.py:39
  13.7 22.2 %collective-permute-start.9 = (bf16[16,4096]{1,0:T(8,128)(2,1)S(1)}, bf16[16,4096]{1,0:T(8,128)(2,1)S(1)}, u32[]{:S(2)}, u32[]{:S(2)}) collective-permute-start(bf16[16,4096]{1,0:T(8,128)(2,1)S(1)} %constant_dynamic-update-slice_fusion), channel_id=1, source_target_pairs={{0,1},{1,2},{2,3},{3,0},{4,5},{5,6},{6,7},{7,4},{8,9},{9,10},{10,1... | collective-permute-start | bytes 393224 | tf_op jit(solution)/shard_map/ppermute | solution.py:49
  16.8 19.1 %collective-permute-start.8 = (bf16[16,4096]{1,0:T(8,128)(2,1)S(1)}, bf16[16,4096]{1,0:T(8,128)(2,1)S(1)}, u32[]{:S(2)}, u32[]{:S(2)}) collective-permute-start(bf16[16,4096]{1,0:T(8,128)(2,1)S(1)} %constant_dynamic-update-slice_fusion), channel_id=1, source_target_pairs={{0,2},{1,3},{2,0},{3,1},{4,6},{5,7},{6,4},{7,5},{8,10},{9,11},{10,... | collective-permute-start | bytes 393224 | tf_op jit(solution)/shard_map/ppermute | solution.py:49
  21.1 14.7 %collective-permute-start.7 = (bf16[16,4096]{1,0:T(8,128)(2,1)S(1)}, bf16[16,4096]{1,0:T(8,128)(2,1)S(1)}, u32[]{:S(2)}, u32[]{:S(2)}) collective-permute-start(bf16[16,4096]{1,0:T(8,128)(2,1)S(1)} %constant_dynamic-update-slice_fusion), channel_id=1, source_target_pairs={{0,3},{1,0},{2,1},{3,2},{4,7},{5,4},{6,5},{7,6},{8,11},{9,8},{10,9... | collective-permute-start | bytes 393224 | tf_op jit(solution)/shard_map/ppermute | solution.py:49
  24.2 4.7 %collective-permute-start.2 = (f32[2,4,32]{2,1,0:T(4,128)S(1)}, f32[2,4,32]{2,1,0:T(4,128)S(1)}, u32[]{:S(2)}, u32[]{:S(2)}) collective-permute-start(f32[2,4,32]{2,1,0:T(4,128)S(1)} %fusion.104), channel_id=1, source_target_pairs={{0,1},{1,0},{2,3},{3,2},{4,5},{5,4},{6,7},{7,6},{8,9},{9,8},{10,11... | collective-permute-start | bytes 3080 | tf_op jit(solution)/shard_map/ppermute | solution.py:39
  28.9 5.8 %collective-permute-start.3 = (f32[2,4,32]{2,1,0:T(4,128)S(1)}, f32[2,4,32]{2,1,0:T(4,128)S(1)}, u32[]{:S(2)}, u32[]{:S(2)}) collective-permute-start(f32[2,4,32]{2,1,0:T(4,128)S(1)} %add.122), channel_id=1, source_target_pairs={{0,2},{1,3},{2,0},{3,1},{4,6},{5,7},{6,4},{7,5},{8,10},{9,11},{10,... | collective-permute-start | bytes 3080 | tf_op jit(solution)/shard_map/ppermute | solution.py:39
  36.1 25.0 %collective-permute-start.10 = (bf16[64,4096]{1,0:T(8,128)(2,1)S(1)}, bf16[64,4096]{1,0:T(8,128)(2,1)S(1)}, u32[]{:S(2)}, u32[]{:S(2)}) collective-permute-start(bf16[64,4096]{1,0:T(8,128)(2,1)S(1)} %bitcast.179), channel_id=1, source_target_pairs={{0,12},{4,0},{8,4},{12,8},{1,13},{5,1},{9,5},{13,9},{2,14},{6,2},{... | collective-permute-start | bytes 1572872 | tf_op jit(solution)/shard_map/ppermute | solution.py:49
  38.0 4.7 %collective-permute-start.4 = (bf16[4,1,32,256]{3,2,1,0:T(8,128)(2,1)S(1)}, bf16[4,1,32,256]{3,2,1,0:T(8,128)(2,1)S(1)}, u32[]{:S(2)}, u32[]{:S(2)}) collective-permute-start(bf16[4,1,32,256]{3,2,1,0:T(8,128)(2,1)S(1)} %get-tuple-element.13), channel_id=1, source_target_pairs={{0,4},{4,8},{8,12},{1,5},{5,9},{9,13},{2,6},{6,10},{10,14},{3,7},{... | collective-permute-start | bytes 196616 | tf_op jit(solution)/shard_map/ppermute | solution.py:21
  41.4 7.4 %collective-permute-start.5 = (bf16[4,1,32,256]{3,2,1,0:T(8,128)(2,1)S(1)}, bf16[4,1,32,256]{3,2,1,0:T(8,128)(2,1)S(1)}, u32[]{:S(2)}, u32[]{:S(2)}) collective-permute-start(bf16[4,1,32,256]{3,2,1,0:T(8,128)(2,1)S(1)} %get-tuple-element.14), channel_id=1, source_target_pairs={{4,0},{8,4},{12,8},{5,1},{9,5},{13,9},{6,2},{10,6},{14,10},{7,3},{... | collective-permute-start | bytes 196616 | tf_op jit(solution)/shard_map/ppermute | solution.py:22
  48.9 5.9 %collective-permute-start.13 = (bf16[4,18,1,256]{3,2,1,0:T(2,128)(2,1)S(1)}, bf16[4,18,1,256]{3,2,1,0:T(2,128)(2,1)S(1)}, u32[]{:S(2)}, u32[]{:S(2)}) collective-permute-start(bf16[4,18,1,256]{3,2,1,0:T(2,128)(2,1)S(1)} %get-tuple-element.11), channel_id=1, source_target_pairs={{1,0},{2,1},{3,2},{5,4},{6,5},{7,6},{9,8},{10,9},{11,10},{13,12},{... | collective-permute-start | bytes 110600 | tf_op jit(solution)/shard_map/ppermute | solution.py:22
  50.2 5.4 %collective-permute-start.6 = (bf16[4,18,1,256]{3,2,1,0:T(2,128)(2,1)S(1)}, bf16[4,18,1,256]{3,2,1,0:T(2,128)(2,1)}, u32[]{:S(2)}, u32[]{:S(2)}) collective-permute-start(bf16[4,18,1,256]{3,2,1,0:T(2,128)(2,1)S(1)} %get-tuple-element.12), channel_id=1, source_target_pairs={{0,1},{1,2},{2,3},{4,5},{5,6},{6,7},{8,9},{9,10},{10,11},{12,13},{... | collective-permute-start | bytes 110600 | tf_op jit(solution)/shard_map/ppermute | solution.py:21
  57.2 25.2 %collective-permute-start.12 = (bf16[64,4096]{1,0:T(8,128)(2,1)S(1)}, bf16[64,4096]{1,0:T(8,128)(2,1)S(1)}, u32[]{:S(2)}, u32[]{:S(2)}) collective-permute-start(bf16[64,4096]{1,0:T(8,128)(2,1)S(1)} %bitcast.180), channel_id=1, source_target_pairs={{0,4},{4,8},{8,12},{12,0},{1,5},{5,9},{9,13},{13,1},{2,6},{6,10},{... | collective-permute-start | bytes 1572872 | tf_op jit(solution)/shard_map/ppermute | solution.py:49
  59.2 16.6 %collective-permute-start.11 = (bf16[64,4096]{1,0:T(8,128)(2,1)S(1)}, bf16[64,4096]{1,0:T(8,128)(2,1)S(1)}, u32[]{:S(2)}, u32[]{:S(2)}) collective-permute-start(bf16[64,4096]{1,0:T(8,128)(2,1)S(1)} %bitcast.181), channel_id=1, source_target_pairs={{0,8},{4,12},{8,0},{12,4},{1,9},{5,13},{9,1},{13,5},{2,10},{6,14},... | collective-permute-start | bytes 1572872 | tf_op jit(solution)/shard_map/ppermute | solution.py:49
  82.9 3.6 %copy-start.1 = (bf16[4,64,4096]{2,1,0:T(8,128)(2,1)}, bf16[4,64,4096]{2,1,0:T(8,128)(2,1)S(1)}, u32[]{:S(2)}) copy-start(bf16[4,64,4096]{2,1,0:T(8,128)(2,1)S(1)} %constant_dynamic-slice_fusion) | copy-start | bytes 6291460
  86.5 8.2 %copy-start.2 = (s32[16]{0:T(128)S(1)}, s32[16]{0:T(128)}, u32[]{:S(2)}) copy-start(s32[16]{0:T(128)} %param.8) | copy-start | bytes 196
  87.6 13.0 %collective-permute-start.14 = (bf16[2,16,32,256]{3,2,1,0:T(8,128)(2,1)S(1)}, bf16[2,16,32,256]{3,2,1,0:T(8,128)(2,1)S(1)}, u32[]{:S(2)}, u32[]{:S(2)}) collective-permute-start(bf16[2,16,32,256]{3,2,1,0:T(8,128)(2,1)S(1)} %slice.193), channel_id=1, source_target_pairs={{0,16},{16,32},{32,48},{48,64},{64,80},{80,96},{96,112},{112,128},... | collective-permute-start | bytes 1572872 | tf_op jit(solution)/shard_map/ppermute | solution.py:30
  109.9 90.1 %all-to-all-start = ((bf16[32,4,16,256]{3,2,1,0:T(8,128)(2,1)}), bf16[32,4,16,256]{3,2,1,0:T(8,128)(2,1)S(1)}, u32[]{:S(2)}, u32[]{:S(2)}) async-start(bf16[32,4,16,256]{3,2,1,0:T(8,128)(2,1)} %bitcast.162), calls=%async_computation | async-start | bytes 2097152 | tf_op jit(solution)/shard_map/all_to_all | solution.py:135
  127.8 4.6 %collective-permute-start.15 = (f32[2,4,32]{2,1,0:T(4,128)S(1)}, f32[2,4,32]{2,1,0:T(4,128)S(1)}, u32[]{:S(2)}, u32[]{:S(2)}) collective-permute-start(f32[2,4,32]{2,1,0:T(4,128)S(1)} %pad_maximum_fusion.6), channel_id=1, source_target_pairs={{0,4},{4,0},{8,12},{12,8},{1,5},{5,1},{9,13},{13,9},{2,6},{6,2},{1... | collective-permute-start | bytes 3080 | tf_op jit(solution)/shard_map/ppermute | solution.py:39
  132.4 6.1 %collective-permute-start.16 = (f32[2,4,32]{2,1,0:T(4,128)S(1)}, f32[2,4,32]{2,1,0:T(4,128)S(1)}, u32[]{:S(2)}, u32[]{:S(2)}) collective-permute-start(f32[2,4,32]{2,1,0:T(4,128)S(1)} %fusion.92), channel_id=1, source_target_pairs={{0,8},{4,12},{8,0},{12,4},{1,9},{5,13},{9,1},{13,5},{2,10},{6,14},... | collective-permute-start | bytes 3080 | tf_op jit(solution)/shard_map/ppermute | solution.py:39
  138.6 5.1 %collective-permute-start.17 = (f32[2,4,32]{2,1,0:T(4,128)S(1)}, f32[2,4,32]{2,1,0:T(4,128)S(1)}, u32[]{:S(2)}, u32[]{:S(2)}) collective-permute-start(f32[2,4,32]{2,1,0:T(4,128)S(1)} %fusion.103), channel_id=1, source_target_pairs={{0,1},{1,0},{2,3},{3,2},{4,5},{5,4},{6,7},{7,6},{8,9},{9,8},{10,11... | collective-permute-start | bytes 3080 | tf_op jit(solution)/shard_map/ppermute | solution.py:39
  143.6 6.1 %collective-permute-start.18 = (f32[2,4,32]{2,1,0:T(4,128)S(1)}, f32[2,4,32]{2,1,0:T(4,128)S(1)}, u32[]{:S(2)}, u32[]{:S(2)}) collective-permute-start(f32[2,4,32]{2,1,0:T(4,128)S(1)} %add.147), channel_id=1, source_target_pairs={{0,2},{1,3},{2,0},{3,1},{4,6},{5,7},{6,4},{7,5},{8,10},{9,11},{10,... | collective-permute-start | bytes 3080 | tf_op jit(solution)/shard_map/ppermute | solution.py:39

commit v6 on v5

--- a/solution.py
+++ b/solution.py
@@ -3,9 +3,12 @@
 import jax
 import jax.numpy as jnp
 from jax import lax
+from jax.sharding import Mesh
 from jax.sharding import PartitionSpec as P
 
+
 GROUPS = 32
+TM = ("z", "core")
 
 
 EPS = 1e-06
@@ -87,14 +90,15 @@
     frames, height, width, chans = video.shape
     widths = [w.shape[1] for w in (spatial_kernel_weight, w_time, w_qkv, w_out)]
     packed = jnp.concatenate([spatial_kernel_weight, w_time, w_qkv, w_out], axis=1)
-    gathered = ring_gather(ring_gather(packed, "fsdp"), "band")
+    first_stage = ring_gather(packed, "fsdp")
+    gathered = ring_gather(first_stage, "band")
     offsets = [sum(widths[:i]) for i in range(4)]
     space_full, time_full, qkv_full, output_complete = [
         gathered[:, o : o + w] for o, w in zip(offsets, widths)
     ]
-    ranks = lax.axis_size("tm")
+    ranks = lax.axis_size(TM)
     total_frames = frames * ranks
-    first = lax.axis_index("tm") * frames
+    first = lax.axis_index(TM) * frames
     starts = frame_starts(clip_lengths, total_frames)
     local_starts = lax.dynamic_slice_in_dim(starts, first, frames)
     mean_one, scale_one = group_moments(video)
@@ -111,7 +115,7 @@
             preferred_element_type=jnp.float32,
         )
     spatial = spatial.astype(jnp.bfloat16)
-    carried = from_behind(spatial[frames - 2 :], "tm", 1)
+    carried = from_behind(spatial[frames - 2 :], TM, 1)
     extended = jnp.concatenate([carried, spatial], axis=0)
     position = first + jnp.arange(frames, dtype=jnp.int32)
     slots = jnp.arange(frames + 2, dtype=jnp.int32)
@@ -132,12 +136,12 @@
     pixels = height * width
     group_pixels = pixels // ranks
     flat_resid = resid.reshape(frames, ranks, group_pixels, chans).transpose(1, 0, 2, 3)
-    received = lax.all_to_all(flat_resid, "tm", split_axis=0, concat_axis=0, tiled=True)
+    received = lax.all_to_all(flat_resid, TM, split_axis=0, concat_axis=0, tiled=True)
     resid_time = received.reshape(total_frames, group_pixels, chans)
     mean_two, scale_two = group_moments(resid)
-    moments = lax.all_gather(
-        jnp.concatenate([mean_two, scale_two], axis=1), "tm", axis=0, tiled=True
-    )
+    moments = jnp.concatenate([mean_two, scale_two], axis=1)
+    for axis in TM[::-1]:
+        moments = lax.all_gather(moments, axis, axis=0, tiled=True)
     mean_all, scale_all = moments[:, :GROUPS], moments[:, GROUPS:]
     flat_norm = apply_norm(resid_time, mean_all, scale_all, norm_gains[1]).astype(jnp.bfloat16)
     qkv_time = jnp.einsum(
@@ -168,11 +172,16 @@
 
 
 def solution(mesh):
+    devices = mesh.devices
+    split = Mesh(
+        devices.reshape((devices.shape[0] // 2, 2) + devices.shape[1:]),
+        ("z", "core", "band", "fsdp"),
+    )
     return jax.shard_map(
         body,
-        mesh=mesh,
+        mesh=split,
         in_specs=(
-            P("tm", "band", "fsdp", None),
+            P(TM, "band", "fsdp", None),
             P(),
             P(),
             P(("band", "fsdp"), None),
@@ -180,6 +189,6 @@
             P(("band", "fsdp"), None),
             P(("band", "fsdp"), None),
         ),
-        out_specs=P("band", "fsdp", "tm", None, None),
+        out_specs=P("band", "fsdp", TM, None, None),
         check_vma=False,
     )

time: 212 us -> 211 us (level)
  the two profiles are of different devices: /device:TPU:1 before, /device:TPU:2 now
where the time goes in v6:
time: 211 us; the launch traced here: 210 us
  starting transfers between devices  79 us (37%)
  waiting for transfers between devices  48.6 us (23%)
  blocking collectives  46 us (22%)
  matrix products  23.3 us (11%)
  local copies, waits for them, and re-layouts  6.89 us (3%)
  other arithmetic  5.35 us (3%)
    all_gather x2, blocking collectives, body(): moments = lax.all_gather(moments, axis, axis=0, tiled=True)  46 us
    all_to_all x1, starting transfers between devices, body(): lax.all_to_all(flat_resid, TM, split_axis=0, concat_axis=0, tiled=True)  24.4 us
    ppermute x8, starting transfers between devices, butterfly_sum(): x = x + lax.ppermute(x, axis, pairs)  23.4 us
    ppermute x8, waiting for transfers between devices, butterfly_sum(): x = x + lax.ppermute(x, axis, pairs)  21.5 us
    ppermute x6, starting transfers between devices, ring_gather(): lax.ppermute(x, axis, [(i, (i + shift) % size) for i in range(size)])  21.3 us
    ppermute x6, waiting for transfers between devices, ring_gather(): lax.ppermute(x, axis, [(i, (i + shift) % size) for i in range(size)])  16.8 us
    ppermute x2, waiting for transfers between devices, with_halo(): after = lax.ppermute(initial, axis, down)  5.08 us
    ppermute x2, starting transfers between devices, with_halo(): after = lax.ppermute(initial, axis, down)  4.97 us
  transfers between devices with their start and end apart: 20, of which 13 were waited for; matrix products, arithmetic and copies ran while one was open for 4% of the time, Pallas kernels for 0%

profile of v6, /device:TPU:2, one launch (start us, length us, event | category | flops | bytes accessed | tf_op | source)
XLA Modules:
  0.0 209.8 jit_solution(5537028611598286514)
XLA Ops:
  0.0 1.6 convert_reduce_fusion
  2.0 3.5 %collective-permute-start = (f32[2,4,32]{2,1,0:T(4,128)S(1)}, f32[2,4,32]{2,1,0:T(4,128)S(1)}, u32[]{:S(2)}, u32[]{:S(2)}) collective-permute-start(f32[2,4,32]{2,1,0:T(4,128)S(1)} %pad_maximum_fusion.5), channel_id=1, source_target_pairs={{0,4},{4,0},{8,12},{12,8},{1,5},{5,1},{9,13},{13,9},{2,6},{6,2},{1... | collective-permute-start | bytes 3080 | tf_op jit(solution)/shard_map/ppermute | solution.py:42
  5.5 0.9 constant_dynamic-update-slice_fusion.3
  7.9 4.8 %collective-permute-start.1 = (f32[2,4,32]{2,1,0:T(4,128)S(1)}, f32[2,4,32]{2,1,0:T(4,128)S(1)}, u32[]{:S(2)}, u32[]{:S(2)}) collective-permute-start(f32[2,4,32]{2,1,0:T(4,128)S(1)} %fusion.93), channel_id=1, source_target_pairs={{0,8},{4,12},{8,0},{12,4},{1,9},{5,13},{9,1},{13,5},{2,10},{6,14},... | collective-permute-start | bytes 3080 | tf_op jit(solution)/shard_map/ppermute | solution.py:42
  13.4 3.4 %collective-permute-start.9 = (bf16[16,4096]{1,0:T(8,128)(2,1)S(1)}, bf16[16,4096]{1,0:T(8,128)(2,1)S(1)}, u32[]{:S(2)}, u32[]{:S(2)}) collective-permute-start(bf16[16,4096]{1,0:T(8,128)(2,1)S(1)} %constant_dynamic-update-slice_fusion), channel_id=1, source_target_pairs={{0,1},{1,2},{2,3},{3,0},{4,5},{5,6},{6,7},{7,4},{8,9},{9,10},{10,1... | collective-permute-start | bytes 393224 | tf_op jit(solution)/shard_map/ppermute | solution.py:52
  16.8 5.1 %collective-permute-start.8 = (bf16[16,4096]{1,0:T(8,128)(2,1)S(1)}, bf16[16,4096]{1,0:T(8,128)(2,1)S(1)}, u32[]{:S(2)}, u32[]{:S(2)}) collective-permute-start(bf16[16,4096]{1,0:T(8,128)(2,1)S(1)} %constant_dynamic-update-slice_fusion), channel_id=1, source_target_pairs={{0,2},{1,3},{2,0},{3,1},{4,6},{5,7},{6,4},{7,5},{8,10},{9,11},{10,... | collective-permute-start | bytes 393224 | tf_op jit(solution)/shard_map/ppermute | solution.py:52
  21.9 2.0 collective-permute-start.7
  23.9 3.3 %collective-permute-start.2 = (f32[2,4,32]{2,1,0:T(4,128)S(1)}, f32[2,4,32]{2,1,0:T(4,128)S(1)}, u32[]{:S(2)}, u32[]{:S(2)}) collective-permute-start(f32[2,4,32]{2,1,0:T(4,128)S(1)} %fusion.104), channel_id=1, source_target_pairs={{0,1},{1,0},{2,3},{3,2},{4,5},{5,4},{6,7},{7,6},{8,9},{9,8},{10,11... | collective-permute-start | bytes 3080 | tf_op jit(solution)/shard_map/ppermute | solution.py:42
  27.3 0.8 fusion.96
  28.0 1.4 collective-permute-done.2
  29.4 3.3 %collective-permute-start.3 = (f32[2,4,32]{2,1,0:T(4,128)S(1)}, f32[2,4,32]{2,1,0:T(4,128)S(1)}, u32[]{:S(2)}, u32[]{:S(2)}) collective-permute-start(f32[2,4,32]{2,1,0:T(4,128)S(1)} %add.126), channel_id=1, source_target_pairs={{0,2},{1,3},{2,0},{3,1},{4,6},{5,7},{6,4},{7,5},{8,10},{9,11},{10,... | collective-permute-start | bytes 3080 | tf_op jit(solution)/shard_map/ppermute | solution.py:42
  32.7 3.7 %collective-permute-done.3 = f32[2,4,32]{2,1,0:T(4,128)S(1)} collective-permute-done((f32[2,4,32]{2,1,0:T(4,128)S(1)}, f32[2,4,32]{2,1,0:T(4,128)S(1)}, u32[]{:S(2)}, u32[]{:S(2)}) %collective-permute-start.3) | collective-permute-done | bytes 1056 | tf_op jit(solution)/shard_map/ppermute | solution.py:42
  37.7 5.3 %collective-permute-start.10 = (bf16[64,4096]{1,0:T(8,128)(2,1)S(1)}, bf16[64,4096]{1,0:T(8,128)(2,1)S(1)}, u32[]{:S(2)}, u32[]{:S(2)}) collective-permute-start(bf16[64,4096]{1,0:T(8,128)(2,1)S(1)} %bitcast.179), channel_id=1, source_target_pairs={{0,12},{4,0},{8,4},{12,8},{1,13},{5,1},{9,5},{13,9},{2,14},{6,2},{... | collective-permute-start | bytes 1572872 | tf_op jit(solution)/shard_map/ppermute | solution.py:52
  43.1 1.3 collective-permute-start.4
  44.4 1.3 collective-permute-start.5
  46.3 4.7 %collective-permute-done.5 = bf16[4,1,32,256]{3,2,1,0:T(8,128)(2,1)S(1)} collective-permute-done((bf16[4,1,32,256]{3,2,1,0:T(8,128)(2,1)S(1)}, bf16[4,1,32,256]{3,2,1,0:T(8,128)(2,1)S(1)}, u32[]{:S(2)}, u32[]{:S(2)}) %collective-permute-start.5) | collective-permute-done | bytes 65568 | tf_op jit(solution)/shard_map/ppermute | solution.py:25
  51.1 3.7 %collective-permute-start.13 = (bf16[4,18,1,256]{3,2,1,0:T(2,128)(2,1)S(1)}, bf16[4,18,1,256]{3,2,1,0:T(2,128)(2,1)S(1)}, u32[]{:S(2)}, u32[]{:S(2)}) collective-permute-start(bf16[4,18,1,256]{3,2,1,0:T(2,128)(2,1)S(1)} %get-tuple-element.11), channel_id=1, source_target_pairs={{1,0},{2,1},{3,2},{5,4},{6,5},{7,6},{9,8},{10,9},{11,10},{13,12},{... | collective-permute-start | bytes 110600 | tf_op jit(solution)/shard_map/ppermute | solution.py:25
  54.8 2.2 %collective-permute-start.6 = (bf16[4,18,1,256]{3,2,1,0:T(2,128)(2,1)S(1)}, bf16[4,18,1,256]{3,2,1,0:T(2,128)(2,1)}, u32[]{:S(2)}, u32[]{:S(2)}) collective-permute-start(bf16[4,18,1,256]{3,2,1,0:T(2,128)(2,1)S(1)} %get-tuple-element.12), channel_id=1, source_target_pairs={{0,1},{1,2},{2,3},{4,5},{5,6},{6,7},{8,9},{9,10},{10,11},{12,13},{... | collective-permute-start | bytes 110600 | tf_op jit(solution)/shard_map/ppermute | solution.py:24
  57.4 3.8 %collective-permute-done.6 = bf16[4,18,1,256]{3,2,1,0:T(2,128)(2,1)} collective-permute-done((bf16[4,18,1,256]{3,2,1,0:T(2,128)(2,1)S(1)}, bf16[4,18,1,256]{3,2,1,0:T(2,128)(2,1)}, u32[]{:S(2)}, u32[]{:S(2)}) %collective-permute-start.6) | collective-permute-done | bytes 36896 | tf_op jit(solution)/shard_map/ppermute | solution.py:24
  61.1 1.6 pad_maximum_fusion.1
  62.8 2.0 collective-permute-start.12
  64.8 3.4 %collective-permute-start.11 = (bf16[64,4096]{1,0:T(8,128)(2,1)S(1)}, bf16[64,4096]{1,0:T(8,128)(2,1)S(1)}, u32[]{:S(2)}, u32[]{:S(2)}) collective-permute-start(bf16[64,4096]{1,0:T(8,128)(2,1)S(1)} %bitcast.181), channel_id=1, source_target_pairs={{0,8},{4,12},{8,0},{12,4},{1,9},{5,13},{9,1},{13,5},{2,10},{6,14},... | collective-permute-start | bytes 1572872 | tf_op jit(solution)/shard_map/ppermute | solution.py:52
  68.3 13.6 %collective-permute-done.11 = bf16[64,4096]{1,0:T(8,128)(2,1)S(1)} collective-permute-done((bf16[64,4096]{1,0:T(8,128)(2,1)S(1)}, bf16[64,4096]{1,0:T(8,128)(2,1)S(1)}, u32[]{:S(2)}, u32[]{:S(2)}) %collective-permute-start.11) | collective-permute-done | bytes 524320 | tf_op jit(solution)/shard_map/ppermute | solution.py:52
  81.9 3.2 %collective-permute-done.12 = bf16[64,4096]{1,0:T(8,128)(2,1)S(1)} collective-permute-done((bf16[64,4096]{1,0:T(8,128)(2,1)S(1)}, bf16[64,4096]{1,0:T(8,128)(2,1)S(1)}, u32[]{:S(2)}, u32[]{:S(2)}) %collective-permute-start.12) | collective-permute-done | bytes 524320 | tf_op jit(solution)/shard_map/ppermute | solution.py:52
  89.2 1.0 add_convert_fusion
  90.3 1.5 collective-permute-start.14
  92.2 0.9 collective-permute-done.14
  93.2 1.2 fusion.22
  94.4 1.2 fusion.25
  95.6 1.2 fusion.19
  96.8 1.3 fusion.62
  98.2 1.3 fusion.60
  99.5 1.8 convert_reduce_fusion.1
  101.3 1.1 copy.100
  102.4 24.4 %all-to-all-start = ((bf16[32,4,16,256]{3,2,1,0:T(8,128)(2,1)}), bf16[32,4,16,256]{3,2,1,0:T(8,128)(2,1)S(1)}, u32[]{:S(2)}, u32[]{:S(2)}) async-start(bf16[32,4,16,256]{3,2,1,0:T(8,128)(2,1)} %bitcast.162), calls=%async_computation | async-start | bytes 2097152 | tf_op jit(solution)/shard_map/all_to_all | solution.py:139
  127.2 1.9 collective-permute-start.15
  129.1 3.6 %collective-permute-done.15 = f32[2,4,32]{2,1,0:T(4,128)S(1)} collective-permute-done((f32[2,4,32]{2,1,0:T(4,128)S(1)}, f32[2,4,32]{2,1,0:T(4,128)S(1)}, u32[]{:S(2)}, u32[]{:S(2)}) %collective-permute-start.15) | collective-permute-done | bytes 1056 | tf_op jit(solution)/shard_map/ppermute | solution.py:42
  132.7 2.6 %collective-permute-start.16 = (f32[2,4,32]{2,1,0:T(4,128)S(1)}, f32[2,4,32]{2,1,0:T(4,128)S(1)}, u32[]{:S(2)}, u32[]{:S(2)}) collective-permute-start(f32[2,4,32]{2,1,0:T(4,128)S(1)} %fusion.92), channel_id=1, source_target_pairs={{0,8},{4,12},{8,0},{12,4},{1,9},{5,13},{9,1},{13,5},{2,10},{6,14},... | collective-permute-start | bytes 3080 | tf_op jit(solution)/shard_map/ppermute | solution.py:42
  135.3 4.4 %collective-permute-done.16 = f32[2,4,32]{2,1,0:T(4,128)S(1)} collective-permute-done((f32[2,4,32]{2,1,0:T(4,128)S(1)}, f32[2,4,32]{2,1,0:T(4,128)S(1)}, u32[]{:S(2)}, u32[]{:S(2)}) %collective-permute-start.16) | collective-permute-done | bytes 1056 | tf_op jit(solution)/shard_map/ppermute | solution.py:42
  139.7 1.9 collective-permute-start.17
  141.6 3.6 %collective-permute-done.17 = f32[2,4,32]{2,1,0:T(4,128)S(1)} collective-permute-done((f32[2,4,32]{2,1,0:T(4,128)S(1)}, f32[2,4,32]{2,1,0:T(4,128)S(1)}, u32[]{:S(2)}, u32[]{:S(2)}) %collective-permute-start.17) | collective-permute-done | bytes 1056 | tf_op jit(solution)/shard_map/ppermute | solution.py:42
  145.2 2.1 %collective-permute-start.18 = (f32[2,4,32]{2,1,0:T(4,128)S(1)}, f32[2,4,32]{2,1,0:T(4,128)S(1)}, u32[]{:S(2)}, u32[]{:S(2)}) collective-permute-start(f32[2,4,32]{2,1,0:T(4,128)S(1)} %add.151), channel_id=1, source_target_pairs={{0,2},{1,3},{2,0},{3,1},{4,6},{5,7},{6,4},{7,5},{8,10},{9,11},{10,... | collective-permute-start | bytes 3080 | tf_op jit(solution)/shard_map/ppermute | solution.py:42
  147.3 4.9 %collective-permute-done.18 = f32[2,4,32]{2,1,0:T(4,128)S(1)} collective-permute-done((f32[2,4,32]{2,1,0:T(4,128)S(1)}, f32[2,4,32]{2,1,0:T(4,128)S(1)}, u32[]{:S(2)}, u32[]{:S(2)}) %collective-permute-start.18) | collective-permute-done | bytes 1056 | tf_op jit(solution)/shard_map/ppermute | solution.py:42
  152.3 1.8 all-gather
  154.1 44.2 %all_gather.7 = f32[128,64]{1,0:T(8,128)S(1)} all-gather(f32[8,64]{1,0:T(8,128)S(1)} %bitcast.197), channel_id=1, replica_groups=mesh['z'=16,'core'=2,'band'=4,'fsdp'=4] {'z'}, dimensions={0}, use_global_device_ids=true | all-gather | bytes 34816 | tf_op jit(solution)/shard_map/all_gather | solution.py:144
  199.2 4.6 %convolution_convert_fusion = bf16[128,16,768]{2,0,1:T(8,128)(2,1)} fusion(f32[128,16,256]{2,1,0:T(8,128)S(1)} %bitcast_convert_fusion, f32[256]{0:T(256)S(1)} %bitcast.198, f32[128,256]{1,0:T(8,128)S(1)} %copy.55, f32[128,256]{1,0:T(8,128)S(1)} %copy.53, bf16[256,4096]{1,0:T(8,128)(2,1)} %bitcast.177), kind=kOutput, calls=%fused_computation.7 | convolution fusion | flops 808976384 | bytes 5899264 | tf_op jit(solution)/shard_map/fpc,cd->fpd/dot_general | solution.py:147
  203.8 2.1 %fusion.97 = (f32[16,128]{1,0:T(8,128)S(1)}, f32[16,128,128]{1,2,0:T(8,128)S(1)}) fusion(pred[128,128]{0,1:T(8,128)(4,1)S(1)} %fusion.70, bf16[128,16,768]{2,0,1:T(8,128)(2,1)} %convolution_convert_fusion), kind=kOutput, calls=%fused_computation.161 | convolution fusion | flops 135528576 | bytes 3186688 | tf_op jit(solution)/shard_map/sub | solution.py:160
  205.9 3.9 %fusion.31 = bf16[1,1,16,128,256]{4,3,2,1,0:T(8,128)(2,1)} fusion(f32[128,16,256]{2,1,0:T(8,128)S(1)} %bitcast_convert_fusion, bf16[128,16,768]{2,0,1:T(8,128)(2,1)} %convolution_convert_fusion, f32[16,128,128]{1,2,0:T(8,128)S(1)} %get-tuple-element.24, f32[16,128]{1,0:T(8,128)S(1)} %get-tuple-element.23, bf16[256,4096]{1,0:T(8,128)(2,1)} %bitcast.178), kind=kOutput, calls=%fused_computation.39 | convolution fusion | flops 404750336 | bytes 5382144 | tf_op jit(solution)/shard_map/axi,iy->axy/dot_general | solution.py:165
  (91 shorter events, 10.8 us)
Async XLA Ops:
  0.0 36.8 %copy-start = (bf16[4,16,32,256]{3,2,1,0:T(8,128)(2,1)S(1)}, bf16[4,16,32,256]{3,2,1,0:T(8,128)(2,1)}, u32[]{:S(2)}) copy-start(bf16[4,16,32,256]{3,2,1,0:T(8,128)(2,1)} %param.7) | copy-start | bytes 3145732
  2.0 5.9 %collective-permute-start = (f32[2,4,32]{2,1,0:T(4,128)S(1)}, f32[2,4,32]{2,1,0:T(4,128)S(1)}, u32[]{:S(2)}, u32[]{:S(2)}) collective-permute-start(f32[2,4,32]{2,1,0:T(4,128)S(1)} %pad_maximum_fusion.5), channel_id=1, source_target_pairs={{0,4},{4,0},{8,12},{12,8},{1,5},{5,1},{9,13},{13,9},{2,6},{6,2},{1... | collective-permute-start | bytes 3080 | tf_op jit(solution)/shard_map/ppermute | solution.py:42
  7.9 16.0 %collective-permute-start.1 = (f32[2,4,32]{2,1,0:T(4,128)S(1)}, f32[2,4,32]{2,1,0:T(4,128)S(1)}, u32[]{:S(2)}, u32[]{:S(2)}) collective-permute-start(f32[2,4,32]{2,1,0:T(4,128)S(1)} %fusion.93), channel_id=1, source_target_pairs={{0,8},{4,12},{8,0},{12,4},{1,9},{5,13},{9,1},{13,5},{2,10},{6,14},... | collective-permute-start | bytes 3080 | tf_op jit(solution)/shard_map/ppermute | solution.py:42
  13.4 24.1 %collective-permute-start.9 = (bf16[16,4096]{1,0:T(8,128)(2,1)S(1)}, bf16[16,4096]{1,0:T(8,128)(2,1)S(1)}, u32[]{:S(2)}, u32[]{:S(2)}) collective-permute-start(bf16[16,4096]{1,0:T(8,128)(2,1)S(1)} %constant_dynamic-update-slice_fusion), channel_id=1, source_target_pairs={{0,1},{1,2},{2,3},{3,0},{4,5},{5,6},{6,7},{7,4},{8,9},{9,10},{10,1... | collective-permute-start | bytes 393224 | tf_op jit(solution)/shard_map/ppermute | solution.py:52
  16.8 20.7 %collective-permute-start.8 = (bf16[16,4096]{1,0:T(8,128)(2,1)S(1)}, bf16[16,4096]{1,0:T(8,128)(2,1)S(1)}, u32[]{:S(2)}, u32[]{:S(2)}) collective-permute-start(bf16[16,4096]{1,0:T(8,128)(2,1)S(1)} %constant_dynamic-update-slice_fusion), channel_id=1, source_target_pairs={{0,2},{1,3},{2,0},{3,1},{4,6},{5,7},{6,4},{7,5},{8,10},{9,11},{10,... | collective-permute-start | bytes 393224 | tf_op jit(solution)/shard_map/ppermute | solution.py:52
  21.9 15.6 %collective-permute-start.7 = (bf16[16,4096]{1,0:T(8,128)(2,1)S(1)}, bf16[16,4096]{1,0:T(8,128)(2,1)S(1)}, u32[]{:S(2)}, u32[]{:S(2)}) collective-permute-start(bf16[16,4096]{1,0:T(8,128)(2,1)S(1)} %constant_dynamic-update-slice_fusion), channel_id=1, source_target_pairs={{0,3},{1,0},{2,1},{3,2},{4,7},{5,4},{6,5},{7,6},{8,11},{9,8},{10,9... | collective-permute-start | bytes 393224 | tf_op jit(solution)/shard_map/ppermute | solution.py:52
  23.9 5.5 %collective-permute-start.2 = (f32[2,4,32]{2,1,0:T(4,128)S(1)}, f32[2,4,32]{2,1,0:T(4,128)S(1)}, u32[]{:S(2)}, u32[]{:S(2)}) collective-permute-start(f32[2,4,32]{2,1,0:T(4,128)S(1)} %fusion.104), channel_id=1, source_target_pairs={{0,1},{1,0},{2,3},{3,2},{4,5},{5,4},{6,7},{7,6},{8,9},{9,8},{10,11... | collective-permute-start | bytes 3080 | tf_op jit(solution)/shard_map/ppermute | solution.py:42
  29.4 7.0 %collective-permute-start.3 = (f32[2,4,32]{2,1,0:T(4,128)S(1)}, f32[2,4,32]{2,1,0:T(4,128)S(1)}, u32[]{:S(2)}, u32[]{:S(2)}) collective-permute-start(f32[2,4,32]{2,1,0:T(4,128)S(1)} %add.126), channel_id=1, source_target_pairs={{0,2},{1,3},{2,0},{3,1},{4,6},{5,7},{6,4},{7,5},{8,10},{9,11},{10,... | collective-permute-start | bytes 3080 | tf_op jit(solution)/shard_map/ppermute | solution.py:42
  37.7 30.5 %collective-permute-start.10 = (bf16[64,4096]{1,0:T(8,128)(2,1)S(1)}, bf16[64,4096]{1,0:T(8,128)(2,1)S(1)}, u32[]{:S(2)}, u32[]{:S(2)}) collective-permute-start(bf16[64,4096]{1,0:T(8,128)(2,1)S(1)} %bitcast.179), channel_id=1, source_target_pairs={{0,12},{4,0},{8,4},{12,8},{1,13},{5,1},{9,5},{13,9},{2,14},{6,2},{... | collective-permute-start | bytes 1572872 | tf_op jit(solution)/shard_map/ppermute | solution.py:52
  43.1 3.2 %collective-permute-start.4 = (bf16[4,1,32,256]{3,2,1,0:T(8,128)(2,1)S(1)}, bf16[4,1,32,256]{3,2,1,0:T(8,128)(2,1)S(1)}, u32[]{:S(2)}, u32[]{:S(2)}) collective-permute-start(bf16[4,1,32,256]{3,2,1,0:T(8,128)(2,1)S(1)} %get-tuple-element.13), channel_id=1, source_target_pairs={{0,4},{4,8},{8,12},{1,5},{5,9},{9,13},{2,6},{6,10},{10,14},{3,7},{... | collective-permute-start | bytes 196616 | tf_op jit(solution)/shard_map/ppermute | solution.py:24
  44.4 6.6 %collective-permute-start.5 = (bf16[4,1,32,256]{3,2,1,0:T(8,128)(2,1)S(1)}, bf16[4,1,32,256]{3,2,1,0:T(8,128)(2,1)S(1)}, u32[]{:S(2)}, u32[]{:S(2)}) collective-permute-start(bf16[4,1,32,256]{3,2,1,0:T(8,128)(2,1)S(1)} %get-tuple-element.14), channel_id=1, source_target_pairs={{4,0},{8,4},{12,8},{5,1},{9,5},{13,9},{6,2},{10,6},{14,10},{7,3},{... | collective-permute-start | bytes 196616 | tf_op jit(solution)/shard_map/ppermute | solution.py:25
  51.1 6.2 %collective-permute-start.13 = (bf16[4,18,1,256]{3,2,1,0:T(2,128)(2,1)S(1)}, bf16[4,18,1,256]{3,2,1,0:T(2,128)(2,1)S(1)}, u32[]{:S(2)}, u32[]{:S(2)}) collective-permute-start(bf16[4,18,1,256]{3,2,1,0:T(2,128)(2,1)S(1)} %get-tuple-element.11), channel_id=1, source_target_pairs={{1,0},{2,1},{3,2},{5,4},{6,5},{7,6},{9,8},{10,9},{11,10},{13,12},{... | collective-permute-start | bytes 110600 | tf_op jit(solution)/shard_map/ppermute | solution.py:25
  54.8 6.4 %collective-permute-start.6 = (bf16[4,18,1,256]{3,2,1,0:T(2,128)(2,1)S(1)}, bf16[4,18,1,256]{3,2,1,0:T(2,128)(2,1)}, u32[]{:S(2)}, u32[]{:S(2)}) collective-permute-start(bf16[4,18,1,256]{3,2,1,0:T(2,128)(2,1)S(1)} %get-tuple-element.12), channel_id=1, source_target_pairs={{0,1},{1,2},{2,3},{4,5},{5,6},{6,7},{8,9},{9,10},{10,11},{12,13},{... | collective-permute-start | bytes 110600 | tf_op jit(solution)/shard_map/ppermute | solution.py:24
  62.8 22.4 %collective-permute-start.12 = (bf16[64,4096]{1,0:T(8,128)(2,1)S(1)}, bf16[64,4096]{1,0:T(8,128)(2,1)S(1)}, u32[]{:S(2)}, u32[]{:S(2)}) collective-permute-start(bf16[64,4096]{1,0:T(8,128)(2,1)S(1)} %bitcast.180), channel_id=1, source_target_pairs={{0,4},{4,8},{8,12},{12,0},{1,5},{5,9},{9,13},{13,1},{2,6},{6,10},{... | collective-permute-start | bytes 1572872 | tf_op jit(solution)/shard_map/ppermute | solution.py:52
  64.8 17.1 %collective-permute-start.11 = (bf16[64,4096]{1,0:T(8,128)(2,1)S(1)}, bf16[64,4096]{1,0:T(8,128)(2,1)S(1)}, u32[]{:S(2)}, u32[]{:S(2)}) collective-permute-start(bf16[64,4096]{1,0:T(8,128)(2,1)S(1)} %bitcast.181), channel_id=1, source_target_pairs={{0,8},{4,12},{8,0},{12,4},{1,9},{5,13},{9,1},{13,5},{2,10},{6,14},... | collective-permute-start | bytes 1572872 | tf_op jit(solution)/shard_map/ppermute | solution.py:52
  85.6 3.5 %copy-start.1 = (bf16[4,64,4096]{2,1,0:T(8,128)(2,1)}, bf16[4,64,4096]{2,1,0:T(8,128)(2,1)S(1)}, u32[]{:S(2)}) copy-start(bf16[4,64,4096]{2,1,0:T(8,128)(2,1)S(1)} %constant_dynamic-slice_fusion) | copy-start | bytes 6291460
  89.1 2.6 %copy-start.2 = (s32[16]{0:T(128)S(1)}, s32[16]{0:T(128)}, u32[]{:S(2)}) copy-start(s32[16]{0:T(128)} %param.8) | copy-start | bytes 196
  90.3 2.8 %collective-permute-start.14 = (bf16[2,16,32,256]{3,2,1,0:T(8,128)(2,1)S(1)}, bf16[2,16,32,256]{3,2,1,0:T(8,128)(2,1)S(1)}, u32[]{:S(2)}, u32[]{:S(2)}) collective-permute-start(bf16[2,16,32,256]{3,2,1,0:T(8,128)(2,1)S(1)} %slice.193), channel_id=1, source_target_pairs={{0,16},{16,32},{32,48},{48,64},{64,80},{80,96},{96,112},{112,128},... | collective-permute-start | bytes 1572872 | tf_op jit(solution)/shard_map/ppermute | solution.py:33
  102.4 96.4 %all-to-all-start = ((bf16[32,4,16,256]{3,2,1,0:T(8,128)(2,1)}), bf16[32,4,16,256]{3,2,1,0:T(8,128)(2,1)S(1)}, u32[]{:S(2)}, u32[]{:S(2)}) async-start(bf16[32,4,16,256]{3,2,1,0:T(8,128)(2,1)} %bitcast.162), calls=%async_computation | async-start | bytes 2097152 | tf_op jit(solution)/shard_map/all_to_all | solution.py:139
  127.2 5.5 %collective-permute-start.15 = (f32[2,4,32]{2,1,0:T(4,128)S(1)}, f32[2,4,32]{2,1,0:T(4,128)S(1)}, u32[]{:S(2)}, u32[]{:S(2)}) collective-permute-start(f32[2,4,32]{2,1,0:T(4,128)S(1)} %pad_maximum_fusion.6), channel_id=1, source_target_pairs={{0,4},{4,0},{8,12},{12,8},{1,5},{5,1},{9,13},{13,9},{2,6},{6,2},{1... | collective-permute-start | bytes 3080 | tf_op jit(solution)/shard_map/ppermute | solution.py:42
  132.7 7.0 %collective-permute-start.16 = (f32[2,4,32]{2,1,0:T(4,128)S(1)}, f32[2,4,32]{2,1,0:T(4,128)S(1)}, u32[]{:S(2)}, u32[]{:S(2)}) collective-permute-start(f32[2,4,32]{2,1,0:T(4,128)S(1)} %fusion.92), channel_id=1, source_target_pairs={{0,8},{4,12},{8,0},{12,4},{1,9},{5,13},{9,1},{13,5},{2,10},{6,14},... | collective-permute-start | bytes 3080 | tf_op jit(solution)/shard_map/ppermute | solution.py:42
  139.7 5.5 %collective-permute-start.17 = (f32[2,4,32]{2,1,0:T(4,128)S(1)}, f32[2,4,32]{2,1,0:T(4,128)S(1)}, u32[]{:S(2)}, u32[]{:S(2)}) collective-permute-start(f32[2,4,32]{2,1,0:T(4,128)S(1)} %fusion.103), channel_id=1, source_target_pairs={{0,1},{1,0},{2,3},{3,2},{4,5},{5,4},{6,7},{7,6},{8,9},{9,8},{10,11... | collective-permute-start | bytes 3080 | tf_op jit(solution)/shard_map/ppermute | solution.py:42
  145.2 7.0 %collective-permute-start.18 = (f32[2,4,32]{2,1,0:T(4,128)S(1)}, f32[2,4,32]{2,1,0:T(4,128)S(1)}, u32[]{:S(2)}, u32[]{:S(2)}) collective-permute-start(f32[2,4,32]{2,1,0:T(4,128)S(1)} %add.151), channel_id=1, source_target_pairs={{0,2},{1,3},{2,0},{3,1},{4,6},{5,7},{6,4},{7,5},{8,10},{9,11},{10,... | collective-permute-start | bytes 3080 | tf_op jit(solution)/shard_map/ppermute | solution.py:42

commit v7 on v6

--- a/solution.py
+++ b/solution.py
@@ -90,8 +90,18 @@
     frames, height, width, chans = video.shape
     widths = [w.shape[1] for w in (spatial_kernel_weight, w_time, w_qkv, w_out)]
     packed = jnp.concatenate([spatial_kernel_weight, w_time, w_qkv, w_out], axis=1)
-    first_stage = ring_gather(packed, "fsdp")
-    gathered = ring_gather(first_stage, "band")
+    half = packed.shape[1] // 2
+    core = lax.axis_index("core")
+    mine = lax.dynamic_slice_in_dim(packed, core * half, half, axis=1)
+    first_stage = ring_gather(mine, "fsdp")
+    second_stage = ring_gather(first_stage, "band")
+    other = lax.ppermute(second_stage, "core", [(0, 1), (1, 0)])
+    both = jnp.stack([second_stage, other, second_stage])
+    gathered = jnp.concatenate(
+        [lax.dynamic_index_in_dim(both, core, 0, keepdims=False),
+         lax.dynamic_index_in_dim(both, core + 1, 0, keepdims=False)],
+        axis=1,
+    )
     offsets = [sum(widths[:i]) for i in range(4)]
     space_full, time_full, qkv_full, output_complete = [
         gathered[:, o : o + w] for o, w in zip(offsets, widths)

time: 211 us -> 202 us (0.957)
  the two profiles are of different devices: /device:TPU:2 before, /device:TPU:12 now
where the time goes in v7:
time: 202 us; the launch traced here: 201 us
  starting transfers between devices  76.9 us (38%)
  blocking collectives  46 us (23%)
  waiting for transfers between devices  43.6 us (22%)
  matrix products  20.6 us (10%)
  other arithmetic  8.79 us (4%)
  local copies, waits for them, and re-layouts  4.46 us (2%)
    all_gather x2, blocking collectives, body(): moments = lax.all_gather(moments, axis, axis=0, tiled=True)  46 us
    ppermute x8, waiting for transfers between devices, butterfly_sum(): x = x + lax.ppermute(x, axis, pairs)  29.7 us
    ppermute x6, starting transfers between devices, ring_gather(): lax.ppermute(x, axis, [(i, (i + shift) % size) for i in range(size)])  22.6 us
    all_to_all x1, starting transfers between devices, body(): lax.all_to_all(flat_resid, TM, split_axis=0, concat_axis=0, tiled=True)  22 us
    ppermute x8, starting transfers between devices, butterfly_sum(): x = x + lax.ppermute(x, axis, pairs)  16.3 us
    ppermute x6, waiting for transfers between devices, ring_gather(): lax.ppermute(x, axis, [(i, (i + shift) % size) for i in range(size)])  6.65 us
    ppermute x2, starting transfers between devices, with_halo(): after = lax.ppermute(initial, axis, down)  6.14 us
    ppermute x2, waiting for transfers between devices, with_halo(): before = lax.ppermute(last, axis, up)  6.03 us
  transfers between devices with their start and end apart: 21, of which 14 were waited for; matrix products, arithmetic and copies ran while one was open for 3% of the time, Pallas kernels for 0%

profile of v7, /device:TPU:12, one launch (start us, length us, event | category | flops | bytes accessed | tf_op | source)
XLA Modules:
  0.0 201.1 jit_solution(12675656828624264576)
XLA Ops:
  0.0 1.5 convert_reduce_fusion
  1.9 2.4 %collective-permute-start = (f32[2,4,32]{2,1,0:T(4,128)S(1)}, f32[2,4,32]{2,1,0:T(4,128)S(1)}, u32[]{:S(2)}, u32[]{:S(2)}) collective-permute-start(f32[2,4,32]{2,1,0:T(4,128)S(1)} %pad_maximum_fusion.6), channel_id=1, source_target_pairs={{0,4},{4,0},{8,12},{12,8},{1,5},{5,1},{9,13},{13,9},{2,6},{6,2},{1... | collective-permute-start | bytes 3080 | tf_op jit(solution)/shard_map/ppermute | solution.py:42
  4.3 0.9 fusion.72
  5.2 2.4 %collective-permute-start.7 = (bf16[16,2048]{1,0:T(8,128)(2,1)S(1)}, bf16[16,2048]{1,0:T(8,128)(2,1)S(1)}, u32[]{:S(2)}, u32[]{:S(2)}) collective-permute-start(bf16[16,2048]{1,0:T(8,128)(2,1)S(1)} %fusion.72), channel_id=1, source_target_pairs={{0,3},{1,0},{2,1},{3,2},{4,7},{5,4},{6,5},{7,6},{8,11},{9,8},{10,9... | collective-permute-start | bytes 196616 | tf_op jit(solution)/shard_map/ppermute | solution.py:52
  7.7 7.2 %collective-permute-start.8 = (bf16[16,2048]{1,0:T(8,128)(2,1)S(1)}, bf16[16,2048]{1,0:T(8,128)(2,1)S(1)}, u32[]{:S(2)}, u32[]{:S(2)}) collective-permute-start(bf16[16,2048]{1,0:T(8,128)(2,1)S(1)} %fusion.72), channel_id=1, source_target_pairs={{0,2},{1,3},{2,0},{3,1},{4,6},{5,7},{6,4},{7,5},{8,10},{9,11},{10,... | collective-permute-start | bytes 196616 | tf_op jit(solution)/shard_map/ppermute | solution.py:52
  14.9 4.5 %collective-permute-start.9 = (bf16[16,2048]{1,0:T(8,128)(2,1)S(1)}, bf16[16,2048]{1,0:T(8,128)(2,1)S(1)}, u32[]{:S(2)}, u32[]{:S(2)}) collective-permute-start(bf16[16,2048]{1,0:T(8,128)(2,1)S(1)} %fusion.72), channel_id=1, source_target_pairs={{0,1},{1,2},{2,3},{3,0},{4,5},{5,6},{6,7},{7,4},{8,9},{9,10},{10,1... | collective-permute-start | bytes 196616 | tf_op jit(solution)/shard_map/ppermute | solution.py:52
  19.5 1.9 collective-permute-start.1
  22.2 4.3 %collective-permute-done.1 = f32[2,4,32]{2,1,0:T(4,128)S(1)} collective-permute-done((f32[2,4,32]{2,1,0:T(4,128)S(1)}, f32[2,4,32]{2,1,0:T(4,128)S(1)}, u32[]{:S(2)}, u32[]{:S(2)}) %collective-permute-start.1) | collective-permute-done | bytes 1056 | tf_op jit(solution)/shard_map/ppermute | solution.py:42
  26.5 1.9 collective-permute-start.2
  28.4 3.6 %collective-permute-done.2 = f32[2,4,32]{2,1,0:T(4,128)S(1)} collective-permute-done((f32[2,4,32]{2,1,0:T(4,128)S(1)}, f32[2,4,32]{2,1,0:T(4,128)S(1)}, u32[]{:S(2)}, u32[]{:S(2)}) %collective-permute-start.2) | collective-permute-done | bytes 1056 | tf_op jit(solution)/shard_map/ppermute | solution.py:42
  32.0 1.9 collective-permute-start.3
  33.9 5.0 %collective-permute-done.3 = f32[2,4,32]{2,1,0:T(4,128)S(1)} collective-permute-done((f32[2,4,32]{2,1,0:T(4,128)S(1)}, f32[2,4,32]{2,1,0:T(4,128)S(1)}, u32[]{:S(2)}, u32[]{:S(2)}) %collective-permute-start.3) | collective-permute-done | bytes 1056 | tf_op jit(solution)/shard_map/ppermute | solution.py:42
  39.1 1.9 collective-permute-start.10
  41.5 1.9 collective-permute-start.11
  43.4 4.5 %collective-permute-start.12 = (bf16[64,2048]{1,0:T(8,128)(2,1)S(1)}, bf16[64,2048]{1,0:T(8,128)(2,1)S(1)}, u32[]{:S(2)}, u32[]{:S(2)}) collective-permute-start(bf16[64,2048]{1,0:T(8,128)(2,1)S(1)} %bitcast.176), channel_id=1, source_target_pairs={{0,4},{4,8},{8,12},{12,0},{1,5},{5,9},{9,13},{13,1},{2,6},{6,10},{... | collective-permute-start | bytes 786440 | tf_op jit(solution)/shard_map/ppermute | solution.py:52
  48.0 3.3 %collective-permute-done.11 = bf16[64,2048]{1,0:T(8,128)(2,1)S(1)} collective-permute-done((bf16[64,2048]{1,0:T(8,128)(2,1)S(1)}, bf16[64,2048]{1,0:T(8,128)(2,1)S(1)}, u32[]{:S(2)}, u32[]{:S(2)}) %collective-permute-start.11) | collective-permute-done | bytes 262176 | tf_op jit(solution)/shard_map/ppermute | solution.py:52
  51.3 3.4 %collective-permute-done.12 = bf16[64,2048]{1,0:T(8,128)(2,1)S(1)} collective-permute-done((bf16[64,2048]{1,0:T(8,128)(2,1)S(1)}, bf16[64,2048]{1,0:T(8,128)(2,1)S(1)}, u32[]{:S(2)}, u32[]{:S(2)}) %collective-permute-start.12) | collective-permute-done | bytes 262176 | tf_op jit(solution)/shard_map/ppermute | solution.py:52
  54.9 2.1 %collective-permute-start.13 = (bf16[256,2048]{1,0:T(8,128)(2,1)S(1)}, bf16[256,2048]{1,0:T(8,128)(2,1)}, u32[]{:S(2)}, u32[]{:S(2)}) collective-permute-start(bf16[256,2048]{1,0:T(8,128)(2,1)S(1)} %bitcast.171), channel_id=1, source_target_pairs={{0,16},{16,0},{1,17},{17,1},{2,18},{18,2},{3,19},{19,3},{4,20},{20... | collective-permute-start | bytes 3145736 | tf_op jit(solution)/shard_map/ppermute | solution.py:98
  57.7 4.2 %collective-permute-start.5 = (bf16[4,1,32,256]{3,2,1,0:T(8,128)(2,1)S(1)}, bf16[4,1,32,256]{3,2,1,0:T(8,128)(2,1)S(1)}, u32[]{:S(2)}, u32[]{:S(2)}) collective-permute-start(bf16[4,1,32,256]{3,2,1,0:T(8,128)(2,1)S(1)} %get-tuple-element.16), channel_id=1, source_target_pairs={{4,0},{8,4},{12,8},{5,1},{9,5},{13,9},{6,2},{10,6},{14,10},{7,3},{... | collective-permute-start | bytes 196616 | tf_op jit(solution)/shard_map/ppermute | solution.py:25
  61.9 1.9 collective-permute-start.4
  64.1 4.0 %collective-permute-done.4 = bf16[4,1,32,256]{3,2,1,0:T(8,128)(2,1)S(1)} collective-permute-done((bf16[4,1,32,256]{3,2,1,0:T(8,128)(2,1)S(1)}, bf16[4,1,32,256]{3,2,1,0:T(8,128)(2,1)S(1)}, u32[]{:S(2)}, u32[]{:S(2)}) %collective-permute-start.4) | collective-permute-done | bytes 65568 | tf_op jit(solution)/shard_map/ppermute | solution.py:24
  68.2 1.9 collective-permute-start.14
  70.1 3.9 %collective-permute-start.6 = (bf16[4,18,1,256]{3,2,1,0:T(2,128)(2,1)S(1)}, bf16[4,18,1,256]{3,2,1,0:T(2,128)(2,1)}, u32[]{:S(2)}, u32[]{:S(2)}) collective-permute-start(bf16[4,18,1,256]{3,2,1,0:T(2,128)(2,1)S(1)} %get-tuple-element.14), channel_id=1, source_target_pairs={{0,1},{1,2},{2,3},{4,5},{5,6},{6,7},{8,9},{9,10},{10,11},{12,13},{... | collective-permute-start | bytes 110600 | tf_op jit(solution)/shard_map/ppermute | solution.py:24
  74.4 2.0 %collective-permute-done.6 = bf16[4,18,1,256]{3,2,1,0:T(2,128)(2,1)} collective-permute-done((bf16[4,18,1,256]{3,2,1,0:T(2,128)(2,1)S(1)}, bf16[4,18,1,256]{3,2,1,0:T(2,128)(2,1)}, u32[]{:S(2)}, u32[]{:S(2)}) %collective-permute-start.6) | collective-permute-done | bytes 36896 | tf_op jit(solution)/shard_map/ppermute | solution.py:24
  76.5 1.6 pad_maximum_fusion.2
  78.1 1.6 pad_maximum_fusion
  83.4 1.1 add_convert_fusion
  85.2 2.1 %collective-permute-start.15 = (bf16[2,16,32,256]{3,2,1,0:T(8,128)(2,1)}, bf16[2,16,32,256]{3,2,1,0:T(8,128)(2,1)}, u32[]{:S(2)}, u32[]{:S(2)}) collective-permute-start(bf16[2,16,32,256]{3,2,1,0:T(8,128)(2,1)} %slice.202), channel_id=1, source_target_pairs={{0,16},{16,32},{32,48},{48,64},{64,80},{80,96},{96,112},{112,128},... | collective-permute-start | bytes 1572872 | tf_op jit(solution)/shard_map/ppermute | solution.py:33
  88.4 1.2 pad_maximum_fusion.1
  89.6 1.2 fusion.25
  90.8 1.2 fusion.19
  92.4 1.2 fusion.22
  94.1 0.9 convert_reduce_fusion.1
  95.0 1.1 copy.100
  96.1 22.0 %all-to-all-start = ((bf16[32,4,16,256]{3,2,1,0:T(8,128)(2,1)}), bf16[32,4,16,256]{3,2,1,0:T(8,128)(2,1)S(1)}, u32[]{:S(2)}, u32[]{:S(2)}) async-start(bf16[32,4,16,256]{3,2,1,0:T(8,128)(2,1)} %bitcast.168), calls=%async_computation | async-start | bytes 2097152 | tf_op jit(solution)/shard_map/all_to_all | solution.py:149
  118.5 1.9 collective-permute-start.16
  120.4 3.6 %collective-permute-done.16 = f32[2,4,32]{2,1,0:T(4,128)S(1)} collective-permute-done((f32[2,4,32]{2,1,0:T(4,128)S(1)}, f32[2,4,32]{2,1,0:T(4,128)S(1)}, u32[]{:S(2)}, u32[]{:S(2)}) %collective-permute-start.16) | collective-permute-done | bytes 1056 | tf_op jit(solution)/shard_map/ppermute | solution.py:42
  124.0 2.4 %collective-permute-start.17 = (f32[2,4,32]{2,1,0:T(4,128)S(1)}, f32[2,4,32]{2,1,0:T(4,128)S(1)}, u32[]{:S(2)}, u32[]{:S(2)}) collective-permute-start(f32[2,4,32]{2,1,0:T(4,128)S(1)} %fusion.95), channel_id=1, source_target_pairs={{0,8},{4,12},{8,0},{12,4},{1,9},{5,13},{9,1},{13,5},{2,10},{6,14},... | collective-permute-start | bytes 3080 | tf_op jit(solution)/shard_map/ppermute | solution.py:42
  126.4 4.6 %collective-permute-done.17 = f32[2,4,32]{2,1,0:T(4,128)S(1)} collective-permute-done((f32[2,4,32]{2,1,0:T(4,128)S(1)}, f32[2,4,32]{2,1,0:T(4,128)S(1)}, u32[]{:S(2)}, u32[]{:S(2)}) %collective-permute-start.17) | collective-permute-done | bytes 1056 | tf_op jit(solution)/shard_map/ppermute | solution.py:42
  131.0 1.9 collective-permute-start.18
  132.9 3.6 %collective-permute-done.18 = f32[2,4,32]{2,1,0:T(4,128)S(1)} collective-permute-done((f32[2,4,32]{2,1,0:T(4,128)S(1)}, f32[2,4,32]{2,1,0:T(4,128)S(1)}, u32[]{:S(2)}, u32[]{:S(2)}) %collective-permute-start.18) | collective-permute-done | bytes 1056 | tf_op jit(solution)/shard_map/ppermute | solution.py:42
  136.5 1.9 collective-permute-start.19
  138.4 5.0 %collective-permute-done.19 = f32[2,4,32]{2,1,0:T(4,128)S(1)} collective-permute-done((f32[2,4,32]{2,1,0:T(4,128)S(1)}, f32[2,4,32]{2,1,0:T(4,128)S(1)}, u32[]{:S(2)}, u32[]{:S(2)}) %collective-permute-start.19) | collective-permute-done | bytes 1056 | tf_op jit(solution)/shard_map/ppermute | solution.py:42
  143.6 1.8 all-gather
  145.4 44.2 %all_gather.7 = f32[128,64]{1,0:T(8,128)S(1)} all-gather(f32[8,64]{1,0:T(8,128)S(1)} %bitcast.191), channel_id=1, replica_groups=mesh['z'=16,'core'=2,'band'=4,'fsdp'=4] {'z'}, dimensions={0}, use_global_device_ids=true | all-gather | bytes 34816 | tf_op jit(solution)/shard_map/all_gather | solution.py:154
  190.5 4.6 %convolution_convert_fusion = bf16[128,16,768]{2,0,1:T(8,128)(2,1)} fusion(f32[128,16,256]{2,1,0:T(8,128)S(1)} %bitcast_convert_fusion, f32[256]{0:T(256)S(1)} %bitcast.192, f32[128,256]{1,0:T(8,128)S(1)} %copy.55, f32[128,256]{1,0:T(8,128)S(1)} %copy.53, bf16[256,2048]{1,0:T(8,128)(2,1)} %copy-done.1), kind=kOutput, calls=%fused_computation.8 | convolution fusion | flops 808976384 | bytes 5899264 | tf_op jit(solution)/shard_map/fpc,cd->fpd/dot_general | solution.py:157
  195.1 2.1 %fusion.100 = (f32[16,128]{1,0:T(8,128)S(1)}, f32[16,128,128]{1,2,0:T(8,128)S(1)}) fusion(pred[128,128]{0,1:T(8,128)(4,1)S(1)} %fusion.73, bf16[128,16,768]{2,0,1:T(8,128)(2,1)} %convolution_convert_fusion), kind=kOutput, calls=%fused_computation.167 | convolution fusion | flops 135528576 | bytes 3186688 | tf_op jit(solution)/shard_map/sub | solution.py:170
  197.2 3.9 %fusion.31 = bf16[1,1,16,128,256]{4,3,2,1,0:T(8,128)(2,1)} fusion(f32[128,16,256]{2,1,0:T(8,128)S(1)} %bitcast_convert_fusion, bf16[128,16,768]{2,0,1:T(8,128)(2,1)} %convolution_convert_fusion, f32[16,128,128]{1,2,0:T(8,128)S(1)} %get-tuple-element.26, f32[16,128]{1,0:T(8,128)S(1)} %get-tuple-element.25, bf16[256,2048]{1,0:T(8,128)(2,1)} %copy-done.1), kind=kOutput, calls=%fused_computation.40 | convolution fusion | flops 404750336 | bytes 5382144 | tf_op jit(solution)/shard_map/axi,iy->axy/dot_general | solution.py:175
  (92 shorter events, 11.0 us)
Async XLA Ops:
  1.9 17.5 %collective-permute-start = (f32[2,4,32]{2,1,0:T(4,128)S(1)}, f32[2,4,32]{2,1,0:T(4,128)S(1)}, u32[]{:S(2)}, u32[]{:S(2)}) collective-permute-start(f32[2,4,32]{2,1,0:T(4,128)S(1)} %pad_maximum_fusion.6), channel_id=1, source_target_pairs={{0,4},{4,0},{8,12},{12,8},{1,5},{5,1},{9,13},{13,9},{2,6},{6,2},{1... | collective-permute-start | bytes 3080 | tf_op jit(solution)/shard_map/ppermute | solution.py:42
  5.2 33.8 %collective-permute-start.7 = (bf16[16,2048]{1,0:T(8,128)(2,1)S(1)}, bf16[16,2048]{1,0:T(8,128)(2,1)S(1)}, u32[]{:S(2)}, u32[]{:S(2)}) collective-permute-start(bf16[16,2048]{1,0:T(8,128)(2,1)S(1)} %fusion.72), channel_id=1, source_target_pairs={{0,3},{1,0},{2,1},{3,2},{4,7},{5,4},{6,5},{7,6},{8,11},{9,8},{10,9... | collective-permute-start | bytes 196616 | tf_op jit(solution)/shard_map/ppermute | solution.py:52
  7.7 31.3 %collective-permute-start.8 = (bf16[16,2048]{1,0:T(8,128)(2,1)S(1)}, bf16[16,2048]{1,0:T(8,128)(2,1)S(1)}, u32[]{:S(2)}, u32[]{:S(2)}) collective-permute-start(bf16[16,2048]{1,0:T(8,128)(2,1)S(1)} %fusion.72), channel_id=1, source_target_pairs={{0,2},{1,3},{2,0},{3,1},{4,6},{5,7},{6,4},{7,5},{8,10},{9,11},{10,... | collective-permute-start | bytes 196616 | tf_op jit(solution)/shard_map/ppermute | solution.py:52
  14.9 24.1 %collective-permute-start.9 = (bf16[16,2048]{1,0:T(8,128)(2,1)S(1)}, bf16[16,2048]{1,0:T(8,128)(2,1)S(1)}, u32[]{:S(2)}, u32[]{:S(2)}) collective-permute-start(bf16[16,2048]{1,0:T(8,128)(2,1)S(1)} %fusion.72), channel_id=1, source_target_pairs={{0,1},{1,2},{2,3},{3,0},{4,5},{5,6},{6,7},{7,4},{8,9},{9,10},{10,1... | collective-permute-start | bytes 196616 | tf_op jit(solution)/shard_map/ppermute | solution.py:52
  19.5 7.0 %collective-permute-start.1 = (f32[2,4,32]{2,1,0:T(4,128)S(1)}, f32[2,4,32]{2,1,0:T(4,128)S(1)}, u32[]{:S(2)}, u32[]{:S(2)}) collective-permute-start(f32[2,4,32]{2,1,0:T(4,128)S(1)} %fusion.96), channel_id=1, source_target_pairs={{0,8},{4,12},{8,0},{12,4},{1,9},{5,13},{9,1},{13,5},{2,10},{6,14},... | collective-permute-start | bytes 3080 | tf_op jit(solution)/shard_map/ppermute | solution.py:42
  26.5 5.5 %collective-permute-start.2 = (f32[2,4,32]{2,1,0:T(4,128)S(1)}, f32[2,4,32]{2,1,0:T(4,128)S(1)}, u32[]{:S(2)}, u32[]{:S(2)}) collective-permute-start(f32[2,4,32]{2,1,0:T(4,128)S(1)} %fusion.107), channel_id=1, source_target_pairs={{0,1},{1,0},{2,3},{3,2},{4,5},{5,4},{6,7},{7,6},{8,9},{9,8},{10,11... | collective-permute-start | bytes 3080 | tf_op jit(solution)/shard_map/ppermute | solution.py:42
  32.0 7.0 %collective-permute-start.3 = (f32[2,4,32]{2,1,0:T(4,128)S(1)}, f32[2,4,32]{2,1,0:T(4,128)S(1)}, u32[]{:S(2)}, u32[]{:S(2)}) collective-permute-start(f32[2,4,32]{2,1,0:T(4,128)S(1)} %add.141), channel_id=1, source_target_pairs={{0,2},{1,3},{2,0},{3,1},{4,6},{5,7},{6,4},{7,5},{8,10},{9,11},{10,... | collective-permute-start | bytes 3080 | tf_op jit(solution)/shard_map/ppermute | solution.py:42
  39.1 8.8 %collective-permute-start.10 = (bf16[64,2048]{1,0:T(8,128)(2,1)S(1)}, bf16[64,2048]{1,0:T(8,128)(2,1)S(1)}, u32[]{:S(2)}, u32[]{:S(2)}) collective-permute-start(bf16[64,2048]{1,0:T(8,128)(2,1)S(1)} %bitcast.174), channel_id=1, source_target_pairs={{0,12},{4,0},{8,4},{12,8},{1,13},{5,1},{9,5},{13,9},{2,14},{6,2},{... | collective-permute-start | bytes 786440 | tf_op jit(solution)/shard_map/ppermute | solution.py:52
  41.5 9.8 %collective-permute-start.11 = (bf16[64,2048]{1,0:T(8,128)(2,1)S(1)}, bf16[64,2048]{1,0:T(8,128)(2,1)S(1)}, u32[]{:S(2)}, u32[]{:S(2)}) collective-permute-start(bf16[64,2048]{1,0:T(8,128)(2,1)S(1)} %bitcast.175), channel_id=1, source_target_pairs={{0,8},{4,12},{8,0},{12,4},{1,9},{5,13},{9,1},{13,5},{2,10},{6,14},... | collective-permute-start | bytes 786440 | tf_op jit(solution)/shard_map/ppermute | solution.py:52
  43.4 11.2 %collective-permute-start.12 = (bf16[64,2048]{1,0:T(8,128)(2,1)S(1)}, bf16[64,2048]{1,0:T(8,128)(2,1)S(1)}, u32[]{:S(2)}, u32[]{:S(2)}) collective-permute-start(bf16[64,2048]{1,0:T(8,128)(2,1)S(1)} %bitcast.176), channel_id=1, source_target_pairs={{0,4},{4,8},{8,12},{12,0},{1,5},{5,9},{9,13},{13,1},{2,6},{6,10},{... | collective-permute-start | bytes 786440 | tf_op jit(solution)/shard_map/ppermute | solution.py:52
  54.7 2.3 %copy-start = (bf16[4,16,32,256]{3,2,1,0:T(8,128)(2,1)S(1)}, bf16[4,16,32,256]{3,2,1,0:T(8,128)(2,1)}, u32[]{:S(2)}) copy-start(bf16[4,16,32,256]{3,2,1,0:T(8,128)(2,1)} %param.7) | copy-start | bytes 3145732
  54.9 23.2 %collective-permute-start.13 = (bf16[256,2048]{1,0:T(8,128)(2,1)S(1)}, bf16[256,2048]{1,0:T(8,128)(2,1)}, u32[]{:S(2)}, u32[]{:S(2)}) collective-permute-start(bf16[256,2048]{1,0:T(8,128)(2,1)S(1)} %bitcast.171), channel_id=1, source_target_pairs={{0,16},{16,0},{1,17},{17,1},{2,18},{18,2},{3,19},{19,3},{4,20},{20... | collective-permute-start | bytes 3145736 | tf_op jit(solution)/shard_map/ppermute | solution.py:98
  57.7 6.4 %collective-permute-start.5 = (bf16[4,1,32,256]{3,2,1,0:T(8,128)(2,1)S(1)}, bf16[4,1,32,256]{3,2,1,0:T(8,128)(2,1)S(1)}, u32[]{:S(2)}, u32[]{:S(2)}) collective-permute-start(bf16[4,1,32,256]{3,2,1,0:T(8,128)(2,1)S(1)} %get-tuple-element.16), channel_id=1, source_target_pairs={{4,0},{8,4},{12,8},{5,1},{9,5},{13,9},{6,2},{10,6},{14,10},{7,3},{... | collective-permute-start | bytes 196616 | tf_op jit(solution)/shard_map/ppermute | solution.py:25
  61.9 6.2 %collective-permute-start.4 = (bf16[4,1,32,256]{3,2,1,0:T(8,128)(2,1)S(1)}, bf16[4,1,32,256]{3,2,1,0:T(8,128)(2,1)S(1)}, u32[]{:S(2)}, u32[]{:S(2)}) collective-permute-start(bf16[4,1,32,256]{3,2,1,0:T(8,128)(2,1)S(1)} %get-tuple-element.15), channel_id=1, source_target_pairs={{0,4},{4,8},{8,12},{1,5},{5,9},{9,13},{2,6},{6,10},{10,14},{3,7},{... | collective-permute-start | bytes 196616 | tf_op jit(solution)/shard_map/ppermute | solution.py:24
  68.2 6.2 %collective-permute-start.14 = (bf16[4,18,1,256]{3,2,1,0:T(2,128)(2,1)S(1)}, bf16[4,18,1,256]{3,2,1,0:T(2,128)(2,1)S(1)}, u32[]{:S(2)}, u32[]{:S(2)}) collective-permute-start(bf16[4,18,1,256]{3,2,1,0:T(2,128)(2,1)S(1)} %get-tuple-element.13), channel_id=1, source_target_pairs={{1,0},{2,1},{3,2},{5,4},{6,5},{7,6},{9,8},{10,9},{11,10},{13,12},{... | collective-permute-start | bytes 110600 | tf_op jit(solution)/shard_map/ppermute | solution.py:25
  70.1 6.4 %collective-permute-start.6 = (bf16[4,18,1,256]{3,2,1,0:T(2,128)(2,1)S(1)}, bf16[4,18,1,256]{3,2,1,0:T(2,128)(2,1)}, u32[]{:S(2)}, u32[]{:S(2)}) collective-permute-start(bf16[4,18,1,256]{3,2,1,0:T(2,128)(2,1)S(1)} %get-tuple-element.14), channel_id=1, source_target_pairs={{0,1},{1,2},{2,3},{4,5},{5,6},{6,7},{8,9},{9,10},{10,11},{12,13},{... | collective-permute-start | bytes 110600 | tf_op jit(solution)/shard_map/ppermute | solution.py:24
  79.8 14.3 %copy-start.1 = (bf16[256,2048]{1,0:T(8,128)(2,1)}, bf16[256,2048]{1,0:T(8,128)(2,1)S(1)}, u32[]{:S(2)}) copy-start(bf16[256,2048]{1,0:T(8,128)(2,1)S(1)} %get-tuple-element.9) | copy-start | bytes 3145732
  83.3 4.0 %copy-start.2 = (s32[16]{0:T(128)S(1)}, s32[16]{0:T(128)}, u32[]{:S(2)}) copy-start(s32[16]{0:T(128)} %param.8) | copy-start | bytes 196
  85.2 3.1 %collective-permute-start.15 = (bf16[2,16,32,256]{3,2,1,0:T(8,128)(2,1)}, bf16[2,16,32,256]{3,2,1,0:T(8,128)(2,1)}, u32[]{:S(2)}, u32[]{:S(2)}) collective-permute-start(bf16[2,16,32,256]{3,2,1,0:T(8,128)(2,1)} %slice.202), channel_id=1, source_target_pairs={{0,16},{16,32},{32,48},{48,64},{64,80},{80,96},{96,112},{112,128},... | collective-permute-start | bytes 1572872 | tf_op jit(solution)/shard_map/ppermute | solution.py:33
  96.1 94.0 %all-to-all-start = ((bf16[32,4,16,256]{3,2,1,0:T(8,128)(2,1)}), bf16[32,4,16,256]{3,2,1,0:T(8,128)(2,1)S(1)}, u32[]{:S(2)}, u32[]{:S(2)}) async-start(bf16[32,4,16,256]{3,2,1,0:T(8,128)(2,1)} %bitcast.168), calls=%async_computation | async-start | bytes 2097152 | tf_op jit(solution)/shard_map/all_to_all | solution.py:149
  118.5 5.5 %collective-permute-start.16 = (f32[2,4,32]{2,1,0:T(4,128)S(1)}, f32[2,4,32]{2,1,0:T(4,128)S(1)}, u32[]{:S(2)}, u32[]{:S(2)}) collective-permute-start(f32[2,4,32]{2,1,0:T(4,128)S(1)} %pad_maximum_fusion.7), channel_id=1, source_target_pairs={{0,4},{4,0},{8,12},{12,8},{1,5},{5,1},{9,13},{13,9},{2,6},{6,2},{1... | collective-permute-start | bytes 3080 | tf_op jit(solution)/shard_map/ppermute | solution.py:42
  124.0 7.0 %collective-permute-start.17 = (f32[2,4,32]{2,1,0:T(4,128)S(1)}, f32[2,4,32]{2,1,0:T(4,128)S(1)}, u32[]{:S(2)}, u32[]{:S(2)}) collective-permute-start(f32[2,4,32]{2,1,0:T(4,128)S(1)} %fusion.95), channel_id=1, source_target_pairs={{0,8},{4,12},{8,0},{12,4},{1,9},{5,13},{9,1},{13,5},{2,10},{6,14},... | collective-permute-start | bytes 3080 | tf_op jit(solution)/shard_map/ppermute | solution.py:42
  131.0 5.5 %collective-permute-start.18 = (f32[2,4,32]{2,1,0:T(4,128)S(1)}, f32[2,4,32]{2,1,0:T(4,128)S(1)}, u32[]{:S(2)}, u32[]{:S(2)}) collective-permute-start(f32[2,4,32]{2,1,0:T(4,128)S(1)} %fusion.106), channel_id=1, source_target_pairs={{0,1},{1,0},{2,3},{3,2},{4,5},{5,4},{6,7},{7,6},{8,9},{9,8},{10,11... | collective-permute-start | bytes 3080 | tf_op jit(solution)/shard_map/ppermute | solution.py:42
  136.5 7.0 %collective-permute-start.19 = (f32[2,4,32]{2,1,0:T(4,128)S(1)}, f32[2,4,32]{2,1,0:T(4,128)S(1)}, u32[]{:S(2)}, u32[]{:S(2)}) collective-permute-start(f32[2,4,32]{2,1,0:T(4,128)S(1)} %add.170), channel_id=1, source_target_pairs={{0,2},{1,3},{2,0},{3,1},{4,6},{5,7},{6,4},{7,5},{8,10},{9,11},{10,... | collective-permute-start | bytes 3080 | tf_op jit(solution)/shard_map/ppermute | solution.py:42

commit v8 on v7

--- a/solution.py
+++ b/solution.py
@@ -144,10 +144,8 @@
         )
     resid = (video.astype(jnp.float32) + temporal).astype(jnp.bfloat16)
     pixels = height * width
-    group_pixels = pixels // ranks
-    flat_resid = resid.reshape(frames, ranks, group_pixels, chans).transpose(1, 0, 2, 3)
-    received = lax.all_to_all(flat_resid, TM, split_axis=0, concat_axis=0, tiled=True)
-    resid_time = received.reshape(total_frames, group_pixels, chans)
+    flat_resid = resid.reshape(frames, pixels, chans)
+    resid_time = lax.all_to_all(flat_resid, TM, split_axis=1, concat_axis=0, tiled=True)
     mean_two, scale_two = group_moments(resid)
     moments = jnp.concatenate([mean_two, scale_two], axis=1)
     for axis in TM[::-1]:

time: 202 us -> 205 us (1.015)
  local copies, waits for them, and re-layouts: 4.46 us -> 7.1 us
where the time goes in v8:
time: 205 us; the launch traced here: 204 us
  starting transfers between devices  76.9 us (38%)
  blocking collectives  46 us (22%)
  waiting for transfers between devices  43.6 us (21%)
  matrix products  19 us (9%)
  other arithmetic  10.3 us (5%)
  local copies, waits for them, and re-layouts  7.1 us (3%)
    all_gather x2, blocking collectives, body(): moments = lax.all_gather(moments, axis, axis=0, tiled=True)  46 us
    ppermute x8, waiting for transfers between devices, butterfly_sum(): x = x + lax.ppermute(x, axis, pairs)  29.7 us
    ppermute x6, starting transfers between devices, ring_gather(): lax.ppermute(x, axis, [(i, (i + shift) % size) for i in range(size)])  22.6 us
    all_to_all x1, starting transfers between devices, body(): lax.all_to_all(flat_resid, TM, split_axis=1, concat_axis=0, tiled=True)  22 us
    ppermute x8, starting transfers between devices, butterfly_sum(): x = x + lax.ppermute(x, axis, pairs)  16.2 us
    ppermute x6, waiting for transfers between devices, ring_gather(): lax.ppermute(x, axis, [(i, (i + shift) % size) for i in range(size)])  6.65 us
    ppermute x2, starting transfers between devices, with_halo(): after = lax.ppermute(initial, axis, down)  6.14 us
    ppermute x2, waiting for transfers between devices, with_halo(): before = lax.ppermute(last, axis, up)  6.03 us
  transfers between devices with their start and end apart: 21, of which 14 were waited for; matrix products, arithmetic and copies ran while one was open for 3% of the time, Pallas kernels for 0%

profile of v8, /device:TPU:12, one launch (start us, length us, event | category | flops | bytes accessed | tf_op | source)
XLA Modules:
  0.0 203.7 jit_solution(3275242488533237355)
XLA Ops:
  0.0 1.5 convert_reduce_fusion
  1.9 2.4 %collective-permute-start = (f32[2,4,32]{2,1,0:T(4,128)S(1)}, f32[2,4,32]{2,1,0:T(4,128)S(1)}, u32[]{:S(2)}, u32[]{:S(2)}) collective-permute-start(f32[2,4,32]{2,1,0:T(4,128)S(1)} %pad_maximum_fusion.6), channel_id=1, source_target_pairs={{0,4},{4,0},{8,12},{12,8},{1,5},{5,1},{9,13},{13,9},{2,6},{6,2},{1... | collective-permute-start | bytes 3080 | tf_op jit(solution)/shard_map/ppermute | solution.py:42
  5.2 2.4 %collective-permute-start.7 = (bf16[16,2048]{1,0:T(8,128)(2,1)S(1)}, bf16[16,2048]{1,0:T(8,128)(2,1)S(1)}, u32[]{:S(2)}, u32[]{:S(2)}) collective-permute-start(bf16[16,2048]{1,0:T(8,128)(2,1)S(1)} %fusion.72), channel_id=1, source_target_pairs={{0,3},{1,0},{2,1},{3,2},{4,7},{5,4},{6,5},{7,6},{8,11},{9,8},{10,9... | collective-permute-start | bytes 196616 | tf_op jit(solution)/shard_map/ppermute | solution.py:52
  7.7 7.2 %collective-permute-start.8 = (bf16[16,2048]{1,0:T(8,128)(2,1)S(1)}, bf16[16,2048]{1,0:T(8,128)(2,1)S(1)}, u32[]{:S(2)}, u32[]{:S(2)}) collective-permute-start(bf16[16,2048]{1,0:T(8,128)(2,1)S(1)} %fusion.72), channel_id=1, source_target_pairs={{0,2},{1,3},{2,0},{3,1},{4,6},{5,7},{6,4},{7,5},{8,10},{9,11},{10,... | collective-permute-start | bytes 196616 | tf_op jit(solution)/shard_map/ppermute | solution.py:52
  14.9 4.5 %collective-permute-start.9 = (bf16[16,2048]{1,0:T(8,128)(2,1)S(1)}, bf16[16,2048]{1,0:T(8,128)(2,1)S(1)}, u32[]{:S(2)}, u32[]{:S(2)}) collective-permute-start(bf16[16,2048]{1,0:T(8,128)(2,1)S(1)} %fusion.72), channel_id=1, source_target_pairs={{0,1},{1,2},{2,3},{3,0},{4,5},{5,6},{6,7},{7,4},{8,9},{9,10},{10,1... | collective-permute-start | bytes 196616 | tf_op jit(solution)/shard_map/ppermute | solution.py:52
  19.5 1.9 collective-permute-start.1
  22.2 4.3 %collective-permute-done.1 = f32[2,4,32]{2,1,0:T(4,128)S(1)} collective-permute-done((f32[2,4,32]{2,1,0:T(4,128)S(1)}, f32[2,4,32]{2,1,0:T(4,128)S(1)}, u32[]{:S(2)}, u32[]{:S(2)}) %collective-permute-start.1) | collective-permute-done | bytes 1056 | tf_op jit(solution)/shard_map/ppermute | solution.py:42
  26.5 1.9 collective-permute-start.2
  28.4 3.6 %collective-permute-done.2 = f32[2,4,32]{2,1,0:T(4,128)S(1)} collective-permute-done((f32[2,4,32]{2,1,0:T(4,128)S(1)}, f32[2,4,32]{2,1,0:T(4,128)S(1)}, u32[]{:S(2)}, u32[]{:S(2)}) %collective-permute-start.2) | collective-permute-done | bytes 1056 | tf_op jit(solution)/shard_map/ppermute | solution.py:42
  32.0 1.9 collective-permute-start.3
  33.9 5.0 %collective-permute-done.3 = f32[2,4,32]{2,1,0:T(4,128)S(1)} collective-permute-done((f32[2,4,32]{2,1,0:T(4,128)S(1)}, f32[2,4,32]{2,1,0:T(4,128)S(1)}, u32[]{:S(2)}, u32[]{:S(2)}) %collective-permute-start.3) | collective-permute-done | bytes 1056 | tf_op jit(solution)/shard_map/ppermute | solution.py:42
  39.1 1.9 collective-permute-start.10
  41.5 1.9 collective-permute-start.11
  43.4 4.5 %collective-permute-start.12 = (bf16[64,2048]{1,0:T(8,128)(2,1)S(1)}, bf16[64,2048]{1,0:T(8,128)(2,1)S(1)}, u32[]{:S(2)}, u32[]{:S(2)}) collective-permute-start(bf16[64,2048]{1,0:T(8,128)(2,1)S(1)} %bitcast.177), channel_id=1, source_target_pairs={{0,4},{4,8},{8,12},{12,0},{1,5},{5,9},{9,13},{13,1},{2,6},{6,10},{... | collective-permute-start | bytes 786440 | tf_op jit(solution)/shard_map/ppermute | solution.py:52
  48.0 3.3 %collective-permute-done.11 = bf16[64,2048]{1,0:T(8,128)(2,1)S(1)} collective-permute-done((bf16[64,2048]{1,0:T(8,128)(2,1)S(1)}, bf16[64,2048]{1,0:T(8,128)(2,1)S(1)}, u32[]{:S(2)}, u32[]{:S(2)}) %collective-permute-start.11) | collective-permute-done | bytes 262176 | tf_op jit(solution)/shard_map/ppermute | solution.py:52
  51.3 3.4 %collective-permute-done.12 = bf16[64,2048]{1,0:T(8,128)(2,1)S(1)} collective-permute-done((bf16[64,2048]{1,0:T(8,128)(2,1)S(1)}, bf16[64,2048]{1,0:T(8,128)(2,1)S(1)}, u32[]{:S(2)}, u32[]{:S(2)}) %collective-permute-start.12) | collective-permute-done | bytes 262176 | tf_op jit(solution)/shard_map/ppermute | solution.py:52
  54.9 2.1 %collective-permute-start.13 = (bf16[256,2048]{1,0:T(8,128)(2,1)S(1)}, bf16[256,2048]{1,0:T(8,128)(2,1)}, u32[]{:S(2)}, u32[]{:S(2)}) collective-permute-start(bf16[256,2048]{1,0:T(8,128)(2,1)S(1)} %bitcast.171), channel_id=1, source_target_pairs={{0,16},{16,0},{1,17},{17,1},{2,18},{18,2},{3,19},{19,3},{4,20},{20... | collective-permute-start | bytes 3145736 | tf_op jit(solution)/shard_map/ppermute | solution.py:98
  57.7 4.2 %collective-permute-start.5 = (bf16[4,1,32,256]{3,2,1,0:T(8,128)(2,1)S(1)}, bf16[4,1,32,256]{3,2,1,0:T(8,128)(2,1)S(1)}, u32[]{:S(2)}, u32[]{:S(2)}) collective-permute-start(bf16[4,1,32,256]{3,2,1,0:T(8,128)(2,1)S(1)} %get-tuple-element.16), channel_id=1, source_target_pairs={{4,0},{8,4},{12,8},{5,1},{9,5},{13,9},{6,2},{10,6},{14,10},{7,3},{... | collective-permute-start | bytes 196616 | tf_op jit(solution)/shard_map/ppermute | solution.py:25
  61.9 1.9 collective-permute-start.4
  64.1 4.0 %collective-permute-done.4 = bf16[4,1,32,256]{3,2,1,0:T(8,128)(2,1)S(1)} collective-permute-done((bf16[4,1,32,256]{3,2,1,0:T(8,128)(2,1)S(1)}, bf16[4,1,32,256]{3,2,1,0:T(8,128)(2,1)S(1)}, u32[]{:S(2)}, u32[]{:S(2)}) %collective-permute-start.4) | collective-permute-done | bytes 65568 | tf_op jit(solution)/shard_map/ppermute | solution.py:24
  68.2 1.9 collective-permute-start.14
  70.1 3.9 %collective-permute-start.6 = (bf16[4,18,1,256]{3,2,1,0:T(2,128)(2,1)S(1)}, bf16[4,18,1,256]{3,2,1,0:T(2,128)(2,1)}, u32[]{:S(2)}, u32[]{:S(2)}) collective-permute-start(bf16[4,18,1,256]{3,2,1,0:T(2,128)(2,1)S(1)} %get-tuple-element.14), channel_id=1, source_target_pairs={{0,1},{1,2},{2,3},{4,5},{5,6},{6,7},{8,9},{9,10},{10,11},{12,13},{... | collective-permute-start | bytes 110600 | tf_op jit(solution)/shard_map/ppermute | solution.py:24
  74.4 2.0 collective-permute-done.6
  76.5 1.6 pad_maximum_fusion.2
  78.1 1.6 pad_maximum_fusion
  83.3 1.1 add_convert_fusion
  85.2 2.1 %collective-permute-start.15 = (bf16[2,16,32,256]{3,2,1,0:T(8,128)(2,1)}, bf16[2,16,32,256]{3,2,1,0:T(8,128)(2,1)}, u32[]{:S(2)}, u32[]{:S(2)}) collective-permute-start(bf16[2,16,32,256]{3,2,1,0:T(8,128)(2,1)} %slice.202), channel_id=1, source_target_pairs={{0,16},{16,32},{32,48},{48,64},{64,80},{80,96},{96,112},{112,128},... | collective-permute-start | bytes 1572872 | tf_op jit(solution)/shard_map/ppermute | solution.py:33
  88.4 1.2 pad_maximum_fusion.1
  89.6 1.2 fusion.25
  90.8 1.2 fusion.19
  92.4 1.2 fusion.22
  95.0 1.8 copy.50
  96.7 22.0 %all-to-all-start = ((bf16[4,512,256]{2,0,1:T(4,128)(2,1)}), bf16[4,512,256]{2,0,1:T(4,128)(2,1)S(1)}, u32[]{:S(2)}, u32[]{:S(2)}) async-start(bf16[4,512,256]{2,0,1:T(4,128)(2,1)} %copy.50), calls=%async_computation | async-start | bytes 2097152 | tf_op jit(solution)/shard_map/all_to_all | solution.py:148
  119.1 1.9 collective-permute-start.16
  121.1 3.6 %collective-permute-done.16 = f32[2,4,32]{2,1,0:T(4,128)S(1)} collective-permute-done((f32[2,4,32]{2,1,0:T(4,128)S(1)}, f32[2,4,32]{2,1,0:T(4,128)S(1)}, u32[]{:S(2)}, u32[]{:S(2)}) %collective-permute-start.16) | collective-permute-done | bytes 1056 | tf_op jit(solution)/shard_map/ppermute | solution.py:42
  124.6 2.4 %collective-permute-start.17 = (f32[2,4,32]{2,1,0:T(4,128)S(1)}, f32[2,4,32]{2,1,0:T(4,128)S(1)}, u32[]{:S(2)}, u32[]{:S(2)}) collective-permute-start(f32[2,4,32]{2,1,0:T(4,128)S(1)} %fusion.95), channel_id=1, source_target_pairs={{0,8},{4,12},{8,0},{12,4},{1,9},{5,13},{9,1},{13,5},{2,10},{6,14},... | collective-permute-start | bytes 3080 | tf_op jit(solution)/shard_map/ppermute | solution.py:42
  127.1 4.6 %collective-permute-done.17 = f32[2,4,32]{2,1,0:T(4,128)S(1)} collective-permute-done((f32[2,4,32]{2,1,0:T(4,128)S(1)}, f32[2,4,32]{2,1,0:T(4,128)S(1)}, u32[]{:S(2)}, u32[]{:S(2)}) %collective-permute-start.17) | collective-permute-done | bytes 1056 | tf_op jit(solution)/shard_map/ppermute | solution.py:42
  131.6 1.9 collective-permute-start.18
  133.6 3.6 %collective-permute-done.18 = f32[2,4,32]{2,1,0:T(4,128)S(1)} collective-permute-done((f32[2,4,32]{2,1,0:T(4,128)S(1)}, f32[2,4,32]{2,1,0:T(4,128)S(1)}, u32[]{:S(2)}, u32[]{:S(2)}) %collective-permute-start.18) | collective-permute-done | bytes 1056 | tf_op jit(solution)/shard_map/ppermute | solution.py:42
  137.1 1.9 collective-permute-start.19
  139.1 5.0 %collective-permute-done.19 = f32[2,4,32]{2,1,0:T(4,128)S(1)} collective-permute-done((f32[2,4,32]{2,1,0:T(4,128)S(1)}, f32[2,4,32]{2,1,0:T(4,128)S(1)}, u32[]{:S(2)}, u32[]{:S(2)}) %collective-permute-start.19) | collective-permute-done | bytes 1056 | tf_op jit(solution)/shard_map/ppermute | solution.py:42
  144.2 1.8 all-gather
  146.1 44.2 %all_gather.7 = f32[128,64]{1,0:T(8,128)S(1)} all-gather(f32[8,64]{1,0:T(8,128)S(1)} %bitcast.192), channel_id=1, replica_groups=mesh['z'=16,'core'=2,'band'=4,'fsdp'=4] {'z'}, dimensions={0}, use_global_device_ids=true | all-gather | bytes 34816 | tf_op jit(solution)/shard_map/all_gather | solution.py:152
  190.7 1.9 copy_bitcast_fusion
  192.6 2.0 reshape.135
  194.6 2.7 %convolution_convert_fusion = bf16[128,16,768]{2,0,1:T(8,128)(2,1)} fusion(f32[128,16,256]{2,0,1:T(8,128)S(1)} %reshape.135, f32[256]{0:T(256)S(1)} %bitcast.193, f32[128,256]{1,0:T(8,128)S(1)} %copy.55, f32[128,256]{1,0:T(8,128)S(1)} %copy.53, bf16[256,2048]{1,0:T(8,128)(2,1)S(1)} %get-tuple-element.9), kind=kOutput, calls=%fused_computation.8 | convolution fusion | flops 808976384 | bytes 5899264 | tf_op jit(solution)/shard_map/fpc,cd->fpd/dot_general | solution.py:155
  197.3 3.1 %fusion.100 = (f32[16,128]{1,0:T(8,128)S(1)}, f32[16,128,128]{1,2,0:T(8,128)}) fusion(pred[128,128]{0,1:T(8,128)(4,1)S(1)} %fusion.73, bf16[128,16,768]{2,0,1:T(8,128)(2,1)} %convolution_convert_fusion), kind=kOutput, calls=%fused_computation.166 | convolution fusion | flops 135528576 | bytes 3186688 | tf_op jit(solution)/shard_map/sub | solution.py:168
  200.4 3.3 %fusion.31 = bf16[1,1,16,128,256]{4,3,2,1,0:T(8,128)(2,1)} fusion(f32[128,16,256]{2,0,1:T(8,128)S(1)} %reshape.135, bf16[128,16,768]{2,0,1:T(8,128)(2,1)} %convolution_convert_fusion, f32[16,128,128]{1,2,0:T(8,128)} %get-tuple-element.26, f32[16,128]{1,0:T(8,128)S(1)} %get-tuple-element.25, bf16[256,2048]{1,0:T(8,128)(2,1)S(1)} %get-tuple-element.9), kind=kOutput, calls=%fused_computation.41 | convolution fusion | flops 404750336 | bytes 5382144 | tf_op jit(solution)/shard_map/axi,iy->axy/dot_general | solution.py:173
  (91 shorter events, 12.5 us)
Async XLA Ops:
  1.9 17.5 %collective-permute-start = (f32[2,4,32]{2,1,0:T(4,128)S(1)}, f32[2,4,32]{2,1,0:T(4,128)S(1)}, u32[]{:S(2)}, u32[]{:S(2)}) collective-permute-start(f32[2,4,32]{2,1,0:T(4,128)S(1)} %pad_maximum_fusion.6), channel_id=1, source_target_pairs={{0,4},{4,0},{8,12},{12,8},{1,5},{5,1},{9,13},{13,9},{2,6},{6,2},{1... | collective-permute-start | bytes 3080 | tf_op jit(solution)/shard_map/ppermute | solution.py:42
  5.2 33.8 %collective-permute-start.7 = (bf16[16,2048]{1,0:T(8,128)(2,1)S(1)}, bf16[16,2048]{1,0:T(8,128)(2,1)S(1)}, u32[]{:S(2)}, u32[]{:S(2)}) collective-permute-start(bf16[16,2048]{1,0:T(8,128)(2,1)S(1)} %fusion.72), channel_id=1, source_target_pairs={{0,3},{1,0},{2,1},{3,2},{4,7},{5,4},{6,5},{7,6},{8,11},{9,8},{10,9... | collective-permute-start | bytes 196616 | tf_op jit(solution)/shard_map/ppermute | solution.py:52
  7.7 31.3 %collective-permute-start.8 = (bf16[16,2048]{1,0:T(8,128)(2,1)S(1)}, bf16[16,2048]{1,0:T(8,128)(2,1)S(1)}, u32[]{:S(2)}, u32[]{:S(2)}) collective-permute-start(bf16[16,2048]{1,0:T(8,128)(2,1)S(1)} %fusion.72), channel_id=1, source_target_pairs={{0,2},{1,3},{2,0},{3,1},{4,6},{5,7},{6,4},{7,5},{8,10},{9,11},{10,... | collective-permute-start | bytes 196616 | tf_op jit(solution)/shard_map/ppermute | solution.py:52
  14.9 24.1 %collective-permute-start.9 = (bf16[16,2048]{1,0:T(8,128)(2,1)S(1)}, bf16[16,2048]{1,0:T(8,128)(2,1)S(1)}, u32[]{:S(2)}, u32[]{:S(2)}) collective-permute-start(bf16[16,2048]{1,0:T(8,128)(2,1)S(1)} %fusion.72), channel_id=1, source_target_pairs={{0,1},{1,2},{2,3},{3,0},{4,5},{5,6},{6,7},{7,4},{8,9},{9,10},{10,1... | collective-permute-start | bytes 196616 | tf_op jit(solution)/shard_map/ppermute | solution.py:52
  19.5 7.0 %collective-permute-start.1 = (f32[2,4,32]{2,1,0:T(4,128)S(1)}, f32[2,4,32]{2,1,0:T(4,128)S(1)}, u32[]{:S(2)}, u32[]{:S(2)}) collective-permute-start(f32[2,4,32]{2,1,0:T(4,128)S(1)} %fusion.96), channel_id=1, source_target_pairs={{0,8},{4,12},{8,0},{12,4},{1,9},{5,13},{9,1},{13,5},{2,10},{6,14},... | collective-permute-start | bytes 3080 | tf_op jit(solution)/shard_map/ppermute | solution.py:42
  26.5 5.5 %collective-permute-start.2 = (f32[2,4,32]{2,1,0:T(4,128)S(1)}, f32[2,4,32]{2,1,0:T(4,128)S(1)}, u32[]{:S(2)}, u32[]{:S(2)}) collective-permute-start(f32[2,4,32]{2,1,0:T(4,128)S(1)} %fusion.107), channel_id=1, source_target_pairs={{0,1},{1,0},{2,3},{3,2},{4,5},{5,4},{6,7},{7,6},{8,9},{9,8},{10,11... | collective-permute-start | bytes 3080 | tf_op jit(solution)/shard_map/ppermute | solution.py:42
  32.0 7.0 %collective-permute-start.3 = (f32[2,4,32]{2,1,0:T(4,128)S(1)}, f32[2,4,32]{2,1,0:T(4,128)S(1)}, u32[]{:S(2)}, u32[]{:S(2)}) collective-permute-start(f32[2,4,32]{2,1,0:T(4,128)S(1)} %add.141), channel_id=1, source_target_pairs={{0,2},{1,3},{2,0},{3,1},{4,6},{5,7},{6,4},{7,5},{8,10},{9,11},{10,... | collective-permute-start | bytes 3080 | tf_op jit(solution)/shard_map/ppermute | solution.py:42
  39.1 8.8 %collective-permute-start.10 = (bf16[64,2048]{1,0:T(8,128)(2,1)S(1)}, bf16[64,2048]{1,0:T(8,128)(2,1)S(1)}, u32[]{:S(2)}, u32[]{:S(2)}) collective-permute-start(bf16[64,2048]{1,0:T(8,128)(2,1)S(1)} %bitcast.175), channel_id=1, source_target_pairs={{0,12},{4,0},{8,4},{12,8},{1,13},{5,1},{9,5},{13,9},{2,14},{6,2},{... | collective-permute-start | bytes 786440 | tf_op jit(solution)/shard_map/ppermute | solution.py:52
  41.5 9.8 %collective-permute-start.11 = (bf16[64,2048]{1,0:T(8,128)(2,1)S(1)}, bf16[64,2048]{1,0:T(8,128)(2,1)S(1)}, u32[]{:S(2)}, u32[]{:S(2)}) collective-permute-start(bf16[64,2048]{1,0:T(8,128)(2,1)S(1)} %bitcast.176), channel_id=1, source_target_pairs={{0,8},{4,12},{8,0},{12,4},{1,9},{5,13},{9,1},{13,5},{2,10},{6,14},... | collective-permute-start | bytes 786440 | tf_op jit(solution)/shard_map/ppermute | solution.py:52
  43.4 11.2 %collective-permute-start.12 = (bf16[64,2048]{1,0:T(8,128)(2,1)S(1)}, bf16[64,2048]{1,0:T(8,128)(2,1)S(1)}, u32[]{:S(2)}, u32[]{:S(2)}) collective-permute-start(bf16[64,2048]{1,0:T(8,128)(2,1)S(1)} %bitcast.177), channel_id=1, source_target_pairs={{0,4},{4,8},{8,12},{12,0},{1,5},{5,9},{9,13},{13,1},{2,6},{6,10},{... | collective-permute-start | bytes 786440 | tf_op jit(solution)/shard_map/ppermute | solution.py:52
  54.7 2.3 %copy-start = (bf16[4,16,32,256]{3,2,1,0:T(8,128)(2,1)S(1)}, bf16[4,16,32,256]{3,2,1,0:T(8,128)(2,1)}, u32[]{:S(2)}) copy-start(bf16[4,16,32,256]{3,2,1,0:T(8,128)(2,1)} %param.7) | copy-start | bytes 3145732
  54.9 23.2 %collective-permute-start.13 = (bf16[256,2048]{1,0:T(8,128)(2,1)S(1)}, bf16[256,2048]{1,0:T(8,128)(2,1)}, u32[]{:S(2)}, u32[]{:S(2)}) collective-permute-start(bf16[256,2048]{1,0:T(8,128)(2,1)S(1)} %bitcast.171), channel_id=1, source_target_pairs={{0,16},{16,0},{1,17},{17,1},{2,18},{18,2},{3,19},{19,3},{4,20},{20... | collective-permute-start | bytes 3145736 | tf_op jit(solution)/shard_map/ppermute | solution.py:98
  57.7 6.4 %collective-permute-start.5 = (bf16[4,1,32,256]{3,2,1,0:T(8,128)(2,1)S(1)}, bf16[4,1,32,256]{3,2,1,0:T(8,128)(2,1)S(1)}, u32[]{:S(2)}, u32[]{:S(2)}) collective-permute-start(bf16[4,1,32,256]{3,2,1,0:T(8,128)(2,1)S(1)} %get-tuple-element.16), channel_id=1, source_target_pairs={{4,0},{8,4},{12,8},{5,1},{9,5},{13,9},{6,2},{10,6},{14,10},{7,3},{... | collective-permute-start | bytes 196616 | tf_op jit(solution)/shard_map/ppermute | solution.py:25
  61.9 6.2 %collective-permute-start.4 = (bf16[4,1,32,256]{3,2,1,0:T(8,128)(2,1)S(1)}, bf16[4,1,32,256]{3,2,1,0:T(8,128)(2,1)S(1)}, u32[]{:S(2)}, u32[]{:S(2)}) collective-permute-start(bf16[4,1,32,256]{3,2,1,0:T(8,128)(2,1)S(1)} %get-tuple-element.15), channel_id=1, source_target_pairs={{0,4},{4,8},{8,12},{1,5},{5,9},{9,13},{2,6},{6,10},{10,14},{3,7},{... | collective-permute-start | bytes 196616 | tf_op jit(solution)/shard_map/ppermute | solution.py:24
  68.2 6.2 %collective-permute-start.14 = (bf16[4,18,1,256]{3,2,1,0:T(2,128)(2,1)S(1)}, bf16[4,18,1,256]{3,2,1,0:T(2,128)(2,1)S(1)}, u32[]{:S(2)}, u32[]{:S(2)}) collective-permute-start(bf16[4,18,1,256]{3,2,1,0:T(2,128)(2,1)S(1)} %get-tuple-element.13), channel_id=1, source_target_pairs={{1,0},{2,1},{3,2},{5,4},{6,5},{7,6},{9,8},{10,9},{11,10},{13,12},{... | collective-permute-start | bytes 110600 | tf_op jit(solution)/shard_map/ppermute | solution.py:25
  70.1 6.4 %collective-permute-start.6 = (bf16[4,18,1,256]{3,2,1,0:T(2,128)(2,1)S(1)}, bf16[4,18,1,256]{3,2,1,0:T(2,128)(2,1)}, u32[]{:S(2)}, u32[]{:S(2)}) collective-permute-start(bf16[4,18,1,256]{3,2,1,0:T(2,128)(2,1)S(1)} %get-tuple-element.14), channel_id=1, source_target_pairs={{0,1},{1,2},{2,3},{4,5},{5,6},{6,7},{8,9},{9,10},{10,11},{12,13},{... | collective-permute-start | bytes 110600 | tf_op jit(solution)/shard_map/ppermute | solution.py:24
  83.3 4.0 %copy-start.1 = (s32[16]{0:T(128)S(1)}, s32[16]{0:T(128)}, u32[]{:S(2)}) copy-start(s32[16]{0:T(128)} %param.8) | copy-start | bytes 196
  85.2 3.1 %collective-permute-start.15 = (bf16[2,16,32,256]{3,2,1,0:T(8,128)(2,1)}, bf16[2,16,32,256]{3,2,1,0:T(8,128)(2,1)}, u32[]{:S(2)}, u32[]{:S(2)}) collective-permute-start(bf16[2,16,32,256]{3,2,1,0:T(8,128)(2,1)} %slice.202), channel_id=1, source_target_pairs={{0,16},{16,32},{32,48},{48,64},{64,80},{80,96},{96,112},{112,128},... | collective-permute-start | bytes 1572872 | tf_op jit(solution)/shard_map/ppermute | solution.py:33
  96.7 94.0 %all-to-all-start = ((bf16[4,512,256]{2,0,1:T(4,128)(2,1)}), bf16[4,512,256]{2,0,1:T(4,128)(2,1)S(1)}, u32[]{:S(2)}, u32[]{:S(2)}) async-start(bf16[4,512,256]{2,0,1:T(4,128)(2,1)} %copy.50), calls=%async_computation | async-start | bytes 2097152 | tf_op jit(solution)/shard_map/all_to_all | solution.py:148
  119.1 5.5 %collective-permute-start.16 = (f32[2,4,32]{2,1,0:T(4,128)S(1)}, f32[2,4,32]{2,1,0:T(4,128)S(1)}, u32[]{:S(2)}, u32[]{:S(2)}) collective-permute-start(f32[2,4,32]{2,1,0:T(4,128)S(1)} %pad_maximum_fusion.7), channel_id=1, source_target_pairs={{0,4},{4,0},{8,12},{12,8},{1,5},{5,1},{9,13},{13,9},{2,6},{6,2},{1... | collective-permute-start | bytes 3080 | tf_op jit(solution)/shard_map/ppermute | solution.py:42
  124.6 7.0 %collective-permute-start.17 = (f32[2,4,32]{2,1,0:T(4,128)S(1)}, f32[2,4,32]{2,1,0:T(4,128)S(1)}, u32[]{:S(2)}, u32[]{:S(2)}) collective-permute-start(f32[2,4,32]{2,1,0:T(4,128)S(1)} %fusion.95), channel_id=1, source_target_pairs={{0,8},{4,12},{8,0},{12,4},{1,9},{5,13},{9,1},{13,5},{2,10},{6,14},... | collective-permute-start | bytes 3080 | tf_op jit(solution)/shard_map/ppermute | solution.py:42
  131.6 5.5 %collective-permute-start.18 = (f32[2,4,32]{2,1,0:T(4,128)S(1)}, f32[2,4,32]{2,1,0:T(4,128)S(1)}, u32[]{:S(2)}, u32[]{:S(2)}) collective-permute-start(f32[2,4,32]{2,1,0:T(4,128)S(1)} %fusion.106), channel_id=1, source_target_pairs={{0,1},{1,0},{2,3},{3,2},{4,5},{5,4},{6,7},{7,6},{8,9},{9,8},{10,11... | collective-permute-start | bytes 3080 | tf_op jit(solution)/shard_map/ppermute | solution.py:42
  137.1 7.0 %collective-permute-start.19 = (f32[2,4,32]{2,1,0:T(4,128)S(1)}, f32[2,4,32]{2,1,0:T(4,128)S(1)}, u32[]{:S(2)}, u32[]{:S(2)}) collective-permute-start(f32[2,4,32]{2,1,0:T(4,128)S(1)} %add.170), channel_id=1, source_target_pairs={{0,2},{1,3},{2,0},{3,1},{4,6},{5,7},{6,4},{7,5},{8,10},{9,11},{10,... | collective-permute-start | bytes 3080 | tf_op jit(solution)/shard_map/ppermute | solution.py:42

commit v9 on v7

--- a/solution.py
+++ b/solution.py
@@ -33,17 +33,6 @@
     return lax.ppermute(x, axis, pairs)
 
 
-def butterfly_sum(x, axes):
-    for axis in axes:
-        size = lax.axis_size(axis)
-        step = 1
-        while step < size:
-            pairs = [(i, i ^ step) for i in range(size)]
-            x = x + lax.ppermute(x, axis, pairs)
-            step *= 2
-    return x
-
-
 def ring_gather(x, axis):
     size = lax.axis_size(axis)
     me = lax.axis_index(axis)
@@ -69,7 +58,8 @@
     vals = field.astype(jnp.float32).reshape(frames, height * width, GROUPS, group_width)
     sums = jnp.sum(vals, axis=(1, 3))
     squares = jnp.sum(vals * vals, axis=(1, 3))
-    both = butterfly_sum(jnp.stack([sums, squares]), ("band", "fsdp"))
+    both = lax.psum(jnp.stack([sums, squares]), "band")
+    both = lax.psum(lax.optimization_barrier(both), "fsdp")
     sums, squares = both[0], both[1]
     count = height * width * group_width * lax.axis_size("band") * lax.axis_size("fsdp")
     mean = sums / count

time: 202 us -> 198 us (0.980)
  the two profiles are of different devices: /device:TPU:12 before, /device:TPU:18 now
where the time goes in v9:
time: 198 us; the launch traced here: 197 us
  blocking collectives  89.1 us (45%)
  starting transfers between devices  60.5 us (31%)
  matrix products  20.6 us (10%)
  waiting for transfers between devices  13.4 us (7%)
  other arithmetic  8.76 us (4%)
  local copies, waits for them, and re-layouts  3.7 us (2%)
    all_gather x2, blocking collectives, body(): moments = lax.all_gather(moments, axis, axis=0, tiled=True)  56.9 us
    all_to_all x1, starting transfers between devices, body(): lax.all_to_all(flat_resid, TM, split_axis=0, concat_axis=0, tiled=True)  23.5 us
    ppermute x6, starting transfers between devices, ring_gather(): lax.ppermute(x, axis, [(i, (i + shift) % size) for i in range(size)])  21.2 us
    psum x2, blocking collectives, group_moments(): both = lax.psum(lax.optimization_barrier(both), 'fsdp')  16.9 us
    psum x2, blocking collectives, group_moments(): both = lax.psum(jnp.stack([sums, squares]), 'band')  15.2 us
    ppermute x2, starting transfers between devices, with_halo(): after = lax.ppermute(initial, axis, down)  7.05 us
    ppermute x6, waiting for transfers between devices, ring_gather(): lax.ppermute(x, axis, [(i, (i + shift) % size) for i in range(size)])  6.61 us
    dot_general x1, matrix products, body(): jnp.einsum('fpc,cd->fpd', flat_norm, qkv_full, preferred_element_type=jnp...  4.64 us
  transfers between devices with their start and end apart: 13, of which 7 were waited for; matrix products, arithmetic and copies ran while one was open for 3% of the time, Pallas kernels for 0%

profile of v9, /device:TPU:18, one launch (start us, length us, event | category | flops | bytes accessed | tf_op | source)
XLA Modules:
  0.0 196.6 jit_solution(13003015931968332106)
XLA Ops:
  0.0 0.9 fusion.72
  0.9 2.4 %collective-permute-start.3 = (bf16[16,2048]{1,0:T(8,128)(2,1)S(1)}, bf16[16,2048]{1,0:T(8,128)(2,1)S(1)}, u32[]{:S(2)}, u32[]{:S(2)}) collective-permute-start(bf16[16,2048]{1,0:T(8,128)(2,1)S(1)} %fusion.72), channel_id=1, source_target_pairs={{0,3},{1,0},{2,1},{3,2},{4,7},{5,4},{6,5},{7,6},{8,11},{9,8},{10,9... | collective-permute-start | bytes 196616 | tf_op jit(solution)/shard_map/ppermute | solution.py:41
  3.4 4.3 %collective-permute-start.4 = (bf16[16,2048]{1,0:T(8,128)(2,1)S(1)}, bf16[16,2048]{1,0:T(8,128)(2,1)S(1)}, u32[]{:S(2)}, u32[]{:S(2)}) collective-permute-start(bf16[16,2048]{1,0:T(8,128)(2,1)S(1)} %fusion.72), channel_id=1, source_target_pairs={{0,2},{1,3},{2,0},{3,1},{4,6},{5,7},{6,4},{7,5},{8,10},{9,11},{10,... | collective-permute-start | bytes 196616 | tf_op jit(solution)/shard_map/ppermute | solution.py:41
  7.7 3.7 %collective-permute-start.5 = (bf16[16,2048]{1,0:T(8,128)(2,1)S(1)}, bf16[16,2048]{1,0:T(8,128)(2,1)S(1)}, u32[]{:S(2)}, u32[]{:S(2)}) collective-permute-start(bf16[16,2048]{1,0:T(8,128)(2,1)S(1)} %fusion.72), channel_id=1, source_target_pairs={{0,1},{1,2},{2,3},{3,0},{4,5},{5,6},{6,7},{7,4},{8,9},{9,10},{10,1... | collective-permute-start | bytes 196616 | tf_op jit(solution)/shard_map/ppermute | solution.py:41
  11.4 1.5 convert_reduce_fusion
  13.4 8.4 %psum.28 = f32[2,4,32]{2,1,0:T(4,128)S(1)} all-reduce(f32[2,4,32]{2,1,0:T(4,128)S(1)} %pad_maximum_fusion.6), channel_id=1, replica_groups=mesh['z'=16,'core'=2,'band'=4,'fsdp'=4] {'band'}, use_global_device_ids=true, to_apply=%region_6.7 | all-reduce | flops 256 | bytes 2048 | tf_op jit(solution)/shard_map/psum | solution.py:61
  21.8 9.7 %psum.29 = f32[2,4,32]{2,1,0:T(4,128)S(1)} all-reduce(f32[2,4,32]{2,1,0:T(4,128)S(1)} %psum.28), channel_id=1, replica_groups=mesh['z'=16,'core'=2,'band'=4,'fsdp'=4] {'fsdp'}, use_global_device_ids=true, to_apply=%region_7.8 | all-reduce | flops 256 | bytes 2048 | tf_op jit(solution)/shard_map/psum | solution.py:62
  31.6 4.8 %collective-permute-start.6 = (bf16[64,2048]{1,0:T(8,128)(2,1)S(1)}, bf16[64,2048]{1,0:T(8,128)(2,1)S(1)}, u32[]{:S(2)}, u32[]{:S(2)}) collective-permute-start(bf16[64,2048]{1,0:T(8,128)(2,1)S(1)} %bitcast.174), channel_id=1, source_target_pairs={{0,12},{4,0},{8,4},{12,8},{1,13},{5,1},{9,5},{13,9},{2,14},{6,2},{... | collective-permute-start | bytes 786440 | tf_op jit(solution)/shard_map/ppermute | solution.py:41
  36.9 3.4 %collective-permute-start.7 = (bf16[64,2048]{1,0:T(8,128)(2,1)S(1)}, bf16[64,2048]{1,0:T(8,128)(2,1)S(1)}, u32[]{:S(2)}, u32[]{:S(2)}) collective-permute-start(bf16[64,2048]{1,0:T(8,128)(2,1)S(1)} %bitcast.175), channel_id=1, source_target_pairs={{0,8},{4,12},{8,0},{12,4},{1,9},{5,13},{9,1},{13,5},{2,10},{6,14},... | collective-permute-start | bytes 786440 | tf_op jit(solution)/shard_map/ppermute | solution.py:41
  40.2 2.5 %collective-permute-start.8 = (bf16[64,2048]{1,0:T(8,128)(2,1)S(1)}, bf16[64,2048]{1,0:T(8,128)(2,1)S(1)}, u32[]{:S(2)}, u32[]{:S(2)}) collective-permute-start(bf16[64,2048]{1,0:T(8,128)(2,1)S(1)} %bitcast.176), channel_id=1, source_target_pairs={{0,4},{4,8},{8,12},{12,0},{1,5},{5,9},{9,13},{13,1},{2,6},{6,10},{... | collective-permute-start | bytes 786440 | tf_op jit(solution)/shard_map/ppermute | solution.py:41
  42.8 3.9 %collective-permute-done.7 = bf16[64,2048]{1,0:T(8,128)(2,1)S(1)} collective-permute-done((bf16[64,2048]{1,0:T(8,128)(2,1)S(1)}, bf16[64,2048]{1,0:T(8,128)(2,1)S(1)}, u32[]{:S(2)}, u32[]{:S(2)}) %collective-permute-start.7) | collective-permute-done | bytes 262176 | tf_op jit(solution)/shard_map/ppermute | solution.py:41
  46.8 2.7 %collective-permute-done.8 = bf16[64,2048]{1,0:T(8,128)(2,1)S(1)} collective-permute-done((bf16[64,2048]{1,0:T(8,128)(2,1)S(1)}, bf16[64,2048]{1,0:T(8,128)(2,1)S(1)}, u32[]{:S(2)}, u32[]{:S(2)}) %collective-permute-start.8) | collective-permute-done | bytes 262176 | tf_op jit(solution)/shard_map/ppermute | solution.py:41
  49.7 2.1 %collective-permute-start.9 = (bf16[256,2048]{1,0:T(8,128)(2,1)S(1)}, bf16[256,2048]{1,0:T(8,128)(2,1)}, u32[]{:S(2)}, u32[]{:S(2)}) collective-permute-start(bf16[256,2048]{1,0:T(8,128)(2,1)S(1)} %bitcast.171), channel_id=1, source_target_pairs={{0,16},{16,0},{1,17},{17,1},{2,18},{18,2},{3,19},{19,3},{4,20},{20... | collective-permute-start | bytes 3145736 | tf_op jit(solution)/shard_map/ppermute | solution.py:88
  51.8 0.7 fusion.16
  52.5 1.9 collective-permute-start
  54.4 3.9 %collective-permute-start.1 = (bf16[4,1,32,256]{3,2,1,0:T(8,128)(2,1)S(1)}, bf16[4,1,32,256]{3,2,1,0:T(8,128)(2,1)S(1)}, u32[]{:S(2)}, u32[]{:S(2)}) collective-permute-start(bf16[4,1,32,256]{3,2,1,0:T(8,128)(2,1)S(1)} %get-tuple-element.16), channel_id=1, source_target_pairs={{4,0},{8,4},{12,8},{5,1},{9,5},{13,9},{6,2},{10,6},{14,10},{7,3},{... | collective-permute-start | bytes 196616 | tf_op jit(solution)/shard_map/ppermute | solution.py:25
  58.3 0.5 collective-permute-done
  58.9 1.9 collective-permute-done.1
  60.9 3.1 %collective-permute-start.10 = (bf16[4,18,1,256]{3,2,1,0:T(2,128)(2,1)S(1)}, bf16[4,18,1,256]{3,2,1,0:T(2,128)(2,1)S(1)}, u32[]{:S(2)}, u32[]{:S(2)}) collective-permute-start(bf16[4,18,1,256]{3,2,1,0:T(2,128)(2,1)S(1)} %get-tuple-element.13), channel_id=1, source_target_pairs={{1,0},{2,1},{3,2},{5,4},{6,5},{7,6},{9,8},{10,9},{11,10},{13,12},{... | collective-permute-start | bytes 110600 | tf_op jit(solution)/shard_map/ppermute | solution.py:25
  64.1 2.7 %collective-permute-start.2 = (bf16[4,18,1,256]{3,2,1,0:T(2,128)(2,1)S(1)}, bf16[4,18,1,256]{3,2,1,0:T(2,128)(2,1)}, u32[]{:S(2)}, u32[]{:S(2)}) collective-permute-start(bf16[4,18,1,256]{3,2,1,0:T(2,128)(2,1)S(1)} %get-tuple-element.14), channel_id=1, source_target_pairs={{0,1},{1,2},{2,3},{4,5},{5,6},{6,7},{8,9},{9,10},{10,11},{12,13},{... | collective-permute-start | bytes 110600 | tf_op jit(solution)/shard_map/ppermute | solution.py:24
  67.2 3.2 %collective-permute-done.2 = bf16[4,18,1,256]{3,2,1,0:T(2,128)(2,1)} collective-permute-done((bf16[4,18,1,256]{3,2,1,0:T(2,128)(2,1)S(1)}, bf16[4,18,1,256]{3,2,1,0:T(2,128)(2,1)}, u32[]{:S(2)}, u32[]{:S(2)}) %collective-permute-start.2) | collective-permute-done | bytes 36896 | tf_op jit(solution)/shard_map/ppermute | solution.py:24
  70.4 1.6 pad_maximum_fusion.2
  72.0 1.6 pad_maximum_fusion
  74.2 0.4 fusion.53
  74.6 0.5 fusion.55
  75.1 0.5 fusion.51
  75.5 0.4 fusion.49
  76.0 0.4 fusion.69
  77.3 1.1 add_convert_fusion
  78.4 0.8 slice.202
  79.2 2.1 %collective-permute-start.11 = (bf16[2,16,32,256]{3,2,1,0:T(8,128)(2,1)}, bf16[2,16,32,256]{3,2,1,0:T(8,128)(2,1)}, u32[]{:S(2)}, u32[]{:S(2)}) collective-permute-start(bf16[2,16,32,256]{3,2,1,0:T(8,128)(2,1)} %slice.202), channel_id=1, source_target_pairs={{0,16},{16,32},{32,48},{48,64},{64,80},{80,96},{96,112},{112,128},... | collective-permute-start | bytes 1572872 | tf_op jit(solution)/shard_map/ppermute | solution.py:33
  81.7 0.6 collective-permute-done.11
  82.3 1.2 pad_maximum_fusion.1
  83.5 1.2 fusion.22
  84.7 0.4 fusion.60
  85.2 1.2 fusion.19
  86.4 0.4 fusion.62
  86.8 1.2 fusion.25
  88.0 0.9 convert_reduce_fusion.1
  88.9 1.1 copy.100
  90.0 23.5 %all-to-all-start = ((bf16[32,4,16,256]{3,2,1,0:T(8,128)(2,1)}), bf16[32,4,16,256]{3,2,1,0:T(8,128)(2,1)S(1)}, u32[]{:S(2)}, u32[]{:S(2)}) async-start(bf16[32,4,16,256]{3,2,1,0:T(8,128)(2,1)} %bitcast.168), calls=%async_computation | async-start | bytes 2097152 | tf_op jit(solution)/shard_map/all_to_all | solution.py:139
  114.0 6.8 %psum.30 = f32[2,4,32]{2,1,0:T(4,128)S(1)} all-reduce(f32[2,4,32]{2,1,0:T(4,128)S(1)} %pad_maximum_fusion.7), channel_id=1, replica_groups=mesh['z'=16,'core'=2,'band'=4,'fsdp'=4] {'band'}, use_global_device_ids=true, to_apply=%region_12.13 | all-reduce | flops 256 | bytes 2048 | tf_op jit(solution)/shard_map/psum | solution.py:61
  120.8 7.3 %psum.31 = f32[2,4,32]{2,1,0:T(4,128)S(1)} all-reduce(f32[2,4,32]{2,1,0:T(4,128)S(1)} %psum.30), channel_id=1, replica_groups=mesh['z'=16,'core'=2,'band'=4,'fsdp'=4] {'fsdp'}, use_global_device_ids=true, to_apply=%region_13.14 | all-reduce | flops 256 | bytes 2048 | tf_op jit(solution)/shard_map/psum | solution.py:62
  128.2 1.8 all-gather
  130.0 55.1 %all_gather.7 = f32[128,64]{1,0:T(8,128)S(1)} all-gather(f32[8,64]{1,0:T(8,128)S(1)} %bitcast.179), channel_id=1, replica_groups=mesh['z'=16,'core'=2,'band'=4,'fsdp'=4] {'z'}, dimensions={0}, use_global_device_ids=true | all-gather | bytes 34816 | tf_op jit(solution)/shard_map/all_gather | solution.py:144
  185.9 4.6 %convolution_convert_fusion = bf16[128,16,768]{2,0,1:T(8,128)(2,1)} fusion(f32[128,16,256]{2,1,0:T(8,128)S(1)} %bitcast_convert_fusion, f32[256]{0:T(256)S(1)} %bitcast.184, f32[128,256]{1,0:T(8,128)S(1)} %copy.55, f32[128,256]{1,0:T(8,128)S(1)} %copy.53, bf16[256,2048]{1,0:T(8,128)(2,1)} %copy-done.1), kind=kOutput, calls=%fused_computation.8 | convolution fusion | flops 808976384 | bytes 5899264 | tf_op jit(solution)/shard_map/fpc,cd->fpd/dot_general | solution.py:147
  190.6 2.1 %fusion.98 = (f32[16,128]{1,0:T(8,128)S(1)}, f32[16,128,128]{1,2,0:T(8,128)S(1)}) fusion(pred[128,128]{0,1:T(8,128)(4,1)S(1)} %fusion.73, bf16[128,16,768]{2,0,1:T(8,128)(2,1)} %convolution_convert_fusion), kind=kOutput, calls=%fused_computation.165 | convolution fusion | flops 135528576 | bytes 3186688 | tf_op jit(solution)/shard_map/sub | solution.py:160
  192.7 3.9 %fusion.31 = bf16[1,1,16,128,256]{4,3,2,1,0:T(8,128)(2,1)} fusion(f32[128,16,256]{2,1,0:T(8,128)S(1)} %bitcast_convert_fusion, bf16[128,16,768]{2,0,1:T(8,128)(2,1)} %convolution_convert_fusion, f32[16,128,128]{1,2,0:T(8,128)S(1)} %get-tuple-element.26, f32[16,128]{1,0:T(8,128)S(1)} %get-tuple-element.25, bf16[256,2048]{1,0:T(8,128)(2,1)} %copy-done.1), kind=kOutput, calls=%fused_computation.40 | convolution fusion | flops 404750336 | bytes 5382144 | tf_op jit(solution)/shard_map/axi,iy->axy/dot_general | solution.py:165
  (74 shorter events, 4.8 us)
Async XLA Ops:
  0.0 36.8 %copy-start.2 = (f32[2,256]{1,0:T(2,128)S(1)}, f32[2,256]{1,0:T(2,128)}, u32[]{:S(2)}) copy-start(f32[2,256]{1,0:T(2,128)} %param.9) | copy-start | bytes 6148
  0.9 30.5 %collective-permute-start.3 = (bf16[16,2048]{1,0:T(8,128)(2,1)S(1)}, bf16[16,2048]{1,0:T(8,128)(2,1)S(1)}, u32[]{:S(2)}, u32[]{:S(2)}) collective-permute-start(bf16[16,2048]{1,0:T(8,128)(2,1)S(1)} %fusion.72), channel_id=1, source_target_pairs={{0,3},{1,0},{2,1},{3,2},{4,7},{5,4},{6,5},{7,6},{8,11},{9,8},{10,9... | collective-permute-start | bytes 196616 | tf_op jit(solution)/shard_map/ppermute | solution.py:41
  3.4 28.1 %collective-permute-start.4 = (bf16[16,2048]{1,0:T(8,128)(2,1)S(1)}, bf16[16,2048]{1,0:T(8,128)(2,1)S(1)}, u32[]{:S(2)}, u32[]{:S(2)}) collective-permute-start(bf16[16,2048]{1,0:T(8,128)(2,1)S(1)} %fusion.72), channel_id=1, source_target_pairs={{0,2},{1,3},{2,0},{3,1},{4,6},{5,7},{6,4},{7,5},{8,10},{9,11},{10,... | collective-permute-start | bytes 196616 | tf_op jit(solution)/shard_map/ppermute | solution.py:41
  7.7 23.8 %collective-permute-start.5 = (bf16[16,2048]{1,0:T(8,128)(2,1)S(1)}, bf16[16,2048]{1,0:T(8,128)(2,1)S(1)}, u32[]{:S(2)}, u32[]{:S(2)}) collective-permute-start(bf16[16,2048]{1,0:T(8,128)(2,1)S(1)} %fusion.72), channel_id=1, source_target_pairs={{0,1},{1,2},{2,3},{3,0},{4,5},{5,6},{6,7},{7,4},{8,9},{9,10},{10,1... | collective-permute-start | bytes 196616 | tf_op jit(solution)/shard_map/ppermute | solution.py:41
  31.6 11.2 %collective-permute-start.6 = (bf16[64,2048]{1,0:T(8,128)(2,1)S(1)}, bf16[64,2048]{1,0:T(8,128)(2,1)S(1)}, u32[]{:S(2)}, u32[]{:S(2)}) collective-permute-start(bf16[64,2048]{1,0:T(8,128)(2,1)S(1)} %bitcast.174), channel_id=1, source_target_pairs={{0,12},{4,0},{8,4},{12,8},{1,13},{5,1},{9,5},{13,9},{2,14},{6,2},{... | collective-permute-start | bytes 786440 | tf_op jit(solution)/shard_map/ppermute | solution.py:41
  36.9 9.9 %collective-permute-start.7 = (bf16[64,2048]{1,0:T(8,128)(2,1)S(1)}, bf16[64,2048]{1,0:T(8,128)(2,1)S(1)}, u32[]{:S(2)}, u32[]{:S(2)}) collective-permute-start(bf16[64,2048]{1,0:T(8,128)(2,1)S(1)} %bitcast.175), channel_id=1, source_target_pairs={{0,8},{4,12},{8,0},{12,4},{1,9},{5,13},{9,1},{13,5},{2,10},{6,14},... | collective-permute-start | bytes 786440 | tf_op jit(solution)/shard_map/ppermute | solution.py:41
  40.2 9.2 %collective-permute-start.8 = (bf16[64,2048]{1,0:T(8,128)(2,1)S(1)}, bf16[64,2048]{1,0:T(8,128)(2,1)S(1)}, u32[]{:S(2)}, u32[]{:S(2)}) collective-permute-start(bf16[64,2048]{1,0:T(8,128)(2,1)S(1)} %bitcast.176), channel_id=1, source_target_pairs={{0,4},{4,8},{8,12},{12,0},{1,5},{5,9},{9,13},{13,1},{2,6},{6,10},{... | collective-permute-start | bytes 786440 | tf_op jit(solution)/shard_map/ppermute | solution.py:41
  49.5 2.3 %copy-start = (bf16[4,16,32,256]{3,2,1,0:T(8,128)(2,1)S(1)}, bf16[4,16,32,256]{3,2,1,0:T(8,128)(2,1)}, u32[]{:S(2)}) copy-start(bf16[4,16,32,256]{3,2,1,0:T(8,128)(2,1)} %param.7) | copy-start | bytes 3145732
  49.7 22.3 %collective-permute-start.9 = (bf16[256,2048]{1,0:T(8,128)(2,1)S(1)}, bf16[256,2048]{1,0:T(8,128)(2,1)}, u32[]{:S(2)}, u32[]{:S(2)}) collective-permute-start(bf16[256,2048]{1,0:T(8,128)(2,1)S(1)} %bitcast.171), channel_id=1, source_target_pairs={{0,16},{16,0},{1,17},{17,1},{2,18},{18,2},{3,19},{19,3},{4,20},{20... | collective-permute-start | bytes 3145736 | tf_op jit(solution)/shard_map/ppermute | solution.py:88
  52.5 6.4 %collective-permute-start = (bf16[4,1,32,256]{3,2,1,0:T(8,128)(2,1)S(1)}, bf16[4,1,32,256]{3,2,1,0:T(8,128)(2,1)S(1)}, u32[]{:S(2)}, u32[]{:S(2)}) collective-permute-start(bf16[4,1,32,256]{3,2,1,0:T(8,128)(2,1)S(1)} %get-tuple-element.15), channel_id=1, source_target_pairs={{0,4},{4,8},{8,12},{1,5},{5,9},{9,13},{2,6},{6,10},{10,14},{3,7},{... | collective-permute-start | bytes 196616 | tf_op jit(solution)/shard_map/ppermute | solution.py:24
  54.4 6.4 %collective-permute-start.1 = (bf16[4,1,32,256]{3,2,1,0:T(8,128)(2,1)S(1)}, bf16[4,1,32,256]{3,2,1,0:T(8,128)(2,1)S(1)}, u32[]{:S(2)}, u32[]{:S(2)}) collective-permute-start(bf16[4,1,32,256]{3,2,1,0:T(8,128)(2,1)S(1)} %get-tuple-element.16), channel_id=1, source_target_pairs={{4,0},{8,4},{12,8},{5,1},{9,5},{13,9},{6,2},{10,6},{14,10},{7,3},{... | collective-permute-start | bytes 196616 | tf_op jit(solution)/shard_map/ppermute | solution.py:25
  60.9 6.2 %collective-permute-start.10 = (bf16[4,18,1,256]{3,2,1,0:T(2,128)(2,1)S(1)}, bf16[4,18,1,256]{3,2,1,0:T(2,128)(2,1)S(1)}, u32[]{:S(2)}, u32[]{:S(2)}) collective-permute-start(bf16[4,18,1,256]{3,2,1,0:T(2,128)(2,1)S(1)} %get-tuple-element.13), channel_id=1, source_target_pairs={{1,0},{2,1},{3,2},{5,4},{6,5},{7,6},{9,8},{10,9},{11,10},{13,12},{... | collective-permute-start | bytes 110600 | tf_op jit(solution)/shard_map/ppermute | solution.py:25
  64.1 6.4 %collective-permute-start.2 = (bf16[4,18,1,256]{3,2,1,0:T(2,128)(2,1)S(1)}, bf16[4,18,1,256]{3,2,1,0:T(2,128)(2,1)}, u32[]{:S(2)}, u32[]{:S(2)}) collective-permute-start(bf16[4,18,1,256]{3,2,1,0:T(2,128)(2,1)S(1)} %get-tuple-element.14), channel_id=1, source_target_pairs={{0,1},{1,2},{2,3},{4,5},{5,6},{6,7},{8,9},{9,10},{10,11},{12,13},{... | collective-permute-start | bytes 110600 | tf_op jit(solution)/shard_map/ppermute | solution.py:24
  73.8 14.2 %copy-start.1 = (bf16[256,2048]{1,0:T(8,128)(2,1)}, bf16[256,2048]{1,0:T(8,128)(2,1)S(1)}, u32[]{:S(2)}) copy-start(bf16[256,2048]{1,0:T(8,128)(2,1)S(1)} %get-tuple-element.9) | copy-start | bytes 3145732
  77.3 4.0 %copy-start.3 = (s32[16]{0:T(128)S(1)}, s32[16]{0:T(128)}, u32[]{:S(2)}) copy-start(s32[16]{0:T(128)} %param.8) | copy-start | bytes 196
  79.2 3.1 %collective-permute-start.11 = (bf16[2,16,32,256]{3,2,1,0:T(8,128)(2,1)}, bf16[2,16,32,256]{3,2,1,0:T(8,128)(2,1)}, u32[]{:S(2)}, u32[]{:S(2)}) collective-permute-start(bf16[2,16,32,256]{3,2,1,0:T(8,128)(2,1)} %slice.202), channel_id=1, source_target_pairs={{0,16},{16,32},{32,48},{48,64},{64,80},{80,96},{96,112},{112,128},... | collective-permute-start | bytes 1572872 | tf_op jit(solution)/shard_map/ppermute | solution.py:33
  90.0 95.5 %all-to-all-start = ((bf16[32,4,16,256]{3,2,1,0:T(8,128)(2,1)}), bf16[32,4,16,256]{3,2,1,0:T(8,128)(2,1)S(1)}, u32[]{:S(2)}, u32[]{:S(2)}) async-start(bf16[32,4,16,256]{3,2,1,0:T(8,128)(2,1)} %bitcast.168), calls=%async_computation | async-start | bytes 2097152 | tf_op jit(solution)/shard_map/all_to_all | solution.py:139

commit v10 on v9

--- a/solution.py
+++ b/solution.py
@@ -8,7 +8,7 @@
 
 
 GROUPS = 32
-TM = ("z", "core")
+TM = ("zh", "zl", "core")
 
 
 EPS = 1e-06
@@ -174,8 +174,8 @@
 def solution(mesh):
     devices = mesh.devices
     split = Mesh(
-        devices.reshape((devices.shape[0] // 2, 2) + devices.shape[1:]),
-        ("z", "core", "band", "fsdp"),
+        devices.reshape((4, devices.shape[0] // 8, 2) + devices.shape[1:]),
+        ("zh", "zl", "core", "band", "fsdp"),
     )
     return jax.shard_map(
         body,

time: 198 us -> 202 us (1.020)
  blocking collectives: 89.1 us -> 93.2 us
    all_gather x2 -> x3, blocking collectives: 56.9 us -> 61.1 us  [body(): moments = lax.all_gather(moments, axis, axis=0, tiled=True)]
where the time goes in v10:
time: 202 us; the launch traced here: 201 us
  blocking collectives  93.2 us (46%)
  starting transfers between devices  60.5 us (30%)
  matrix products  20.6 us (10%)
  waiting for transfers between devices  13.4 us (7%)
  other arithmetic  8.76 us (4%)
  local copies, waits for them, and re-layouts  3.7 us (2%)
    all_gather x3, blocking collectives, body(): moments = lax.all_gather(moments, axis, axis=0, tiled=True)  61.1 us
    all_to_all x1, starting transfers between devices, body(): lax.all_to_all(flat_resid, TM, split_axis=0, concat_axis=0, tiled=True)  23.5 us
    ppermute x6, starting transfers between devices, ring_gather(): lax.ppermute(x, axis, [(i, (i + shift) % size) for i in range(size)])  21.2 us
    psum x2, blocking collectives, group_moments(): both = lax.psum(lax.optimization_barrier(both), 'fsdp')  16.9 us
    psum x2, blocking collectives, group_moments(): both = lax.psum(jnp.stack([sums, squares]), 'band')  15.2 us
    ppermute x2, starting transfers between devices, with_halo(): after = lax.ppermute(initial, axis, down)  7.05 us
    ppermute x6, waiting for transfers between devices, ring_gather(): lax.ppermute(x, axis, [(i, (i + shift) % size) for i in range(size)])  6.61 us
    dot_general x1, matrix products, body(): jnp.einsum('fpc,cd->fpd', flat_norm, qkv_full, preferred_element_type=jnp...  4.64 us
  transfers between devices with their start and end apart: 13, of which 7 were waited for; matrix products, arithmetic and copies ran while one was open for 3% of the time, Pallas kernels for 0%

profile of v10, /device:TPU:18, one launch (start us, length us, event | category | flops | bytes accessed | tf_op | source)
XLA Modules:
  0.0 200.7 jit_solution(17054096332086258857)
XLA Ops:
  0.0 0.9 fusion.72
  0.9 2.4 %collective-permute-start.3 = (bf16[16,2048]{1,0:T(8,128)(2,1)S(1)}, bf16[16,2048]{1,0:T(8,128)(2,1)S(1)}, u32[]{:S(2)}, u32[]{:S(2)}) collective-permute-start(bf16[16,2048]{1,0:T(8,128)(2,1)S(1)} %fusion.72), channel_id=1, source_target_pairs={{0,3},{1,0},{2,1},{3,2},{4,7},{5,4},{6,5},{7,6},{8,11},{9,8},{10,9... | collective-permute-start | bytes 196616 | tf_op jit(solution)/shard_map/ppermute | solution.py:41
  3.4 4.3 %collective-permute-start.4 = (bf16[16,2048]{1,0:T(8,128)(2,1)S(1)}, bf16[16,2048]{1,0:T(8,128)(2,1)S(1)}, u32[]{:S(2)}, u32[]{:S(2)}) collective-permute-start(bf16[16,2048]{1,0:T(8,128)(2,1)S(1)} %fusion.72), channel_id=1, source_target_pairs={{0,2},{1,3},{2,0},{3,1},{4,6},{5,7},{6,4},{7,5},{8,10},{9,11},{10,... | collective-permute-start | bytes 196616 | tf_op jit(solution)/shard_map/ppermute | solution.py:41
  7.7 3.7 %collective-permute-start.5 = (bf16[16,2048]{1,0:T(8,128)(2,1)S(1)}, bf16[16,2048]{1,0:T(8,128)(2,1)S(1)}, u32[]{:S(2)}, u32[]{:S(2)}) collective-permute-start(bf16[16,2048]{1,0:T(8,128)(2,1)S(1)} %fusion.72), channel_id=1, source_target_pairs={{0,1},{1,2},{2,3},{3,0},{4,5},{5,6},{6,7},{7,4},{8,9},{9,10},{10,1... | collective-permute-start | bytes 196616 | tf_op jit(solution)/shard_map/ppermute | solution.py:41
  11.4 1.5 convert_reduce_fusion
  13.4 8.4 %psum.28 = f32[2,4,32]{2,1,0:T(4,128)S(1)} all-reduce(f32[2,4,32]{2,1,0:T(4,128)S(1)} %pad_maximum_fusion.6), channel_id=1, replica_groups=mesh['zh'=4,'zl'=4,'core'=2,'band'=4,'fsdp'=4] {'band'}, use_global_device_ids=true, to_apply=%region_6.7 | all-reduce | flops 256 | bytes 2048 | tf_op jit(solution)/shard_map/psum | solution.py:61
  21.8 9.7 %psum.29 = f32[2,4,32]{2,1,0:T(4,128)S(1)} all-reduce(f32[2,4,32]{2,1,0:T(4,128)S(1)} %psum.28), channel_id=1, replica_groups=mesh['zh'=4,'zl'=4,'core'=2,'band'=4,'fsdp'=4] {'fsdp'}, use_global_device_ids=true, to_apply=%region_7.8 | all-reduce | flops 256 | bytes 2048 | tf_op jit(solution)/shard_map/psum | solution.py:62
  31.6 4.8 %collective-permute-start.6 = (bf16[64,2048]{1,0:T(8,128)(2,1)S(1)}, bf16[64,2048]{1,0:T(8,128)(2,1)S(1)}, u32[]{:S(2)}, u32[]{:S(2)}) collective-permute-start(bf16[64,2048]{1,0:T(8,128)(2,1)S(1)} %bitcast.174), channel_id=1, source_target_pairs={{0,12},{4,0},{8,4},{12,8},{1,13},{5,1},{9,5},{13,9},{2,14},{6,2},{... | collective-permute-start | bytes 786440 | tf_op jit(solution)/shard_map/ppermute | solution.py:41
  36.9 3.4 %collective-permute-start.7 = (bf16[64,2048]{1,0:T(8,128)(2,1)S(1)}, bf16[64,2048]{1,0:T(8,128)(2,1)S(1)}, u32[]{:S(2)}, u32[]{:S(2)}) collective-permute-start(bf16[64,2048]{1,0:T(8,128)(2,1)S(1)} %bitcast.175), channel_id=1, source_target_pairs={{0,8},{4,12},{8,0},{12,4},{1,9},{5,13},{9,1},{13,5},{2,10},{6,14},... | collective-permute-start | bytes 786440 | tf_op jit(solution)/shard_map/ppermute | solution.py:41
  40.2 2.5 %collective-permute-start.8 = (bf16[64,2048]{1,0:T(8,128)(2,1)S(1)}, bf16[64,2048]{1,0:T(8,128)(2,1)S(1)}, u32[]{:S(2)}, u32[]{:S(2)}) collective-permute-start(bf16[64,2048]{1,0:T(8,128)(2,1)S(1)} %bitcast.176), channel_id=1, source_target_pairs={{0,4},{4,8},{8,12},{12,0},{1,5},{5,9},{9,13},{13,1},{2,6},{6,10},{... | collective-permute-start | bytes 786440 | tf_op jit(solution)/shard_map/ppermute | solution.py:41
  42.8 3.9 %collective-permute-done.7 = bf16[64,2048]{1,0:T(8,128)(2,1)S(1)} collective-permute-done((bf16[64,2048]{1,0:T(8,128)(2,1)S(1)}, bf16[64,2048]{1,0:T(8,128)(2,1)S(1)}, u32[]{:S(2)}, u32[]{:S(2)}) %collective-permute-start.7) | collective-permute-done | bytes 262176 | tf_op jit(solution)/shard_map/ppermute | solution.py:41
  46.8 2.7 %collective-permute-done.8 = bf16[64,2048]{1,0:T(8,128)(2,1)S(1)} collective-permute-done((bf16[64,2048]{1,0:T(8,128)(2,1)S(1)}, bf16[64,2048]{1,0:T(8,128)(2,1)S(1)}, u32[]{:S(2)}, u32[]{:S(2)}) %collective-permute-start.8) | collective-permute-done | bytes 262176 | tf_op jit(solution)/shard_map/ppermute | solution.py:41
  49.7 2.1 %collective-permute-start.9 = (bf16[256,2048]{1,0:T(8,128)(2,1)S(1)}, bf16[256,2048]{1,0:T(8,128)(2,1)}, u32[]{:S(2)}, u32[]{:S(2)}) collective-permute-start(bf16[256,2048]{1,0:T(8,128)(2,1)S(1)} %bitcast.171), channel_id=1, source_target_pairs={{0,16},{16,0},{1,17},{17,1},{2,18},{18,2},{3,19},{19,3},{4,20},{20... | collective-permute-start | bytes 3145736 | tf_op jit(solution)/shard_map/ppermute | solution.py:88
  51.8 0.7 fusion.16
  52.5 1.9 collective-permute-start
  54.4 3.9 %collective-permute-start.1 = (bf16[4,1,32,256]{3,2,1,0:T(8,128)(2,1)S(1)}, bf16[4,1,32,256]{3,2,1,0:T(8,128)(2,1)S(1)}, u32[]{:S(2)}, u32[]{:S(2)}) collective-permute-start(bf16[4,1,32,256]{3,2,1,0:T(8,128)(2,1)S(1)} %get-tuple-element.16), channel_id=1, source_target_pairs={{4,0},{8,4},{12,8},{5,1},{9,5},{13,9},{6,2},{10,6},{14,10},{7,3},{... | collective-permute-start | bytes 196616 | tf_op jit(solution)/shard_map/ppermute | solution.py:25
  58.3 0.5 collective-permute-done
  58.9 1.9 collective-permute-done.1
  60.9 3.1 %collective-permute-start.10 = (bf16[4,18,1,256]{3,2,1,0:T(2,128)(2,1)S(1)}, bf16[4,18,1,256]{3,2,1,0:T(2,128)(2,1)S(1)}, u32[]{:S(2)}, u32[]{:S(2)}) collective-permute-start(bf16[4,18,1,256]{3,2,1,0:T(2,128)(2,1)S(1)} %get-tuple-element.13), channel_id=1, source_target_pairs={{1,0},{2,1},{3,2},{5,4},{6,5},{7,6},{9,8},{10,9},{11,10},{13,12},{... | collective-permute-start | bytes 110600 | tf_op jit(solution)/shard_map/ppermute | solution.py:25
  64.1 2.7 %collective-permute-start.2 = (bf16[4,18,1,256]{3,2,1,0:T(2,128)(2,1)S(1)}, bf16[4,18,1,256]{3,2,1,0:T(2,128)(2,1)}, u32[]{:S(2)}, u32[]{:S(2)}) collective-permute-start(bf16[4,18,1,256]{3,2,1,0:T(2,128)(2,1)S(1)} %get-tuple-element.14), channel_id=1, source_target_pairs={{0,1},{1,2},{2,3},{4,5},{5,6},{6,7},{8,9},{9,10},{10,11},{12,13},{... | collective-permute-start | bytes 110600 | tf_op jit(solution)/shard_map/ppermute | solution.py:24
  67.2 3.2 %collective-permute-done.2 = bf16[4,18,1,256]{3,2,1,0:T(2,128)(2,1)} collective-permute-done((bf16[4,18,1,256]{3,2,1,0:T(2,128)(2,1)S(1)}, bf16[4,18,1,256]{3,2,1,0:T(2,128)(2,1)}, u32[]{:S(2)}, u32[]{:S(2)}) %collective-permute-start.2) | collective-permute-done | bytes 36896 | tf_op jit(solution)/shard_map/ppermute | solution.py:24
  70.4 1.6 pad_maximum_fusion.2
  72.0 1.6 pad_maximum_fusion
  74.2 0.4 fusion.53
  74.6 0.5 fusion.55
  75.1 0.5 fusion.51
  75.5 0.4 fusion.49
  76.0 0.4 fusion.69
  77.3 1.1 add_convert_fusion
  78.4 0.8 slice.202
  79.2 2.1 %collective-permute-start.11 = (bf16[2,16,32,256]{3,2,1,0:T(8,128)(2,1)}, bf16[2,16,32,256]{3,2,1,0:T(8,128)(2,1)}, u32[]{:S(2)}, u32[]{:S(2)}) collective-permute-start(bf16[2,16,32,256]{3,2,1,0:T(8,128)(2,1)} %slice.202), channel_id=1, source_target_pairs={{0,16},{16,32},{32,48},{48,64},{64,80},{80,96},{96,112},{112,128},... | collective-permute-start | bytes 1572872 | tf_op jit(solution)/shard_map/ppermute | solution.py:33
  81.7 0.6 collective-permute-done.11
  82.3 1.2 pad_maximum_fusion.1
  83.5 1.2 fusion.22
  85.2 1.2 fusion.19
  86.4 0.4 fusion.62
  86.8 1.2 fusion.25
  88.0 0.9 convert_reduce_fusion.1
  88.9 1.1 copy.100
  90.0 23.5 %all-to-all-start = ((bf16[32,4,16,256]{3,2,1,0:T(8,128)(2,1)}), bf16[32,4,16,256]{3,2,1,0:T(8,128)(2,1)S(1)}, u32[]{:S(2)}, u32[]{:S(2)}) async-start(bf16[32,4,16,256]{3,2,1,0:T(8,128)(2,1)} %bitcast.168), calls=%async_computation | async-start | bytes 2097152 | tf_op jit(solution)/shard_map/all_to_all | solution.py:139
  114.0 6.8 %psum.30 = f32[2,4,32]{2,1,0:T(4,128)S(1)} all-reduce(f32[2,4,32]{2,1,0:T(4,128)S(1)} %pad_maximum_fusion.7), channel_id=1, replica_groups=mesh['zh'=4,'zl'=4,'core'=2,'band'=4,'fsdp'=4] {'band'}, use_global_device_ids=true, to_apply=%region_12.13 | all-reduce | flops 256 | bytes 2048 | tf_op jit(solution)/shard_map/psum | solution.py:61
  120.8 7.3 %psum.31 = f32[2,4,32]{2,1,0:T(4,128)S(1)} all-reduce(f32[2,4,32]{2,1,0:T(4,128)S(1)} %psum.30), channel_id=1, replica_groups=mesh['zh'=4,'zl'=4,'core'=2,'band'=4,'fsdp'=4] {'fsdp'}, use_global_device_ids=true, to_apply=%region_13.14 | all-reduce | flops 256 | bytes 2048 | tf_op jit(solution)/shard_map/psum | solution.py:62
  128.2 1.8 all-gather
  130.0 36.7 %all_gather.10 = f32[32,64]{1,0:T(8,128)S(1)} all-gather(f32[8,64]{1,0:T(8,128)S(1)} %bitcast.179), channel_id=1, replica_groups=mesh['zh'=4,'zl'=4,'core'=2,'band'=4,'fsdp'=4] {'zl'}, dimensions={0}, use_global_device_ids=true | all-gather | bytes 10240 | tf_op jit(solution)/shard_map/all_gather | solution.py:144
  166.7 22.6 %all_gather.11 = f32[128,64]{1,0:T(8,128)S(1)} all-gather(f32[32,64]{1,0:T(8,128)S(1)} %all_gather.10), channel_id=1, replica_groups=mesh['zh'=4,'zl'=4,'core'=2,'band'=4,'fsdp'=4] {'zh'}, dimensions={0}, use_global_device_ids=true | all-gather | bytes 40960 | tf_op jit(solution)/shard_map/all_gather | solution.py:144
  190.1 4.6 %convolution_convert_fusion = bf16[128,16,768]{2,0,1:T(8,128)(2,1)} fusion(f32[128,16,256]{2,1,0:T(8,128)S(1)} %bitcast_convert_fusion, f32[256]{0:T(256)S(1)} %bitcast.184, f32[128,256]{1,0:T(8,128)S(1)} %copy.55, f32[128,256]{1,0:T(8,128)S(1)} %copy.53, bf16[256,2048]{1,0:T(8,128)(2,1)} %copy-done.1), kind=kOutput, calls=%fused_computation.8 | convolution fusion | flops 808976384 | bytes 5899264 | tf_op jit(solution)/shard_map/fpc,cd->fpd/dot_general | solution.py:147
  194.7 2.1 %fusion.98 = (f32[16,128]{1,0:T(8,128)S(1)}, f32[16,128,128]{1,2,0:T(8,128)S(1)}) fusion(pred[128,128]{0,1:T(8,128)(4,1)S(1)} %fusion.73, bf16[128,16,768]{2,0,1:T(8,128)(2,1)} %convolution_convert_fusion), kind=kOutput, calls=%fused_computation.165 | convolution fusion | flops 135528576 | bytes 3186688 | tf_op jit(solution)/shard_map/sub | solution.py:160
  196.9 3.9 %fusion.31 = bf16[1,1,16,128,256]{4,3,2,1,0:T(8,128)(2,1)} fusion(f32[128,16,256]{2,1,0:T(8,128)S(1)} %bitcast_convert_fusion, bf16[128,16,768]{2,0,1:T(8,128)(2,1)} %convolution_convert_fusion, f32[16,128,128]{1,2,0:T(8,128)S(1)} %get-tuple-element.26, f32[16,128]{1,0:T(8,128)S(1)} %get-tuple-element.25, bf16[256,2048]{1,0:T(8,128)(2,1)} %copy-done.1), kind=kOutput, calls=%fused_computation.40 | convolution fusion | flops 404750336 | bytes 5382144 | tf_op jit(solution)/shard_map/axi,iy->axy/dot_general | solution.py:165
  (75 shorter events, 5.2 us)
Async XLA Ops:
  0.0 36.8 %copy-start.2 = (f32[2,256]{1,0:T(2,128)S(1)}, f32[2,256]{1,0:T(2,128)}, u32[]{:S(2)}) copy-start(f32[2,256]{1,0:T(2,128)} %param.9) | copy-start | bytes 6148
  0.9 30.5 %collective-permute-start.3 = (bf16[16,2048]{1,0:T(8,128)(2,1)S(1)}, bf16[16,2048]{1,0:T(8,128)(2,1)S(1)}, u32[]{:S(2)}, u32[]{:S(2)}) collective-permute-start(bf16[16,2048]{1,0:T(8,128)(2,1)S(1)} %fusion.72), channel_id=1, source_target_pairs={{0,3},{1,0},{2,1},{3,2},{4,7},{5,4},{6,5},{7,6},{8,11},{9,8},{10,9... | collective-permute-start | bytes 196616 | tf_op jit(solution)/shard_map/ppermute | solution.py:41
  3.4 28.1 %collective-permute-start.4 = (bf16[16,2048]{1,0:T(8,128)(2,1)S(1)}, bf16[16,2048]{1,0:T(8,128)(2,1)S(1)}, u32[]{:S(2)}, u32[]{:S(2)}) collective-permute-start(bf16[16,2048]{1,0:T(8,128)(2,1)S(1)} %fusion.72), channel_id=1, source_target_pairs={{0,2},{1,3},{2,0},{3,1},{4,6},{5,7},{6,4},{7,5},{8,10},{9,11},{10,... | collective-permute-start | bytes 196616 | tf_op jit(solution)/shard_map/ppermute | solution.py:41
  7.7 23.8 %collective-permute-start.5 = (bf16[16,2048]{1,0:T(8,128)(2,1)S(1)}, bf16[16,2048]{1,0:T(8,128)(2,1)S(1)}, u32[]{:S(2)}, u32[]{:S(2)}) collective-permute-start(bf16[16,2048]{1,0:T(8,128)(2,1)S(1)} %fusion.72), channel_id=1, source_target_pairs={{0,1},{1,2},{2,3},{3,0},{4,5},{5,6},{6,7},{7,4},{8,9},{9,10},{10,1... | collective-permute-start | bytes 196616 | tf_op jit(solution)/shard_map/ppermute | solution.py:41
  31.6 11.2 %collective-permute-start.6 = (bf16[64,2048]{1,0:T(8,128)(2,1)S(1)}, bf16[64,2048]{1,0:T(8,128)(2,1)S(1)}, u32[]{:S(2)}, u32[]{:S(2)}) collective-permute-start(bf16[64,2048]{1,0:T(8,128)(2,1)S(1)} %bitcast.174), channel_id=1, source_target_pairs={{0,12},{4,0},{8,4},{12,8},{1,13},{5,1},{9,5},{13,9},{2,14},{6,2},{... | collective-permute-start | bytes 786440 | tf_op jit(solution)/shard_map/ppermute | solution.py:41
  36.9 9.9 %collective-permute-start.7 = (bf16[64,2048]{1,0:T(8,128)(2,1)S(1)}, bf16[64,2048]{1,0:T(8,128)(2,1)S(1)}, u32[]{:S(2)}, u32[]{:S(2)}) collective-permute-start(bf16[64,2048]{1,0:T(8,128)(2,1)S(1)} %bitcast.175), channel_id=1, source_target_pairs={{0,8},{4,12},{8,0},{12,4},{1,9},{5,13},{9,1},{13,5},{2,10},{6,14},... | collective-permute-start | bytes 786440 | tf_op jit(solution)/shard_map/ppermute | solution.py:41
  40.2 9.2 %collective-permute-start.8 = (bf16[64,2048]{1,0:T(8,128)(2,1)S(1)}, bf16[64,2048]{1,0:T(8,128)(2,1)S(1)}, u32[]{:S(2)}, u32[]{:S(2)}) collective-permute-start(bf16[64,2048]{1,0:T(8,128)(2,1)S(1)} %bitcast.176), channel_id=1, source_target_pairs={{0,4},{4,8},{8,12},{12,0},{1,5},{5,9},{9,13},{13,1},{2,6},{6,10},{... | collective-permute-start | bytes 786440 | tf_op jit(solution)/shard_map/ppermute | solution.py:41
  49.5 2.3 %copy-start = (bf16[4,16,32,256]{3,2,1,0:T(8,128)(2,1)S(1)}, bf16[4,16,32,256]{3,2,1,0:T(8,128)(2,1)}, u32[]{:S(2)}) copy-start(bf16[4,16,32,256]{3,2,1,0:T(8,128)(2,1)} %param.7) | copy-start | bytes 3145732
  49.7 22.3 %collective-permute-start.9 = (bf16[256,2048]{1,0:T(8,128)(2,1)S(1)}, bf16[256,2048]{1,0:T(8,128)(2,1)}, u32[]{:S(2)}, u32[]{:S(2)}) collective-permute-start(bf16[256,2048]{1,0:T(8,128)(2,1)S(1)} %bitcast.171), channel_id=1, source_target_pairs={{0,16},{16,0},{1,17},{17,1},{2,18},{18,2},{3,19},{19,3},{4,20},{20... | collective-permute-start | bytes 3145736 | tf_op jit(solution)/shard_map/ppermute | solution.py:88
  52.5 6.4 %collective-permute-start = (bf16[4,1,32,256]{3,2,1,0:T(8,128)(2,1)S(1)}, bf16[4,1,32,256]{3,2,1,0:T(8,128)(2,1)S(1)}, u32[]{:S(2)}, u32[]{:S(2)}) collective-permute-start(bf16[4,1,32,256]{3,2,1,0:T(8,128)(2,1)S(1)} %get-tuple-element.15), channel_id=1, source_target_pairs={{0,4},{4,8},{8,12},{1,5},{5,9},{9,13},{2,6},{6,10},{10,14},{3,7},{... | collective-permute-start | bytes 196616 | tf_op jit(solution)/shard_map/ppermute | solution.py:24
  54.4 6.4 %collective-permute-start.1 = (bf16[4,1,32,256]{3,2,1,0:T(8,128)(2,1)S(1)}, bf16[4,1,32,256]{3,2,1,0:T(8,128)(2,1)S(1)}, u32[]{:S(2)}, u32[]{:S(2)}) collective-permute-start(bf16[4,1,32,256]{3,2,1,0:T(8,128)(2,1)S(1)} %get-tuple-element.16), channel_id=1, source_target_pairs={{4,0},{8,4},{12,8},{5,1},{9,5},{13,9},{6,2},{10,6},{14,10},{7,3},{... | collective-permute-start | bytes 196616 | tf_op jit(solution)/shard_map/ppermute | solution.py:25
  60.9 6.2 %collective-permute-start.10 = (bf16[4,18,1,256]{3,2,1,0:T(2,128)(2,1)S(1)}, bf16[4,18,1,256]{3,2,1,0:T(2,128)(2,1)S(1)}, u32[]{:S(2)}, u32[]{:S(2)}) collective-permute-start(bf16[4,18,1,256]{3,2,1,0:T(2,128)(2,1)S(1)} %get-tuple-element.13), channel_id=1, source_target_pairs={{1,0},{2,1},{3,2},{5,4},{6,5},{7,6},{9,8},{10,9},{11,10},{13,12},{... | collective-permute-start | bytes 110600 | tf_op jit(solution)/shard_map/ppermute | solution.py:25
  64.1 6.4 %collective-permute-start.2 = (bf16[4,18,1,256]{3,2,1,0:T(2,128)(2,1)S(1)}, bf16[4,18,1,256]{3,2,1,0:T(2,128)(2,1)}, u32[]{:S(2)}, u32[]{:S(2)}) collective-permute-start(bf16[4,18,1,256]{3,2,1,0:T(2,128)(2,1)S(1)} %get-tuple-element.14), channel_id=1, source_target_pairs={{0,1},{1,2},{2,3},{4,5},{5,6},{6,7},{8,9},{9,10},{10,11},{12,13},{... | collective-permute-start | bytes 110600 | tf_op jit(solution)/shard_map/ppermute | solution.py:24
  73.8 14.2 %copy-start.1 = (bf16[256,2048]{1,0:T(8,128)(2,1)}, bf16[256,2048]{1,0:T(8,128)(2,1)S(1)}, u32[]{:S(2)}) copy-start(bf16[256,2048]{1,0:T(8,128)(2,1)S(1)} %get-tuple-element.9) | copy-start | bytes 3145732
  77.3 4.0 %copy-start.3 = (s32[16]{0:T(128)S(1)}, s32[16]{0:T(128)}, u32[]{:S(2)}) copy-start(s32[16]{0:T(128)} %param.8) | copy-start | bytes 196
  79.2 3.1 %collective-permute-start.11 = (bf16[2,16,32,256]{3,2,1,0:T(8,128)(2,1)}, bf16[2,16,32,256]{3,2,1,0:T(8,128)(2,1)}, u32[]{:S(2)}, u32[]{:S(2)}) collective-permute-start(bf16[2,16,32,256]{3,2,1,0:T(8,128)(2,1)} %slice.202), channel_id=1, source_target_pairs={{0,16},{16,32},{32,48},{48,64},{64,80},{80,96},{96,112},{112,128},... | collective-permute-start | bytes 1572872 | tf_op jit(solution)/shard_map/ppermute | solution.py:33
  90.0 99.7 %all-to-all-start = ((bf16[32,4,16,256]{3,2,1,0:T(8,128)(2,1)}), bf16[32,4,16,256]{3,2,1,0:T(8,128)(2,1)S(1)}, u32[]{:S(2)}, u32[]{:S(2)}) async-start(bf16[32,4,16,256]{3,2,1,0:T(8,128)(2,1)} %bitcast.168), calls=%async_computation | async-start | bytes 2097152 | tf_op jit(solution)/shard_map/all_to_all | solution.py:139

commit v11 on v9

--- a/solution.py
+++ b/solution.py
@@ -119,19 +119,24 @@
     extended = jnp.concatenate([carried, spatial], axis=0)
     position = first + jnp.arange(frames, dtype=jnp.int32)
     slots = jnp.arange(frames + 2, dtype=jnp.int32)
-    temporal = jnp.zeros((frames, height, width, chans), jnp.float32)
+    picks = []
     for tap in range(3):
         source = jnp.maximum(position - 2 + tap, local_starts) - first + 2
         select = (source[:, None] == slots[None, :]).astype(jnp.bfloat16)
-        picked = jnp.einsum(
-            "fe,ehwc->fhwc", select, extended, preferred_element_type=jnp.float32
-        ).astype(jnp.bfloat16)
-        temporal = temporal + jnp.einsum(
-            "fhwc,cd->fhwd",
-            picked,
-            time_full[:, tap * chans : (tap + 1) * chans],
-            preferred_element_type=jnp.float32,
+        picks.append(
+            jnp.einsum(
+                "fe,ehwc->fhwc", select, extended, preferred_element_type=jnp.float32
+            ).astype(jnp.bfloat16)
         )
+    stacked_taps = jnp.concatenate(
+        [time_full[:, tap * chans : (tap + 1) * chans] for tap in range(3)], axis=0
+    )
+    temporal = jnp.einsum(
+        "fhwc,cd->fhwd",
+        jnp.concatenate(picks, axis=-1),
+        stacked_taps,
+        preferred_element_type=jnp.float32,
+    )
     resid = (video.astype(jnp.float32) + temporal).astype(jnp.bfloat16)
     pixels = height * width
     group_pixels = pixels // ranks

time: 198 us -> 202 us (1.020)
  other arithmetic: 8.76 us -> 13.7 us
    concatenate x0 -> x1, other arithmetic: none -> 4.96 us  [body(): jnp.concatenate(picks, axis=-1)]
where the time goes in v11:
time: 202 us; the launch traced here: 201 us
  blocking collectives  89.1 us (44%)
  starting transfers between devices  60.6 us (30%)
  matrix products  19.9 us (10%)
  other arithmetic  13.7 us (7%)
  waiting for transfers between devices  13.3 us (7%)
  local copies, waits for them, and re-layouts  3.73 us (2%)
    all_gather x2, blocking collectives, body(): moments = lax.all_gather(moments, axis, axis=0, tiled=True)  56.9 us
    all_to_all x1, starting transfers between devices, body(): lax.all_to_all(flat_resid, TM, split_axis=0, concat_axis=0, tiled=True)  23.5 us
    ppermute x6, starting transfers between devices, ring_gather(): lax.ppermute(x, axis, [(i, (i + shift) % size) for i in range(size)])  21.2 us
    psum x2, blocking collectives, group_moments(): both = lax.psum(lax.optimization_barrier(both), 'fsdp')  16.9 us
    psum x2, blocking collectives, group_moments(): both = lax.psum(jnp.stack([sums, squares]), 'band')  15.2 us
    ppermute x2, starting transfers between devices, with_halo(): after = lax.ppermute(initial, axis, down)  7.05 us
    ppermute x6, waiting for transfers between devices, ring_gather(): lax.ppermute(x, axis, [(i, (i + shift) % size) for i in range(size)])  6.61 us
    concatenate x1, other arithmetic, body(): jnp.concatenate(picks, axis=-1)  4.96 us
  transfers between devices with their start and end apart: 13, of which 7 were waited for; matrix products, arithmetic and copies ran while one was open for 3% of the time, Pallas kernels for 0%

profile of v11, /device:TPU:18, one launch (start us, length us, event | category | flops | bytes accessed | tf_op | source)
XLA Modules:
  0.0 200.9 jit_solution(16631870989738391539)
XLA Ops:
  0.0 0.9 fusion.75
  0.9 2.4 %collective-permute-start.3 = (bf16[16,2048]{1,0:T(8,128)(2,1)S(1)}, bf16[16,2048]{1,0:T(8,128)(2,1)S(1)}, u32[]{:S(2)}, u32[]{:S(2)}) collective-permute-start(bf16[16,2048]{1,0:T(8,128)(2,1)S(1)} %fusion.75), channel_id=1, source_target_pairs={{0,3},{1,0},{2,1},{3,2},{4,7},{5,4},{6,5},{7,6},{8,11},{9,8},{10,9... | collective-permute-start | bytes 196616 | tf_op jit(solution)/shard_map/ppermute | solution.py:41
  3.4 4.3 %collective-permute-start.4 = (bf16[16,2048]{1,0:T(8,128)(2,1)S(1)}, bf16[16,2048]{1,0:T(8,128)(2,1)S(1)}, u32[]{:S(2)}, u32[]{:S(2)}) collective-permute-start(bf16[16,2048]{1,0:T(8,128)(2,1)S(1)} %fusion.75), channel_id=1, source_target_pairs={{0,2},{1,3},{2,0},{3,1},{4,6},{5,7},{6,4},{7,5},{8,10},{9,11},{10,... | collective-permute-start | bytes 196616 | tf_op jit(solution)/shard_map/ppermute | solution.py:41
  7.7 3.7 %collective-permute-start.5 = (bf16[16,2048]{1,0:T(8,128)(2,1)S(1)}, bf16[16,2048]{1,0:T(8,128)(2,1)S(1)}, u32[]{:S(2)}, u32[]{:S(2)}) collective-permute-start(bf16[16,2048]{1,0:T(8,128)(2,1)S(1)} %fusion.75), channel_id=1, source_target_pairs={{0,1},{1,2},{2,3},{3,0},{4,5},{5,6},{6,7},{7,4},{8,9},{9,10},{10,1... | collective-permute-start | bytes 196616 | tf_op jit(solution)/shard_map/ppermute | solution.py:41
  11.4 1.5 convert_reduce_fusion
  13.4 8.4 %psum.28 = f32[2,4,32]{2,1,0:T(4,128)S(1)} all-reduce(f32[2,4,32]{2,1,0:T(4,128)S(1)} %pad_maximum_fusion.7), channel_id=1, replica_groups=mesh['z'=16,'core'=2,'band'=4,'fsdp'=4] {'band'}, use_global_device_ids=true, to_apply=%region_6.7 | all-reduce | flops 256 | bytes 2048 | tf_op jit(solution)/shard_map/psum | solution.py:61
  21.8 9.7 %psum.29 = f32[2,4,32]{2,1,0:T(4,128)S(1)} all-reduce(f32[2,4,32]{2,1,0:T(4,128)S(1)} %psum.28), channel_id=1, replica_groups=mesh['z'=16,'core'=2,'band'=4,'fsdp'=4] {'fsdp'}, use_global_device_ids=true, to_apply=%region_7.8 | all-reduce | flops 256 | bytes 2048 | tf_op jit(solution)/shard_map/psum | solution.py:62
  31.6 4.8 %collective-permute-start.6 = (bf16[64,2048]{1,0:T(8,128)(2,1)S(1)}, bf16[64,2048]{1,0:T(8,128)(2,1)S(1)}, u32[]{:S(2)}, u32[]{:S(2)}) collective-permute-start(bf16[64,2048]{1,0:T(8,128)(2,1)S(1)} %bitcast.163), channel_id=1, source_target_pairs={{0,12},{4,0},{8,4},{12,8},{1,13},{5,1},{9,5},{13,9},{2,14},{6,2},{... | collective-permute-start | bytes 786440 | tf_op jit(solution)/shard_map/ppermute | solution.py:41
  36.9 3.4 %collective-permute-start.7 = (bf16[64,2048]{1,0:T(8,128)(2,1)S(1)}, bf16[64,2048]{1,0:T(8,128)(2,1)S(1)}, u32[]{:S(2)}, u32[]{:S(2)}) collective-permute-start(bf16[64,2048]{1,0:T(8,128)(2,1)S(1)} %bitcast.164), channel_id=1, source_target_pairs={{0,8},{4,12},{8,0},{12,4},{1,9},{5,13},{9,1},{13,5},{2,10},{6,14},... | collective-permute-start | bytes 786440 | tf_op jit(solution)/shard_map/ppermute | solution.py:41
  40.2 2.5 %collective-permute-start.8 = (bf16[64,2048]{1,0:T(8,128)(2,1)S(1)}, bf16[64,2048]{1,0:T(8,128)(2,1)S(1)}, u32[]{:S(2)}, u32[]{:S(2)}) collective-permute-start(bf16[64,2048]{1,0:T(8,128)(2,1)S(1)} %bitcast.165), channel_id=1, source_target_pairs={{0,4},{4,8},{8,12},{12,0},{1,5},{5,9},{9,13},{13,1},{2,6},{6,10},{... | collective-permute-start | bytes 786440 | tf_op jit(solution)/shard_map/ppermute | solution.py:41
  42.8 3.9 %collective-permute-done.7 = bf16[64,2048]{1,0:T(8,128)(2,1)S(1)} collective-permute-done((bf16[64,2048]{1,0:T(8,128)(2,1)S(1)}, bf16[64,2048]{1,0:T(8,128)(2,1)S(1)}, u32[]{:S(2)}, u32[]{:S(2)}) %collective-permute-start.7) | collective-permute-done | bytes 262176 | tf_op jit(solution)/shard_map/ppermute | solution.py:41
  46.8 2.7 %collective-permute-done.8 = bf16[64,2048]{1,0:T(8,128)(2,1)S(1)} collective-permute-done((bf16[64,2048]{1,0:T(8,128)(2,1)S(1)}, bf16[64,2048]{1,0:T(8,128)(2,1)S(1)}, u32[]{:S(2)}, u32[]{:S(2)}) %collective-permute-start.8) | collective-permute-done | bytes 262176 | tf_op jit(solution)/shard_map/ppermute | solution.py:41
  49.7 2.1 %collective-permute-start.9 = (bf16[256,2048]{1,0:T(8,128)(2,1)S(1)}, bf16[256,2048]{1,0:T(8,128)(2,1)}, u32[]{:S(2)}, u32[]{:S(2)}) collective-permute-start(bf16[256,2048]{1,0:T(8,128)(2,1)S(1)} %bitcast.161), channel_id=1, source_target_pairs={{0,16},{16,0},{1,17},{17,1},{2,18},{18,2},{3,19},{19,3},{4,20},{20... | collective-permute-start | bytes 3145736 | tf_op jit(solution)/shard_map/ppermute | solution.py:88
  51.8 0.7 fusion.18
  52.5 1.9 collective-permute-start
  54.4 3.9 %collective-permute-start.1 = (bf16[4,1,32,256]{3,2,1,0:T(8,128)(2,1)S(1)}, bf16[4,1,32,256]{3,2,1,0:T(8,128)(2,1)S(1)}, u32[]{:S(2)}, u32[]{:S(2)}) collective-permute-start(bf16[4,1,32,256]{3,2,1,0:T(8,128)(2,1)S(1)} %get-tuple-element.19), channel_id=1, source_target_pairs={{4,0},{8,4},{12,8},{5,1},{9,5},{13,9},{6,2},{10,6},{14,10},{7,3},{... | collective-permute-start | bytes 196616 | tf_op jit(solution)/shard_map/ppermute | solution.py:25
  58.3 0.5 collective-permute-done
  58.9 1.9 collective-permute-done.1
  60.9 3.1 %collective-permute-start.10 = (bf16[4,18,1,256]{3,2,1,0:T(2,128)(2,1)S(1)}, bf16[4,18,1,256]{3,2,1,0:T(2,128)(2,1)S(1)}, u32[]{:S(2)}, u32[]{:S(2)}) collective-permute-start(bf16[4,18,1,256]{3,2,1,0:T(2,128)(2,1)S(1)} %get-tuple-element.13), channel_id=1, source_target_pairs={{1,0},{2,1},{3,2},{5,4},{6,5},{7,6},{9,8},{10,9},{11,10},{13,12},{... | collective-permute-start | bytes 110600 | tf_op jit(solution)/shard_map/ppermute | solution.py:25
  64.1 2.7 %collective-permute-start.2 = (bf16[4,18,1,256]{3,2,1,0:T(2,128)(2,1)S(1)}, bf16[4,18,1,256]{3,2,1,0:T(2,128)(2,1)}, u32[]{:S(2)}, u32[]{:S(2)}) collective-permute-start(bf16[4,18,1,256]{3,2,1,0:T(2,128)(2,1)S(1)} %get-tuple-element.14), channel_id=1, source_target_pairs={{0,1},{1,2},{2,3},{4,5},{5,6},{6,7},{8,9},{9,10},{10,11},{12,13},{... | collective-permute-start | bytes 110600 | tf_op jit(solution)/shard_map/ppermute | solution.py:24
  67.2 3.2 %collective-permute-done.2 = bf16[4,18,1,256]{3,2,1,0:T(2,128)(2,1)} collective-permute-done((bf16[4,18,1,256]{3,2,1,0:T(2,128)(2,1)S(1)}, bf16[4,18,1,256]{3,2,1,0:T(2,128)(2,1)}, u32[]{:S(2)}, u32[]{:S(2)}) %collective-permute-start.2) | collective-permute-done | bytes 36896 | tf_op jit(solution)/shard_map/ppermute | solution.py:24
  70.4 1.6 pad_maximum_fusion.3
  72.0 1.6 pad_maximum_fusion
  73.8 0.4 fusion.61
  74.2 0.4 fusion.57
  74.6 0.5 fusion.59
  75.1 0.5 fusion.55
  75.5 0.4 fusion.53
  76.0 0.4 fusion.72
  77.3 1.1 add_convert_fusion
  78.4 0.8 slice.202
  79.2 2.1 %collective-permute-start.11 = (bf16[2,16,32,256]{3,2,1,0:T(8,128)(2,1)}, bf16[2,16,32,256]{3,2,1,0:T(8,128)(2,1)}, u32[]{:S(2)}, u32[]{:S(2)}) collective-permute-start(bf16[2,16,32,256]{3,2,1,0:T(8,128)(2,1)} %slice.202), channel_id=1, source_target_pairs={{0,16},{16,32},{32,48},{48,64},{64,80},{80,96},{96,112},{112,128},... | collective-permute-start | bytes 1572872 | tf_op jit(solution)/shard_map/ppermute | solution.py:33
  81.7 0.6 collective-permute-done.11
  82.3 1.2 pad_maximum_fusion.2
  83.5 1.2 fusion.23
  84.7 1.2 fusion.26
  85.9 1.2 fusion.29
  87.1 5.0 %pad_maximum_fusion.1 = bf16[4,16,32,768]{3,0,2,1:T(4,128)(2,1)S(1)} fusion(bf16[4,16,32,256]{3,0,2,1:T(4,128)(2,1)S(1)} %fusion.29, bf16[4,16,32,256]{3,0,2,1:T(4,128)(2,1)S(1)} %fusion.26, bf16[4,16,32,256]{3,0,2,1:T(4,128)(2,1)S(1)} %fusion.23), kind=kLoop, calls=%fused_computation.6 | loop fusion | flops 9437184 | bytes 6291456 | tf_op jit(solution)/shard_map/concatenate | solution.py:136
  92.1 1.1 convert_reduce_fusion.1
  93.2 1.1 copy.90
  94.3 23.5 %all-to-all-start = ((bf16[32,4,16,256]{3,2,1,0:T(8,128)(2,1)}), bf16[32,4,16,256]{3,2,1,0:T(8,128)(2,1)S(1)}, u32[]{:S(2)}, u32[]{:S(2)}) async-start(bf16[32,4,16,256]{3,2,1,0:T(8,128)(2,1)} %bitcast.158), calls=%async_computation | async-start | bytes 2097152 | tf_op jit(solution)/shard_map/all_to_all | solution.py:144
  118.3 6.8 %psum.30 = f32[2,4,32]{2,1,0:T(4,128)S(1)} all-reduce(f32[2,4,32]{2,1,0:T(4,128)S(1)} %pad_maximum_fusion.8), channel_id=1, replica_groups=mesh['z'=16,'core'=2,'band'=4,'fsdp'=4] {'band'}, use_global_device_ids=true, to_apply=%region_12.13 | all-reduce | flops 256 | bytes 2048 | tf_op jit(solution)/shard_map/psum | solution.py:61
  125.1 7.3 %psum.31 = f32[2,4,32]{2,1,0:T(4,128)S(1)} all-reduce(f32[2,4,32]{2,1,0:T(4,128)S(1)} %psum.30), channel_id=1, replica_groups=mesh['z'=16,'core'=2,'band'=4,'fsdp'=4] {'fsdp'}, use_global_device_ids=true, to_apply=%region_13.14 | all-reduce | flops 256 | bytes 2048 | tf_op jit(solution)/shard_map/psum | solution.py:62
  132.5 1.8 all-gather
  134.3 55.1 %all_gather.7 = f32[128,64]{1,0:T(8,128)S(1)} all-gather(f32[8,64]{1,0:T(8,128)S(1)} %bitcast.169), channel_id=1, replica_groups=mesh['z'=16,'core'=2,'band'=4,'fsdp'=4] {'z'}, dimensions={0}, use_global_device_ids=true | all-gather | bytes 34816 | tf_op jit(solution)/shard_map/all_gather | solution.py:149
  190.2 4.6 %convolution_convert_fusion = bf16[128,16,768]{2,0,1:T(8,128)(2,1)} fusion(f32[128,16,256]{2,1,0:T(8,128)S(1)} %bitcast_convert_fusion, f32[256]{0:T(256)S(1)} %bitcast.174, f32[128,256]{1,0:T(8,128)S(1)} %copy.49, f32[128,256]{1,0:T(8,128)S(1)} %copy.47, bf16[256,2048]{1,0:T(8,128)(2,1)} %copy-done.1), kind=kOutput, calls=%fused_computation.11 | convolution fusion | flops 808976384 | bytes 5899264 | tf_op jit(solution)/shard_map/fpc,cd->fpd/dot_general | solution.py:152
  194.9 2.1 %fusion.103 = (f32[16,128]{1,0:T(8,128)S(1)}, f32[16,128,128]{1,2,0:T(8,128)S(1)}) fusion(pred[128,128]{0,1:T(8,128)(4,1)S(1)} %fusion.76, bf16[128,16,768]{2,0,1:T(8,128)(2,1)} %convolution_convert_fusion), kind=kOutput, calls=%fused_computation.167 | convolution fusion | flops 135528576 | bytes 3186688 | tf_op jit(solution)/shard_map/sub | solution.py:165
  197.0 3.9 %fusion.35 = bf16[1,1,16,128,256]{4,3,2,1,0:T(8,128)(2,1)} fusion(f32[128,16,256]{2,1,0:T(8,128)S(1)} %bitcast_convert_fusion, bf16[128,16,768]{2,0,1:T(8,128)(2,1)} %convolution_convert_fusion, f32[16,128,128]{1,2,0:T(8,128)S(1)} %get-tuple-element.29, f32[16,128]{1,0:T(8,128)S(1)} %get-tuple-element.28, bf16[256,2048]{1,0:T(8,128)(2,1)} %copy-done.1), kind=kOutput, calls=%fused_computation.43 | convolution fusion | flops 404750336 | bytes 5382144 | tf_op jit(solution)/shard_map/axi,iy->axy/dot_general | solution.py:170
  (74 shorter events, 4.4 us)
Async XLA Ops:
  0.0 36.8 %copy-start.2 = (f32[2,256]{1,0:T(2,128)S(1)}, f32[2,256]{1,0:T(2,128)}, u32[]{:S(2)}) copy-start(f32[2,256]{1,0:T(2,128)} %param.9) | copy-start | bytes 6148
  0.9 30.5 %collective-permute-start.3 = (bf16[16,2048]{1,0:T(8,128)(2,1)S(1)}, bf16[16,2048]{1,0:T(8,128)(2,1)S(1)}, u32[]{:S(2)}, u32[]{:S(2)}) collective-permute-start(bf16[16,2048]{1,0:T(8,128)(2,1)S(1)} %fusion.75), channel_id=1, source_target_pairs={{0,3},{1,0},{2,1},{3,2},{4,7},{5,4},{6,5},{7,6},{8,11},{9,8},{10,9... | collective-permute-start | bytes 196616 | tf_op jit(solution)/shard_map/ppermute | solution.py:41
  3.4 28.1 %collective-permute-start.4 = (bf16[16,2048]{1,0:T(8,128)(2,1)S(1)}, bf16[16,2048]{1,0:T(8,128)(2,1)S(1)}, u32[]{:S(2)}, u32[]{:S(2)}) collective-permute-start(bf16[16,2048]{1,0:T(8,128)(2,1)S(1)} %fusion.75), channel_id=1, source_target_pairs={{0,2},{1,3},{2,0},{3,1},{4,6},{5,7},{6,4},{7,5},{8,10},{9,11},{10,... | collective-permute-start | bytes 196616 | tf_op jit(solution)/shard_map/ppermute | solution.py:41
  7.7 23.8 %collective-permute-start.5 = (bf16[16,2048]{1,0:T(8,128)(2,1)S(1)}, bf16[16,2048]{1,0:T(8,128)(2,1)S(1)}, u32[]{:S(2)}, u32[]{:S(2)}) collective-permute-start(bf16[16,2048]{1,0:T(8,128)(2,1)S(1)} %fusion.75), channel_id=1, source_target_pairs={{0,1},{1,2},{2,3},{3,0},{4,5},{5,6},{6,7},{7,4},{8,9},{9,10},{10,1... | collective-permute-start | bytes 196616 | tf_op jit(solution)/shard_map/ppermute | solution.py:41
  31.6 11.2 %collective-permute-start.6 = (bf16[64,2048]{1,0:T(8,128)(2,1)S(1)}, bf16[64,2048]{1,0:T(8,128)(2,1)S(1)}, u32[]{:S(2)}, u32[]{:S(2)}) collective-permute-start(bf16[64,2048]{1,0:T(8,128)(2,1)S(1)} %bitcast.163), channel_id=1, source_target_pairs={{0,12},{4,0},{8,4},{12,8},{1,13},{5,1},{9,5},{13,9},{2,14},{6,2},{... | collective-permute-start | bytes 786440 | tf_op jit(solution)/shard_map/ppermute | solution.py:41
  36.9 9.9 %collective-permute-start.7 = (bf16[64,2048]{1,0:T(8,128)(2,1)S(1)}, bf16[64,2048]{1,0:T(8,128)(2,1)S(1)}, u32[]{:S(2)}, u32[]{:S(2)}) collective-permute-start(bf16[64,2048]{1,0:T(8,128)(2,1)S(1)} %bitcast.164), channel_id=1, source_target_pairs={{0,8},{4,12},{8,0},{12,4},{1,9},{5,13},{9,1},{13,5},{2,10},{6,14},... | collective-permute-start | bytes 786440 | tf_op jit(solution)/shard_map/ppermute | solution.py:41
  40.2 9.2 %collective-permute-start.8 = (bf16[64,2048]{1,0:T(8,128)(2,1)S(1)}, bf16[64,2048]{1,0:T(8,128)(2,1)S(1)}, u32[]{:S(2)}, u32[]{:S(2)}) collective-permute-start(bf16[64,2048]{1,0:T(8,128)(2,1)S(1)} %bitcast.165), channel_id=1, source_target_pairs={{0,4},{4,8},{8,12},{12,0},{1,5},{5,9},{9,13},{13,1},{2,6},{6,10},{... | collective-permute-start | bytes 786440 | tf_op jit(solution)/shard_map/ppermute | solution.py:41
  49.5 2.3 %copy-start = (bf16[4,16,32,256]{3,2,1,0:T(8,128)(2,1)S(1)}, bf16[4,16,32,256]{3,2,1,0:T(8,128)(2,1)}, u32[]{:S(2)}) copy-start(bf16[4,16,32,256]{3,2,1,0:T(8,128)(2,1)} %param.7) | copy-start | bytes 3145732
  49.7 22.3 %collective-permute-start.9 = (bf16[256,2048]{1,0:T(8,128)(2,1)S(1)}, bf16[256,2048]{1,0:T(8,128)(2,1)}, u32[]{:S(2)}, u32[]{:S(2)}) collective-permute-start(bf16[256,2048]{1,0:T(8,128)(2,1)S(1)} %bitcast.161), channel_id=1, source_target_pairs={{0,16},{16,0},{1,17},{17,1},{2,18},{18,2},{3,19},{19,3},{4,20},{20... | collective-permute-start | bytes 3145736 | tf_op jit(solution)/shard_map/ppermute | solution.py:88
  52.5 6.4 %collective-permute-start = (bf16[4,1,32,256]{3,2,1,0:T(8,128)(2,1)S(1)}, bf16[4,1,32,256]{3,2,1,0:T(8,128)(2,1)S(1)}, u32[]{:S(2)}, u32[]{:S(2)}) collective-permute-start(bf16[4,1,32,256]{3,2,1,0:T(8,128)(2,1)S(1)} %get-tuple-element.18), channel_id=1, source_target_pairs={{0,4},{4,8},{8,12},{1,5},{5,9},{9,13},{2,6},{6,10},{10,14},{3,7},{... | collective-permute-start | bytes 196616 | tf_op jit(solution)/shard_map/ppermute | solution.py:24
  54.4 6.4 %collective-permute-start.1 = (bf16[4,1,32,256]{3,2,1,0:T(8,128)(2,1)S(1)}, bf16[4,1,32,256]{3,2,1,0:T(8,128)(2,1)S(1)}, u32[]{:S(2)}, u32[]{:S(2)}) collective-permute-start(bf16[4,1,32,256]{3,2,1,0:T(8,128)(2,1)S(1)} %get-tuple-element.19), channel_id=1, source_target_pairs={{4,0},{8,4},{12,8},{5,1},{9,5},{13,9},{6,2},{10,6},{14,10},{7,3},{... | collective-permute-start | bytes 196616 | tf_op jit(solution)/shard_map/ppermute | solution.py:25
  60.9 6.2 %collective-permute-start.10 = (bf16[4,18,1,256]{3,2,1,0:T(2,128)(2,1)S(1)}, bf16[4,18,1,256]{3,2,1,0:T(2,128)(2,1)S(1)}, u32[]{:S(2)}, u32[]{:S(2)}) collective-permute-start(bf16[4,18,1,256]{3,2,1,0:T(2,128)(2,1)S(1)} %get-tuple-element.13), channel_id=1, source_target_pairs={{1,0},{2,1},{3,2},{5,4},{6,5},{7,6},{9,8},{10,9},{11,10},{13,12},{... | collective-permute-start | bytes 110600 | tf_op jit(solution)/shard_map/ppermute | solution.py:25
  64.1 6.4 %collective-permute-start.2 = (bf16[4,18,1,256]{3,2,1,0:T(2,128)(2,1)S(1)}, bf16[4,18,1,256]{3,2,1,0:T(2,128)(2,1)}, u32[]{:S(2)}, u32[]{:S(2)}) collective-permute-start(bf16[4,18,1,256]{3,2,1,0:T(2,128)(2,1)S(1)} %get-tuple-element.14), channel_id=1, source_target_pairs={{0,1},{1,2},{2,3},{4,5},{5,6},{6,7},{8,9},{9,10},{10,11},{12,13},{... | collective-permute-start | bytes 110600 | tf_op jit(solution)/shard_map/ppermute | solution.py:24
  73.8 7.9 %copy-start.1 = (bf16[256,2048]{1,0:T(8,128)(2,1)}, bf16[256,2048]{1,0:T(8,128)(2,1)S(1)}, u32[]{:S(2)}) copy-start(bf16[256,2048]{1,0:T(8,128)(2,1)S(1)} %get-tuple-element.9) | copy-start | bytes 3145732
  77.3 4.0 %copy-start.3 = (s32[16]{0:T(128)S(1)}, s32[16]{0:T(128)}, u32[]{:S(2)}) copy-start(s32[16]{0:T(128)} %param.8) | copy-start | bytes 196
  79.2 3.1 %collective-permute-start.11 = (bf16[2,16,32,256]{3,2,1,0:T(8,128)(2,1)}, bf16[2,16,32,256]{3,2,1,0:T(8,128)(2,1)}, u32[]{:S(2)}, u32[]{:S(2)}) collective-permute-start(bf16[2,16,32,256]{3,2,1,0:T(8,128)(2,1)} %slice.202), channel_id=1, source_target_pairs={{0,16},{16,32},{32,48},{48,64},{64,80},{80,96},{96,112},{112,128},... | collective-permute-start | bytes 1572872 | tf_op jit(solution)/shard_map/ppermute | solution.py:33
  94.3 95.5 %all-to-all-start = ((bf16[32,4,16,256]{3,2,1,0:T(8,128)(2,1)}), bf16[32,4,16,256]{3,2,1,0:T(8,128)(2,1)S(1)}, u32[]{:S(2)}, u32[]{:S(2)}) async-start(bf16[32,4,16,256]{3,2,1,0:T(8,128)(2,1)} %bitcast.158), calls=%async_computation | async-start | bytes 2097152 | tf_op jit(solution)/shard_map/all_to_all | solution.py:144

commit v12 on v9

--- a/solution.py
+++ b/solution.py
@@ -118,14 +118,10 @@
     carried = from_behind(spatial[frames - 2 :], TM, 1)
     extended = jnp.concatenate([carried, spatial], axis=0)
     position = first + jnp.arange(frames, dtype=jnp.int32)
-    slots = jnp.arange(frames + 2, dtype=jnp.int32)
     temporal = jnp.zeros((frames, height, width, chans), jnp.float32)
     for tap in range(3):
         source = jnp.maximum(position - 2 + tap, local_starts) - first + 2
-        select = (source[:, None] == slots[None, :]).astype(jnp.bfloat16)
-        picked = jnp.einsum(
-            "fe,ehwc->fhwc", select, extended, preferred_element_type=jnp.float32
-        ).astype(jnp.bfloat16)
+        picked = jnp.take(extended, source, axis=0, mode="clip")
         temporal = temporal + jnp.einsum(
             "fhwc,cd->fhwd",
             picked,

time: 198 us -> 206 us (1.040)
  local copies, waits for them, and re-layouts: 3.7 us -> 8.66 us
  matrix products: 20.6 us -> 24.5 us
    dot_general x3, matrix products: 1.77 us -> 9.29 us  [body(): jnp.einsum('fhwc,cd->fhwd', picked, time_full[:, tap * chans:(tap + 1) *...]
    gather x0 -> x3, local copies, waits for them, and re-layouts: none -> 4.75 us  [body(): picked = jnp.take(extended, source, axis=0, mode='clip')]
    dot_general x3 -> x0, matrix products: 3.6 us -> none  [body(): jnp.einsum('fe,ehwc->fhwc', select, extended, preferred_element_type=jnp....]
where the time goes in v12:
time: 206 us; the launch traced here: 205 us
  blocking collectives  89.1 us (43%)
  starting transfers between devices  59.8 us (29%)
  matrix products  24.5 us (12%)
  waiting for transfers between devices  13.7 us (7%)
  other arithmetic  8.95 us (4%)
  local copies, waits for them, and re-layouts  8.66 us (4%)
    all_gather x2, blocking collectives, body(): moments = lax.all_gather(moments, axis, axis=0, tiled=True)  57 us
    all_to_all x1, starting transfers between devices, body(): lax.all_to_all(flat_resid, TM, split_axis=0, concat_axis=0, tiled=True)  23.6 us
    ppermute x6, starting transfers between devices, ring_gather(): lax.ppermute(x, axis, [(i, (i + shift) % size) for i in range(size)])  21.2 us
    psum x2, blocking collectives, group_moments(): both = lax.psum(lax.optimization_barrier(both), 'fsdp')  16.9 us
    psum x2, blocking collectives, group_moments(): both = lax.psum(jnp.stack([sums, squares]), 'band')  15.2 us
    dot_general x3, matrix products, body(): jnp.einsum('fhwc,cd->fhwd', picked, time_full[:, tap * chans:(tap + 1) *...  9.29 us
    ppermute x2, starting transfers between devices, with_halo(): after = lax.ppermute(initial, axis, down)  7.05 us
    ppermute x6, waiting for transfers between devices, ring_gather(): lax.ppermute(x, axis, [(i, (i + shift) % size) for i in range(size)])  6.61 us
  transfers between devices with their start and end apart: 13, of which 7 were waited for; matrix products, arithmetic and copies ran while one was open for 3% of the time, Pallas kernels for 0%

profile of v12, /device:TPU:18, one launch (start us, length us, event | category | flops | bytes accessed | tf_op | source)
XLA Modules:
  0.0 205.3 jit_solution(15277167575362373177)
XLA Ops:
  0.0 0.9 fusion.55
  0.9 2.4 %collective-permute-start.3 = (bf16[16,2048]{1,0:T(8,128)(2,1)S(1)}, bf16[16,2048]{1,0:T(8,128)(2,1)S(1)}, u32[]{:S(2)}, u32[]{:S(2)}) collective-permute-start(bf16[16,2048]{1,0:T(8,128)(2,1)S(1)} %fusion.55), channel_id=1, source_target_pairs={{0,3},{1,0},{2,1},{3,2},{4,7},{5,4},{6,5},{7,6},{8,11},{9,8},{10,9... | collective-permute-start | bytes 196616 | tf_op jit(solution)/shard_map/ppermute | solution.py:41
  3.4 4.3 %collective-permute-start.4 = (bf16[16,2048]{1,0:T(8,128)(2,1)S(1)}, bf16[16,2048]{1,0:T(8,128)(2,1)S(1)}, u32[]{:S(2)}, u32[]{:S(2)}) collective-permute-start(bf16[16,2048]{1,0:T(8,128)(2,1)S(1)} %fusion.55), channel_id=1, source_target_pairs={{0,2},{1,3},{2,0},{3,1},{4,6},{5,7},{6,4},{7,5},{8,10},{9,11},{10,... | collective-permute-start | bytes 196616 | tf_op jit(solution)/shard_map/ppermute | solution.py:41
  7.7 3.7 %collective-permute-start.5 = (bf16[16,2048]{1,0:T(8,128)(2,1)S(1)}, bf16[16,2048]{1,0:T(8,128)(2,1)S(1)}, u32[]{:S(2)}, u32[]{:S(2)}) collective-permute-start(bf16[16,2048]{1,0:T(8,128)(2,1)S(1)} %fusion.55), channel_id=1, source_target_pairs={{0,1},{1,2},{2,3},{3,0},{4,5},{5,6},{6,7},{7,4},{8,9},{9,10},{10,1... | collective-permute-start | bytes 196616 | tf_op jit(solution)/shard_map/ppermute | solution.py:41
  11.4 1.5 convert_reduce_fusion
  13.4 8.4 %psum.28 = f32[2,4,32]{2,1,0:T(4,128)S(1)} all-reduce(f32[2,4,32]{2,1,0:T(4,128)S(1)} %pad_maximum_fusion.6), channel_id=1, replica_groups=mesh['z'=16,'core'=2,'band'=4,'fsdp'=4] {'band'}, use_global_device_ids=true, to_apply=%region_4.5 | all-reduce | flops 256 | bytes 2048 | tf_op jit(solution)/shard_map/psum | solution.py:61
  21.8 9.7 %psum.29 = f32[2,4,32]{2,1,0:T(4,128)S(1)} all-reduce(f32[2,4,32]{2,1,0:T(4,128)S(1)} %psum.28), channel_id=1, replica_groups=mesh['z'=16,'core'=2,'band'=4,'fsdp'=4] {'fsdp'}, use_global_device_ids=true, to_apply=%region_5.6 | all-reduce | flops 256 | bytes 2048 | tf_op jit(solution)/shard_map/psum | solution.py:62
  31.6 4.8 %collective-permute-start.6 = (bf16[64,2048]{1,0:T(8,128)(2,1)S(1)}, bf16[64,2048]{1,0:T(8,128)(2,1)S(1)}, u32[]{:S(2)}, u32[]{:S(2)}) collective-permute-start(bf16[64,2048]{1,0:T(8,128)(2,1)S(1)} %bitcast.164), channel_id=1, source_target_pairs={{0,12},{4,0},{8,4},{12,8},{1,13},{5,1},{9,5},{13,9},{2,14},{6,2},{... | collective-permute-start | bytes 786440 | tf_op jit(solution)/shard_map/ppermute | solution.py:41
  36.9 3.4 %collective-permute-start.7 = (bf16[64,2048]{1,0:T(8,128)(2,1)S(1)}, bf16[64,2048]{1,0:T(8,128)(2,1)S(1)}, u32[]{:S(2)}, u32[]{:S(2)}) collective-permute-start(bf16[64,2048]{1,0:T(8,128)(2,1)S(1)} %bitcast.165), channel_id=1, source_target_pairs={{0,8},{4,12},{8,0},{12,4},{1,9},{5,13},{9,1},{13,5},{2,10},{6,14},... | collective-permute-start | bytes 786440 | tf_op jit(solution)/shard_map/ppermute | solution.py:41
  40.2 2.5 %collective-permute-start.8 = (bf16[64,2048]{1,0:T(8,128)(2,1)S(1)}, bf16[64,2048]{1,0:T(8,128)(2,1)S(1)}, u32[]{:S(2)}, u32[]{:S(2)}) collective-permute-start(bf16[64,2048]{1,0:T(8,128)(2,1)S(1)} %bitcast.166), channel_id=1, source_target_pairs={{0,4},{4,8},{8,12},{12,0},{1,5},{5,9},{9,13},{13,1},{2,6},{6,10},{... | collective-permute-start | bytes 786440 | tf_op jit(solution)/shard_map/ppermute | solution.py:41
  42.8 3.9 %collective-permute-done.7 = bf16[64,2048]{1,0:T(8,128)(2,1)S(1)} collective-permute-done((bf16[64,2048]{1,0:T(8,128)(2,1)S(1)}, bf16[64,2048]{1,0:T(8,128)(2,1)S(1)}, u32[]{:S(2)}, u32[]{:S(2)}) %collective-permute-start.7) | collective-permute-done | bytes 262176 | tf_op jit(solution)/shard_map/ppermute | solution.py:41
  46.8 2.7 %collective-permute-done.8 = bf16[64,2048]{1,0:T(8,128)(2,1)S(1)} collective-permute-done((bf16[64,2048]{1,0:T(8,128)(2,1)S(1)}, bf16[64,2048]{1,0:T(8,128)(2,1)S(1)}, u32[]{:S(2)}, u32[]{:S(2)}) %collective-permute-start.8) | collective-permute-done | bytes 262176 | tf_op jit(solution)/shard_map/ppermute | solution.py:41
  49.7 2.1 collective-permute-start.9
  51.8 0.7 fusion.10
  52.5 1.9 collective-permute-start
  54.4 3.9 %collective-permute-start.1 = (bf16[4,1,32,256]{3,2,1,0:T(8,128)(2,1)S(1)}, bf16[4,1,32,256]{3,2,1,0:T(8,128)(2,1)S(1)}, u32[]{:S(2)}, u32[]{:S(2)}) collective-permute-start(bf16[4,1,32,256]{3,2,1,0:T(8,128)(2,1)S(1)} %get-tuple-element.16), channel_id=1, source_target_pairs={{4,0},{8,4},{12,8},{5,1},{9,5},{13,9},{6,2},{10,6},{14,10},{7,3},{... | collective-permute-start | bytes 196616 | tf_op jit(solution)/shard_map/ppermute | solution.py:25
  58.3 0.5 collective-permute-done
  58.9 1.9 collective-permute-done.1
  60.9 3.1 %collective-permute-start.10 = (bf16[4,18,1,256]{3,2,1,0:T(2,128)(2,1)S(1)}, bf16[4,18,1,256]{3,2,1,0:T(2,128)(2,1)S(1)}, u32[]{:S(2)}, u32[]{:S(2)}) collective-permute-start(bf16[4,18,1,256]{3,2,1,0:T(2,128)(2,1)S(1)} %get-tuple-element.13), channel_id=1, source_target_pairs={{1,0},{2,1},{3,2},{5,4},{6,5},{7,6},{9,8},{10,9},{11,10},{13,12},{... | collective-permute-start | bytes 110600 | tf_op jit(solution)/shard_map/ppermute | solution.py:25
  64.1 2.7 %collective-permute-start.2 = (bf16[4,18,1,256]{3,2,1,0:T(2,128)(2,1)S(1)}, bf16[4,18,1,256]{3,2,1,0:T(2,128)(2,1)}, u32[]{:S(2)}, u32[]{:S(2)}) collective-permute-start(bf16[4,18,1,256]{3,2,1,0:T(2,128)(2,1)S(1)} %get-tuple-element.14), channel_id=1, source_target_pairs={{0,1},{1,2},{2,3},{4,5},{5,6},{6,7},{8,9},{9,10},{10,11},{12,13},{... | collective-permute-start | bytes 110600 | tf_op jit(solution)/shard_map/ppermute | solution.py:24
  67.2 3.2 %collective-permute-done.2 = bf16[4,18,1,256]{3,2,1,0:T(2,128)(2,1)} collective-permute-done((bf16[4,18,1,256]{3,2,1,0:T(2,128)(2,1)S(1)}, bf16[4,18,1,256]{3,2,1,0:T(2,128)(2,1)}, u32[]{:S(2)}, u32[]{:S(2)}) %collective-permute-start.2) | collective-permute-done | bytes 36896 | tf_op jit(solution)/shard_map/ppermute | solution.py:24
  70.4 1.6 pad_maximum_fusion.2
  72.0 1.6 pad_maximum_fusion
  74.2 0.4 fusion.38
  74.7 0.5 fusion.40
  75.1 0.5 fusion.36
  75.6 0.4 fusion.34
  76.0 0.4 fusion.52
  77.3 1.0 add_convert_fusion
  78.4 1.0 copy-done.1
  79.4 1.3 collective-permute-start.11
  81.2 1.0 collective-permute-done.11
  82.2 1.4 pad_maximum_fusion.1
  83.6 1.6 gather_fusion.1
  85.2 3.0 %fusion.50 = f32[4,16,32,256]{3,2,1,0:T(8,128)} fusion(bf16[4,16,32,256]{3,2,1,0:T(8,128)(2,1)} %gather_fusion.1, bf16[256,2048]{1,0:T(8,128)(2,1)} %copy-done.2), kind=kOutput, calls=%fused_computation.82 | convolution fusion | flops 268435456 | bytes 3276800 | tf_op jit(solution)/shard_map/fhwc,cd->fhwd/dot_general | solution.py:125
  88.1 1.6 gather_fusion
  89.7 3.0 %fusion.51 = f32[4,16,32,256]{3,2,1,0:T(8,128)} fusion(bf16[4,16,32,256]{3,2,1,0:T(8,128)(2,1)} %gather_fusion, bf16[256,2048]{1,0:T(8,128)(2,1)} %copy-done.2), kind=kOutput, calls=%fused_computation.84 | convolution fusion | flops 268435456 | bytes 3276800 | tf_op jit(solution)/shard_map/fhwc,cd->fhwd/dot_general | solution.py:125
  92.7 1.6 gather_fusion.2
  94.3 3.3 %convert_reduce_fusion.1 = (f32[4,256]{1,0:T(4,128)S(1)}, f32[4,256]{1,0:T(4,128)S(1)}, bf16[4,16,32,256]{3,2,1,0:T(8,128)(2,1)S(1)}) fusion(bf16[4,16,32,256]{3,2,1,0:T(8,128)(2,1)} %gather_fusion.2, bf16[256,2048]{1,0:T(8,128)(2,1)} %copy-done.2, f32[4,16,32,256]{3,2,1,0:T(8,128)} %fusion.51, f32[4,16,32,256]{3,2,1,0:T(8,128)} %fusion.50, ...), kind=kOutput, calls=%fused_computation.10 | convolution fusion | flops 273152000 | bytes 7479296 | tf_op jit(solution)/shard_map/fhwc,cd->fhwd/dot_general | solution.py:125
  97.6 1.1 copy.59
  98.7 23.6 %all-to-all-start = ((bf16[32,4,16,256]{3,2,1,0:T(8,128)(2,1)}), bf16[32,4,16,256]{3,2,1,0:T(8,128)(2,1)S(1)}, u32[]{:S(2)}, u32[]{:S(2)}) async-start(bf16[32,4,16,256]{3,2,1,0:T(8,128)(2,1)} %bitcast.158), calls=%async_computation | async-start | bytes 2097152 | tf_op jit(solution)/shard_map/all_to_all | solution.py:135
  122.8 6.8 %psum.30 = f32[2,4,32]{2,1,0:T(4,128)S(1)} all-reduce(f32[2,4,32]{2,1,0:T(4,128)S(1)} %pad_maximum_fusion.7), channel_id=1, replica_groups=mesh['z'=16,'core'=2,'band'=4,'fsdp'=4] {'band'}, use_global_device_ids=true, to_apply=%region_12.13 | all-reduce | flops 256 | bytes 2048 | tf_op jit(solution)/shard_map/psum | solution.py:61
  129.6 7.2 %psum.31 = f32[2,4,32]{2,1,0:T(4,128)S(1)} all-reduce(f32[2,4,32]{2,1,0:T(4,128)S(1)} %psum.30), channel_id=1, replica_groups=mesh['z'=16,'core'=2,'band'=4,'fsdp'=4] {'fsdp'}, use_global_device_ids=true, to_apply=%region_13.14 | all-reduce | flops 256 | bytes 2048 | tf_op jit(solution)/shard_map/psum | solution.py:62
  136.9 1.8 all-gather
  138.7 55.1 %all_gather.7 = f32[128,64]{1,0:T(8,128)S(1)} all-gather(f32[8,64]{1,0:T(8,128)S(1)} %bitcast.169), channel_id=1, replica_groups=mesh['z'=16,'core'=2,'band'=4,'fsdp'=4] {'z'}, dimensions={0}, use_global_device_ids=true | all-gather | bytes 34816 | tf_op jit(solution)/shard_map/all_gather | solution.py:140
  194.7 4.6 %convolution_convert_fusion = bf16[128,16,768]{2,0,1:T(8,128)(2,1)} fusion(f32[128,16,256]{2,1,0:T(8,128)S(1)} %bitcast_convert_fusion, f32[256]{0:T(256)S(1)} %bitcast.174, f32[128,256]{1,0:T(8,128)S(1)} %copy.37, f32[128,256]{1,0:T(8,128)S(1)} %copy.35, bf16[256,2048]{1,0:T(8,128)(2,1)} %copy-done.2), kind=kOutput, calls=%fused_computation.11 | convolution fusion | flops 808976384 | bytes 5899264 | tf_op jit(solution)/shard_map/fpc,cd->fpd/dot_general | solution.py:143
  199.3 2.1 %fusion.72 = (f32[16,128]{1,0:T(8,128)S(1)}, f32[16,128,128]{1,2,0:T(8,128)S(1)}) fusion(pred[128,128]{0,1:T(8,128)(4,1)S(1)} %fusion.56, bf16[128,16,768]{2,0,1:T(8,128)(2,1)} %convolution_convert_fusion), kind=kOutput, calls=%fused_computation.151 | convolution fusion | flops 135528576 | bytes 3186688 | tf_op jit(solution)/shard_map/sub | solution.py:156
  201.5 3.9 %fusion.16 = bf16[1,1,16,128,256]{4,3,2,1,0:T(8,128)(2,1)} fusion(f32[128,16,256]{2,1,0:T(8,128)S(1)} %bitcast_convert_fusion, bf16[128,16,768]{2,0,1:T(8,128)(2,1)} %convolution_convert_fusion, f32[16,128,128]{1,2,0:T(8,128)S(1)} %get-tuple-element.26, f32[16,128]{1,0:T(8,128)S(1)} %get-tuple-element.25, bf16[256,2048]{1,0:T(8,128)(2,1)} %copy-done.2), kind=kOutput, calls=%fused_computation.34 | convolution fusion | flops 404750336 | bytes 5382144 | tf_op jit(solution)/shard_map/axi,iy->axy/dot_general | solution.py:161
  (78 shorter events, 4.9 us)
Async XLA Ops:
  0.0 36.8 %copy-start.3 = (f32[2,256]{1,0:T(2,128)S(1)}, f32[2,256]{1,0:T(2,128)}, u32[]{:S(2)}) copy-start(f32[2,256]{1,0:T(2,128)} %param.9) | copy-start | bytes 6148
  0.9 30.5 %collective-permute-start.3 = (bf16[16,2048]{1,0:T(8,128)(2,1)S(1)}, bf16[16,2048]{1,0:T(8,128)(2,1)S(1)}, u32[]{:S(2)}, u32[]{:S(2)}) collective-permute-start(bf16[16,2048]{1,0:T(8,128)(2,1)S(1)} %fusion.55), channel_id=1, source_target_pairs={{0,3},{1,0},{2,1},{3,2},{4,7},{5,4},{6,5},{7,6},{8,11},{9,8},{10,9... | collective-permute-start | bytes 196616 | tf_op jit(solution)/shard_map/ppermute | solution.py:41
  3.4 28.1 %collective-permute-start.4 = (bf16[16,2048]{1,0:T(8,128)(2,1)S(1)}, bf16[16,2048]{1,0:T(8,128)(2,1)S(1)}, u32[]{:S(2)}, u32[]{:S(2)}) collective-permute-start(bf16[16,2048]{1,0:T(8,128)(2,1)S(1)} %fusion.55), channel_id=1, source_target_pairs={{0,2},{1,3},{2,0},{3,1},{4,6},{5,7},{6,4},{7,5},{8,10},{9,11},{10,... | collective-permute-start | bytes 196616 | tf_op jit(solution)/shard_map/ppermute | solution.py:41
  7.7 23.8 %collective-permute-start.5 = (bf16[16,2048]{1,0:T(8,128)(2,1)S(1)}, bf16[16,2048]{1,0:T(8,128)(2,1)S(1)}, u32[]{:S(2)}, u32[]{:S(2)}) collective-permute-start(bf16[16,2048]{1,0:T(8,128)(2,1)S(1)} %fusion.55), channel_id=1, source_target_pairs={{0,1},{1,2},{2,3},{3,0},{4,5},{5,6},{6,7},{7,4},{8,9},{9,10},{10,1... | collective-permute-start | bytes 196616 | tf_op jit(solution)/shard_map/ppermute | solution.py:41
  31.6 11.2 %collective-permute-start.6 = (bf16[64,2048]{1,0:T(8,128)(2,1)S(1)}, bf16[64,2048]{1,0:T(8,128)(2,1)S(1)}, u32[]{:S(2)}, u32[]{:S(2)}) collective-permute-start(bf16[64,2048]{1,0:T(8,128)(2,1)S(1)} %bitcast.164), channel_id=1, source_target_pairs={{0,12},{4,0},{8,4},{12,8},{1,13},{5,1},{9,5},{13,9},{2,14},{6,2},{... | collective-permute-start | bytes 786440 | tf_op jit(solution)/shard_map/ppermute | solution.py:41
  36.9 9.9 %collective-permute-start.7 = (bf16[64,2048]{1,0:T(8,128)(2,1)S(1)}, bf16[64,2048]{1,0:T(8,128)(2,1)S(1)}, u32[]{:S(2)}, u32[]{:S(2)}) collective-permute-start(bf16[64,2048]{1,0:T(8,128)(2,1)S(1)} %bitcast.165), channel_id=1, source_target_pairs={{0,8},{4,12},{8,0},{12,4},{1,9},{5,13},{9,1},{13,5},{2,10},{6,14},... | collective-permute-start | bytes 786440 | tf_op jit(solution)/shard_map/ppermute | solution.py:41
  40.2 9.2 %collective-permute-start.8 = (bf16[64,2048]{1,0:T(8,128)(2,1)S(1)}, bf16[64,2048]{1,0:T(8,128)(2,1)S(1)}, u32[]{:S(2)}, u32[]{:S(2)}) collective-permute-start(bf16[64,2048]{1,0:T(8,128)(2,1)S(1)} %bitcast.166), channel_id=1, source_target_pairs={{0,4},{4,8},{8,12},{12,0},{1,5},{5,9},{9,13},{13,1},{2,6},{6,10},{... | collective-permute-start | bytes 786440 | tf_op jit(solution)/shard_map/ppermute | solution.py:41
  49.5 2.3 %copy-start = (bf16[4,16,32,256]{3,2,1,0:T(8,128)(2,1)S(1)}, bf16[4,16,32,256]{3,2,1,0:T(8,128)(2,1)}, u32[]{:S(2)}) copy-start(bf16[4,16,32,256]{3,2,1,0:T(8,128)(2,1)} %param.7) | copy-start | bytes 3145732
  49.7 22.3 %collective-permute-start.9 = (bf16[256,2048]{1,0:T(8,128)(2,1)S(1)}, bf16[256,2048]{1,0:T(8,128)(2,1)}, u32[]{:S(2)}, u32[]{:S(2)}) collective-permute-start(bf16[256,2048]{1,0:T(8,128)(2,1)S(1)} %bitcast.161), channel_id=1, source_target_pairs={{0,16},{16,0},{1,17},{17,1},{2,18},{18,2},{3,19},{19,3},{4,20},{20... | collective-permute-start | bytes 3145736 | tf_op jit(solution)/shard_map/ppermute | solution.py:88
  52.5 6.4 %collective-permute-start = (bf16[4,1,32,256]{3,2,1,0:T(8,128)(2,1)S(1)}, bf16[4,1,32,256]{3,2,1,0:T(8,128)(2,1)S(1)}, u32[]{:S(2)}, u32[]{:S(2)}) collective-permute-start(bf16[4,1,32,256]{3,2,1,0:T(8,128)(2,1)S(1)} %get-tuple-element.15), channel_id=1, source_target_pairs={{0,4},{4,8},{8,12},{1,5},{5,9},{9,13},{2,6},{6,10},{10,14},{3,7},{... | collective-permute-start | bytes 196616 | tf_op jit(solution)/shard_map/ppermute | solution.py:24
  54.4 6.4 %collective-permute-start.1 = (bf16[4,1,32,256]{3,2,1,0:T(8,128)(2,1)S(1)}, bf16[4,1,32,256]{3,2,1,0:T(8,128)(2,1)S(1)}, u32[]{:S(2)}, u32[]{:S(2)}) collective-permute-start(bf16[4,1,32,256]{3,2,1,0:T(8,128)(2,1)S(1)} %get-tuple-element.16), channel_id=1, source_target_pairs={{4,0},{8,4},{12,8},{5,1},{9,5},{13,9},{6,2},{10,6},{14,10},{7,3},{... | collective-permute-start | bytes 196616 | tf_op jit(solution)/shard_map/ppermute | solution.py:25
  60.9 6.2 %collective-permute-start.10 = (bf16[4,18,1,256]{3,2,1,0:T(2,128)(2,1)S(1)}, bf16[4,18,1,256]{3,2,1,0:T(2,128)(2,1)S(1)}, u32[]{:S(2)}, u32[]{:S(2)}) collective-permute-start(bf16[4,18,1,256]{3,2,1,0:T(2,128)(2,1)S(1)} %get-tuple-element.13), channel_id=1, source_target_pairs={{1,0},{2,1},{3,2},{5,4},{6,5},{7,6},{9,8},{10,9},{11,10},{13,12},{... | collective-permute-start | bytes 110600 | tf_op jit(solution)/shard_map/ppermute | solution.py:25
  64.1 6.4 %collective-permute-start.2 = (bf16[4,18,1,256]{3,2,1,0:T(2,128)(2,1)S(1)}, bf16[4,18,1,256]{3,2,1,0:T(2,128)(2,1)}, u32[]{:S(2)}, u32[]{:S(2)}) collective-permute-start(bf16[4,18,1,256]{3,2,1,0:T(2,128)(2,1)S(1)} %get-tuple-element.14), channel_id=1, source_target_pairs={{0,1},{1,2},{2,3},{4,5},{5,6},{6,7},{8,9},{9,10},{10,11},{12,13},{... | collective-permute-start | bytes 110600 | tf_op jit(solution)/shard_map/ppermute | solution.py:24
  73.8 3.5 %copy-start.2 = (bf16[256,2048]{1,0:T(8,128)(2,1)}, bf16[256,2048]{1,0:T(8,128)(2,1)S(1)}, u32[]{:S(2)}) copy-start(bf16[256,2048]{1,0:T(8,128)(2,1)S(1)} %get-tuple-element.9) | copy-start | bytes 3145732
  77.3 3.4 %copy-start.4 = (s32[16]{0:T(128)S(1)}, s32[16]{0:T(128)}, u32[]{:S(2)}) copy-start(s32[16]{0:T(128)} %param.8) | copy-start | bytes 196
  78.4 1.0 copy-start.1
  79.4 2.8 %collective-permute-start.11 = (bf16[2,16,32,256]{3,2,1,0:T(8,128)(2,1)S(1)}, bf16[2,16,32,256]{3,2,1,0:T(8,128)(2,1)S(1)}, u32[]{:S(2)}, u32[]{:S(2)}) collective-permute-start(bf16[2,16,32,256]{3,2,1,0:T(8,128)(2,1)S(1)} %slice.208), channel_id=1, source_target_pairs={{0,16},{16,32},{32,48},{48,64},{64,80},{80,96},{96,112},{112,128},... | collective-permute-start | bytes 1572872 | tf_op jit(solution)/shard_map/ppermute | solution.py:33
  98.7 95.6 %all-to-all-start = ((bf16[32,4,16,256]{3,2,1,0:T(8,128)(2,1)}), bf16[32,4,16,256]{3,2,1,0:T(8,128)(2,1)S(1)}, u32[]{:S(2)}, u32[]{:S(2)}) async-start(bf16[32,4,16,256]{3,2,1,0:T(8,128)(2,1)} %bitcast.158), calls=%async_computation | async-start | bytes 2097152 | tf_op jit(solution)/shard_map/all_to_all | solution.py:135

commit v13 on v9

--- a/solution.py
+++ b/solution.py
@@ -52,14 +52,14 @@
     return jnp.max(chosen, axis=1)
 
 
-def group_moments(field):
+def group_moments(field, order=("band", "fsdp")):
     frames, height, width, chans = field.shape
     group_width = chans // GROUPS
     vals = field.astype(jnp.float32).reshape(frames, height * width, GROUPS, group_width)
     sums = jnp.sum(vals, axis=(1, 3))
     squares = jnp.sum(vals * vals, axis=(1, 3))
-    both = lax.psum(jnp.stack([sums, squares]), "band")
-    both = lax.psum(lax.optimization_barrier(both), "fsdp")
+    both = lax.psum(jnp.stack([sums, squares]), order[0])
+    both = lax.psum(lax.optimization_barrier(both), order[1])
     sums, squares = both[0], both[1]
     count = height * width * group_width * lax.axis_size("band") * lax.axis_size("fsdp")
     mean = sums / count
@@ -101,7 +101,7 @@
     first = lax.axis_index(TM) * frames
     starts = frame_starts(clip_lengths, total_frames)
     local_starts = lax.dynamic_slice_in_dim(starts, first, frames)
-    mean_one, scale_one = group_moments(video)
+    mean_one, scale_one = group_moments(video, ("fsdp", "band"))
     act = jax.nn.silu(apply_norm(video, mean_one, scale_one, norm_gains[0])).astype(jnp.bfloat16)
     padded = with_halo(act, (("band", 1), ("fsdp", 2)), 1)
     spatial = jnp.zeros((frames, height, width, chans), jnp.float32)

time: 198 us -> 198 us (level)
  no operation moved by 1% of the time
where the time goes in v13:
time: 198 us; the launch traced here: 197 us
  blocking collectives  89.1 us (45%)
  starting transfers between devices  60.5 us (31%)
  matrix products  20.6 us (10%)
  waiting for transfers between devices  13.4 us (7%)
  other arithmetic  8.76 us (4%)
  local copies, waits for them, and re-layouts  3.7 us (2%)
    all_gather x2, blocking collectives, body(): moments = lax.all_gather(moments, axis, axis=0, tiled=True)  56.9 us
    all_to_all x1, starting transfers between devices, body(): lax.all_to_all(flat_resid, TM, split_axis=0, concat_axis=0, tiled=True)  23.5 us
    ppermute x6, starting transfers between devices, ring_gather(): lax.ppermute(x, axis, [(i, (i + shift) % size) for i in range(size)])  21.1 us
    psum x2, blocking collectives, group_moments(): both = lax.psum(lax.optimization_barrier(both), order[1])  17.4 us
    psum x2, blocking collectives, group_moments(): both = lax.psum(jnp.stack([sums, squares]), order[0])  14.8 us
    ppermute x2, starting transfers between devices, with_halo(): after = lax.ppermute(initial, axis, down)  7.05 us
    ppermute x6, waiting for transfers between devices, ring_gather(): lax.ppermute(x, axis, [(i, (i + shift) % size) for i in range(size)])  6.61 us
    dot_general x1, matrix products, body(): jnp.einsum('fpc,cd->fpd', flat_norm, qkv_full, preferred_element_type=jnp...  4.64 us
  transfers between devices with their start and end apart: 13, of which 7 were waited for; matrix products, arithmetic and copies ran while one was open for 3% of the time, Pallas kernels for 0%

profile of v13, /device:TPU:18, one launch (start us, length us, event | category | flops | bytes accessed | tf_op | source)
XLA Modules:
  0.0 196.6 jit_solution(4988583009457498089)
XLA Ops:
  0.0 0.9 fusion.72
  0.9 2.4 %collective-permute-start.3 = (bf16[16,2048]{1,0:T(8,128)(2,1)S(1)}, bf16[16,2048]{1,0:T(8,128)(2,1)S(1)}, u32[]{:S(2)}, u32[]{:S(2)}) collective-permute-start(bf16[16,2048]{1,0:T(8,128)(2,1)S(1)} %fusion.72), channel_id=1, source_target_pairs={{0,3},{1,0},{2,1},{3,2},{4,7},{5,4},{6,5},{7,6},{8,11},{9,8},{10,9... | collective-permute-start | bytes 196616 | tf_op jit(solution)/shard_map/ppermute | solution.py:41
  3.4 4.3 %collective-permute-start.4 = (bf16[16,2048]{1,0:T(8,128)(2,1)S(1)}, bf16[16,2048]{1,0:T(8,128)(2,1)S(1)}, u32[]{:S(2)}, u32[]{:S(2)}) collective-permute-start(bf16[16,2048]{1,0:T(8,128)(2,1)S(1)} %fusion.72), channel_id=1, source_target_pairs={{0,2},{1,3},{2,0},{3,1},{4,6},{5,7},{6,4},{7,5},{8,10},{9,11},{10,... | collective-permute-start | bytes 196616 | tf_op jit(solution)/shard_map/ppermute | solution.py:41
  7.7 3.7 %collective-permute-start.5 = (bf16[16,2048]{1,0:T(8,128)(2,1)S(1)}, bf16[16,2048]{1,0:T(8,128)(2,1)S(1)}, u32[]{:S(2)}, u32[]{:S(2)}) collective-permute-start(bf16[16,2048]{1,0:T(8,128)(2,1)S(1)} %fusion.72), channel_id=1, source_target_pairs={{0,1},{1,2},{2,3},{3,0},{4,5},{5,6},{6,7},{7,4},{8,9},{9,10},{10,1... | collective-permute-start | bytes 196616 | tf_op jit(solution)/shard_map/ppermute | solution.py:41
  11.4 1.5 convert_reduce_fusion
  13.4 8.0 %psum.28 = f32[2,4,32]{2,1,0:T(4,128)S(1)} all-reduce(f32[2,4,32]{2,1,0:T(4,128)S(1)} %pad_maximum_fusion.6), channel_id=1, replica_groups=mesh['z'=16,'core'=2,'band'=4,'fsdp'=4] {'fsdp'}, use_global_device_ids=true, to_apply=%region_6.7 | all-reduce | flops 256 | bytes 2048 | tf_op jit(solution)/shard_map/psum | solution.py:61
  21.3 10.2 %psum.29 = f32[2,4,32]{2,1,0:T(4,128)S(1)} all-reduce(f32[2,4,32]{2,1,0:T(4,128)S(1)} %psum.28), channel_id=1, replica_groups=mesh['z'=16,'core'=2,'band'=4,'fsdp'=4] {'band'}, use_global_device_ids=true, to_apply=%region_7.8 | all-reduce | flops 256 | bytes 2048 | tf_op jit(solution)/shard_map/psum | solution.py:62
  31.7 4.8 %collective-permute-start.6 = (bf16[64,2048]{1,0:T(8,128)(2,1)S(1)}, bf16[64,2048]{1,0:T(8,128)(2,1)S(1)}, u32[]{:S(2)}, u32[]{:S(2)}) collective-permute-start(bf16[64,2048]{1,0:T(8,128)(2,1)S(1)} %bitcast.174), channel_id=1, source_target_pairs={{0,12},{4,0},{8,4},{12,8},{1,13},{5,1},{9,5},{13,9},{2,14},{6,2},{... | collective-permute-start | bytes 786440 | tf_op jit(solution)/shard_map/ppermute | solution.py:41
  36.9 3.4 %collective-permute-start.7 = (bf16[64,2048]{1,0:T(8,128)(2,1)S(1)}, bf16[64,2048]{1,0:T(8,128)(2,1)S(1)}, u32[]{:S(2)}, u32[]{:S(2)}) collective-permute-start(bf16[64,2048]{1,0:T(8,128)(2,1)S(1)} %bitcast.175), channel_id=1, source_target_pairs={{0,8},{4,12},{8,0},{12,4},{1,9},{5,13},{9,1},{13,5},{2,10},{6,14},... | collective-permute-start | bytes 786440 | tf_op jit(solution)/shard_map/ppermute | solution.py:41
  40.3 2.5 %collective-permute-start.8 = (bf16[64,2048]{1,0:T(8,128)(2,1)S(1)}, bf16[64,2048]{1,0:T(8,128)(2,1)S(1)}, u32[]{:S(2)}, u32[]{:S(2)}) collective-permute-start(bf16[64,2048]{1,0:T(8,128)(2,1)S(1)} %bitcast.176), channel_id=1, source_target_pairs={{0,4},{4,8},{8,12},{12,0},{1,5},{5,9},{9,13},{13,1},{2,6},{6,10},{... | collective-permute-start | bytes 786440 | tf_op jit(solution)/shard_map/ppermute | solution.py:41
  42.8 3.9 %collective-permute-done.7 = bf16[64,2048]{1,0:T(8,128)(2,1)S(1)} collective-permute-done((bf16[64,2048]{1,0:T(8,128)(2,1)S(1)}, bf16[64,2048]{1,0:T(8,128)(2,1)S(1)}, u32[]{:S(2)}, u32[]{:S(2)}) %collective-permute-start.7) | collective-permute-done | bytes 262176 | tf_op jit(solution)/shard_map/ppermute | solution.py:41
  46.8 2.7 %collective-permute-done.8 = bf16[64,2048]{1,0:T(8,128)(2,1)S(1)} collective-permute-done((bf16[64,2048]{1,0:T(8,128)(2,1)S(1)}, bf16[64,2048]{1,0:T(8,128)(2,1)S(1)}, u32[]{:S(2)}, u32[]{:S(2)}) %collective-permute-start.8) | collective-permute-done | bytes 262176 | tf_op jit(solution)/shard_map/ppermute | solution.py:41
  49.7 2.1 %collective-permute-start.9 = (bf16[256,2048]{1,0:T(8,128)(2,1)S(1)}, bf16[256,2048]{1,0:T(8,128)(2,1)}, u32[]{:S(2)}, u32[]{:S(2)}) collective-permute-start(bf16[256,2048]{1,0:T(8,128)(2,1)S(1)} %bitcast.171), channel_id=1, source_target_pairs={{0,16},{16,0},{1,17},{17,1},{2,18},{18,2},{3,19},{19,3},{4,20},{20... | collective-permute-start | bytes 3145736 | tf_op jit(solution)/shard_map/ppermute | solution.py:88
  51.8 0.7 fusion.16
  52.5 1.9 collective-permute-start
  54.4 3.9 %collective-permute-start.1 = (bf16[4,1,32,256]{3,2,1,0:T(8,128)(2,1)S(1)}, bf16[4,1,32,256]{3,2,1,0:T(8,128)(2,1)S(1)}, u32[]{:S(2)}, u32[]{:S(2)}) collective-permute-start(bf16[4,1,32,256]{3,2,1,0:T(8,128)(2,1)S(1)} %get-tuple-element.16), channel_id=1, source_target_pairs={{4,0},{8,4},{12,8},{5,1},{9,5},{13,9},{6,2},{10,6},{14,10},{7,3},{... | collective-permute-start | bytes 196616 | tf_op jit(solution)/shard_map/ppermute | solution.py:25
  58.3 0.5 collective-permute-done
  58.9 1.9 collective-permute-done.1
  60.9 3.1 %collective-permute-start.10 = (bf16[4,18,1,256]{3,2,1,0:T(2,128)(2,1)S(1)}, bf16[4,18,1,256]{3,2,1,0:T(2,128)(2,1)S(1)}, u32[]{:S(2)}, u32[]{:S(2)}) collective-permute-start(bf16[4,18,1,256]{3,2,1,0:T(2,128)(2,1)S(1)} %get-tuple-element.13), channel_id=1, source_target_pairs={{1,0},{2,1},{3,2},{5,4},{6,5},{7,6},{9,8},{10,9},{11,10},{13,12},{... | collective-permute-start | bytes 110600 | tf_op jit(solution)/shard_map/ppermute | solution.py:25
  64.1 2.7 %collective-permute-start.2 = (bf16[4,18,1,256]{3,2,1,0:T(2,128)(2,1)S(1)}, bf16[4,18,1,256]{3,2,1,0:T(2,128)(2,1)}, u32[]{:S(2)}, u32[]{:S(2)}) collective-permute-start(bf16[4,18,1,256]{3,2,1,0:T(2,128)(2,1)S(1)} %get-tuple-element.14), channel_id=1, source_target_pairs={{0,1},{1,2},{2,3},{4,5},{5,6},{6,7},{8,9},{9,10},{10,11},{12,13},{... | collective-permute-start | bytes 110600 | tf_op jit(solution)/shard_map/ppermute | solution.py:24
  67.2 3.2 %collective-permute-done.2 = bf16[4,18,1,256]{3,2,1,0:T(2,128)(2,1)} collective-permute-done((bf16[4,18,1,256]{3,2,1,0:T(2,128)(2,1)S(1)}, bf16[4,18,1,256]{3,2,1,0:T(2,128)(2,1)}, u32[]{:S(2)}, u32[]{:S(2)}) %collective-permute-start.2) | collective-permute-done | bytes 36896 | tf_op jit(solution)/shard_map/ppermute | solution.py:24
  70.4 1.6 pad_maximum_fusion.2
  72.0 1.6 pad_maximum_fusion
  74.2 0.4 fusion.53
  74.6 0.5 fusion.55
  75.1 0.5 fusion.51
  75.5 0.4 fusion.49
  76.0 0.4 fusion.69
  77.3 1.1 add_convert_fusion
  78.4 0.8 slice.202
  79.2 2.1 %collective-permute-start.11 = (bf16[2,16,32,256]{3,2,1,0:T(8,128)(2,1)}, bf16[2,16,32,256]{3,2,1,0:T(8,128)(2,1)}, u32[]{:S(2)}, u32[]{:S(2)}) collective-permute-start(bf16[2,16,32,256]{3,2,1,0:T(8,128)(2,1)} %slice.202), channel_id=1, source_target_pairs={{0,16},{16,32},{32,48},{48,64},{64,80},{80,96},{96,112},{112,128},... | collective-permute-start | bytes 1572872 | tf_op jit(solution)/shard_map/ppermute | solution.py:33
  81.7 0.6 collective-permute-done.11
  82.3 1.2 pad_maximum_fusion.1
  83.5 1.2 fusion.22
  84.7 0.4 fusion.60
  85.2 1.2 fusion.19
  86.4 0.4 fusion.62
  86.8 1.2 fusion.25
  88.0 0.9 convert_reduce_fusion.1
  88.9 1.1 copy.100
  90.0 23.5 %all-to-all-start = ((bf16[32,4,16,256]{3,2,1,0:T(8,128)(2,1)}), bf16[32,4,16,256]{3,2,1,0:T(8,128)(2,1)S(1)}, u32[]{:S(2)}, u32[]{:S(2)}) async-start(bf16[32,4,16,256]{3,2,1,0:T(8,128)(2,1)} %bitcast.168), calls=%async_computation | async-start | bytes 2097152 | tf_op jit(solution)/shard_map/all_to_all | solution.py:139
  114.0 6.8 %psum.30 = f32[2,4,32]{2,1,0:T(4,128)S(1)} all-reduce(f32[2,4,32]{2,1,0:T(4,128)S(1)} %pad_maximum_fusion.7), channel_id=1, replica_groups=mesh['z'=16,'core'=2,'band'=4,'fsdp'=4] {'band'}, use_global_device_ids=true, to_apply=%region_12.13 | all-reduce | flops 256 | bytes 2048 | tf_op jit(solution)/shard_map/psum | solution.py:61
  120.8 7.3 %psum.31 = f32[2,4,32]{2,1,0:T(4,128)S(1)} all-reduce(f32[2,4,32]{2,1,0:T(4,128)S(1)} %psum.30), channel_id=1, replica_groups=mesh['z'=16,'core'=2,'band'=4,'fsdp'=4] {'fsdp'}, use_global_device_ids=true, to_apply=%region_13.14 | all-reduce | flops 256 | bytes 2048 | tf_op jit(solution)/shard_map/psum | solution.py:62
  128.2 1.8 all-gather
  130.0 55.1 %all_gather.7 = f32[128,64]{1,0:T(8,128)S(1)} all-gather(f32[8,64]{1,0:T(8,128)S(1)} %bitcast.179), channel_id=1, replica_groups=mesh['z'=16,'core'=2,'band'=4,'fsdp'=4] {'z'}, dimensions={0}, use_global_device_ids=true | all-gather | bytes 34816 | tf_op jit(solution)/shard_map/all_gather | solution.py:144
  185.9 4.6 %convolution_convert_fusion = bf16[128,16,768]{2,0,1:T(8,128)(2,1)} fusion(f32[128,16,256]{2,1,0:T(8,128)S(1)} %bitcast_convert_fusion, f32[256]{0:T(256)S(1)} %bitcast.184, f32[128,256]{1,0:T(8,128)S(1)} %copy.55, f32[128,256]{1,0:T(8,128)S(1)} %copy.53, bf16[256,2048]{1,0:T(8,128)(2,1)} %copy-done.1), kind=kOutput, calls=%fused_computation.8 | convolution fusion | flops 808976384 | bytes 5899264 | tf_op jit(solution)/shard_map/fpc,cd->fpd/dot_general | solution.py:147
  190.6 2.1 %fusion.98 = (f32[16,128]{1,0:T(8,128)S(1)}, f32[16,128,128]{1,2,0:T(8,128)S(1)}) fusion(pred[128,128]{0,1:T(8,128)(4,1)S(1)} %fusion.73, bf16[128,16,768]{2,0,1:T(8,128)(2,1)} %convolution_convert_fusion), kind=kOutput, calls=%fused_computation.165 | convolution fusion | flops 135528576 | bytes 3186688 | tf_op jit(solution)/shard_map/sub | solution.py:160
  192.7 3.9 %fusion.31 = bf16[1,1,16,128,256]{4,3,2,1,0:T(8,128)(2,1)} fusion(f32[128,16,256]{2,1,0:T(8,128)S(1)} %bitcast_convert_fusion, bf16[128,16,768]{2,0,1:T(8,128)(2,1)} %convolution_convert_fusion, f32[16,128,128]{1,2,0:T(8,128)S(1)} %get-tuple-element.26, f32[16,128]{1,0:T(8,128)S(1)} %get-tuple-element.25, bf16[256,2048]{1,0:T(8,128)(2,1)} %copy-done.1), kind=kOutput, calls=%fused_computation.40 | convolution fusion | flops 404750336 | bytes 5382144 | tf_op jit(solution)/shard_map/axi,iy->axy/dot_general | solution.py:165
  (74 shorter events, 4.8 us)
Async XLA Ops:
  0.0 36.8 %copy-start.2 = (f32[2,256]{1,0:T(2,128)S(1)}, f32[2,256]{1,0:T(2,128)}, u32[]{:S(2)}) copy-start(f32[2,256]{1,0:T(2,128)} %param.9) | copy-start | bytes 6148
  0.9 30.6 %collective-permute-start.3 = (bf16[16,2048]{1,0:T(8,128)(2,1)S(1)}, bf16[16,2048]{1,0:T(8,128)(2,1)S(1)}, u32[]{:S(2)}, u32[]{:S(2)}) collective-permute-start(bf16[16,2048]{1,0:T(8,128)(2,1)S(1)} %fusion.72), channel_id=1, source_target_pairs={{0,3},{1,0},{2,1},{3,2},{4,7},{5,4},{6,5},{7,6},{8,11},{9,8},{10,9... | collective-permute-start | bytes 196616 | tf_op jit(solution)/shard_map/ppermute | solution.py:41
  3.4 28.1 %collective-permute-start.4 = (bf16[16,2048]{1,0:T(8,128)(2,1)S(1)}, bf16[16,2048]{1,0:T(8,128)(2,1)S(1)}, u32[]{:S(2)}, u32[]{:S(2)}) collective-permute-start(bf16[16,2048]{1,0:T(8,128)(2,1)S(1)} %fusion.72), channel_id=1, source_target_pairs={{0,2},{1,3},{2,0},{3,1},{4,6},{5,7},{6,4},{7,5},{8,10},{9,11},{10,... | collective-permute-start | bytes 196616 | tf_op jit(solution)/shard_map/ppermute | solution.py:41
  7.7 23.8 %collective-permute-start.5 = (bf16[16,2048]{1,0:T(8,128)(2,1)S(1)}, bf16[16,2048]{1,0:T(8,128)(2,1)S(1)}, u32[]{:S(2)}, u32[]{:S(2)}) collective-permute-start(bf16[16,2048]{1,0:T(8,128)(2,1)S(1)} %fusion.72), channel_id=1, source_target_pairs={{0,1},{1,2},{2,3},{3,0},{4,5},{5,6},{6,7},{7,4},{8,9},{9,10},{10,1... | collective-permute-start | bytes 196616 | tf_op jit(solution)/shard_map/ppermute | solution.py:41
  31.7 11.1 %collective-permute-start.6 = (bf16[64,2048]{1,0:T(8,128)(2,1)S(1)}, bf16[64,2048]{1,0:T(8,128)(2,1)S(1)}, u32[]{:S(2)}, u32[]{:S(2)}) collective-permute-start(bf16[64,2048]{1,0:T(8,128)(2,1)S(1)} %bitcast.174), channel_id=1, source_target_pairs={{0,12},{4,0},{8,4},{12,8},{1,13},{5,1},{9,5},{13,9},{2,14},{6,2},{... | collective-permute-start | bytes 786440 | tf_op jit(solution)/shard_map/ppermute | solution.py:41
  36.9 9.9 %collective-permute-start.7 = (bf16[64,2048]{1,0:T(8,128)(2,1)S(1)}, bf16[64,2048]{1,0:T(8,128)(2,1)S(1)}, u32[]{:S(2)}, u32[]{:S(2)}) collective-permute-start(bf16[64,2048]{1,0:T(8,128)(2,1)S(1)} %bitcast.175), channel_id=1, source_target_pairs={{0,8},{4,12},{8,0},{12,4},{1,9},{5,13},{9,1},{13,5},{2,10},{6,14},... | collective-permute-start | bytes 786440 | tf_op jit(solution)/shard_map/ppermute | solution.py:41
  40.3 9.2 %collective-permute-start.8 = (bf16[64,2048]{1,0:T(8,128)(2,1)S(1)}, bf16[64,2048]{1,0:T(8,128)(2,1)S(1)}, u32[]{:S(2)}, u32[]{:S(2)}) collective-permute-start(bf16[64,2048]{1,0:T(8,128)(2,1)S(1)} %bitcast.176), channel_id=1, source_target_pairs={{0,4},{4,8},{8,12},{12,0},{1,5},{5,9},{9,13},{13,1},{2,6},{6,10},{... | collective-permute-start | bytes 786440 | tf_op jit(solution)/shard_map/ppermute | solution.py:41
  49.5 2.3 %copy-start = (bf16[4,16,32,256]{3,2,1,0:T(8,128)(2,1)S(1)}, bf16[4,16,32,256]{3,2,1,0:T(8,128)(2,1)}, u32[]{:S(2)}) copy-start(bf16[4,16,32,256]{3,2,1,0:T(8,128)(2,1)} %param.7) | copy-start | bytes 3145732
  49.7 22.3 %collective-permute-start.9 = (bf16[256,2048]{1,0:T(8,128)(2,1)S(1)}, bf16[256,2048]{1,0:T(8,128)(2,1)}, u32[]{:S(2)}, u32[]{:S(2)}) collective-permute-start(bf16[256,2048]{1,0:T(8,128)(2,1)S(1)} %bitcast.171), channel_id=1, source_target_pairs={{0,16},{16,0},{1,17},{17,1},{2,18},{18,2},{3,19},{19,3},{4,20},{20... | collective-permute-start | bytes 3145736 | tf_op jit(solution)/shard_map/ppermute | solution.py:88
  52.5 6.4 %collective-permute-start = (bf16[4,1,32,256]{3,2,1,0:T(8,128)(2,1)S(1)}, bf16[4,1,32,256]{3,2,1,0:T(8,128)(2,1)S(1)}, u32[]{:S(2)}, u32[]{:S(2)}) collective-permute-start(bf16[4,1,32,256]{3,2,1,0:T(8,128)(2,1)S(1)} %get-tuple-element.15), channel_id=1, source_target_pairs={{0,4},{4,8},{8,12},{1,5},{5,9},{9,13},{2,6},{6,10},{10,14},{3,7},{... | collective-permute-start | bytes 196616 | tf_op jit(solution)/shard_map/ppermute | solution.py:24
  54.4 6.4 %collective-permute-start.1 = (bf16[4,1,32,256]{3,2,1,0:T(8,128)(2,1)S(1)}, bf16[4,1,32,256]{3,2,1,0:T(8,128)(2,1)S(1)}, u32[]{:S(2)}, u32[]{:S(2)}) collective-permute-start(bf16[4,1,32,256]{3,2,1,0:T(8,128)(2,1)S(1)} %get-tuple-element.16), channel_id=1, source_target_pairs={{4,0},{8,4},{12,8},{5,1},{9,5},{13,9},{6,2},{10,6},{14,10},{7,3},{... | collective-permute-start | bytes 196616 | tf_op jit(solution)/shard_map/ppermute | solution.py:25
  60.9 6.2 %collective-permute-start.10 = (bf16[4,18,1,256]{3,2,1,0:T(2,128)(2,1)S(1)}, bf16[4,18,1,256]{3,2,1,0:T(2,128)(2,1)S(1)}, u32[]{:S(2)}, u32[]{:S(2)}) collective-permute-start(bf16[4,18,1,256]{3,2,1,0:T(2,128)(2,1)S(1)} %get-tuple-element.13), channel_id=1, source_target_pairs={{1,0},{2,1},{3,2},{5,4},{6,5},{7,6},{9,8},{10,9},{11,10},{13,12},{... | collective-permute-start | bytes 110600 | tf_op jit(solution)/shard_map/ppermute | solution.py:25
  64.1 6.4 %collective-permute-start.2 = (bf16[4,18,1,256]{3,2,1,0:T(2,128)(2,1)S(1)}, bf16[4,18,1,256]{3,2,1,0:T(2,128)(2,1)}, u32[]{:S(2)}, u32[]{:S(2)}) collective-permute-start(bf16[4,18,1,256]{3,2,1,0:T(2,128)(2,1)S(1)} %get-tuple-element.14), channel_id=1, source_target_pairs={{0,1},{1,2},{2,3},{4,5},{5,6},{6,7},{8,9},{9,10},{10,11},{12,13},{... | collective-permute-start | bytes 110600 | tf_op jit(solution)/shard_map/ppermute | solution.py:24
  73.8 14.2 %copy-start.1 = (bf16[256,2048]{1,0:T(8,128)(2,1)}, bf16[256,2048]{1,0:T(8,128)(2,1)S(1)}, u32[]{:S(2)}) copy-start(bf16[256,2048]{1,0:T(8,128)(2,1)S(1)} %get-tuple-element.9) | copy-start | bytes 3145732
  77.3 4.0 %copy-start.3 = (s32[16]{0:T(128)S(1)}, s32[16]{0:T(128)}, u32[]{:S(2)}) copy-start(s32[16]{0:T(128)} %param.8) | copy-start | bytes 196
  79.2 3.1 %collective-permute-start.11 = (bf16[2,16,32,256]{3,2,1,0:T(8,128)(2,1)}, bf16[2,16,32,256]{3,2,1,0:T(8,128)(2,1)}, u32[]{:S(2)}, u32[]{:S(2)}) collective-permute-start(bf16[2,16,32,256]{3,2,1,0:T(8,128)(2,1)} %slice.202), channel_id=1, source_target_pairs={{0,16},{16,32},{32,48},{48,64},{64,80},{80,96},{96,112},{112,128},... | collective-permute-start | bytes 1572872 | tf_op jit(solution)/shard_map/ppermute | solution.py:33
  90.0 95.5 %all-to-all-start = ((bf16[32,4,16,256]{3,2,1,0:T(8,128)(2,1)}), bf16[32,4,16,256]{3,2,1,0:T(8,128)(2,1)S(1)}, u32[]{:S(2)}, u32[]{:S(2)}) async-start(bf16[32,4,16,256]{3,2,1,0:T(8,128)(2,1)} %bitcast.168), calls=%async_computation | async-start | bytes 2097152 | tf_op jit(solution)/shard_map/all_to_all | solution.py:139
